TPU v7x, 256 devices: a whole 4x4x8 slice. The times are simulated.
256 devices in a mesh: dp: 4 (over y), seq: 64 (over z, x, core).
Axes of the slice: x: 4, y: 4, z: 8, core: 2. Of those that a mesh axis runs over, the one named last changes fastest.
Arguments:
- features: bfloat16 [49152, 1408], P(('dp', 'seq')), parts along dimension 0, may hold values from -6 to 6
- norm_gain: float32 [1408], replicated, may hold values from 0.1 to 1.9
- conv_weight: bfloat16 [5, 1408, 1536], P(None, None, 'seq'), may hold values from -0.0625 to 0.0625
- conv_bias: float32 [1536], replicated, may hold values from -3 to 3
- attn_gain: float32 [1536], replicated, may hold values from 0.1 to 1.9
- query_weight: bfloat16 [1536, 1024], P('seq'), may hold values from -1 to 1
- keyval_weight: bfloat16 [1536, 256], P('seq'), may hold values from -1 to 1
- head_scale: float32 [8], replicated, may hold values from 1 to 4
- output_weight: bfloat16 [1024, 1536], P('seq'), may hold values from -0.1875 to 0.1875
Outputs:
- coarse: bfloat16 [24576, 1536], P(('dp', 'seq')), parts along dimension 0
- attended: bfloat16 [24576, 1536], P(('dp', 'seq')), parts along dimension 0
There are 4 independent parts, one for each index of `dp`. A program takes and returns all parts, laid end to end along the dimension named above; an argument that names none is the same for every part. Nothing has to cross between parts.
All inputs are finite; a program needn't handle non-finite values.
Results may differ from a plain program's by a relative error of at most 0.007.
Values may be sent and summed in bfloat16 or wider, within the bound.
No kernel may reach another device: no remote copies, remote signals or barrier semaphores. Data moves between devices by JAX's collectives and lax.ppermute only.
A program may use at most 128 MiB of HBM per device.

v0:
```python
import jax
import jax.numpy as jnp
from jax import lax
from jax.sharding import PartitionSpec as P

HEAD_DIM = 128


def with_halo(block, sides, width):
    for axis, dim in sides:
        count = lax.axis_size(axis)
        forward = [(i, i + 1) for i in range(count - 1)]
        backward = [(target, source) for source, target in forward]
        low = lax.ppermute(
            lax.slice_in_dim(block, block.shape[dim] - width, None, axis=dim), axis, forward
        )
        high = lax.ppermute(lax.slice_in_dim(block, 0, width, axis=dim), axis, backward)
        block = jnp.concatenate([low, block, high], axis=dim)
    return block


def normalize(values_in, channel_gain):
    meansq = jnp.mean(values_in * values_in, axis=-1, keepdims=True)
    return values_in * lax.rsqrt(meansq + 1e-06) * channel_gain


def convolve(padded, kernel, row_count):
    summed = jnp.zeros((row_count, kernel.shape[2]), jnp.float32)
    for kernel_tap in range(kernel.shape[0]):
        summed = summed + jnp.dot(
            padded[kernel_tap : kernel_tap + row_count],
            kernel[kernel_tap],
            preferred_element_type=jnp.float32,
        )
    return summed


def pool_pairs(levels):
    return jnp.max(levels.reshape(-1, 2, levels.shape[1]), axis=1)


def attend(queries, keyvals, scales):
    row_count = queries.shape[0]
    head_count = scales.shape[0]
    shaped = queries.reshape(row_count, head_count, HEAD_DIM)
    key_block = lax.all_gather(keyvals, "seq", axis=0, tiled=True)
    running_max = jnp.full((head_count, row_count), -1e30, jnp.float32)
    key_part = key_block[:, :HEAD_DIM]
    value_part = key_block[:, HEAD_DIM:]
    scores = (
        jnp.einsum("qhd,kd->hqk", shaped, key_part, preferred_element_type=jnp.float32)
        * scales[:, None, None]
        * HEAD_DIM ** (-0.5)
    )
    newest = jnp.maximum(running_max, jnp.max(scores, axis=2))
    expon = jnp.exp(scores - newest[:, :, None])
    running_sum = jnp.sum(expon, axis=2)
    running_ctx = jnp.einsum(
        "hqk,kd->hqd", expon.astype(jnp.bfloat16), value_part, preferred_element_type=jnp.float32
    )
    context = running_ctx / running_sum[:, :, None]
    return context.transpose(1, 0, 2).reshape(row_count, head_count * HEAD_DIM).astype(jnp.bfloat16)


def shards(
    features,
    norm_gain,
    conv_weight,
    conv_bias,
    attn_gain,
    query_weight,
    keyval_weight,
    head_scale,
    output_weight,
):
    normed = jax.nn.gelu(normalize(features.astype(jnp.float32), norm_gain)).astype(jnp.bfloat16)
    fine_rows = normed.shape[0]
    padded = with_halo(normed, (("seq", 0),), 2)
    levels = (
        convolve(padded, lax.all_gather(conv_weight, "seq", axis=2, tiled=True), fine_rows)
        + conv_bias[None, :]
    )
    coarse = pool_pairs(levels).astype(jnp.bfloat16)
    attn_in = normalize(coarse.astype(jnp.float32), attn_gain).astype(jnp.bfloat16)
    columns = attn_in
    query_sum = jnp.dot(
        columns,
        lax.all_gather(query_weight, "seq", axis=0, tiled=True),
        preferred_element_type=jnp.float32,
    )
    keyval_sum = jnp.dot(
        columns,
        lax.all_gather(keyval_weight, "seq", axis=0, tiled=True),
        preferred_element_type=jnp.float32,
    )
    queries = query_sum.astype(jnp.bfloat16)
    keyvals = keyval_sum.astype(jnp.bfloat16)
    context = attend(queries, keyvals, head_scale)
    columns = context
    projected = jnp.dot(
        columns,
        lax.all_gather(output_weight, "seq", axis=0, tiled=True),
        preferred_element_type=jnp.float32,
    )
    return (coarse, projected.astype(jnp.bfloat16))


def solution(mesh):
    return jax.shard_map(
        shards,
        mesh=mesh,
        in_specs=(
            P(("dp", "seq"), None),
            P(),
            P(None, None, "seq"),
            P(),
            P(),
            P("seq", None),
            P("seq", None),
            P(),
            P("seq", None),
        ),
        out_specs=(P(("dp", "seq"), None), P(("dp", "seq"), None)),
        check_vma=False,
    )
```

profile of v0, /device:TPU:1, one launch (start us, length us, event | category | flops | bytes accessed | tf_op | source)
XLA Modules:
  0.0 370.9 jit_solution(2090418662259818749)
XLA Ops:
  7.2 0.7 all-gather.5.cloned.1.call-update
  7.9 0.7 all-gather.9.cloned.1.call-update
  8.7 1.2 fusion.20
  9.9 1.6 fusion.24
  11.5 5.1 %collective-permute-start.1 = (bf16[2,1408]{1,0:T(2,128)(2,1)S(1)}, bf16[2,1408]{1,0:T(2,128)(2,1)S(1)}, u32[]{:S(2)}, u32[]{:S(2)}) collective-permute-start(bf16[2,1408]{1,0:T(2,128)(2,1)S(1)} %get-tuple-element.3), channel_id=1, source_target_pairs={{1,0},{2,1},{3,2},{4,3},{5,4},{6,5},{7,6},{8,7},{9,8},{10,9},{11,1... | collective-permute-start | bytes 16904 | tf_op jit(solution)/shard_map/ppermute | solution.py:17
  16.6 1.9 collective-permute-start
  18.6 54.5 %all_gather.16 = bf16[1536,256]{1,0:T(8,128)(2,1)S(1)} all-gather(bf16[24,256]{1,0:T(8,128)(2,1)} %param.15), channel_id=1, replica_groups=mesh['dp'=4,'seq'=64] {'seq'}, dimensions={0}, use_global_device_ids=true | all-gather | bytes 798720 | tf_op jit(solution)/shard_map/all_gather | solution.py:93
  73.1 53.4 %all-gather.5.cloned.1.call-done = bf16[5,1408,1536]{1,2,0:T(8,128)(2,1)} async-done(((bf16[5,1408,24]{1,2,0:T(8,128)(2,1)}), bf16[5,1408,1536]{1,2,0:T(8,128)(2,1)}) %all-gather.5.cloned.1.call-update) | async-done | bytes 21626896 | tf_op jit(solution)/shard_map/all_gather | solution.py:80
  126.6 3.8 %fusion.8 = f32[192,1536]{1,0:T(8,128)S(1)} fusion(bf16[5,1408,1536]{1,2,0:T(8,128)(2,1)} %all-gather.5.cloned.1.call-done, bf16[192,1408]{1,0:T(8,128)(2,1)S(1)} %fusion.24, bf16[2,1408]{1,0:T(2,128)(2,1)S(1)} %collective-permute-done), kind=kOutput, calls=%fused_computation.14 | convolution fusion | flops 831553536 | bytes 6051328 | tf_op jit(solution)/shard_map/dot_general | solution.py:30
  130.4 3.8 %fusion.5 = f32[192,1536]{1,0:T(8,128)S(1)} fusion(bf16[5,1408,1536]{1,2,0:T(8,128)(2,1)} %all-gather.5.cloned.1.call-done, bf16[2,1408]{1,0:T(2,128)(2,1)S(1)} %collective-permute-done.1, bf16[192,1408]{1,0:T(8,128)(2,1)S(1)} %fusion.24), kind=kOutput, calls=%fused_computation.8 | convolution fusion | flops 831553536 | bytes 6051328 | tf_op jit(solution)/shard_map/dot_general | solution.py:30
  134.2 3.8 %fusion.7 = f32[192,1536]{1,0:T(8,128)S(1)} fusion(bf16[192,1408]{1,0:T(8,128)(2,1)S(1)} %fusion.24, bf16[5,1408,1536]{1,2,0:T(8,128)(2,1)} %all-gather.5.cloned.1.call-done), kind=kOutput, calls=%fused_computation.12 | convolution fusion | flops 830472192 | bytes 6045696 | tf_op jit(solution)/shard_map/dot_general | solution.py:30
  138.0 3.8 %fusion.6 = f32[192,1536]{1,0:T(8,128)S(1)} fusion(bf16[5,1408,1536]{1,2,0:T(8,128)(2,1)} %all-gather.5.cloned.1.call-done, bf16[192,1408]{1,0:T(8,128)(2,1)S(1)} %fusion.24, bf16[2,1408]{1,0:T(2,128)(2,1)S(1)} %collective-permute-done.1), kind=kOutput, calls=%fused_computation.10 | convolution fusion | flops 831553536 | bytes 6051328 | tf_op jit(solution)/shard_map/dot_general | solution.py:30
  141.9 3.9 %fusion.14 = bf16[192,1536]{1,0:T(8,128)(2,1)S(1)} fusion(f32[192,1536]{1,0:T(8,128)S(1)} %fusion.5, f32[192,1536]{1,0:T(8,128)S(1)} %fusion.6, f32[192,1536]{1,0:T(8,128)S(1)} %fusion.7, f32[192,1536]{1,0:T(8,128)S(1)} %fusion.8, bf16[5,1408,1536]{1,2,0:T(8,128)(2,1)} %all-gather.5.cloned.1.call-done, f32[1536]{0:T(1024)S(1)} %copy-done.4, ...), kind=kOutput, calls=%fused_computation.21 | convolution fusion | flops 833323008 | bytes 10186240 | tf_op jit(solution)/shard_map/dot_general | solution.py:30
  146.1 1.6 reduce_max.18
  147.9 0.9 convolution_convert_fusion.2
  149.0 0.3 all-gather.11.cloned.1.call-update
  149.4 54.9 %all-gather.9.cloned.1.call-done = bf16[1536,1024]{1,0:T(8,128)(2,1)} async-done(((bf16[24,1024]{1,0:T(8,128)(2,1)}), bf16[1536,1024]{1,0:T(8,128)(2,1)}) %all-gather.9.cloned.1.call-update) | async-done | bytes 3145744 | tf_op jit(solution)/shard_map/all_gather | solution.py:88
  204.3 2.6 fusion.19
  206.8 76.2 %all-gather.7.cloned.1.call-done = bf16[6144,256]{1,0:T(8,128)(2,1)} async-done(((bf16[96,256]{1,0:T(8,128)(2,1)}), bf16[6144,256]{1,0:T(8,128)(2,1)}) %all-gather.7.cloned.1.call-update) | async-done | bytes 3145744 | tf_op jit(solution)/shard_map/all_gather | solution.py:46
  283.1 9.3 %bitcast_reduce_fusion = (f32[8,96]{1,0:T(8,128)S(1)}, f32[6144,96,8]{0,1,2:T(8,128)}) fusion(f32[8]{0:T(128)S(1)} %copy-done.2, bf16[12,8,8,128]{3,2,1,0:T(8,128)(2,1)S(1)} %fusion.19, bf16[6144,256]{1,0:T(8,128)(2,1)} %all-gather.7.cloned.1.call-done), kind=kOutput, calls=%fused_computation.1 | convolution fusion | flops 1222114560 | bytes 20646944 | tf_op jit(solution)/shard_map/qhd,kd->hqk/dot_general | solution.py:51
  292.3 10.4 %fusion.1 = f32[8,96]{1,0:T(8,128)S(1)} fusion(f32[6144,96,8]{0,1,2:T(8,128)} %get-tuple-element.5, f32[8,96]{1,0:T(8,128)S(1)} %broadcast_maximum_fusion, f32[8]{0:T(128)S(1)} %copy-done.2), kind=kLoop, calls=%fused_computation.4 | loop fusion | flops 18873600 | bytes 18880544 | tf_op jit(solution)/shard_map/reduce_sum | solution.py:57
  302.7 8.5 %fusion.36 = bf16[8,12,8,128]{3,2,1,0:T(8,128)(2,1)S(1)} fusion(bf16[6144,256]{1,0:T(8,128)(2,1)S(1)} %copy-done.1, f32[6144,96,8]{0,1,2:T(8,128)} %get-tuple-element.5, f32[8,96]{1,0:T(8,128)S(1)} %broadcast_maximum_fusion, f32[8]{0:T(128)S(1)} %copy-done.2, f32[96,8]{0,1:T(8,128)S(1)} %bitcast.84), kind=kOutput, calls=%fused_computation.45 | convolution fusion | flops 1227030528 | bytes 20652544 | tf_op jit(solution)/shard_map/hqk,kd->hqd/dot_general | solution.py:58
  311.2 49.9 %all-gather.11.cloned.1.call-done = bf16[1024,1536]{1,0:T(8,128)(2,1)} async-done(((bf16[16,1536]{1,0:T(8,128)(2,1)}), bf16[1024,1536]{1,0:T(8,128)(2,1)}) %all-gather.11.cloned.1.call-update) | async-done | bytes 3145744 | tf_op jit(solution)/shard_map/all_gather | solution.py:102
  361.1 3.2 convolution_convert_fusion
  (23 shorter events, 0.8 us)
Async XLA Ops:
  7.2 119.4 %all-gather.5.cloned.1.call-start = ((), (), s32[]{:S(2)}) async-start(), calls=%async_computation | async-start | bytes 21964800 | tf_op jit(solution)/shard_map/all_gather | solution.py:80
  7.9 196.4 %all-gather.9.cloned.1.call-start = ((), (), s32[]{:S(2)}) async-start(), calls=%async_computation.2 | async-start | bytes 3194880 | tf_op jit(solution)/shard_map/all_gather | solution.py:88
  8.6 274.4 %all-gather.7.cloned.1.call-start = ((), (), s32[]{:S(2)}) async-start(), calls=%async_computation.1 | async-start | bytes 3194880 | tf_op jit(solution)/shard_map/all_gather | solution.py:46
  11.5 118.9 %collective-permute-start.1 = (bf16[2,1408]{1,0:T(2,128)(2,1)S(1)}, bf16[2,1408]{1,0:T(2,128)(2,1)S(1)}, u32[]{:S(2)}, u32[]{:S(2)}) collective-permute-start(bf16[2,1408]{1,0:T(2,128)(2,1)S(1)} %get-tuple-element.3), channel_id=1, source_target_pairs={{1,0},{2,1},{3,2},{4,3},{5,4},{6,5},{7,6},{8,7},{9,8},{10,9},{11,1... | collective-permute-start | bytes 16904 | tf_op jit(solution)/shard_map/ppermute | solution.py:17
  16.6 56.5 %collective-permute-start = (bf16[2,1408]{1,0:T(2,128)(2,1)S(1)}, bf16[2,1408]{1,0:T(2,128)(2,1)S(1)}, u32[]{:S(2)}, u32[]{:S(2)}) collective-permute-start(bf16[2,1408]{1,0:T(2,128)(2,1)S(1)} %get-tuple-element.2), channel_id=1, source_target_pairs={{0,1},{1,2},{2,3},{3,4},{4,5},{5,6},{6,7},{7,8},{8,9},{9,10},{10,1... | collective-permute-start | bytes 16904 | tf_op jit(solution)/shard_map/ppermute | solution.py:14
  138.0 3.9 %copy-start.4 = (f32[1536]{0:T(1024)S(1)}, f32[1536]{0:T(1024)}, u32[]{:S(2)}) copy-start(f32[1536]{0:T(1024)} %param.12) | copy-start | bytes 18436
  141.9 6.0 %copy-start.3 = (f32[1536]{0:T(1024)S(1)}, f32[1536]{0:T(1024)}, u32[]{:S(2)}) copy-start(f32[1536]{0:T(1024)} %param.13) | copy-start | bytes 18436
  146.1 137.0 %copy-start.2 = (f32[8]{0:T(128)S(1)}, f32[8]{0:T(128)}, u32[]{:S(2)}) copy-start(f32[8]{0:T(128)} %param.16) | copy-start | bytes 100
  147.7 144.7 %copy-start = (bf16[96,1536]{1,0:T(8,128)(2,1)}, bf16[96,1536]{1,0:T(8,128)(2,1)S(1)}, u32[]{:S(2)}) copy-start(bf16[96,1536]{1,0:T(8,128)(2,1)S(1)} %reduce_max.18) | copy-start | bytes 884740
  148.8 212.3 %all-gather.11.cloned.1.call-start = ((), (), s32[]{:S(2)}) async-start(), calls=%async_computation.3 | async-start | bytes 3194880 | tf_op jit(solution)/shard_map/all_gather | solution.py:102
  292.3 10.4 %copy-start.1 = (bf16[6144,256]{1,0:T(8,128)(2,1)S(1)}, bf16[6144,256]{1,0:T(8,128)(2,1)}, u32[]{:S(2)}) copy-start(bf16[6144,256]{1,0:T(8,128)(2,1)} %all-gather.7.cloned.1.call-done) | copy-start | bytes 9437188
Sparse Core Ops, SparseCore 0:
  10.7 115.8 all-gather.4
  129.3 74.9 all-gather.8
  207.6 75.3 all-gather.6
  285.7 75.3 all-gather.10
where the time goes:
time: 371 us
  waiting for transfers between devices  236 us (64%)
  blocking collectives  54.5 us (15%)
  matrix products  43.7 us (12%)
  other arithmetic  14.9 us (4%)
  between operations  13.9 us (4%)
  starting transfers between devices  7.36 us (2%)
    all_gather x1, waiting for transfers between devices, attend(): key_block = lax.all_gather(keyvals, 'seq', axis=0, tiled=True)  76.2 us
    all_gather x1, waiting for transfers between devices, shards(): lax.all_gather(query_weight, 'seq', axis=0, tiled=True)  54.9 us
    all_gather x1, blocking collectives, shards(): lax.all_gather(keyval_weight, 'seq', axis=0, tiled=True)  54.5 us
    all_gather x1, waiting for transfers between devices, shards(): lax.all_gather(conv_weight, 'seq', axis=2, tiled=True)  53.4 us
    all_gather x1, waiting for transfers between devices, shards(): lax.all_gather(output_weight, 'seq', axis=0, tiled=True)  49.9 us
    dot_general x5, matrix products, convolve(): jnp.dot(padded[kernel_tap:kernel_tap + row_count], kernel[kernel_tap], pr...  19.2 us
    reduce_sum x1, other arithmetic, attend(): running_sum = jnp.sum(expon, axis=2)  10.4 us
    dot_general x1, matrix products, attend(): jnp.einsum('qhd,kd->hqk', shaped, key_part, preferred_element_type=jnp.fl...  9.28 us
  transfers between devices with their start and end apart: 6, of which 4 were waited for; matrix products, arithmetic and copies ran while one was open for 15% of the time, Pallas kernels for 0%

commit v1 on v0

v1 whole, which is shorter than its diff:
```python
import jax
import jax.numpy as jnp
from jax import lax
from jax.sharding import Mesh
from jax.sharding import PartitionSpec as P

HEAD_DIM = 128


def normalize(values_in, channel_gain):
    meansq = jnp.mean(values_in * values_in, axis=-1, keepdims=True)
    return values_in * lax.rsqrt(meansq + 1e-06) * channel_gain


def convolve(padded, kernel, row_count):
    summed = jnp.zeros((row_count, kernel.shape[2]), jnp.float32)
    for kernel_tap in range(kernel.shape[0]):
        summed = summed + jnp.dot(
            padded[kernel_tap : kernel_tap + row_count],
            kernel[kernel_tap],
            preferred_element_type=jnp.float32,
        )
    return summed


def pool_pairs(levels):
    return jnp.max(levels.reshape(-1, 2, levels.shape[1]), axis=1)


def gather_rows(block):
    inner = lax.all_gather(block, "sx", axis=0, tiled=True)
    return lax.all_gather(inner, "sz", axis=0, tiled=True)


def attend(queries, key_block, scales):
    row_count = queries.shape[0]
    head_count = scales.shape[0]
    shaped = queries.reshape(row_count, head_count, HEAD_DIM)
    key_part = key_block[:, :HEAD_DIM]
    value_part = key_block[:, HEAD_DIM:]
    scores = (
        jnp.einsum("qhd,kd->hqk", shaped, key_part, preferred_element_type=jnp.float32)
        * scales[:, None, None]
        * HEAD_DIM ** (-0.5)
    )
    biggest = jnp.max(scores, axis=2)
    expon = jnp.exp(scores - biggest[:, :, None])
    total = jnp.sum(expon, axis=2)
    context = jnp.einsum(
        "hqk,kd->hqd", expon.astype(jnp.bfloat16), value_part, preferred_element_type=jnp.float32
    )
    context = context / total[:, :, None]
    return context.transpose(1, 0, 2).reshape(row_count, head_count * HEAD_DIM).astype(jnp.bfloat16)


def shards(
    features,
    norm_gain,
    conv_weight,
    conv_bias,
    attn_gain,
    query_weight,
    keyval_weight,
    head_scale,
    output_weight,
):
    nz = lax.axis_size("sz")
    nx = lax.axis_size("sx")
    me_x = lax.axis_index("sx")
    rows_here = features.shape[0]
    width = conv_weight.shape[2]
    ch_out = conv_bias.shape[0]

    kernel = lax.all_gather(conv_weight, "sz", axis=2, tiled=True)
    proj_weight = gather_rows(jnp.concatenate([query_weight, keyval_weight], axis=1))
    out_weight = gather_rows(output_weight)

    normed = jax.nn.gelu(normalize(features.astype(jnp.float32), norm_gain)).astype(jnp.bfloat16)
    plane = lax.all_gather(normed, "sx", axis=0, tiled=True)
    plane_rows = plane.shape[0]
    forward = [(i, i + 1) for i in range(nz - 1)]
    backward = [(i + 1, i) for i in range(nz - 1)]
    low = lax.ppermute(plane[plane_rows - 2 :], "sz", forward)
    high = lax.ppermute(plane[:2], "sz", backward)
    padded = jnp.concatenate([low, plane, high], axis=0)

    bias_all = conv_bias.reshape(nz, nx, width).transpose(1, 0, 2)
    bias = lax.dynamic_index_in_dim(bias_all, me_x, axis=0, keepdims=False).reshape(nz * width)
    levels = convolve(padded, kernel, plane_rows) + bias[None, :]
    pooled = pool_pairs(levels).astype(jnp.bfloat16)

    coarse_rows = rows_here // 2
    pieces = pooled.reshape(nx, coarse_rows, nz * width)
    received = lax.all_to_all(pieces, "sx", 0, 0, tiled=False)
    coarse = (
        received.reshape(nx, coarse_rows, nz, width)
        .transpose(1, 2, 0, 3)
        .reshape(coarse_rows, ch_out)
    )

    attn_in = normalize(coarse.astype(jnp.float32), attn_gain).astype(jnp.bfloat16)
    proj = jnp.dot(attn_in, proj_weight, preferred_element_type=jnp.float32)
    q_cols = query_weight.shape[1]
    queries = proj[:, :q_cols].astype(jnp.bfloat16)
    keyvals = proj[:, q_cols:].astype(jnp.bfloat16)
    key_block = gather_rows(keyvals)
    context = attend(queries, key_block, head_scale)
    projected = jnp.dot(context, out_weight, preferred_element_type=jnp.float32)
    return (coarse, projected.astype(jnp.bfloat16))


def solution(mesh):
    dp = mesh.shape["dp"]
    seq = mesh.shape["seq"]
    nx = 8 if seq % 8 == 0 else seq
    nz = seq // nx
    grid = Mesh(mesh.devices.reshape(dp, nz, nx), ("dp", "sz", "sx"))
    rows = P(("dp", "sz", "sx"), None)
    return jax.shard_map(
        shards,
        mesh=grid,
        in_specs=(
            rows,
            P(),
            P(None, None, ("sz", "sx")),
            P(),
            P(),
            P(("sz", "sx"), None),
            P(("sz", "sx"), None),
            P(),
            P(("sz", "sx"), None),
        ),
        out_specs=(rows, rows),
        check_vma=False,
    )
```

time: 371 us -> 263 us (0.71)
  waiting for transfers between devices: 236 us -> 119 us
  local copies, waits for them, and re-layouts: 0.27 us -> 9.68 us
  matrix products: 43.7 us -> 34.6 us
  blocking collectives: 54.5 us -> 62.5 us
    all_gather x4 -> x5, waiting for transfers between devices: 234 us -> 118 us  [the longest x3 67.8 us: gather_rows(): return lax.all_gather(inner, 'sz', axis=0, tiled=True)]
    all_to_all x0 -> x1, blocking collectives: none -> 16.2 us  [shards(): received = lax.all_to_all(pieces, 'sx', 0, 0, tiled=False)]
    dot_general x5, matrix products: 19.2 us -> 10.5 us  [convolve(): jnp.dot(padded[kernel_tap:kernel_tap + row_count], kernel[kernel_tap], pr...]
    all_gather x1 -> x3, blocking collectives: 54.5 us -> 46.3 us  [gather_rows(): inner = lax.all_gather(block, 'sx', axis=0, tiled=True)]
    unnamed x10 -> x16, local copies, waits for them, and re-layouts: 0.03 us -> 6.09 us
  transfers between devices with their start and end apart: 6 -> 7, of which waited for: 4 -> 5; matrix products, arithmetic and copies ran while one was open for 15% -> 20% of each run, Pallas kernels for 0% -> 0%
where the time goes in v1:
time: 263 us; the launch traced here: 262 us
  waiting for transfers between devices  119 us (45%)
  blocking collectives  62.5 us (24%)
  matrix products  34.6 us (13%)
  other arithmetic  17.3 us (7%)
  between operations  14 us (5%)
  local copies, waits for them, and re-layouts  9.68 us (4%)
  starting transfers between devices  4.67 us (2%)
    all_gather x3, waiting for transfers between devices, gather_rows(): return lax.all_gather(inner, 'sz', axis=0, tiled=True)  67.8 us
    all_gather x3, blocking collectives, gather_rows(): inner = lax.all_gather(block, 'sx', axis=0, tiled=True)  46.3 us
    all_gather x1, waiting for transfers between devices, shards(): kernel = lax.all_gather(conv_weight, 'sz', axis=2, tiled=True)  31.1 us
    all_gather x1, waiting for transfers between devices, shards(): plane = lax.all_gather(normed, 'sx', axis=0, tiled=True)  19.7 us
    all_to_all x1, blocking collectives, shards(): received = lax.all_to_all(pieces, 'sx', 0, 0, tiled=False)  16.2 us
    dot_general x5, matrix products, convolve(): jnp.dot(padded[kernel_tap:kernel_tap + row_count], kernel[kernel_tap], pr...  10.5 us
    reduce_sum x1, other arithmetic, attend(): total = jnp.sum(expon, axis=2)  10.4 us
    dot_general x1, matrix products, attend(): jnp.einsum('qhd,kd->hqk', shaped, key_part, preferred_element_type=jnp.fl...  9.28 us
  transfers between devices with their start and end apart: 7, of which 5 were waited for; matrix products, arithmetic and copies ran while one was open for 20% of the time, Pallas kernels for 0%

profile of v1, /device:TPU:1, one launch (start us, length us, event | category | flops | bytes accessed | tf_op | source)
XLA Modules:
  0.0 262.1 jit_solution(17511630093383080673)
XLA Ops:
  8.5 2.4 fusion.37
  12.5 17.2 %all_gather.26 = bf16[192,1280]{1,0:T(8,128)(2,1)} all-gather(bf16[24,1280]{1,0:T(8,128)(2,1)S(1)} %pad_maximum_fusion.2), channel_id=1, replica_groups=mesh['dp'=4,'sz'=8,'sx'=8] {'sx'}, dimensions={0}, use_global_device_ids=true | all-gather | bytes 552960 | tf_op jit(solution)/shard_map/all_gather | solution.py:31
  30.7 19.7 %all-gather.6.cloned.1.call-done = bf16[1536,1408]{1,0:T(8,128)(2,1)} async-done(((bf16[192,1408]{1,0:T(8,128)(2,1)}), bf16[1536,1408]{1,0:T(8,128)(2,1)}) %all-gather.6.cloned.1.call-update) | async-done | bytes 4325392 | tf_op jit(solution)/shard_map/all_gather | solution.py:79
  51.1 3.2 %collective-permute-start = (bf16[2,1408]{1,0:T(2,128)(2,1)S(1)}, bf16[2,1408]{1,0:T(2,128)(2,1)S(1)}, u32[]{:S(2)}, u32[]{:S(2)}) collective-permute-start(bf16[2,1408]{1,0:T(2,128)(2,1)S(1)} %get-tuple-element.10), channel_id=1, source_target_pairs={{0,8},{8,16},{16,24},{24,32},{32,40},{40,48},{48,56},{1,9},{9,17},... | collective-permute-start | bytes 16904 | tf_op jit(solution)/shard_map/ppermute | solution.py:83
  54.3 1.3 collective-permute-start.1
  55.6 4.6 %constant_dynamic-update-slice_fusion.1 = bf16[1538,1408]{1,0:T(8,128)(2,1)} fusion(bf16[1536,1408]{1,0:T(8,128)(2,1)} %all-gather.6.cloned.1.call-done), kind=kLoop, calls=%fused_computation.62 | loop fusion | bytes 8650752
  60.1 31.1 %all-gather.8.cloned.1.call-done = bf16[5,1408,192]{1,2,0:T(8,128)(2,1)} async-done(((bf16[5,1408,24]{1,2,0:T(8,128)(2,1)}), bf16[5,1408,192]{1,2,0:T(8,128)(2,1)}) %all-gather.8.cloned.1.call-update) | async-done | bytes 2703376 | tf_op jit(solution)/shard_map/all_gather | solution.py:74
  91.2 4.1 %fusion.52 = f32[1536,192]{0,1:T(8,128)S(1)} fusion(bf16[1536,1408]{1,0:T(8,128)(2,1)} %all-gather.6.cloned.1.call-done, bf16[5,1408,192]{1,2,0:T(8,128)(2,1)} %all-gather.8.cloned.1.call-done), kind=kOutput, calls=%fused_computation.50 | convolution fusion | flops 830472192 | bytes 6045696 | tf_op jit(solution)/shard_map/dot_general | solution.py:18
  95.9 1.6 fusion.12
  98.1 1.6 fusion.8
  99.7 1.6 fusion.26
  101.3 1.6 fusion.20
  103.7 2.2 reduce_max.18
  106.6 16.2 %all_to_all.5 = bf16[8,96,192]{1,2,0:T(8,128)(2,1)S(1)} all-to-all(bf16[8,96,192]{1,2,0:T(8,128)(2,1)S(1)} %copy.32), channel_id=1, replica_groups=mesh['dp'=4,'sz'=8,'sx'=8] {'sx'}, dimensions={0} | all-to-all | bytes 589824 | tf_op jit(solution)/shard_map/all_to_all | solution.py:94
  123.1 23.8 %all-gather.10.cloned.1.call-done = bf16[1536,1280]{1,0:T(8,128)(2,1)} async-done(((bf16[192,1280]{1,0:T(8,128)(2,1)}), bf16[1536,1280]{1,0:T(8,128)(2,1)}) %all-gather.10.cloned.1.call-update) | async-done | bytes 3932176 | tf_op jit(solution)/shard_map/all_gather | solution.py:32
  146.9 3.0 %convolution_convert_fusion.1 = bf16[96,1280]{1,0:T(8,128)(2,1)S(1)} fusion(bf16[1536,1280]{1,0:T(8,128)(2,1)} %all-gather.10.cloned.1.call-done, bf16[96,1536]{0,1:T(8,128)(2,1)S(1)} %bitcast.81, f32[1536]{0:T(1024)S(1)} %copy-done.5, f32[96]{0:T(128)S(1)} %add_rsqrt_fusion.1), kind=kOutput, calls=%fused_computation.24 | convolution fusion | flops 378200064 | bytes 4479360 | tf_op jit(solution)/shard_map/dot_general | solution.py:102
  149.9 15.0 %all_gather.28 = bf16[768,256]{1,0:T(8,128)(2,1)} all-gather(bf16[96,256]{1,0:T(8,128)(2,1)S(1)} %slice.77), channel_id=1, replica_groups=mesh['dp'=4,'sz'=8,'sx'=8] {'sx'}, dimensions={0}, use_global_device_ids=true | all-gather | bytes 442368 | tf_op jit(solution)/shard_map/all_gather | solution.py:31
  165.0 14.1 %all_gather.30 = bf16[128,1536]{1,0:T(8,128)(2,1)} all-gather(bf16[16,1536]{1,0:T(8,128)(2,1)S(1)} %copy-done.3), channel_id=1, replica_groups=mesh['dp'=4,'sz'=8,'sx'=8] {'sx'}, dimensions={0}, use_global_device_ids=true | all-gather | bytes 442368 | tf_op jit(solution)/shard_map/all_gather | solution.py:31
  180.0 27.1 %all-gather.12.cloned.1.call-done = bf16[6144,256]{1,0:T(8,128)(2,1)} async-done(((bf16[768,256]{1,0:T(8,128)(2,1)}), bf16[6144,256]{1,0:T(8,128)(2,1)}) %all-gather.12.cloned.1.call-update) | async-done | bytes 3145744 | tf_op jit(solution)/shard_map/all_gather | solution.py:32
  207.0 9.3 %bitcast_reduce_fusion = (f32[8,96]{1,0:T(8,128)S(1)}, f32[6144,96,8]{0,1,2:T(8,128)}) fusion(f32[8]{0:T(128)S(1)} %copy-done.4, bf16[6144,256]{1,0:T(8,128)(2,1)} %all-gather.12.cloned.1.call-done, bf16[96,1280]{1,0:T(8,128)(2,1)S(1)} %convolution_convert_fusion.1), kind=kOutput, calls=%fused_computation.1 | convolution fusion | flops 1222114560 | bytes 20647424 | tf_op jit(solution)/shard_map/qhd,kd->hqk/dot_general | solution.py:42
  216.3 10.4 %fusion.1 = f32[8,96]{1,0:T(8,128)S(1)} fusion(f32[6144,96,8]{0,1,2:T(8,128)} %get-tuple-element.13, f32[8,96]{1,0:T(8,128)S(1)} %get-tuple-element.12, f32[8]{0:T(128)S(1)} %copy-done.4), kind=kLoop, calls=%fused_computation.4 | loop fusion | flops 18873600 | bytes 18880544 | tf_op jit(solution)/shard_map/reduce_sum | solution.py:48
  226.8 8.6 %fusion.49 = bf16[8,12,8,128]{3,2,1,0:T(8,128)(2,1)S(1)} fusion(bf16[6144,256]{1,0:T(8,128)(2,1)S(1)} %copy-done.2, f32[6144,96,8]{0,1,2:T(8,128)} %get-tuple-element.13, f32[8,96]{1,0:T(8,128)S(1)} %get-tuple-element.12, f32[8]{0:T(128)S(1)} %copy-done.4, f32[96,8]{0,1:T(8,128)S(1)} %bitcast.85), kind=kOutput, calls=%fused_computation.44 | convolution fusion | flops 1227030528 | bytes 20652544 | tf_op jit(solution)/shard_map/hqk,kd->hqd/dot_general | solution.py:49
  235.4 16.9 %all-gather.14.cloned.1.call-done = bf16[1024,1536]{1,0:T(8,128)(2,1)} async-done(((bf16[128,1536]{1,0:T(8,128)(2,1)}), bf16[1024,1536]{1,0:T(8,128)(2,1)}) %all-gather.14.cloned.1.call-update) | async-done | bytes 3145744 | tf_op jit(solution)/shard_map/all_gather | solution.py:32
  252.3 3.2 %convolution_convert_fusion = bf16[96,1536]{1,0:T(8,128)(2,1)} fusion(bf16[1024,1536]{1,0:T(8,128)(2,1)} %all-gather.14.cloned.1.call-done, bf16[8,12,8,128]{3,2,1,0:T(8,128)(2,1)S(1)} %fusion.49), kind=kOutput, calls=%fused_computation.23 | convolution fusion | flops 302137344 | bytes 3637248 | tf_op jit(solution)/shard_map/dot_general | solution.py:108
  (44 shorter events, 8.4 us)
Async XLA Ops:
  7.2 43.2 %all-gather.6.cloned.1.call-start = ((), (), s32[]{:S(2)}) async-start(), calls=%async_computation.1 | async-start | bytes 4866048 | tf_op jit(solution)/shard_map/all_gather | solution.py:79
  10.9 80.3 %all-gather.8.cloned.1.call-start = ((), (), s32[]{:S(2)}) async-start(), calls=%async_computation.2 | async-start | bytes 3041280 | tf_op jit(solution)/shard_map/all_gather | solution.py:74
  11.6 135.3 %all-gather.10.cloned.1.call-start = ((), (), s32[]{:S(2)}) async-start(), calls=%async_computation.3 | async-start | bytes 4423680 | tf_op jit(solution)/shard_map/all_gather | solution.py:32
  29.7 177.3 %all-gather.12.cloned.1.call-start = ((), (), s32[]{:S(2)}) async-start(), calls=%async_computation.4 | async-start | bytes 3538944 | tf_op jit(solution)/shard_map/all_gather | solution.py:32
  51.1 44.8 %collective-permute-start = (bf16[2,1408]{1,0:T(2,128)(2,1)S(1)}, bf16[2,1408]{1,0:T(2,128)(2,1)S(1)}, u32[]{:S(2)}, u32[]{:S(2)}) collective-permute-start(bf16[2,1408]{1,0:T(2,128)(2,1)S(1)} %get-tuple-element.10), channel_id=1, source_target_pairs={{0,8},{8,16},{16,24},{24,32},{32,40},{40,48},{48,56},{1,9},{9,17},... | collective-permute-start | bytes 16904 | tf_op jit(solution)/shard_map/ppermute | solution.py:83
  54.3 41.0 %collective-permute-start.1 = (bf16[2,1408]{1,0:T(2,128)(2,1)S(1)}, bf16[2,1408]{1,0:T(2,128)(2,1)S(1)}, u32[]{:S(2)}, u32[]{:S(2)}) collective-permute-start(bf16[2,1408]{1,0:T(2,128)(2,1)S(1)} %get-tuple-element.11), channel_id=1, source_target_pairs={{8,0},{16,8},{24,16},{32,24},{40,32},{48,40},{56,48},{9,1},{17,9},... | collective-permute-start | bytes 16904 | tf_op jit(solution)/shard_map/ppermute | solution.py:84
  91.2 4.7 %copy-start = (bf16[1536,1408]{1,0:T(8,128)(2,1)S(1)}, bf16[1536,1408]{1,0:T(8,128)(2,1)}, u32[]{:S(2)}) copy-start(bf16[1536,1408]{1,0:T(8,128)(2,1)} %all-gather.6.cloned.1.call-done) | copy-start | bytes 12976132
  91.2 4.7 %copy-start.6 = (bf16[5,1408,192]{1,2,0:T(8,128)(2,1)S(1)}, bf16[5,1408,192]{1,2,0:T(8,128)(2,1)}, u32[]{:S(2)}) copy-start(bf16[5,1408,192]{1,2,0:T(8,128)(2,1)} %all-gather.8.cloned.1.call-done) | copy-start | bytes 8110084
  95.9 2.2 copy-start.1
  103.0 43.9 %copy-start.5 = (f32[1536]{0:T(1024)S(1)}, f32[1536]{0:T(1024)}, u32[]{:S(2)}) copy-start(f32[1536]{0:T(1024)} %param.13) | copy-start | bytes 18436
  106.6 58.4 %copy-start.3 = (bf16[16,1536]{1,0:T(8,128)(2,1)S(1)}, bf16[16,1536]{1,0:T(8,128)(2,1)}, u32[]{:S(2)}) copy-start(bf16[16,1536]{1,0:T(8,128)(2,1)} %param.17) | copy-start | bytes 147460
  122.8 84.2 %copy-start.4 = (f32[8]{0:T(128)S(1)}, f32[8]{0:T(128)}, u32[]{:S(2)}) copy-start(f32[8]{0:T(128)} %param.16) | copy-start | bytes 100
  165.0 87.4 %all-gather.14.cloned.1.call-start = ((), (), s32[]{:S(2)}) async-start(), calls=%async_computation.5 | async-start | bytes 3538944 | tf_op jit(solution)/shard_map/all_gather | solution.py:32
  216.3 10.5 %copy-start.2 = (bf16[6144,256]{1,0:T(8,128)(2,1)S(1)}, bf16[6144,256]{1,0:T(8,128)(2,1)}, u32[]{:S(2)}) copy-start(bf16[6144,256]{1,0:T(8,128)(2,1)} %all-gather.12.cloned.1.call-done) | copy-start | bytes 9437188
Sparse Core Ops, SparseCore 0:
  11.0 39.2 all-gather.5
  52.1 39.0 all-gather.7
  93.0 53.8 all-gather.9
  165.1 41.9 all-gather.11
  208.7 43.5 all-gather.13

commit v2 on v1

--- a/solution.py
+++ b/solution.py
@@ -27,9 +27,18 @@
     return jnp.max(levels.reshape(-1, 2, levels.shape[1]), axis=1)
 
 
-def gather_rows(block):
-    inner = lax.all_gather(block, "sx", axis=0, tiled=True)
-    return lax.all_gather(inner, "sz", axis=0, tiled=True)
+def spread_in_plane(block):
+    inner = lax.all_gather(block, "sxx", axis=0, tiled=True)
+    return lax.all_gather(inner, "core", axis=0, tiled=True)
+
+
+def plane_order(columns, nz, nxx, nc):
+    rows = columns.shape[0]
+    return (
+        columns.reshape(rows, nz, nxx, nc, -1)
+        .transpose(0, 3, 2, 1, 4)
+        .reshape(rows, columns.shape[1])
+    )
 
 
 def attend(queries, key_block, scales):
@@ -65,18 +74,30 @@
     output_weight,
 ):
     nz = lax.axis_size("sz")
-    nx = lax.axis_size("sx")
-    me_x = lax.axis_index("sx")
+    nxx = lax.axis_size("sxx")
+    nc = lax.axis_size("core")
+    nx = nxx * nc
+    me_x = lax.axis_index("sxx") * nc + lax.axis_index("core")
     rows_here = features.shape[0]
-    width = conv_weight.shape[2]
+    taps, ch_in, width = conv_weight.shape
     ch_out = conv_bias.shape[0]
 
-    kernel = lax.all_gather(conv_weight, "sz", axis=2, tiled=True)
-    proj_weight = gather_rows(jnp.concatenate([query_weight, keyval_weight], axis=1))
-    out_weight = gather_rows(output_weight)
+    proj_piece = jnp.concatenate([query_weight, keyval_weight], axis=1)
+    pieces = [conv_weight, proj_piece, output_weight]
+    sizes = [p.size for p in pieces]
+    flat = jnp.concatenate([p.reshape(-1) for p in pieces])
+    got = lax.all_gather(flat, "sz", axis=0, tiled=False)
+    kernel = (
+        got[:, : sizes[0]]
+        .reshape(nz, taps, ch_in, width)
+        .transpose(1, 2, 0, 3)
+        .reshape(taps, ch_in, nz * width)
+    )
+    proj_z = got[:, sizes[0] : sizes[0] + sizes[1]].reshape(nz * proj_piece.shape[0], proj_piece.shape[1])
+    out_z = got[:, sizes[0] + sizes[1] :].reshape(nz * output_weight.shape[0], output_weight.shape[1])
 
     normed = jax.nn.gelu(normalize(features.astype(jnp.float32), norm_gain)).astype(jnp.bfloat16)
-    plane = lax.all_gather(normed, "sx", axis=0, tiled=True)
+    plane = lax.all_gather(normed, ("sxx", "core"), axis=0, tiled=True)
     plane_rows = plane.shape[0]
     forward = [(i, i + 1) for i in range(nz - 1)]
     backward = [(i + 1, i) for i in range(nz - 1)]
@@ -89,9 +110,11 @@
     levels = convolve(padded, kernel, plane_rows) + bias[None, :]
     pooled = pool_pairs(levels).astype(jnp.bfloat16)
 
+    proj_weight = spread_in_plane(proj_z)
+
     coarse_rows = rows_here // 2
-    pieces = pooled.reshape(nx, coarse_rows, nz * width)
-    received = lax.all_to_all(pieces, "sx", 0, 0, tiled=False)
+    parts = pooled.reshape(nx, coarse_rows, nz * width)
+    received = lax.all_to_all(parts, ("sxx", "core"), 0, 0, tiled=False)
     coarse = (
         received.reshape(nx, coarse_rows, nz, width)
         .transpose(1, 2, 0, 3)
@@ -99,36 +122,39 @@
     )
 
     attn_in = normalize(coarse.astype(jnp.float32), attn_gain).astype(jnp.bfloat16)
-    proj = jnp.dot(attn_in, proj_weight, preferred_element_type=jnp.float32)
+    proj = jnp.dot(plane_order(attn_in, nz, nxx, nc), proj_weight, preferred_element_type=jnp.float32)
     q_cols = query_weight.shape[1]
     queries = proj[:, :q_cols].astype(jnp.bfloat16)
     keyvals = proj[:, q_cols:].astype(jnp.bfloat16)
-    key_block = gather_rows(keyvals)
+    key_block = spread_in_plane(lax.all_gather(keyvals, "sz", axis=0, tiled=True))
+    out_weight = spread_in_plane(out_z)
     context = attend(queries, key_block, head_scale)
-    projected = jnp.dot(context, out_weight, preferred_element_type=jnp.float32)
+    projected = jnp.dot(plane_order(context, nz, nxx, nc), out_weight, preferred_element_type=jnp.float32)
     return (coarse, projected.astype(jnp.bfloat16))
 
 
 def solution(mesh):
     dp = mesh.shape["dp"]
     seq = mesh.shape["seq"]
-    nx = 8 if seq % 8 == 0 else seq
-    nz = seq // nx
-    grid = Mesh(mesh.devices.reshape(dp, nz, nx), ("dp", "sz", "sx"))
-    rows = P(("dp", "sz", "sx"), None)
+    nc = 2 if seq % 2 == 0 else 1
+    nxx = 4 if (seq // nc) % 4 == 0 else seq // nc
+    nz = seq // (nc * nxx)
+    grid = Mesh(mesh.devices.reshape(dp, nz, nxx, nc), ("dp", "sz", "sxx", "core"))
+    seq_axes = ("sz", "sxx", "core")
+    rows = P(("dp",) + seq_axes, None)
     return jax.shard_map(
         shards,
         mesh=grid,
         in_specs=(
             rows,
             P(),
-            P(None, None, ("sz", "sx")),
+            P(None, None, seq_axes),
             P(),
             P(),
-            P(("sz", "sx"), None),
-            P(("sz", "sx"), None),
+            P(seq_axes, None),
+            P(seq_axes, None),
             P(),
-            P(("sz", "sx"), None),
+            P(seq_axes, None),
         ),
         out_specs=(rows, rows),
         check_vma=False,

time: 263 us -> 314 us (1.19)
  local copies, waits for them, and re-layouts: 9.68 us -> 73.3 us
  blocking collectives: 62.5 us -> 22.5 us
  waiting for transfers between devices: 119 us -> 147 us
    slice x0 -> x11, local copies, waits for them, and re-layouts: none -> 28.1 us  [the longest x6 26.8 us: convolve(): kernel[kernel_tap]]
    reshape x0 -> x6, local copies, waits for them, and re-layouts: none -> 26.9 us  [the longest x1 22.4 us: shards(): kernel = got[:, :sizes[0]].reshape(nz, taps, ch_in, width).transpose(1, 2...]
    all_gather x3 -> x1, blocking collectives: 46.3 us -> 22.5 us  [shards(): lax.all_gather(keyvals, 'sz', axis=0, tiled=True)]
    all_gather x5 -> x8, waiting for transfers between devices: 118 us -> 140 us  [the longest x3 68.2 us: spread_in_plane(): inner = lax.all_gather(block, 'sxx', axis=0, tiled=True)]
    all_to_all x1 -> x0, blocking collectives: 16.2 us -> none  [shards(): received = lax.all_to_all(pieces, 'sx', 0, 0, tiled=False)]
    all_to_all x0 -> x1, waiting for transfers between devices: none -> 7.59 us  [shards(): received = lax.all_to_all(parts, ('sxx', 'core'), 0, 0, tiled=False)]
    all_gather x0 -> x1, local copies, waits for them, and re-layouts: none -> 5.36 us  [shards(): got = lax.all_gather(flat, 'sz', axis=0, tiled=False)]
    all_to_all x0 -> x1, starting transfers between devices: none -> 4.2 us  [shards(): received = lax.all_to_all(parts, ('sxx', 'core'), 0, 0, tiled=False)]
  transfers between devices with their start and end apart: 7 -> 11, of which waited for: 5 -> 6; matrix products, arithmetic and copies ran while one was open for 20% -> 35% of each run, Pallas kernels for 0% -> 0%
where the time goes in v2:
time: 314 us; the launch traced here: 313 us
  waiting for transfers between devices  147 us (47%)
  local copies, waits for them, and re-layouts  73.3 us (23%)
  matrix products  31.8 us (10%)
  blocking collectives  22.5 us (7%)
  other arithmetic  16.2 us (5%)
  between operations  14.6 us (5%)
  starting transfers between devices  7.52 us (2%)
    all_gather x3, waiting for transfers between devices, spread_in_plane(): inner = lax.all_gather(block, 'sxx', axis=0, tiled=True)  68.2 us
    all_gather x1, waiting for transfers between devices, shards(): got = lax.all_gather(flat, 'sz', axis=0, tiled=False)  51.2 us
    slice x6, local copies, waits for them, and re-layouts, convolve(): kernel[kernel_tap]  26.8 us
    all_gather x1, blocking collectives, shards(): lax.all_gather(keyvals, 'sz', axis=0, tiled=True)  22.5 us
    reshape x1, local copies, waits for them, and re-layouts, shards(): kernel = got[:, :sizes[0]].reshape(nz, taps, ch_in, width).transpose(1, 2...  22.4 us
    all_gather x3, waiting for transfers between devices, spread_in_plane(): return lax.all_gather(inner, 'core', axis=0, tiled=True)  20.2 us
    reduce_sum x1, other arithmetic, attend(): total = jnp.sum(expon, axis=2)  11.1 us
    unnamed x34, local copies, waits for them, and re-layouts  9.51 us
  transfers between devices with their start and end apart: 11, of which 6 were waited for; matrix products, arithmetic and copies ran while one was open for 35% of the time, Pallas kernels for 0%

profile of v2, /device:TPU:1, one launch (start us, length us, event | category | flops | bytes accessed | tf_op | source)
XLA Modules:
  0.0 313.2 jit_solution(10841448251101722798)
XLA Ops:
  9.4 2.4 reshape.100
  14.5 51.2 %all-gather.24.cloned.1.call-done = bf16[1794048]{0:T(1024)(128)(2,1)} async-done(((bf16[224256]{0:T(1024)(128)(2,1)}), bf16[1794048]{0:T(1024)(128)(2,1)}) %all-gather.24.cloned.1.call-update) | async-done | bytes 3588112 | tf_op jit(solution)/shard_map/all_gather | solution.py:89
  65.7 5.4 %reshape.114 = bf16[8,224256]{1,0:T(8,128)(2,1)} reshape(bf16[1794048]{0:T(1024)(128)(2,1)} %all-gather.24.cloned.1.call-done) | data formatting | bytes 7176192 | tf_op jit(solution)/shard_map/all_gather | solution.py:89
  73.6 2.8 reshape.124
  76.4 22.4 %reshape.103 = bf16[8,5,1408,24]{3,2,1,0:T(8,128)(2,1)} reshape(bf16[1351680]{0:T(1024)(128)(2,1)} %reshape.124) | data formatting | bytes 5406720 | tf_op jit(solution)/shard_map/reshape | solution.py:92
  98.8 10.0 %fusion.56 = (bf16[1,1408,8,24]{3,1,0,2:T(8,128)(2,1)S(1)}, bf16[1,1408,8,24]{3,1,0,2:T(8,128)(2,1)}, bf16[1,1408,8,24]{3,1,0,2:T(8,128)(2,1)}, bf16[1,1408,8,24]{3,1,0,2:T(8,128)(2,1)}, bf16[1,1408,8,24]{3,1,0,2:T(8,128)(2,1)}) fusion(bf16[5,1408,8,24]{3,1,0,2:T(8,128)(2,1)} %bitcast.78), kind=kLoop, calls=%fused_computation.61 | loop fusion | bytes 5406720 | tf_op jit(solution)/shard_map/slice | solution.py:20
  108.8 3.7 %copy.58 = bf16[1,1408,8,24]{1,3,2,0:T(8,128)(2,1)} copy(bf16[1,1408,8,24]{3,1,0,2:T(8,128)(2,1)} %get-tuple-element.13) | data formatting | bytes 1081344 | tf_op jit(solution)/shard_map/slice | solution.py:20
  112.5 3.8 %copy.59 = bf16[1,1408,8,24]{1,3,2,0:T(8,128)(2,1)} copy(bf16[1,1408,8,24]{3,1,0,2:T(8,128)(2,1)} %get-tuple-element.12) | data formatting | bytes 1081344 | tf_op jit(solution)/shard_map/slice | solution.py:20
  116.4 3.8 %copy.57 = bf16[1,1408,8,24]{1,3,2,0:T(8,128)(2,1)} copy(bf16[1,1408,8,24]{3,1,0,2:T(8,128)(2,1)} %get-tuple-element.14) | data formatting | bytes 1081344 | tf_op jit(solution)/shard_map/slice | solution.py:20
  120.2 3.8 %copy.61 = bf16[1,1408,8,24]{1,3,2,0:T(8,128)(2,1)} copy(bf16[1,1408,8,24]{3,1,0,2:T(8,128)(2,1)} %get-tuple-element.11) | data formatting | bytes 1081344 | tf_op jit(solution)/shard_map/slice | solution.py:20
  129.3 6.1 %all-gather.12.cloned.1.call-done = bf16[768,1280]{1,0:T(8,128)(2,1)} async-done(((bf16[192,1280]{1,0:T(8,128)(2,1)}), bf16[768,1280]{1,0:T(8,128)(2,1)}) %all-gather.12.cloned.1.call-update) | async-done | bytes 1966096 | tf_op jit(solution)/shard_map/all_gather | solution.py:31
  135.4 2.7 constant_dynamic-update-slice_fusion.1
  147.9 2.2 reduce_max.18
  151.6 4.2 %all-to-all-start = ((bf16[8,96,192]{1,2,0:T(8,128)(2,1)}), bf16[8,96,192]{1,2,0:T(8,128)(2,1)S(1)}, u32[]{:S(2)}, u32[]{:S(2)}) async-start(bf16[8,96,192]{1,2,0:T(8,128)(2,1)} %copy.64), calls=%async_computation | async-start | bytes 786432 | tf_op jit(solution)/shard_map/all_to_all | solution.py:117
  155.9 7.6 %all-to-all-done = bf16[8,96,192]{1,2,0:T(8,128)(2,1)S(1)} async-done(((bf16[8,96,192]{1,2,0:T(8,128)(2,1)}), bf16[8,96,192]{1,2,0:T(8,128)(2,1)S(1)}, u32[]{:S(2)}, u32[]{:S(2)}) %all-to-all-start) | async-done | bytes 294944 | tf_op jit(solution)/shard_map/all_to_all | solution.py:117
  164.1 2.8 convolution_convert_fusion.1
  166.9 22.5 %all_gather.35 = bf16[768,256]{1,0:T(8,128)(2,1)} all-gather(bf16[96,256]{1,0:T(8,128)(2,1)S(1)} %slice.96), channel_id=1, replica_groups=mesh['dp'=4,'sz'=8,'sxx'=4,'core'=2] {'sz'}, dimensions={0}, use_global_device_ids=true | all-gather | bytes 442368 | tf_op jit(solution)/shard_map/all_gather | solution.py:129
  190.5 32.7 %all-gather.16.cloned.1.call-done = bf16[3072,256]{1,0:T(8,128)(2,1)} async-done(((bf16[768,256]{1,0:T(8,128)(2,1)}), bf16[3072,256]{1,0:T(8,128)(2,1)}) %all-gather.16.cloned.1.call-update) | async-done | bytes 1572880 | tf_op jit(solution)/shard_map/all_gather | solution.py:31
  224.4 29.5 %all-gather.20.cloned.1.call-done = bf16[512,1536]{1,0:T(8,128)(2,1)} async-done(((bf16[128,1536]{1,0:T(8,128)(2,1)}), bf16[512,1536]{1,0:T(8,128)(2,1)}) %all-gather.20.cloned.1.call-update) | async-done | bytes 1572880 | tf_op jit(solution)/shard_map/all_gather | solution.py:31
  253.9 20.2 %all-gather.18.cloned.1.call-done = bf16[6144,256]{1,0:T(8,128)(2,1)} async-done(((bf16[3072,256]{1,0:T(8,128)(2,1)}), bf16[6144,256]{1,0:T(8,128)(2,1)}) %all-gather.18.cloned.1.call-update) | async-done | bytes 3145744 | tf_op jit(solution)/shard_map/all_gather | solution.py:32
  274.1 9.2 %bitcast_reduce_fusion = (f32[8,96]{1,0:T(8,128)S(1)}, f32[6144,96,8]{0,1,2:T(8,128)}) fusion(f32[8]{0:T(128)S(1)} %copy-done.8, bf16[6144,256]{1,0:T(8,128)(2,1)} %all-gather.18.cloned.1.call-done, bf16[96,1280]{1,0:T(8,128)(2,1)S(1)} %convolution_convert_fusion.1), kind=kOutput, calls=%fused_computation.1 | convolution fusion | flops 1222114560 | bytes 20647424 | tf_op jit(solution)/shard_map/qhd,kd->hqk/dot_general | solution.py:51
  283.3 11.1 %fusion.1 = f32[8,96]{1,0:T(8,128)S(1)} fusion(f32[6144,96,8]{0,1,2:T(8,128)} %get-tuple-element.18, f32[8,96]{1,0:T(8,128)S(1)} %get-tuple-element.17, f32[8]{0:T(128)S(1)} %copy-done.8), kind=kLoop, calls=%fused_computation.4 | loop fusion | flops 18873600 | bytes 18880544 | tf_op jit(solution)/shard_map/reduce_sum | solution.py:57
  294.4 8.4 %fusion.46 = bf16[96,8,128]{2,0,1:T(8,128)(2,1)S(1)} fusion(bf16[6144,256]{1,0:T(8,128)(2,1)S(1)} %copy-done.1, f32[6144,96,8]{0,1,2:T(8,128)} %get-tuple-element.18, f32[8,96]{1,0:T(8,128)S(1)} %get-tuple-element.17, f32[8]{0:T(128)S(1)} %copy-done.8, f32[96,8]{0,1:T(8,128)S(1)} %bitcast.93), kind=kOutput, calls=%fused_computation.43 | convolution fusion | flops 1227030528 | bytes 20652544 | tf_op jit(solution)/shard_map/hqk,kd->hqd/dot_general | solution.py:58
  303.1 3.3 %convolution_convert_fusion = bf16[96,1536]{1,0:T(8,128)(2,1)} fusion(bf16[96,1024]{0,1:T(8,128)(2,1)S(1)} %bitcast.86, bf16[1024,1536]{1,0:T(8,128)(2,1)} %all-gather.22.cloned.1.call-done), kind=kOutput, calls=%fused_computation.23 | convolution fusion | flops 302137344 | bytes 3637248 | tf_op jit(solution)/shard_map/dot_general | solution.py:132
  (95 shorter events, 26.9 us)
Async XLA Ops:
  7.2 4.6 %copy-start.7 = (bf16[24,1024]{1,0:T(8,128)(2,1)S(1)}, bf16[24,1024]{1,0:T(8,128)(2,1)}, u32[]{:S(2)}) copy-start(bf16[24,1024]{1,0:T(8,128)(2,1)} %param.14) | copy-start | bytes 147460
  7.2 4.6 %copy-start.9 = (bf16[24,256]{1,0:T(8,128)(2,1)S(1)}, bf16[24,256]{1,0:T(8,128)(2,1)}, u32[]{:S(2)}) copy-start(bf16[24,256]{1,0:T(8,128)(2,1)} %param.15) | copy-start | bytes 36868
  7.2 4.8 %copy-start.6 = (bf16[16,1536]{1,0:T(8,128)(2,1)S(1)}, bf16[16,1536]{1,0:T(8,128)(2,1)}, u32[]{:S(2)}) copy-start(bf16[16,1536]{1,0:T(8,128)(2,1)} %param.17) | copy-start | bytes 147460
  7.2 5.7 %copy-start = (bf16[192,1408]{1,0:T(8,128)(2,1)S(1)}, bf16[192,1408]{1,0:T(8,128)(2,1)}, u32[]{:S(2)}) copy-start(bf16[192,1408]{1,0:T(8,128)(2,1)} %param.9) | copy-start | bytes 1622020
  7.2 5.9 %copy-start.10 = (f32[1408]{0:T(1024)S(1)}, f32[1408]{0:T(1024)}, u32[]{:S(2)}) copy-start(f32[1408]{0:T(1024)} %param.10) | copy-start | bytes 16900
  7.2 58.5 %all-gather.24.cloned.1.call-start = ((), (), s32[]{:S(2)}) async-start(), calls=%async_computation.8 | async-start | bytes 4036608 | tf_op jit(solution)/shard_map/all_gather | solution.py:89
  12.9 112.8 %all-gather.10.cloned.1.call-start = ((), (), s32[]{:S(2)}) async-start(), calls=%async_computation.1 | async-start | bytes 4866048 | tf_op jit(solution)/shard_map/all_gather | solution.py:100
  14.5 59.0 %copy-start.11 = (f32[1536]{0:T(1024)S(1)}, f32[1536]{0:T(1024)}, u32[]{:S(2)}) copy-start(f32[1536]{0:T(1024)} %param.12) | copy-start | bytes 18436
  14.5 120.9 %all-gather.12.cloned.1.call-start = ((), (), s32[]{:S(2)}) async-start(), calls=%async_computation.2 | async-start | bytes 2457600 | tf_op jit(solution)/shard_map/all_gather | solution.py:31
  73.4 90.7 %all-gather.14.cloned.1.call-start = ((), (), s32[]{:S(2)}) async-start(), calls=%async_computation.3 | async-start | bytes 5898240 | tf_op jit(solution)/shard_map/all_gather | solution.py:32
  126.5 14.2 %collective-permute-start = (bf16[2,1408]{1,0:T(2,128)(2,1)S(1)}, bf16[2,1408]{1,0:T(2,128)(2,1)S(1)}, u32[]{:S(2)}, u32[]{:S(2)}) collective-permute-start(bf16[2,1408]{1,0:T(2,128)(2,1)S(1)} %get-tuple-element.15), channel_id=1, source_target_pairs={{0,8},{8,16},{16,24},{24,32},{32,40},{40,48},{48,56},{1,9},{9,17},... | collective-permute-start | bytes 16904 | tf_op jit(solution)/shard_map/ppermute | solution.py:104
  127.8 12.8 %collective-permute-start.1 = (bf16[2,1408]{1,0:T(2,128)(2,1)S(1)}, bf16[2,1408]{1,0:T(2,128)(2,1)S(1)}, u32[]{:S(2)}, u32[]{:S(2)}) collective-permute-start(bf16[2,1408]{1,0:T(2,128)(2,1)S(1)} %get-tuple-element.16), channel_id=1, source_target_pairs={{8,0},{16,8},{24,16},{32,24},{40,32},{48,40},{56,48},{9,1},{17,9},... | collective-permute-start | bytes 16904 | tf_op jit(solution)/shard_map/ppermute | solution.py:105
  135.4 2.8 slice-start.2
  135.4 3.5 %slice-start.3 = ((s8[4325376]{0:T(1024)(128)(4,1)}), s8[4194304]{0:T(1024)(128)(4,1)S(1)}, s32[]{:S(2)}) async-start(s8[4325376]{0:T(1024)(128)(4,1)} %bitcast.82), calls=%async_computation.12 | async-start | bytes 8388608
  135.4 3.6 %copy-start.5 = (bf16[1,1408,8,24]{1,3,2,0:T(8,128)(2,1)S(1)}, bf16[1,1408,8,24]{1,3,2,0:T(8,128)(2,1)}, u32[]{:S(2)}) copy-start(bf16[1,1408,8,24]{1,3,2,0:T(8,128)(2,1)} %copy.59) | copy-start | bytes 1622020
  147.3 8.5 %copy-start.12 = (f32[1536]{0:T(1024)S(1)}, f32[1536]{0:T(1024)}, u32[]{:S(2)}) copy-start(f32[1536]{0:T(1024)} %param.13) | copy-start | bytes 18436
  151.6 11.9 %all-to-all-start = ((bf16[8,96,192]{1,2,0:T(8,128)(2,1)}), bf16[8,96,192]{1,2,0:T(8,128)(2,1)S(1)}, u32[]{:S(2)}, u32[]{:S(2)}) async-start(bf16[8,96,192]{1,2,0:T(8,128)(2,1)} %copy.64), calls=%async_computation | async-start | bytes 786432 | tf_op jit(solution)/shard_map/all_to_all | solution.py:117
  155.8 33.7 %slice-start.1 = ((bf16[8,224256]{1,0:T(8,128)(2,1)}), bf16[8,24576]{1,0:T(8,128)(2,1)S(1)}, s32[]{:S(2)}) async-start(bf16[8,224256]{1,0:T(8,128)(2,1)} %reshape.114), calls=%async_computation.10 | async-start | bytes 786432 | tf_op jit(solution)/shard_map/slice | solution.py:97
  155.8 67.4 %all-gather.16.cloned.1.call-start = ((), (), s32[]{:S(2)}) async-start(), calls=%async_computation.4 | async-start | bytes 1966080 | tf_op jit(solution)/shard_map/all_gather | solution.py:31
  166.9 107.2 %copy-start.8 = (f32[8]{0:T(128)S(1)}, f32[8]{0:T(128)}, u32[]{:S(2)}) copy-start(f32[8]{0:T(128)} %param.16) | copy-start | bytes 100
  189.4 64.4 %all-gather.20.cloned.1.call-start = ((), (), s32[]{:S(2)}) async-start(), calls=%async_computation.6 | async-start | bytes 1966080 | tf_op jit(solution)/shard_map/all_gather | solution.py:31
  190.4 83.6 %all-gather.18.cloned.1.call-start = ((), (), s32[]{:S(2)}) async-start(), calls=%async_computation.5 | async-start | bytes 4718592 | tf_op jit(solution)/shard_map/all_gather | solution.py:32
  223.2 79.9 %all-gather.22.cloned.1.call-start = ((), (), s32[]{:S(2)}) async-start(), calls=%async_computation.7 | async-start | bytes 4718592 | tf_op jit(solution)/shard_map/all_gather | solution.py:32
  283.3 11.1 %copy-start.1 = (bf16[6144,256]{1,0:T(8,128)(2,1)S(1)}, bf16[6144,256]{1,0:T(8,128)(2,1)}, u32[]{:S(2)}) copy-start(bf16[6144,256]{1,0:T(8,128)(2,1)} %all-gather.18.cloned.1.call-done) | copy-start | bytes 9437188
  (4 other events, 8.3 us)
Sparse Core Ops, SparseCore 0:
  13.0 52.6 all-gather.23
  67.6 34.2 all-gather.9
  103.7 31.6 all-gather.11
  137.0 19.5 all-gather.13
  189.6 33.5 all-gather.15
  224.8 28.9 all-gather.19
  255.7 18.3 all-gather.17
  275.8 18.7 all-gather.21

commit v3 on v1

--- a/solution.py
+++ b/solution.py
@@ -30,6 +30,11 @@
 def gather_rows(block):
     inner = lax.all_gather(block, "sx", axis=0, tiled=True)
     return lax.all_gather(inner, "sz", axis=0, tiled=True)
+
+
+def sx_major(columns, nz, nx):
+    rows = columns.shape[0]
+    return columns.reshape(rows, nz, nx, -1).transpose(0, 2, 1, 3).reshape(rows, columns.shape[1])
 
 
 def attend(queries, key_block, scales):
@@ -71,12 +76,27 @@
     width = conv_weight.shape[2]
     ch_out = conv_bias.shape[0]
 
-    kernel = lax.all_gather(conv_weight, "sz", axis=2, tiled=True)
-    proj_weight = gather_rows(jnp.concatenate([query_weight, keyval_weight], axis=1))
-    out_weight = gather_rows(output_weight)
-
+    me_z = lax.axis_index("sz")
     normed = jax.nn.gelu(normalize(features.astype(jnp.float32), norm_gain)).astype(jnp.bfloat16)
     plane = lax.all_gather(normed, "sx", axis=0, tiled=True)
+
+    slots = [conv_weight]
+    for k in range(1, nz):
+        slots.append(lax.ppermute(conv_weight, "sz", [(i, (i - k) % nz) for i in range(nz)]))
+    kernel = jnp.concatenate(slots, axis=2)
+
+    q_cols = query_weight.shape[1]
+    lane = 256
+    proj_piece = jnp.concatenate([query_weight, keyval_weight], axis=1)
+    proj_n = proj_piece.size // lane
+    both = jnp.concatenate(
+        [proj_piece.reshape(proj_n, lane), output_weight.reshape(-1, lane)], axis=0
+    )
+    both_z = lax.all_gather(both, "sz", axis=0, tiled=False)
+    proj_z = both_z[:, :proj_n].reshape(nz * proj_piece.shape[0], proj_piece.shape[1])
+    out_z = both_z[:, proj_n:].reshape(nz * output_weight.shape[0], output_weight.shape[1])
+    proj_weight = lax.all_gather(proj_z, "sx", axis=0, tiled=True)
+
     plane_rows = plane.shape[0]
     forward = [(i, i + 1) for i in range(nz - 1)]
     backward = [(i + 1, i) for i in range(nz - 1)]
@@ -85,27 +105,26 @@
     padded = jnp.concatenate([low, plane, high], axis=0)
 
     bias_all = conv_bias.reshape(nz, nx, width).transpose(1, 0, 2)
-    bias = lax.dynamic_index_in_dim(bias_all, me_x, axis=0, keepdims=False).reshape(nz * width)
+    bias = lax.dynamic_index_in_dim(bias_all, me_x, axis=0, keepdims=False)
+    bias = jnp.roll(bias, -me_z, axis=0).reshape(nz * width)
     levels = convolve(padded, kernel, plane_rows) + bias[None, :]
     pooled = pool_pairs(levels).astype(jnp.bfloat16)
 
     coarse_rows = rows_here // 2
     pieces = pooled.reshape(nx, coarse_rows, nz * width)
     received = lax.all_to_all(pieces, "sx", 0, 0, tiled=False)
-    coarse = (
-        received.reshape(nx, coarse_rows, nz, width)
-        .transpose(1, 2, 0, 3)
-        .reshape(coarse_rows, ch_out)
-    )
+    received = jnp.roll(received.reshape(nx, coarse_rows, nz, width), me_z, axis=2)
+    coarse = received.transpose(1, 2, 0, 3).reshape(coarse_rows, ch_out)
 
     attn_in = normalize(coarse.astype(jnp.float32), attn_gain).astype(jnp.bfloat16)
-    proj = jnp.dot(attn_in, proj_weight, preferred_element_type=jnp.float32)
-    q_cols = query_weight.shape[1]
+    proj = jnp.dot(sx_major(attn_in, nz, nx), proj_weight, preferred_element_type=jnp.float32)
     queries = proj[:, :q_cols].astype(jnp.bfloat16)
     keyvals = proj[:, q_cols:].astype(jnp.bfloat16)
     key_block = gather_rows(keyvals)
+    key_block, out_z = lax.optimization_barrier((key_block, out_z))
+    out_weight = lax.all_gather(out_z, "sx", axis=0, tiled=True)
     context = attend(queries, key_block, head_scale)
-    projected = jnp.dot(context, out_weight, preferred_element_type=jnp.float32)
+    projected = jnp.dot(sx_major(context, nz, nx), out_weight, preferred_element_type=jnp.float32)
     return (coarse, projected.astype(jnp.bfloat16))
 
 

time: 263 us -> 246 us (0.935)
  blocking collectives: 62.5 us -> 41.6 us
  waiting for transfers between devices: 119 us -> 98.2 us
  starting transfers between devices: 4.67 us -> 22.6 us
  local copies, waits for them, and re-layouts: 9.68 us -> 16.3 us
    ppermute x0 -> x7, waiting for transfers between devices: none -> 51 us  [shards(): lax.ppermute(conv_weight, 'sz', [(i, (i - k) % nz) for i in range(nz)])]
    all_gather x1 -> x2, waiting for transfers between devices: 31.1 us -> 0.04 us  [the longest x1 0.02 us: shards(): proj_weight = lax.all_gather(proj_z, 'sx', axis=0, tiled=True)]
    all_gather x3 -> x1, blocking collectives: 46.3 us -> 15.3 us  [gather_rows(): inner = lax.all_gather(block, 'sx', axis=0, tiled=True)]
    all_gather x3 -> x1, waiting for transfers between devices: 67.8 us -> 39.6 us  [gather_rows(): return lax.all_gather(inner, 'sz', axis=0, tiled=True)]
    all_gather x0 -> x1, blocking collectives: none -> 26.2 us  [shards(): both_z = lax.all_gather(both, 'sz', axis=0, tiled=False)]
    all_gather x1, waiting for transfers between devices: 19.7 us -> 0.01 us  [shards(): plane = lax.all_gather(normed, 'sx', axis=0, tiled=True)]
    all_to_all x1 -> x0, blocking collectives: 16.2 us -> none  [shards(): received = lax.all_to_all(pieces, 'sx', 0, 0, tiled=False)]
    ppermute x0 -> x7, starting transfers between devices: none -> 11.7 us  [shards(): lax.ppermute(conv_weight, 'sz', [(i, (i - k) % nz) for i in range(nz)])]
  transfers between devices with their start and end apart: 7 -> 14, of which waited for: 5 -> 6; matrix products, arithmetic and copies ran while one was open for 20% -> 24% of each run, Pallas kernels for 0% -> 0%
where the time goes in v3:
time: 246 us; the launch traced here: 245 us
  waiting for transfers between devices  98.2 us (40%)
  blocking collectives  41.6 us (17%)
  matrix products  34.3 us (14%)
  starting transfers between devices  22.6 us (9%)
  other arithmetic  18 us (7%)
  local copies, waits for them, and re-layouts  16.3 us (7%)
  between operations  14.1 us (6%)
    ppermute x7, waiting for transfers between devices, shards(): lax.ppermute(conv_weight, 'sz', [(i, (i - k) % nz) for i in range(nz)])  51 us
    all_gather x1, waiting for transfers between devices, gather_rows(): return lax.all_gather(inner, 'sz', axis=0, tiled=True)  39.6 us
    all_gather x1, blocking collectives, shards(): both_z = lax.all_gather(both, 'sz', axis=0, tiled=False)  26.2 us
    all_gather x1, blocking collectives, gather_rows(): inner = lax.all_gather(block, 'sx', axis=0, tiled=True)  15.3 us
    ppermute x7, starting transfers between devices, shards(): lax.ppermute(conv_weight, 'sz', [(i, (i - k) % nz) for i in range(nz)])  11.7 us
    dot_general x1, matrix products, attend(): jnp.einsum('hqk,kd->hqd', expon.astype(jnp.bfloat16), value_part, preferr...  10.7 us
    reduce_sum x1, other arithmetic, attend(): total = jnp.sum(expon, axis=2)  10.7 us
    dot_general x1, matrix products, attend(): jnp.einsum('qhd,kd->hqk', shaped, key_part, preferred_element_type=jnp.fl...  9.28 us
  transfers between devices with their start and end apart: 14, of which 6 were waited for; matrix products, arithmetic and copies ran while one was open for 24% of the time, Pallas kernels for 0%

profile of v3, /device:TPU:1, one launch (start us, length us, event | category | flops | bytes accessed | tf_op | source)
XLA Modules:
  0.0 245.1 jit_solution(2216220209576373742)
XLA Ops:
  8.5 2.4 fusion.43
  12.7 26.2 %all-gather = bf16[1728,256]{1,0:T(8,128)(2,1)S(1)} all-gather(bf16[216,256]{1,0:T(8,128)(2,1)S(1)} %pad_maximum_fusion.2), channel_id=2, replica_groups=mesh['dp'=4,'sz'=8,'sx'=8] {'sz'}, dimensions={0}, use_global_device_ids=true | all-gather | bytes 995328 | tf_op jit(solution)/shard_map/all_gather | solution.py:95
  40.2 1.9 collective-permute-start.1
  42.1 2.8 %collective-permute-start.3 = (bf16[5,1408,24]{1,2,0:T(8,128)(2,1)S(1)}, bf16[5,1408,24]{1,2,0:T(8,128)(2,1)S(1)}, u32[]{:S(2)}, u32[]{:S(2)}) collective-permute-start(bf16[5,1408,24]{1,2,0:T(8,128)(2,1)S(1)} %copy-done), channel_id=1, source_target_pairs={{0,40},{8,48},{16,56},{24,0},{32,8},{40,16},{48,24},{56,32},{1,41}... | collective-permute-start | bytes 1013768 | tf_op jit(solution)/shard_map/ppermute | solution.py:85
  44.9 2.7 %collective-permute-start.4 = (bf16[5,1408,24]{1,2,0:T(8,128)(2,1)S(1)}, bf16[5,1408,24]{1,2,0:T(8,128)(2,1)S(1)}, u32[]{:S(2)}, u32[]{:S(2)}) collective-permute-start(bf16[5,1408,24]{1,2,0:T(8,128)(2,1)S(1)} %copy-done), channel_id=1, source_target_pairs={{0,32},{8,40},{16,48},{24,56},{32,0},{40,8},{48,16},{56,24},{1,33}... | collective-permute-start | bytes 1013768 | tf_op jit(solution)/shard_map/ppermute | solution.py:85
  49.6 2.1 collective-permute-start.6
  52.5 4.4 %collective-permute-done.2 = bf16[5,1408,24]{1,2,0:T(8,128)(2,1)S(1)} collective-permute-done((bf16[5,1408,24]{1,2,0:T(8,128)(2,1)S(1)}, bf16[5,1408,24]{1,2,0:T(8,128)(2,1)S(1)}, u32[]{:S(2)}, u32[]{:S(2)}) %collective-permute-start.2) | collective-permute-done | bytes 337952 | tf_op jit(solution)/shard_map/ppermute | solution.py:85
  58.8 16.1 %collective-permute-done.3 = bf16[5,1408,24]{1,2,0:T(8,128)(2,1)S(1)} collective-permute-done((bf16[5,1408,24]{1,2,0:T(8,128)(2,1)S(1)}, bf16[5,1408,24]{1,2,0:T(8,128)(2,1)S(1)}, u32[]{:S(2)}, u32[]{:S(2)}) %collective-permute-start.3) | collective-permute-done | bytes 337952 | tf_op jit(solution)/shard_map/ppermute | solution.py:85
  76.4 14.2 %collective-permute-done.5 = bf16[5,1408,24]{1,2,0:T(8,128)(2,1)S(1)} collective-permute-done((bf16[5,1408,24]{1,2,0:T(8,128)(2,1)S(1)}, bf16[5,1408,24]{1,2,0:T(8,128)(2,1)S(1)}, u32[]{:S(2)}, u32[]{:S(2)}) %collective-permute-start.5) | collective-permute-done | bytes 337952 | tf_op jit(solution)/shard_map/ppermute | solution.py:85
  92.2 16.3 %collective-permute-done.7 = bf16[5,1408,24]{1,2,0:T(8,128)(2,1)S(1)} collective-permute-done((bf16[5,1408,24]{1,2,0:T(8,128)(2,1)S(1)}, bf16[5,1408,24]{1,2,0:T(8,128)(2,1)S(1)}, u32[]{:S(2)}, u32[]{:S(2)}) %collective-permute-start.7) | collective-permute-done | bytes 337952 | tf_op jit(solution)/shard_map/ppermute | solution.py:85
  111.3 4.4 %collective-permute-start = (bf16[2,1408]{1,0:T(2,128)(2,1)S(1)}, bf16[2,1408]{1,0:T(2,128)(2,1)S(1)}, u32[]{:S(2)}, u32[]{:S(2)}) collective-permute-start(bf16[2,1408]{1,0:T(2,128)(2,1)S(1)} %get-tuple-element.16), channel_id=1, source_target_pairs={{0,8},{8,16},{16,24},{24,32},{32,40},{40,48},{48,56},{1,9},{9,17},... | collective-permute-start | bytes 16904 | tf_op jit(solution)/shard_map/ppermute | solution.py:103
  115.7 2.5 %constant_dynamic-update-slice_fusion.9 = bf16[1538,1408]{1,0:T(8,128)(2,1)S(1)} fusion(bf16[1536,1408]{1,0:T(8,128)(2,1)} %all-gather.6.cloned.1.call-done), kind=kLoop, calls=%fused_computation.71 | loop fusion | bytes 8650752
  121.6 1.6 fusion.10
  124.8 1.8 fusion.26
  127.3 2.2 reduce_max.18
  130.9 5.1 %all-to-all-start = ((bf16[8,96,192]{1,2,0:T(8,128)(2,1)}), bf16[8,96,192]{1,2,0:T(8,128)(2,1)S(1)}, u32[]{:S(2)}, u32[]{:S(2)}) async-start(bf16[8,96,192]{1,2,0:T(8,128)(2,1)} %copy.37), calls=%async_computation | async-start | bytes 786432 | tf_op jit(solution)/shard_map/all_to_all | solution.py:115
  136.2 7.6 %all-to-all-done = bf16[8,96,192]{1,2,0:T(8,128)(2,1)S(1)} async-done(((bf16[8,96,192]{1,2,0:T(8,128)(2,1)}), bf16[8,96,192]{1,2,0:T(8,128)(2,1)S(1)}, u32[]{:S(2)}, u32[]{:S(2)}) %all-to-all-start) | async-done | bytes 294944 | tf_op jit(solution)/shard_map/all_to_all | solution.py:115
  144.4 2.8 %convolution_convert_fusion.1 = bf16[96,1280]{1,0:T(8,128)(2,1)S(1)} fusion(bf16[96,1536]{0,1:T(8,128)(2,1)S(1)} %bitcast.88, bf16[1536,1280]{1,0:T(8,128)(2,1)} %all-gather.8.cloned.1.call-done), kind=kOutput, calls=%fused_computation.24 | convolution fusion | flops 377610240 | bytes 4472832 | tf_op jit(solution)/shard_map/dot_general | solution.py:120
  147.2 15.3 %all_gather.25 = bf16[768,256]{1,0:T(8,128)(2,1)} all-gather(bf16[96,256]{1,0:T(8,128)(2,1)S(1)} %slice.86), channel_id=1, replica_groups=mesh['dp'=4,'sz'=8,'sx'=8] {'sx'}, dimensions={0}, use_global_device_ids=true | all-gather | bytes 442368 | tf_op jit(solution)/shard_map/all_gather | solution.py:31
  163.8 39.6 %all-gather.10.cloned.1.call-done = bf16[6144,256]{1,0:T(8,128)(2,1)} async-done(((bf16[768,256]{1,0:T(8,128)(2,1)}), bf16[6144,256]{1,0:T(8,128)(2,1)}) %all-gather.10.cloned.1.call-update) | async-done | bytes 3145744 | tf_op jit(solution)/shard_map/all_gather | solution.py:32
  204.3 9.3 %bitcast_reduce_fusion = (f32[8,96]{1,0:T(8,128)S(1)}, f32[6144,96,8]{0,1,2:T(8,128)}) fusion(f32[8]{0:T(128)S(1)} %copy-done.2, bf16[6144,256]{1,0:T(8,128)(2,1)} %all-gather.10.cloned.1.call-done, bf16[96,1280]{1,0:T(8,128)(2,1)S(1)} %convolution_convert_fusion.1), kind=kOutput, calls=%fused_computation.1 | convolution fusion | flops 1222114560 | bytes 20647424 | tf_op jit(solution)/shard_map/qhd,kd->hqk/dot_general | solution.py:47
  213.6 10.7 %fusion.1 = f32[8,96]{1,0:T(8,128)S(1)} fusion(f32[6144,96,8]{0,1,2:T(8,128)} %get-tuple-element.19, f32[8,96]{1,0:T(8,128)S(1)} %get-tuple-element.18, f32[8]{0:T(128)S(1)} %copy-done.2), kind=kLoop, calls=%fused_computation.4 | loop fusion | flops 18873600 | bytes 18880544 | tf_op jit(solution)/shard_map/reduce_sum | solution.py:53
  224.3 10.7 %fusion.54 = bf16[96,8,128]{2,0,1:T(8,128)(2,1)S(1)} fusion(bf16[6144,256]{1,0:T(8,128)(2,1)} %all-gather.10.cloned.1.call-done, f32[6144,96,8]{0,1,2:T(8,128)} %get-tuple-element.19, f32[8,96]{1,0:T(8,128)S(1)} %get-tuple-element.18, f32[8]{0:T(128)S(1)} %copy-done.2, f32[96,8]{0,1:T(8,128)S(1)} %bitcast.94), kind=kOutput, calls=%fused_computation.45 | convolution fusion | flops 1227030528 | bytes 20650016 | tf_op jit(solution)/shard_map/hqk,kd->hqd/dot_general | solution.py:54
  235.2 3.3 %convolution_convert_fusion = bf16[96,1536]{1,0:T(8,128)(2,1)} fusion(bf16[96,1024]{0,1:T(8,128)(2,1)S(1)} %bitcast.90, bf16[1024,1536]{1,0:T(8,128)(2,1)} %all-gather.12.cloned.1.call-done), kind=kOutput, calls=%fused_computation.23 | convolution fusion | flops 302137344 | bytes 3637248 | tf_op jit(solution)/shard_map/dot_general | solution.py:127
  (77 shorter events, 24.9 us)
Async XLA Ops:
  7.2 33.0 %copy-start = (bf16[5,1408,24]{1,2,0:T(8,128)(2,1)S(1)}, bf16[5,1408,24]{1,2,0:T(8,128)(2,1)}, u32[]{:S(2)}) copy-start(bf16[5,1408,24]{1,2,0:T(8,128)(2,1)} %param.11) | copy-start | bytes 1013764
  7.2 41.5 %copy-start.3 = (f32[1536]{0:T(1024)S(1)}, f32[1536]{0:T(1024)}, u32[]{:S(2)}) copy-start(f32[1536]{0:T(1024)} %param.12) | copy-start | bytes 18436
  7.2 102.0 %all-gather.6.cloned.1.call-start = ((), (), s32[]{:S(2)}) async-start(), calls=%async_computation.1 | async-start | bytes 4866048 | tf_op jit(solution)/shard_map/all_gather | solution.py:81
  10.9 133.5 %all-gather.8.cloned.1.call-start = ((), (), s32[]{:S(2)}) async-start(), calls=%async_computation.2 | async-start | bytes 4423680 | tf_op jit(solution)/shard_map/all_gather | solution.py:98
  40.2 9.4 %collective-permute-start.1 = (bf16[5,1408,24]{1,2,0:T(8,128)(2,1)S(1)}, bf16[5,1408,24]{1,2,0:T(8,128)(2,1)S(1)}, u32[]{:S(2)}, u32[]{:S(2)}) collective-permute-start(bf16[5,1408,24]{1,2,0:T(8,128)(2,1)S(1)} %copy-done), channel_id=1, source_target_pairs={{0,56},{8,0},{16,8},{24,16},{32,24},{40,32},{48,40},{56,48},{1,57}... | collective-permute-start | bytes 1013768 | tf_op jit(solution)/shard_map/ppermute | solution.py:85
  42.1 14.8 %collective-permute-start.2 = (bf16[5,1408,24]{1,2,0:T(8,128)(2,1)S(1)}, bf16[5,1408,24]{1,2,0:T(8,128)(2,1)S(1)}, u32[]{:S(2)}, u32[]{:S(2)}) collective-permute-start(bf16[5,1408,24]{1,2,0:T(8,128)(2,1)S(1)} %copy-done), channel_id=1, source_target_pairs={{0,48},{8,56},{16,0},{24,8},{32,16},{40,24},{48,32},{56,40},{1,49}... | collective-permute-start | bytes 1013768 | tf_op jit(solution)/shard_map/ppermute | solution.py:85
  42.1 32.8 %collective-permute-start.3 = (bf16[5,1408,24]{1,2,0:T(8,128)(2,1)S(1)}, bf16[5,1408,24]{1,2,0:T(8,128)(2,1)S(1)}, u32[]{:S(2)}, u32[]{:S(2)}) collective-permute-start(bf16[5,1408,24]{1,2,0:T(8,128)(2,1)S(1)} %copy-done), channel_id=1, source_target_pairs={{0,40},{8,48},{16,56},{24,0},{32,8},{40,16},{48,24},{56,32},{1,41}... | collective-permute-start | bytes 1013768 | tf_op jit(solution)/shard_map/ppermute | solution.py:85
  44.9 30.8 %collective-permute-start.4 = (bf16[5,1408,24]{1,2,0:T(8,128)(2,1)S(1)}, bf16[5,1408,24]{1,2,0:T(8,128)(2,1)S(1)}, u32[]{:S(2)}, u32[]{:S(2)}) collective-permute-start(bf16[5,1408,24]{1,2,0:T(8,128)(2,1)S(1)} %copy-done), channel_id=1, source_target_pairs={{0,32},{8,40},{16,48},{24,56},{32,0},{40,8},{48,16},{56,24},{1,33}... | collective-permute-start | bytes 1013768 | tf_op jit(solution)/shard_map/ppermute | solution.py:85
  47.6 43.0 %collective-permute-start.5 = (bf16[5,1408,24]{1,2,0:T(8,128)(2,1)S(1)}, bf16[5,1408,24]{1,2,0:T(8,128)(2,1)S(1)}, u32[]{:S(2)}, u32[]{:S(2)}) collective-permute-start(bf16[5,1408,24]{1,2,0:T(8,128)(2,1)S(1)} %copy-done), channel_id=1, source_target_pairs={{0,24},{8,32},{16,40},{24,48},{32,56},{40,0},{48,8},{56,16},{1,25}... | collective-permute-start | bytes 1013768 | tf_op jit(solution)/shard_map/ppermute | solution.py:85
  49.6 41.8 %collective-permute-start.6 = (bf16[5,1408,24]{1,2,0:T(8,128)(2,1)S(1)}, bf16[5,1408,24]{1,2,0:T(8,128)(2,1)S(1)}, u32[]{:S(2)}, u32[]{:S(2)}) collective-permute-start(bf16[5,1408,24]{1,2,0:T(8,128)(2,1)S(1)} %copy-done), channel_id=1, source_target_pairs={{0,16},{8,24},{16,32},{24,40},{32,48},{40,56},{48,0},{56,8},{1,17}... | collective-permute-start | bytes 1013768 | tf_op jit(solution)/shard_map/ppermute | solution.py:85
  56.9 51.5 %collective-permute-start.7 = (bf16[5,1408,24]{1,2,0:T(8,128)(2,1)S(1)}, bf16[5,1408,24]{1,2,0:T(8,128)(2,1)S(1)}, u32[]{:S(2)}, u32[]{:S(2)}) collective-permute-start(bf16[5,1408,24]{1,2,0:T(8,128)(2,1)S(1)} %copy-done), channel_id=1, source_target_pairs={{0,8},{8,16},{16,24},{24,32},{32,40},{40,48},{48,56},{56,0},{1,9},... | collective-permute-start | bytes 1013768 | tf_op jit(solution)/shard_map/ppermute | solution.py:85
  110.0 9.9 %collective-permute-start.8 = (bf16[2,1408]{1,0:T(2,128)(2,1)S(1)}, bf16[2,1408]{1,0:T(2,128)(2,1)S(1)}, u32[]{:S(2)}, u32[]{:S(2)}) collective-permute-start(bf16[2,1408]{1,0:T(2,128)(2,1)S(1)} %get-tuple-element.17), channel_id=1, source_target_pairs={{8,0},{16,8},{24,16},{32,24},{40,32},{48,40},{56,48},{9,1},{17,9},... | collective-permute-start | bytes 16904 | tf_op jit(solution)/shard_map/ppermute | solution.py:104
  111.3 7.0 %slice-start = ((s8[4325376]{0:T(1024)(128)(4,1)}), s8[4194304]{0:T(1024)(128)(4,1)S(1)}, s32[]{:S(2)}) async-start(s8[4325376]{0:T(1024)(128)(4,1)} %bitcast.82), calls=%async_computation.5 | async-start | bytes 8388608
  111.3 7.0 %slice-start.1 = ((s8[4325376]{0:T(1024)(128)(4,1)}), s8[131072]{0:T(1024)(128)(4,1)S(1)}, s32[]{:S(2)}) async-start(s8[4325376]{0:T(1024)(128)(4,1)} %bitcast.82), calls=%async_computation.6 | async-start | bytes 262144
  111.3 7.0 %copy-start.1 = (bf16[5,1408,192]{1,2,0:T(8,128)(2,1)S(1)}, bf16[5,1408,192]{1,2,0:T(8,128)(2,1)}, u32[]{:S(2)}) copy-start(bf16[5,1408,192]{1,2,0:T(8,128)(2,1)} %constant_dynamic-update-slice_fusion) | copy-start | bytes 8110084
  111.3 8.6 %collective-permute-start = (bf16[2,1408]{1,0:T(2,128)(2,1)S(1)}, bf16[2,1408]{1,0:T(2,128)(2,1)S(1)}, u32[]{:S(2)}, u32[]{:S(2)}) collective-permute-start(bf16[2,1408]{1,0:T(2,128)(2,1)S(1)} %get-tuple-element.16), channel_id=1, source_target_pairs={{0,8},{8,16},{16,24},{24,32},{32,40},{40,48},{48,56},{1,9},{9,17},... | collective-permute-start | bytes 16904 | tf_op jit(solution)/shard_map/ppermute | solution.py:103
  126.9 9.2 %copy-start.4 = (f32[1536]{0:T(1024)S(1)}, f32[1536]{0:T(1024)}, u32[]{:S(2)}) copy-start(f32[1536]{0:T(1024)} %param.13) | copy-start | bytes 18436
  130.9 12.8 %all-to-all-start = ((bf16[8,96,192]{1,2,0:T(8,128)(2,1)}), bf16[8,96,192]{1,2,0:T(8,128)(2,1)S(1)}, u32[]{:S(2)}, u32[]{:S(2)}) async-start(bf16[8,96,192]{1,2,0:T(8,128)(2,1)} %copy.37), calls=%async_computation | async-start | bytes 786432 | tf_op jit(solution)/shard_map/all_to_all | solution.py:115
  136.0 67.3 %all-gather.10.cloned.1.call-start = ((), (), s32[]{:S(2)}) async-start(), calls=%async_computation.3 | async-start | bytes 3538944 | tf_op jit(solution)/shard_map/all_gather | solution.py:32
  147.2 57.1 %copy-start.2 = (f32[8]{0:T(128)S(1)}, f32[8]{0:T(128)}, u32[]{:S(2)}) copy-start(f32[8]{0:T(128)} %param.16) | copy-start | bytes 100
  162.6 72.7 %all-gather.12.cloned.1.call-start = ((), (), s32[]{:S(2)}) async-start(), calls=%async_computation.4 | async-start | bytes 3538944 | tf_op jit(solution)/shard_map/all_gather | solution.py:125
Sparse Core Ops, SparseCore 0:
  11.0 39.2 all-gather.5
  52.2 33.4 all-gather.7
  162.7 40.6 all-gather.9
  205.0 29.7 all-gather.11

commit v4 on v3

--- a/solution.py
+++ b/solution.py
@@ -32,9 +32,10 @@
     return lax.all_gather(inner, "sz", axis=0, tiled=True)
 
 
-def sx_major(columns, nz, nx):
+def sx_major(columns, nz, nx, me_z):
     rows = columns.shape[0]
-    return columns.reshape(rows, nz, nx, -1).transpose(0, 2, 1, 3).reshape(rows, columns.shape[1])
+    split = jnp.roll(columns.reshape(rows, nz, nx, -1), -me_z, axis=1)
+    return split.transpose(0, 2, 1, 3).reshape(rows, columns.shape[1])
 
 
 def attend(queries, key_block, scales):
@@ -80,11 +81,6 @@
     normed = jax.nn.gelu(normalize(features.astype(jnp.float32), norm_gain)).astype(jnp.bfloat16)
     plane = lax.all_gather(normed, "sx", axis=0, tiled=True)
 
-    slots = [conv_weight]
-    for k in range(1, nz):
-        slots.append(lax.ppermute(conv_weight, "sz", [(i, (i - k) % nz) for i in range(nz)]))
-    kernel = jnp.concatenate(slots, axis=2)
-
     q_cols = query_weight.shape[1]
     lane = 256
     proj_piece = jnp.concatenate([query_weight, keyval_weight], axis=1)
@@ -92,7 +88,18 @@
     both = jnp.concatenate(
         [proj_piece.reshape(proj_n, lane), output_weight.reshape(-1, lane)], axis=0
     )
-    both_z = lax.all_gather(both, "sz", axis=0, tiled=False)
+    up = [(i, (i - 1) % nz) for i in range(nz)]
+    down = [(i, (i + 1) % nz) for i in range(nz)]
+    slots = {0: (conv_weight, both)}
+    ahead = behind = slots[0]
+    for step in range(1, nz // 2 + 1):
+        ahead = lax.ppermute(ahead, "sz", up)
+        slots[step % nz] = ahead
+        if step <= (nz - 1) // 2:
+            behind = lax.ppermute(behind, "sz", down)
+            slots[(-step) % nz] = behind
+    kernel = jnp.concatenate([slots[k][0] for k in range(nz)], axis=2)
+    both_z = jnp.stack([slots[k][1] for k in range(nz)])
     proj_z = both_z[:, :proj_n].reshape(nz * proj_piece.shape[0], proj_piece.shape[1])
     out_z = both_z[:, proj_n:].reshape(nz * output_weight.shape[0], output_weight.shape[1])
     proj_weight = lax.all_gather(proj_z, "sx", axis=0, tiled=True)
@@ -117,14 +124,14 @@
     coarse = received.transpose(1, 2, 0, 3).reshape(coarse_rows, ch_out)
 
     attn_in = normalize(coarse.astype(jnp.float32), attn_gain).astype(jnp.bfloat16)
-    proj = jnp.dot(sx_major(attn_in, nz, nx), proj_weight, preferred_element_type=jnp.float32)
+    proj = jnp.dot(sx_major(attn_in, nz, nx, me_z), proj_weight, preferred_element_type=jnp.float32)
     queries = proj[:, :q_cols].astype(jnp.bfloat16)
     keyvals = proj[:, q_cols:].astype(jnp.bfloat16)
     key_block = gather_rows(keyvals)
     key_block, out_z = lax.optimization_barrier((key_block, out_z))
     out_weight = lax.all_gather(out_z, "sx", axis=0, tiled=True)
     context = attend(queries, key_block, head_scale)
-    projected = jnp.dot(sx_major(context, nz, nx), out_weight, preferred_element_type=jnp.float32)
+    projected = jnp.dot(sx_major(context, nz, nx, me_z), out_weight, preferred_element_type=jnp.float32)
     return (coarse, projected.astype(jnp.bfloat16))
 
 

time: 246 us -> 211 us (0.86)
  waiting for transfers between devices: 98.2 us -> 69.7 us
  blocking collectives: 41.6 us -> 15.1 us
  starting transfers between devices: 22.6 us -> 41.4 us
    ppermute x7 -> x14, waiting for transfers between devices: 51 us -> 23.7 us  [the longest x8 20.9 us: shards(): ahead = lax.ppermute(ahead, 'sz', up)]
    all_gather x1 -> x0, blocking collectives: 26.2 us -> none  [shards(): both_z = lax.all_gather(both, 'sz', axis=0, tiled=False)]
    ppermute x7 -> x14, starting transfers between devices: 11.7 us -> 23.5 us  [the longest x8 23.4 us: shards(): ahead = lax.ppermute(ahead, 'sz', up)]
    all_to_all x1, starting transfers between devices: 5.1 us -> 11.9 us  [shards(): received = lax.all_to_all(pieces, 'sx', 0, 0, tiled=False)]
    unnamed x23 -> x29, local copies, waits for them, and re-layouts: 8.86 us -> 9.06 us
  transfers between devices with their start and end apart: 14 -> 21, of which waited for: 6 -> 11; matrix products, arithmetic and copies ran while one was open for 24% -> 28% of each run, Pallas kernels for 0% -> 0%
where the time goes in v4:
time: 211 us; the launch traced here: 210 us
  waiting for transfers between devices  69.7 us (33%)
  starting transfers between devices  41.4 us (20%)
  matrix products  34.1 us (16%)
  other arithmetic  18.4 us (9%)
  local copies, waits for them, and re-layouts  17.1 us (8%)
  blocking collectives  15.1 us (7%)
  between operations  14.2 us (7%)
    all_gather x1, waiting for transfers between devices, gather_rows(): return lax.all_gather(inner, 'sz', axis=0, tiled=True)  38.3 us
    ppermute x8, starting transfers between devices, shards(): ahead = lax.ppermute(ahead, 'sz', up)  23.4 us
    ppermute x8, waiting for transfers between devices, shards(): ahead = lax.ppermute(ahead, 'sz', up)  20.9 us
    all_gather x1, blocking collectives, gather_rows(): inner = lax.all_gather(block, 'sx', axis=0, tiled=True)  15.1 us
    all_to_all x1, starting transfers between devices, shards(): received = lax.all_to_all(pieces, 'sx', 0, 0, tiled=False)  11.9 us
    dot_general x1, matrix products, attend(): jnp.einsum('hqk,kd->hqd', expon.astype(jnp.bfloat16), value_part, preferr...  10.7 us
    reduce_sum x1, other arithmetic, attend(): total = jnp.sum(expon, axis=2)  10.7 us
    dot_general x1, matrix products, attend(): jnp.einsum('qhd,kd->hqk', shaped, key_part, preferred_element_type=jnp.fl...  9.25 us
  transfers between devices with their start and end apart: 21, of which 11 were waited for; matrix products, arithmetic and copies ran while one was open for 28% of the time, Pallas kernels for 0%

profile of v4, /device:TPU:1, one launch (start us, length us, event | category | flops | bytes accessed | tf_op | source)
XLA Modules:
  0.0 210.1 jit_solution(12379791498890986252)
XLA Ops:
  8.5 2.4 %fusion.43 = bf16[192,1408]{1,0:T(8,128)(2,1)} fusion(bf16[192,1408]{1,0:T(8,128)(2,1)} %param.9, f32[1408]{0:T(1024)} %param.10, f32[192]{0:T(256)S(1)} %add_rsqrt_fusion), kind=kLoop, calls=%fused_computation.38 | loop fusion | flops 3244032 | bytes 1087744 | tf_op jit(solution)/shard_map/convert_element_type | solution.py:81
  10.9 6.5 %collective-permute-start.1 = (bf16[5,1408,24]{1,2,0:T(8,128)(2,1)}, bf16[5,1408,24]{1,2,0:T(8,128)(2,1)S(1)}, u32[]{:S(2)}, u32[]{:S(2)}) collective-permute-start(bf16[5,1408,24]{1,2,0:T(8,128)(2,1)} %param.11), channel_id=1, source_target_pairs={{0,56},{8,0},{16,8},{24,16},{32,24},{40,32},{48,40},{56,48},{1,57}... | collective-permute-start | bytes 1013768 | tf_op jit(solution)/shard_map/ppermute | solution.py:96
  19.2 2.7 %collective-permute-start.9 = (bf16[216,256]{1,0:T(8,128)(2,1)S(1)}, bf16[216,256]{1,0:T(8,128)(2,1)S(1)}, u32[]{:S(2)}, u32[]{:S(2)}) collective-permute-start(bf16[216,256]{1,0:T(8,128)(2,1)S(1)} %constant_dynamic-update-slice_fusion.10), channel_id=1, source_target_pairs={{0,56},{8,0},{16,8},{24,16},{32,24},{40,32},{48,40},{56,48},{1,57}... | collective-permute-start | bytes 331784 | tf_op jit(solution)/shard_map/ppermute | solution.py:96
  22.8 3.8 %collective-permute-done.9 = bf16[216,256]{1,0:T(8,128)(2,1)S(1)} collective-permute-done((bf16[216,256]{1,0:T(8,128)(2,1)S(1)}, bf16[216,256]{1,0:T(8,128)(2,1)S(1)}, u32[]{:S(2)}, u32[]{:S(2)}) %collective-permute-start.9) | collective-permute-done | bytes 110624 | tf_op jit(solution)/shard_map/ppermute | solution.py:96
  26.6 3.4 %collective-permute-start.10 = (bf16[216,256]{1,0:T(8,128)(2,1)S(1)}, bf16[216,256]{1,0:T(8,128)(2,1)S(1)}, u32[]{:S(2)}, u32[]{:S(2)}) collective-permute-start(bf16[216,256]{1,0:T(8,128)(2,1)S(1)} %collective-permute-done.9), channel_id=1, source_target_pairs={{0,56},{8,0},{16,8},{24,16},{32,24},{40,32},{48,40},{56,48},{1,57}... | collective-permute-start | bytes 331784 | tf_op jit(solution)/shard_map/ppermute | solution.py:96
  31.8 3.5 %collective-permute-start.11 = (bf16[216,256]{1,0:T(8,128)(2,1)S(1)}, bf16[216,256]{1,0:T(8,128)(2,1)S(1)}, u32[]{:S(2)}, u32[]{:S(2)}) collective-permute-start(bf16[216,256]{1,0:T(8,128)(2,1)S(1)} %collective-permute-done.10), channel_id=1, source_target_pairs={{0,56},{8,0},{16,8},{24,16},{32,24},{40,32},{48,40},{56,48},{1,57}... | collective-permute-start | bytes 331784 | tf_op jit(solution)/shard_map/ppermute | solution.py:96
  37.0 3.5 %collective-permute-start.12 = (bf16[216,256]{1,0:T(8,128)(2,1)S(1)}, bf16[216,256]{1,0:T(8,128)(2,1)S(1)}, u32[]{:S(2)}, u32[]{:S(2)}) collective-permute-start(bf16[216,256]{1,0:T(8,128)(2,1)S(1)} %collective-permute-done.11), channel_id=1, source_target_pairs={{0,56},{8,0},{16,8},{24,16},{32,24},{40,32},{48,40},{56,48},{1,57}... | collective-permute-start | bytes 331784 | tf_op jit(solution)/shard_map/ppermute | solution.py:96
  44.3 4.8 %collective-permute-done.2 = bf16[5,1408,24]{1,2,0:T(8,128)(2,1)S(1)} collective-permute-done((bf16[5,1408,24]{1,2,0:T(8,128)(2,1)S(1)}, bf16[5,1408,24]{1,2,0:T(8,128)(2,1)S(1)}, u32[]{:S(2)}, u32[]{:S(2)}) %collective-permute-start.2) | collective-permute-done | bytes 337952 | tf_op jit(solution)/shard_map/ppermute | solution.py:96
  51.6 4.0 %collective-permute-done.3 = bf16[5,1408,24]{1,2,0:T(8,128)(2,1)S(1)} collective-permute-done((bf16[5,1408,24]{1,2,0:T(8,128)(2,1)S(1)}, bf16[5,1408,24]{1,2,0:T(8,128)(2,1)S(1)}, u32[]{:S(2)}, u32[]{:S(2)}) %collective-permute-start.3) | collective-permute-done | bytes 337952 | tf_op jit(solution)/shard_map/ppermute | solution.py:96
  55.6 2.2 %collective-permute-start.4 = (bf16[5,1408,24]{1,2,0:T(8,128)(2,1)S(1)}, bf16[5,1408,24]{1,2,0:T(8,128)(2,1)S(1)}, u32[]{:S(2)}, u32[]{:S(2)}) collective-permute-start(bf16[5,1408,24]{1,2,0:T(8,128)(2,1)S(1)} %collective-permute-done.3), channel_id=1, source_target_pairs={{0,56},{8,0},{16,8},{24,16},{32,24},{40,32},{48,40},{56,48},{1,57}... | collective-permute-start | bytes 1013768 | tf_op jit(solution)/shard_map/ppermute | solution.py:96
  59.4 3.3 %collective-permute-done.4 = bf16[5,1408,24]{1,2,0:T(8,128)(2,1)S(1)} collective-permute-done((bf16[5,1408,24]{1,2,0:T(8,128)(2,1)S(1)}, bf16[5,1408,24]{1,2,0:T(8,128)(2,1)S(1)}, u32[]{:S(2)}, u32[]{:S(2)}) %collective-permute-start.4) | collective-permute-done | bytes 337952 | tf_op jit(solution)/shard_map/ppermute | solution.py:96
  63.4 2.7 %collective-permute-done.7 = bf16[5,1408,24]{1,2,0:T(8,128)(2,1)S(1)} collective-permute-done((bf16[5,1408,24]{1,2,0:T(8,128)(2,1)S(1)}, bf16[5,1408,24]{1,2,0:T(8,128)(2,1)S(1)}, u32[]{:S(2)}, u32[]{:S(2)}) %collective-permute-start.7) | collective-permute-done | bytes 337952 | tf_op jit(solution)/shard_map/ppermute | solution.py:99
  70.6 4.2 %collective-permute-start = (bf16[2,1408]{1,0:T(2,128)(2,1)S(1)}, bf16[2,1408]{1,0:T(2,128)(2,1)S(1)}, u32[]{:S(2)}, u32[]{:S(2)}) collective-permute-start(bf16[2,1408]{1,0:T(2,128)(2,1)S(1)} %get-tuple-element.16), channel_id=1, source_target_pairs={{0,8},{8,16},{16,24},{24,32},{32,40},{40,48},{48,56},{1,9},{9,17},... | collective-permute-start | bytes 16904 | tf_op jit(solution)/shard_map/ppermute | solution.py:110
  74.8 2.6 %constant_dynamic-update-slice_fusion.9 = bf16[1538,1408]{1,0:T(8,128)(2,1)S(1)} fusion(bf16[1536,1408]{1,0:T(8,128)(2,1)} %all-gather.5.cloned.1.call-done), kind=kLoop, calls=%fused_computation.89 | loop fusion | bytes 8650752
  86.4 2.2 %reduce_max.18 = bf16[768,192]{1,0:T(8,128)(2,1)S(1)} reduce(bf16[768,2,192]{2,1,0:T(2,128)(2,1)S(1)} %reshape.80, bf16[]{:T(256)} %constant.212), dimensions={1}, to_apply=%region_1.2 | reduce | flops 147456 | bytes 884738 | tf_op jit(solution)/shard_map/reduce_max | solution.py:27
  90.0 11.9 %all-to-all-start = ((bf16[8,96,192]{1,2,0:T(8,128)(2,1)}), bf16[8,96,192]{1,2,0:T(8,128)(2,1)S(1)}, u32[]{:S(2)}, u32[]{:S(2)}) async-start(bf16[8,96,192]{1,2,0:T(8,128)(2,1)} %copy.37), calls=%async_computation | async-start | bytes 786432 | tf_op jit(solution)/shard_map/all_to_all | solution.py:122
  102.1 7.6 %all-to-all-done = bf16[8,96,192]{1,2,0:T(8,128)(2,1)S(1)} async-done(((bf16[8,96,192]{1,2,0:T(8,128)(2,1)}), bf16[8,96,192]{1,2,0:T(8,128)(2,1)S(1)}, u32[]{:S(2)}, u32[]{:S(2)}) %all-to-all-start) | async-done | bytes 294944 | tf_op jit(solution)/shard_map/all_to_all | solution.py:122
  110.5 2.8 %convolution_convert_fusion.1 = bf16[96,1280]{1,0:T(8,128)(2,1)S(1)} fusion(bf16[96,1536]{0,1:T(8,128)(2,1)S(1)} %bitcast.100, bf16[1536,1280]{1,0:T(8,128)(2,1)} %all-gather.7.cloned.1.call-done), kind=kOutput, calls=%fused_computation.24 | convolution fusion | flops 377610240 | bytes 4472832 | tf_op jit(solution)/shard_map/dot_general | solution.py:127
  113.4 15.1 %all_gather.17 = bf16[768,256]{1,0:T(8,128)(2,1)} all-gather(bf16[96,256]{1,0:T(8,128)(2,1)S(1)} %slice.86), channel_id=1, replica_groups=mesh['dp'=4,'sz'=8,'sx'=8] {'sx'}, dimensions={0}, use_global_device_ids=true | all-gather | bytes 442368 | tf_op jit(solution)/shard_map/all_gather | solution.py:31
  129.9 38.3 %all-gather.9.cloned.1.call-done = bf16[6144,256]{1,0:T(8,128)(2,1)} async-done(((bf16[768,256]{1,0:T(8,128)(2,1)}), bf16[6144,256]{1,0:T(8,128)(2,1)}) %all-gather.9.cloned.1.call-update) | async-done | bytes 3145744 | tf_op jit(solution)/shard_map/all_gather | solution.py:32
  169.2 9.2 %bitcast_reduce_fusion = (f32[8,96]{1,0:T(8,128)S(1)}, f32[6144,96,8]{0,1,2:T(8,128)}) fusion(f32[8]{0:T(128)S(1)} %copy-done.2, bf16[6144,256]{1,0:T(8,128)(2,1)} %all-gather.9.cloned.1.call-done, bf16[96,1280]{1,0:T(8,128)(2,1)S(1)} %convolution_convert_fusion.1), kind=kOutput, calls=%fused_computation.1 | convolution fusion | flops 1222114560 | bytes 20647424 | tf_op jit(solution)/shard_map/qhd,kd->hqk/dot_general | solution.py:48
  178.5 10.7 %fusion.1 = f32[8,96]{1,0:T(8,128)S(1)} fusion(f32[6144,96,8]{0,1,2:T(8,128)} %get-tuple-element.19, f32[8,96]{1,0:T(8,128)S(1)} %get-tuple-element.18, f32[8]{0:T(128)S(1)} %copy-done.2), kind=kLoop, calls=%fused_computation.4 | loop fusion | flops 18873600 | bytes 18880544 | tf_op jit(solution)/shard_map/reduce_sum | solution.py:54
  189.2 10.7 %fusion.54 = bf16[96,8,128]{2,0,1:T(8,128)(2,1)S(1)} fusion(bf16[6144,256]{1,0:T(8,128)(2,1)} %all-gather.9.cloned.1.call-done, f32[6144,96,8]{0,1,2:T(8,128)} %get-tuple-element.19, f32[8,96]{1,0:T(8,128)S(1)} %get-tuple-element.18, f32[8]{0:T(128)S(1)} %copy-done.2, f32[96,8]{0,1:T(8,128)S(1)} %bitcast.105), kind=kOutput, calls=%fused_computation.45 | convolution fusion | flops 1227030528 | bytes 20650016 | tf_op jit(solution)/shard_map/hqk,kd->hqd/dot_general | solution.py:55
  200.3 3.3 %convolution_convert_fusion = bf16[96,1536]{1,0:T(8,128)(2,1)} fusion(bf16[96,1024]{0,1:T(8,128)(2,1)S(1)} %bitcast.102, bf16[1024,1536]{1,0:T(8,128)(2,1)} %all-gather.11.cloned.1.call-done), kind=kOutput, calls=%fused_computation.23 | convolution fusion | flops 302137344 | bytes 3637248 | tf_op jit(solution)/shard_map/dot_general | solution.py:134
  (99 shorter events, 34.2 us)
Async XLA Ops:
  7.2 61.3 %all-gather.5.cloned.1.call-start = ((), (), s32[]{:S(2)}) async-start(), calls=%async_computation.1 | async-start | bytes 4866048 | tf_op jit(solution)/shard_map/all_gather | solution.py:82
  8.5 35.0 %copy-start = (bf16[5,1408,24]{1,2,0:T(8,128)(2,1)S(1)}, bf16[5,1408,24]{1,2,0:T(8,128)(2,1)}, u32[]{:S(2)}) copy-start(bf16[5,1408,24]{1,2,0:T(8,128)(2,1)} %param.11) | copy-start | bytes 1013764
  10.9 99.6 %all-gather.7.cloned.1.call-start = ((), (), s32[]{:S(2)}) async-start(), calls=%async_computation.2 | async-start | bytes 4423680 | tf_op jit(solution)/shard_map/all_gather | solution.py:105
  10.9 29.5 %collective-permute-start.1 = (bf16[5,1408,24]{1,2,0:T(8,128)(2,1)}, bf16[5,1408,24]{1,2,0:T(8,128)(2,1)S(1)}, u32[]{:S(2)}, u32[]{:S(2)}) collective-permute-start(bf16[5,1408,24]{1,2,0:T(8,128)(2,1)} %param.11), channel_id=1, source_target_pairs={{0,56},{8,0},{16,8},{24,16},{32,24},{40,32},{48,40},{56,48},{1,57}... | collective-permute-start | bytes 1013768 | tf_op jit(solution)/shard_map/ppermute | solution.py:96
  17.4 33.3 %collective-permute-start.5 = (bf16[5,1408,24]{1,2,0:T(8,128)(2,1)}, bf16[5,1408,24]{1,2,0:T(8,128)(2,1)S(1)}, u32[]{:S(2)}, u32[]{:S(2)}) collective-permute-start(bf16[5,1408,24]{1,2,0:T(8,128)(2,1)} %param.11), channel_id=1, source_target_pairs={{0,8},{8,16},{16,24},{24,32},{32,40},{40,48},{48,56},{56,0},{1,9},... | collective-permute-start | bytes 1013768 | tf_op jit(solution)/shard_map/ppermute | solution.py:99
  19.2 7.4 %collective-permute-start.9 = (bf16[216,256]{1,0:T(8,128)(2,1)S(1)}, bf16[216,256]{1,0:T(8,128)(2,1)S(1)}, u32[]{:S(2)}, u32[]{:S(2)}) collective-permute-start(bf16[216,256]{1,0:T(8,128)(2,1)S(1)} %constant_dynamic-update-slice_fusion.10), channel_id=1, source_target_pairs={{0,56},{8,0},{16,8},{24,16},{32,24},{40,32},{48,40},{56,48},{1,57}... | collective-permute-start | bytes 331784 | tf_op jit(solution)/shard_map/ppermute | solution.py:96
  21.9 8.1 %collective-permute-start.13 = (bf16[216,256]{1,0:T(8,128)(2,1)S(1)}, bf16[216,256]{1,0:T(8,128)(2,1)S(1)}, u32[]{:S(2)}, u32[]{:S(2)}) collective-permute-start(bf16[216,256]{1,0:T(8,128)(2,1)S(1)} %constant_dynamic-update-slice_fusion.10), channel_id=1, source_target_pairs={{0,8},{8,16},{16,24},{24,32},{32,40},{40,48},{48,56},{56,0},{1,9},... | collective-permute-start | bytes 331784 | tf_op jit(solution)/shard_map/ppermute | solution.py:99
  26.6 5.2 %collective-permute-start.10 = (bf16[216,256]{1,0:T(8,128)(2,1)S(1)}, bf16[216,256]{1,0:T(8,128)(2,1)S(1)}, u32[]{:S(2)}, u32[]{:S(2)}) collective-permute-start(bf16[216,256]{1,0:T(8,128)(2,1)S(1)} %collective-permute-done.9), channel_id=1, source_target_pairs={{0,56},{8,0},{16,8},{24,16},{32,24},{40,32},{48,40},{56,48},{1,57}... | collective-permute-start | bytes 331784 | tf_op jit(solution)/shard_map/ppermute | solution.py:96
  30.0 5.3 %collective-permute-start.14 = (bf16[216,256]{1,0:T(8,128)(2,1)S(1)}, bf16[216,256]{1,0:T(8,128)(2,1)S(1)}, u32[]{:S(2)}, u32[]{:S(2)}) collective-permute-start(bf16[216,256]{1,0:T(8,128)(2,1)S(1)} %collective-permute-done.13), channel_id=1, source_target_pairs={{0,8},{8,16},{16,24},{24,32},{32,40},{40,48},{48,56},{56,0},{1,9},... | collective-permute-start | bytes 331784 | tf_op jit(solution)/shard_map/ppermute | solution.py:99
  31.8 5.2 %collective-permute-start.11 = (bf16[216,256]{1,0:T(8,128)(2,1)S(1)}, bf16[216,256]{1,0:T(8,128)(2,1)S(1)}, u32[]{:S(2)}, u32[]{:S(2)}) collective-permute-start(bf16[216,256]{1,0:T(8,128)(2,1)S(1)} %collective-permute-done.10), channel_id=1, source_target_pairs={{0,56},{8,0},{16,8},{24,16},{32,24},{40,32},{48,40},{56,48},{1,57}... | collective-permute-start | bytes 331784 | tf_op jit(solution)/shard_map/ppermute | solution.py:96
  35.3 6.9 %collective-permute-start.15 = (bf16[216,256]{1,0:T(8,128)(2,1)S(1)}, bf16[216,256]{1,0:T(8,128)(2,1)S(1)}, u32[]{:S(2)}, u32[]{:S(2)}) collective-permute-start(bf16[216,256]{1,0:T(8,128)(2,1)S(1)} %collective-permute-done.14), channel_id=1, source_target_pairs={{0,8},{8,16},{16,24},{24,32},{32,40},{40,48},{48,56},{56,0},{1,9},... | collective-permute-start | bytes 331784 | tf_op jit(solution)/shard_map/ppermute | solution.py:99
  37.0 5.2 %collective-permute-start.12 = (bf16[216,256]{1,0:T(8,128)(2,1)S(1)}, bf16[216,256]{1,0:T(8,128)(2,1)S(1)}, u32[]{:S(2)}, u32[]{:S(2)}) collective-permute-start(bf16[216,256]{1,0:T(8,128)(2,1)S(1)} %collective-permute-done.11), channel_id=1, source_target_pairs={{0,56},{8,0},{16,8},{24,16},{32,24},{40,32},{48,40},{56,48},{1,57}... | collective-permute-start | bytes 331784 | tf_op jit(solution)/shard_map/ppermute | solution.py:96
  40.5 8.6 %collective-permute-start.2 = (bf16[5,1408,24]{1,2,0:T(8,128)(2,1)S(1)}, bf16[5,1408,24]{1,2,0:T(8,128)(2,1)S(1)}, u32[]{:S(2)}, u32[]{:S(2)}) collective-permute-start(bf16[5,1408,24]{1,2,0:T(8,128)(2,1)S(1)} %collective-permute-done.1), channel_id=1, source_target_pairs={{0,56},{8,0},{16,8},{24,16},{32,24},{40,32},{48,40},{56,48},{1,57}... | collective-permute-start | bytes 1013768 | tf_op jit(solution)/shard_map/ppermute | solution.py:96
  49.1 6.5 %collective-permute-start.3 = (bf16[5,1408,24]{1,2,0:T(8,128)(2,1)S(1)}, bf16[5,1408,24]{1,2,0:T(8,128)(2,1)S(1)}, u32[]{:S(2)}, u32[]{:S(2)}) collective-permute-start(bf16[5,1408,24]{1,2,0:T(8,128)(2,1)S(1)} %collective-permute-done.2), channel_id=1, source_target_pairs={{0,56},{8,0},{16,8},{24,16},{32,24},{40,32},{48,40},{56,48},{1,57}... | collective-permute-start | bytes 1013768 | tf_op jit(solution)/shard_map/ppermute | solution.py:96
  50.7 7.9 %collective-permute-start.6 = (bf16[5,1408,24]{1,2,0:T(8,128)(2,1)S(1)}, bf16[5,1408,24]{1,2,0:T(8,128)(2,1)S(1)}, u32[]{:S(2)}, u32[]{:S(2)}) collective-permute-start(bf16[5,1408,24]{1,2,0:T(8,128)(2,1)S(1)} %collective-permute-done.5), channel_id=1, source_target_pairs={{0,8},{8,16},{16,24},{24,32},{32,40},{40,48},{48,56},{56,0},{1,9},... | collective-permute-start | bytes 1013768 | tf_op jit(solution)/shard_map/ppermute | solution.py:99
  55.6 7.1 %collective-permute-start.4 = (bf16[5,1408,24]{1,2,0:T(8,128)(2,1)S(1)}, bf16[5,1408,24]{1,2,0:T(8,128)(2,1)S(1)}, u32[]{:S(2)}, u32[]{:S(2)}) collective-permute-start(bf16[5,1408,24]{1,2,0:T(8,128)(2,1)S(1)} %collective-permute-done.3), channel_id=1, source_target_pairs={{0,56},{8,0},{16,8},{24,16},{32,24},{40,32},{48,40},{56,48},{1,57}... | collective-permute-start | bytes 1013768 | tf_op jit(solution)/shard_map/ppermute | solution.py:96
  58.6 7.6 %collective-permute-start.7 = (bf16[5,1408,24]{1,2,0:T(8,128)(2,1)S(1)}, bf16[5,1408,24]{1,2,0:T(8,128)(2,1)S(1)}, u32[]{:S(2)}, u32[]{:S(2)}) collective-permute-start(bf16[5,1408,24]{1,2,0:T(8,128)(2,1)S(1)} %collective-permute-done.6), channel_id=1, source_target_pairs={{0,8},{8,16},{16,24},{24,32},{32,40},{40,48},{48,56},{56,0},{1,9},... | collective-permute-start | bytes 1013768 | tf_op jit(solution)/shard_map/ppermute | solution.py:99
  69.2 9.9 %collective-permute-start.8 = (bf16[2,1408]{1,0:T(2,128)(2,1)S(1)}, bf16[2,1408]{1,0:T(2,128)(2,1)S(1)}, u32[]{:S(2)}, u32[]{:S(2)}) collective-permute-start(bf16[2,1408]{1,0:T(2,128)(2,1)S(1)} %get-tuple-element.17), channel_id=1, source_target_pairs={{8,0},{16,8},{24,16},{32,24},{40,32},{48,40},{56,48},{9,1},{17,9},... | collective-permute-start | bytes 16904 | tf_op jit(solution)/shard_map/ppermute | solution.py:111
  70.6 8.6 %collective-permute-start = (bf16[2,1408]{1,0:T(2,128)(2,1)S(1)}, bf16[2,1408]{1,0:T(2,128)(2,1)S(1)}, u32[]{:S(2)}, u32[]{:S(2)}) collective-permute-start(bf16[2,1408]{1,0:T(2,128)(2,1)S(1)} %get-tuple-element.16), channel_id=1, source_target_pairs={{0,8},{8,16},{16,24},{24,32},{32,40},{40,48},{48,56},{1,9},{9,17},... | collective-permute-start | bytes 16904 | tf_op jit(solution)/shard_map/ppermute | solution.py:110
  86.0 16.0 %copy-start.3 = (f32[1536]{0:T(1024)S(1)}, f32[1536]{0:T(1024)}, u32[]{:S(2)}) copy-start(f32[1536]{0:T(1024)} %param.13) | copy-start | bytes 18436
  90.0 19.6 %all-to-all-start = ((bf16[8,96,192]{1,2,0:T(8,128)(2,1)}), bf16[8,96,192]{1,2,0:T(8,128)(2,1)S(1)}, u32[]{:S(2)}, u32[]{:S(2)}) async-start(bf16[8,96,192]{1,2,0:T(8,128)(2,1)} %copy.37), calls=%async_computation | async-start | bytes 786432 | tf_op jit(solution)/shard_map/all_to_all | solution.py:122
  102.0 66.3 %all-gather.9.cloned.1.call-start = ((), (), s32[]{:S(2)}) async-start(), calls=%async_computation.3 | async-start | bytes 3538944 | tf_op jit(solution)/shard_map/all_gather | solution.py:32
  113.3 55.9 %copy-start.2 = (f32[8]{0:T(128)S(1)}, f32[8]{0:T(128)}, u32[]{:S(2)}) copy-start(f32[8]{0:T(128)} %param.16) | copy-start | bytes 100
  128.5 71.8 %all-gather.11.cloned.1.call-start = ((), (), s32[]{:S(2)}) async-start(), calls=%async_computation.4 | async-start | bytes 3538944 | tf_op jit(solution)/shard_map/all_gather | solution.py:132
  (3 other events, 20.8 us)
Sparse Core Ops, SparseCore 0:
  11.0 39.2 all-gather.4
  52.2 33.4 all-gather.6
  128.6 39.5 all-gather.8
  169.9 29.7 all-gather.10

commit v5 on v4

--- a/solution.py
+++ b/solution.py
@@ -1,6 +1,8 @@
 import jax
 import jax.numpy as jnp
 from jax import lax
+from jax.experimental import pallas as pl
+from jax.experimental.pallas import tpu as pltpu
 from jax.sharding import Mesh
 from jax.sharding import PartitionSpec as P
 
@@ -38,25 +40,41 @@
     return split.transpose(0, 2, 1, 3).reshape(rows, columns.shape[1])
 
 
+def head_kernel(scale_ref, q_ref, k_ref, v_ref, o_ref):
+    head = pl.program_id(0)
+    scores = lax.dot_general(
+        q_ref[...], k_ref[...], (((1,), (1,)), ((), ())), preferred_element_type=jnp.float32
+    )
+    scores = scores * scale_ref[head] * HEAD_DIM ** (-0.5)
+    biggest = jnp.max(scores, axis=1, keepdims=True)
+    expon = jnp.exp(scores - biggest)
+    total = jnp.sum(expon, axis=1, keepdims=True)
+    context = jnp.dot(expon.astype(jnp.bfloat16), v_ref[...], preferred_element_type=jnp.float32)
+    o_ref[...] = (context / total).astype(o_ref.dtype)
+
+
 def attend(queries, key_block, scales):
     row_count = queries.shape[0]
     head_count = scales.shape[0]
-    shaped = queries.reshape(row_count, head_count, HEAD_DIM)
-    key_part = key_block[:, :HEAD_DIM]
-    value_part = key_block[:, HEAD_DIM:]
-    scores = (
-        jnp.einsum("qhd,kd->hqk", shaped, key_part, preferred_element_type=jnp.float32)
-        * scales[:, None, None]
-        * HEAD_DIM ** (-0.5)
-    )
-    biggest = jnp.max(scores, axis=2)
-    expon = jnp.exp(scores - biggest[:, :, None])
-    total = jnp.sum(expon, axis=2)
-    context = jnp.einsum(
-        "hqk,kd->hqd", expon.astype(jnp.bfloat16), value_part, preferred_element_type=jnp.float32
-    )
-    context = context / total[:, :, None]
-    return context.transpose(1, 0, 2).reshape(row_count, head_count * HEAD_DIM).astype(jnp.bfloat16)
+    key_count = key_block.shape[0]
+    flops = 4 * head_count * row_count * key_count * HEAD_DIM
+    return pl.pallas_call(
+        head_kernel,
+        grid=(head_count,),
+        in_specs=[
+            pl.BlockSpec(memory_space=pltpu.SMEM),
+            pl.BlockSpec((row_count, HEAD_DIM), lambda h: (0, h)),
+            pl.BlockSpec((key_count, HEAD_DIM), lambda h: (0, 0)),
+            pl.BlockSpec((key_count, HEAD_DIM), lambda h: (0, 1)),
+        ],
+        out_specs=pl.BlockSpec((row_count, HEAD_DIM), lambda h: (0, h)),
+        out_shape=jax.ShapeDtypeStruct((row_count, head_count * HEAD_DIM), jnp.bfloat16),
+        cost_estimate=pl.CostEstimate(
+            flops=flops,
+            transcendentals=head_count * row_count * key_count,
+            bytes_accessed=2 * key_block.size + 4 * queries.size,
+        ),
+    )(scales, queries, key_block, key_block)
 
 
 def shards(

time: 211 us -> 210 us (level)
  matrix products: 34.1 us -> 14.2 us
  Pallas kernels: 0 us -> 15 us
  waiting for transfers between devices: 69.7 us -> 84.2 us
  other arithmetic: 18.4 us -> 7.61 us
    dot_general x2 -> x0, matrix products: 20 us -> none  [the longest x1 10.7 us: attend(): jnp.einsum('hqk,kd->hqd', expon.astype(jnp.bfloat16), value_part, preferr...]
    pallas_call x0 -> x1, Pallas kernels: none -> 15 us  [attend(): pl.pallas_call(head_kernel, grid=(head_count,), in_specs=[pl.BlockSpec(me...]
    all_gather x1, waiting for transfers between devices: 0.02 us -> 13.6 us  [shards(): out_weight = lax.all_gather(out_z, 'sx', axis=0, tiled=True)]
    reduce_sum x1 -> x0, other arithmetic: 10.7 us -> none  [attend(): total = jnp.sum(expon, axis=2)]
  transfers between devices with their start and end apart: 21 -> 21, of which waited for: 11 -> 12; matrix products, arithmetic and copies ran while one was open for 28% -> 14% of each run, Pallas kernels for 0% -> 7%
where the time goes in v5:
time: 210 us
  waiting for transfers between devices  84.2 us (40%)
  starting transfers between devices  41.2 us (20%)
  local copies, waits for them, and re-layouts  18 us (9%)
  blocking collectives  15.1 us (7%)
  Pallas kernels  15 us (7%)
  matrix products  14.2 us (7%)
  between operations  14.2 us (7%)
  other arithmetic  7.61 us (4%)
    all_gather x1, waiting for transfers between devices, gather_rows(): return lax.all_gather(inner, 'sz', axis=0, tiled=True)  38.6 us
    ppermute x8, starting transfers between devices, shards(): ahead = lax.ppermute(ahead, 'sz', up)  23.4 us
    ppermute x8, waiting for transfers between devices, shards(): ahead = lax.ppermute(ahead, 'sz', up)  21.6 us
    all_gather x1, blocking collectives, gather_rows(): inner = lax.all_gather(block, 'sx', axis=0, tiled=True)  15.1 us
    pallas_call x1, Pallas kernels, attend(): pl.pallas_call(head_kernel, grid=(head_count,), in_specs=[pl.BlockSpec(me...  15 us
    all_gather x1, waiting for transfers between devices, shards(): out_weight = lax.all_gather(out_z, 'sx', axis=0, tiled=True)  13.6 us
    all_to_all x1, starting transfers between devices, shards(): received = lax.all_to_all(pieces, 'sx', 0, 0, tiled=False)  12 us
    unnamed x29, local copies, waits for them, and re-layouts  9.03 us
  transfers between devices with their start and end apart: 21, of which 12 were waited for; matrix products, arithmetic and copies ran while one was open for 14% of the time, Pallas kernels for 7%

profile of v5, /device:TPU:1, one launch (start us, length us, event | category | flops | bytes accessed | tf_op | source)
XLA Modules:
  0.0 209.5 jit_solution(5468222547048248873)
XLA Ops:
  8.5 2.4 %fusion.28 = bf16[192,1408]{1,0:T(8,128)(2,1)} fusion(bf16[192,1408]{1,0:T(8,128)(2,1)} %param.9, f32[1408]{0:T(1024)} %param.10, f32[192]{0:T(256)S(1)} %add_rsqrt_fusion), kind=kLoop, calls=%fused_computation.25 | loop fusion | flops 3244032 | bytes 1087744 | tf_op jit(solution)/shard_map/convert_element_type | solution.py:99
  10.9 6.5 %collective-permute-start.1 = (bf16[5,1408,24]{1,2,0:T(8,128)(2,1)}, bf16[5,1408,24]{1,2,0:T(8,128)(2,1)S(1)}, u32[]{:S(2)}, u32[]{:S(2)}) collective-permute-start(bf16[5,1408,24]{1,2,0:T(8,128)(2,1)} %param.11), channel_id=1, source_target_pairs={{0,56},{8,0},{16,8},{24,16},{32,24},{40,32},{48,40},{56,48},{1,57}... | collective-permute-start | bytes 1013768 | tf_op jit(solution)/shard_map/ppermute | solution.py:114
  19.1 2.7 %collective-permute-start.9 = (bf16[216,256]{1,0:T(8,128)(2,1)S(1)}, bf16[216,256]{1,0:T(8,128)(2,1)S(1)}, u32[]{:S(2)}, u32[]{:S(2)}) collective-permute-start(bf16[216,256]{1,0:T(8,128)(2,1)S(1)} %constant_dynamic-update-slice_fusion.10), channel_id=1, source_target_pairs={{0,56},{8,0},{16,8},{24,16},{32,24},{40,32},{48,40},{56,48},{1,57}... | collective-permute-start | bytes 331784 | tf_op jit(solution)/shard_map/ppermute | solution.py:114
  22.0 4.5 %collective-permute-done.9 = bf16[216,256]{1,0:T(8,128)(2,1)S(1)} collective-permute-done((bf16[216,256]{1,0:T(8,128)(2,1)S(1)}, bf16[216,256]{1,0:T(8,128)(2,1)S(1)}, u32[]{:S(2)}, u32[]{:S(2)}) %collective-permute-start.9) | collective-permute-done | bytes 110624 | tf_op jit(solution)/shard_map/ppermute | solution.py:114
  26.6 3.4 %collective-permute-start.10 = (bf16[216,256]{1,0:T(8,128)(2,1)S(1)}, bf16[216,256]{1,0:T(8,128)(2,1)S(1)}, u32[]{:S(2)}, u32[]{:S(2)}) collective-permute-start(bf16[216,256]{1,0:T(8,128)(2,1)S(1)} %collective-permute-done.9), channel_id=1, source_target_pairs={{0,56},{8,0},{16,8},{24,16},{32,24},{40,32},{48,40},{56,48},{1,57}... | collective-permute-start | bytes 331784 | tf_op jit(solution)/shard_map/ppermute | solution.py:114
  31.7 3.5 %collective-permute-start.11 = (bf16[216,256]{1,0:T(8,128)(2,1)S(1)}, bf16[216,256]{1,0:T(8,128)(2,1)S(1)}, u32[]{:S(2)}, u32[]{:S(2)}) collective-permute-start(bf16[216,256]{1,0:T(8,128)(2,1)S(1)} %collective-permute-done.10), channel_id=1, source_target_pairs={{0,56},{8,0},{16,8},{24,16},{32,24},{40,32},{48,40},{56,48},{1,57}... | collective-permute-start | bytes 331784 | tf_op jit(solution)/shard_map/ppermute | solution.py:114
  36.9 3.5 %collective-permute-start.12 = (bf16[216,256]{1,0:T(8,128)(2,1)S(1)}, bf16[216,256]{1,0:T(8,128)(2,1)S(1)}, u32[]{:S(2)}, u32[]{:S(2)}) collective-permute-start(bf16[216,256]{1,0:T(8,128)(2,1)S(1)} %collective-permute-done.11), channel_id=1, source_target_pairs={{0,56},{8,0},{16,8},{24,16},{32,24},{40,32},{48,40},{56,48},{1,57}... | collective-permute-start | bytes 331784 | tf_op jit(solution)/shard_map/ppermute | solution.py:114
  44.2 4.8 %collective-permute-done.2 = bf16[5,1408,24]{1,2,0:T(8,128)(2,1)S(1)} collective-permute-done((bf16[5,1408,24]{1,2,0:T(8,128)(2,1)S(1)}, bf16[5,1408,24]{1,2,0:T(8,128)(2,1)S(1)}, u32[]{:S(2)}, u32[]{:S(2)}) %collective-permute-start.2) | collective-permute-done | bytes 337952 | tf_op jit(solution)/shard_map/ppermute | solution.py:114
  51.5 4.1 %collective-permute-done.3 = bf16[5,1408,24]{1,2,0:T(8,128)(2,1)S(1)} collective-permute-done((bf16[5,1408,24]{1,2,0:T(8,128)(2,1)S(1)}, bf16[5,1408,24]{1,2,0:T(8,128)(2,1)S(1)}, u32[]{:S(2)}, u32[]{:S(2)}) %collective-permute-start.3) | collective-permute-done | bytes 337952 | tf_op jit(solution)/shard_map/ppermute | solution.py:114
  55.5 2.2 %collective-permute-start.4 = (bf16[5,1408,24]{1,2,0:T(8,128)(2,1)S(1)}, bf16[5,1408,24]{1,2,0:T(8,128)(2,1)S(1)}, u32[]{:S(2)}, u32[]{:S(2)}) collective-permute-start(bf16[5,1408,24]{1,2,0:T(8,128)(2,1)S(1)} %collective-permute-done.3), channel_id=1, source_target_pairs={{0,56},{8,0},{16,8},{24,16},{32,24},{40,32},{48,40},{56,48},{1,57}... | collective-permute-start | bytes 1013768 | tf_op jit(solution)/shard_map/ppermute | solution.py:114
  59.3 3.3 %collective-permute-done.4 = bf16[5,1408,24]{1,2,0:T(8,128)(2,1)S(1)} collective-permute-done((bf16[5,1408,24]{1,2,0:T(8,128)(2,1)S(1)}, bf16[5,1408,24]{1,2,0:T(8,128)(2,1)S(1)}, u32[]{:S(2)}, u32[]{:S(2)}) %collective-permute-start.4) | collective-permute-done | bytes 337952 | tf_op jit(solution)/shard_map/ppermute | solution.py:114
  63.4 2.7 %collective-permute-done.7 = bf16[5,1408,24]{1,2,0:T(8,128)(2,1)S(1)} collective-permute-done((bf16[5,1408,24]{1,2,0:T(8,128)(2,1)S(1)}, bf16[5,1408,24]{1,2,0:T(8,128)(2,1)S(1)}, u32[]{:S(2)}, u32[]{:S(2)}) %collective-permute-start.7) | collective-permute-done | bytes 337952 | tf_op jit(solution)/shard_map/ppermute | solution.py:117
  70.5 4.2 %collective-permute-start = (bf16[2,1408]{1,0:T(2,128)(2,1)S(1)}, bf16[2,1408]{1,0:T(2,128)(2,1)S(1)}, u32[]{:S(2)}, u32[]{:S(2)}) collective-permute-start(bf16[2,1408]{1,0:T(2,128)(2,1)S(1)} %get-tuple-element.16), channel_id=1, source_target_pairs={{0,8},{8,16},{16,24},{24,32},{32,40},{40,48},{48,56},{1,9},{9,17},... | collective-permute-start | bytes 16904 | tf_op jit(solution)/shard_map/ppermute | solution.py:128
  74.8 2.6 %constant_dynamic-update-slice_fusion.9 = bf16[1538,1408]{1,0:T(8,128)(2,1)S(1)} fusion(bf16[1536,1408]{1,0:T(8,128)(2,1)} %all-gather.5.cloned.1.call-done), kind=kLoop, calls=%fused_computation.71 | loop fusion | bytes 8650752
  83.9 1.7 fusion.21
  86.3 2.2 %reduce_max.9 = bf16[768,192]{1,0:T(8,128)(2,1)S(1)} reduce(bf16[768,2,192]{2,1,0:T(2,128)(2,1)S(1)} %reshape.73, bf16[]{:T(256)} %constant.198), dimensions={1}, to_apply=%region_1.2 | reduce | flops 147456 | bytes 884738 | tf_op jit(solution)/shard_map/reduce_max | solution.py:29
  90.0 12.0 %all-to-all-start = ((bf16[8,96,192]{1,2,0:T(8,128)(2,1)}), bf16[8,96,192]{1,2,0:T(8,128)(2,1)S(1)}, u32[]{:S(2)}, u32[]{:S(2)}) async-start(bf16[8,96,192]{1,2,0:T(8,128)(2,1)} %copy.33), calls=%async_computation | async-start | bytes 786432 | tf_op jit(solution)/shard_map/all_to_all | solution.py:140
  102.1 7.6 %all-to-all-done = bf16[8,96,192]{1,2,0:T(8,128)(2,1)S(1)} async-done(((bf16[8,96,192]{1,2,0:T(8,128)(2,1)}), bf16[8,96,192]{1,2,0:T(8,128)(2,1)S(1)}, u32[]{:S(2)}, u32[]{:S(2)}) %all-to-all-start) | async-done | bytes 294944 | tf_op jit(solution)/shard_map/all_to_all | solution.py:140
  110.5 2.8 %convolution_convert_fusion.1 = bf16[96,1280]{1,0:T(8,128)(2,1)S(1)} fusion(bf16[96,1536]{0,1:T(8,128)(2,1)S(1)} %bitcast.54, bf16[1536,1280]{1,0:T(8,128)(2,1)} %all-gather.7.cloned.1.call-done), kind=kOutput, calls=%fused_computation.17 | convolution fusion | flops 377610240 | bytes 4472832 | tf_op jit(solution)/shard_map/dot_general | solution.py:145
  113.3 15.1 %all_gather.17 = bf16[768,256]{1,0:T(8,128)(2,1)} all-gather(bf16[96,256]{1,0:T(8,128)(2,1)S(1)} %slice.79), channel_id=1, replica_groups=mesh['dp'=4,'sz'=8,'sx'=8] {'sx'}, dimensions={0}, use_global_device_ids=true | all-gather | bytes 442368 | tf_op jit(solution)/shard_map/all_gather | solution.py:33
  129.6 38.6 %all-gather.9.cloned.1.call-done.k_ref.v_ref = bf16[6144,256]{1,0:T(8,128)(2,1)} async-done(((bf16[768,256]{1,0:T(8,128)(2,1)}), bf16[6144,256]{1,0:T(8,128)(2,1)}) %all-gather.9.cloned.1.call-update) | async-done | bytes 3145744 | tf_op jit(solution)/shard_map/all_gather | solution.py:34
  169.9 15.0 %shard_map.104 = bf16[96,1024]{1,0:T(8,128)(2,1)} custom-call(f32[8]{0:T(128)} %scale_ref.1, bf16[96,1024]{1,0:T(8,128)(2,1)} %slice.78.q_ref, bf16[6144,256]{1,0:T(8,128)(2,1)} %all-gather.9.cloned.1.call-done.k_ref.v_ref, bf16[6144,256]{1,0:T(8,128)(2,1)} %all-gather.9.cloned.1.call-done.k_ref.v_ref), custom_call_target="tpu_custom_call" | custom-call | flops 2415919104 | bytes 3538944 | tf_op jit(solution)/shard_map/pallas_call | solution.py:61
  186.1 13.6 %all-gather.11.cloned.1.call-done = bf16[1024,1536]{1,0:T(8,128)(2,1)} async-done(((bf16[128,1536]{1,0:T(8,128)(2,1)}), bf16[1024,1536]{1,0:T(8,128)(2,1)}) %all-gather.11.cloned.1.call-update) | async-done | bytes 3145744 | tf_op jit(solution)/shard_map/all_gather | solution.py:150
  199.7 3.3 %convolution_convert_fusion = bf16[96,1536]{1,0:T(8,128)(2,1)} fusion(bf16[96,1024]{0,1:T(8,128)(2,1)S(1)} %bitcast.56, bf16[1024,1536]{1,0:T(8,128)(2,1)} %all-gather.11.cloned.1.call-done), kind=kOutput, calls=%fused_computation.16 | convolution fusion | flops 302137344 | bytes 3637248 | tf_op jit(solution)/shard_map/dot_general | solution.py:152
  (98 shorter events, 33.1 us)
Async XLA Ops:
  7.2 14.8 %copy-start.2 = (f32[1536]{0:T(1024)S(1)}, f32[1536]{0:T(1024)}, u32[]{:S(2)}) copy-start(f32[1536]{0:T(1024)} %param.12) | copy-start | bytes 18436
  7.2 61.3 %all-gather.5.cloned.1.call-start = ((), (), s32[]{:S(2)}) async-start(), calls=%async_computation.1 | async-start | bytes 4866048 | tf_op jit(solution)/shard_map/all_gather | solution.py:100
  10.8 32.6 %copy-start = (bf16[5,1408,24]{1,2,0:T(8,128)(2,1)S(1)}, bf16[5,1408,24]{1,2,0:T(8,128)(2,1)}, u32[]{:S(2)}) copy-start(bf16[5,1408,24]{1,2,0:T(8,128)(2,1)} %param.11) | copy-start | bytes 1013764
  10.9 99.6 %all-gather.7.cloned.1.call-start = ((), (), s32[]{:S(2)}) async-start(), calls=%async_computation.2 | async-start | bytes 4423680 | tf_op jit(solution)/shard_map/all_gather | solution.py:123
  10.9 29.5 %collective-permute-start.1 = (bf16[5,1408,24]{1,2,0:T(8,128)(2,1)}, bf16[5,1408,24]{1,2,0:T(8,128)(2,1)S(1)}, u32[]{:S(2)}, u32[]{:S(2)}) collective-permute-start(bf16[5,1408,24]{1,2,0:T(8,128)(2,1)} %param.11), channel_id=1, source_target_pairs={{0,56},{8,0},{16,8},{24,16},{32,24},{40,32},{48,40},{56,48},{1,57}... | collective-permute-start | bytes 1013768 | tf_op jit(solution)/shard_map/ppermute | solution.py:114
  17.4 33.3 %collective-permute-start.5 = (bf16[5,1408,24]{1,2,0:T(8,128)(2,1)}, bf16[5,1408,24]{1,2,0:T(8,128)(2,1)S(1)}, u32[]{:S(2)}, u32[]{:S(2)}) collective-permute-start(bf16[5,1408,24]{1,2,0:T(8,128)(2,1)} %param.11), channel_id=1, source_target_pairs={{0,8},{8,16},{16,24},{24,32},{32,40},{40,48},{48,56},{56,0},{1,9},... | collective-permute-start | bytes 1013768 | tf_op jit(solution)/shard_map/ppermute | solution.py:117
  19.1 7.4 %collective-permute-start.9 = (bf16[216,256]{1,0:T(8,128)(2,1)S(1)}, bf16[216,256]{1,0:T(8,128)(2,1)S(1)}, u32[]{:S(2)}, u32[]{:S(2)}) collective-permute-start(bf16[216,256]{1,0:T(8,128)(2,1)S(1)} %constant_dynamic-update-slice_fusion.10), channel_id=1, source_target_pairs={{0,56},{8,0},{16,8},{24,16},{32,24},{40,32},{48,40},{56,48},{1,57}... | collective-permute-start | bytes 331784 | tf_op jit(solution)/shard_map/ppermute | solution.py:114
  21.9 8.1 %collective-permute-start.13 = (bf16[216,256]{1,0:T(8,128)(2,1)S(1)}, bf16[216,256]{1,0:T(8,128)(2,1)S(1)}, u32[]{:S(2)}, u32[]{:S(2)}) collective-permute-start(bf16[216,256]{1,0:T(8,128)(2,1)S(1)} %constant_dynamic-update-slice_fusion.10), channel_id=1, source_target_pairs={{0,8},{8,16},{16,24},{24,32},{32,40},{40,48},{48,56},{56,0},{1,9},... | collective-permute-start | bytes 331784 | tf_op jit(solution)/shard_map/ppermute | solution.py:117
  26.6 5.2 %collective-permute-start.10 = (bf16[216,256]{1,0:T(8,128)(2,1)S(1)}, bf16[216,256]{1,0:T(8,128)(2,1)S(1)}, u32[]{:S(2)}, u32[]{:S(2)}) collective-permute-start(bf16[216,256]{1,0:T(8,128)(2,1)S(1)} %collective-permute-done.9), channel_id=1, source_target_pairs={{0,56},{8,0},{16,8},{24,16},{32,24},{40,32},{48,40},{56,48},{1,57}... | collective-permute-start | bytes 331784 | tf_op jit(solution)/shard_map/ppermute | solution.py:114
  30.0 5.3 %collective-permute-start.14 = (bf16[216,256]{1,0:T(8,128)(2,1)S(1)}, bf16[216,256]{1,0:T(8,128)(2,1)S(1)}, u32[]{:S(2)}, u32[]{:S(2)}) collective-permute-start(bf16[216,256]{1,0:T(8,128)(2,1)S(1)} %collective-permute-done.13), channel_id=1, source_target_pairs={{0,8},{8,16},{16,24},{24,32},{32,40},{40,48},{48,56},{56,0},{1,9},... | collective-permute-start | bytes 331784 | tf_op jit(solution)/shard_map/ppermute | solution.py:117
  31.7 5.2 %collective-permute-start.11 = (bf16[216,256]{1,0:T(8,128)(2,1)S(1)}, bf16[216,256]{1,0:T(8,128)(2,1)S(1)}, u32[]{:S(2)}, u32[]{:S(2)}) collective-permute-start(bf16[216,256]{1,0:T(8,128)(2,1)S(1)} %collective-permute-done.10), channel_id=1, source_target_pairs={{0,56},{8,0},{16,8},{24,16},{32,24},{40,32},{48,40},{56,48},{1,57}... | collective-permute-start | bytes 331784 | tf_op jit(solution)/shard_map/ppermute | solution.py:114
  35.3 6.9 %collective-permute-start.15 = (bf16[216,256]{1,0:T(8,128)(2,1)S(1)}, bf16[216,256]{1,0:T(8,128)(2,1)S(1)}, u32[]{:S(2)}, u32[]{:S(2)}) collective-permute-start(bf16[216,256]{1,0:T(8,128)(2,1)S(1)} %collective-permute-done.14), channel_id=1, source_target_pairs={{0,8},{8,16},{16,24},{24,32},{32,40},{40,48},{48,56},{56,0},{1,9},... | collective-permute-start | bytes 331784 | tf_op jit(solution)/shard_map/ppermute | solution.py:117
  36.9 5.2 %collective-permute-start.12 = (bf16[216,256]{1,0:T(8,128)(2,1)S(1)}, bf16[216,256]{1,0:T(8,128)(2,1)S(1)}, u32[]{:S(2)}, u32[]{:S(2)}) collective-permute-start(bf16[216,256]{1,0:T(8,128)(2,1)S(1)} %collective-permute-done.11), channel_id=1, source_target_pairs={{0,56},{8,0},{16,8},{24,16},{32,24},{40,32},{48,40},{56,48},{1,57}... | collective-permute-start | bytes 331784 | tf_op jit(solution)/shard_map/ppermute | solution.py:114
  40.4 8.6 %collective-permute-start.2 = (bf16[5,1408,24]{1,2,0:T(8,128)(2,1)S(1)}, bf16[5,1408,24]{1,2,0:T(8,128)(2,1)S(1)}, u32[]{:S(2)}, u32[]{:S(2)}) collective-permute-start(bf16[5,1408,24]{1,2,0:T(8,128)(2,1)S(1)} %collective-permute-done.1), channel_id=1, source_target_pairs={{0,56},{8,0},{16,8},{24,16},{32,24},{40,32},{48,40},{56,48},{1,57}... | collective-permute-start | bytes 1013768 | tf_op jit(solution)/shard_map/ppermute | solution.py:114
  49.0 6.5 %collective-permute-start.3 = (bf16[5,1408,24]{1,2,0:T(8,128)(2,1)S(1)}, bf16[5,1408,24]{1,2,0:T(8,128)(2,1)S(1)}, u32[]{:S(2)}, u32[]{:S(2)}) collective-permute-start(bf16[5,1408,24]{1,2,0:T(8,128)(2,1)S(1)} %collective-permute-done.2), channel_id=1, source_target_pairs={{0,56},{8,0},{16,8},{24,16},{32,24},{40,32},{48,40},{56,48},{1,57}... | collective-permute-start | bytes 1013768 | tf_op jit(solution)/shard_map/ppermute | solution.py:114
  50.6 7.9 %collective-permute-start.6 = (bf16[5,1408,24]{1,2,0:T(8,128)(2,1)S(1)}, bf16[5,1408,24]{1,2,0:T(8,128)(2,1)S(1)}, u32[]{:S(2)}, u32[]{:S(2)}) collective-permute-start(bf16[5,1408,24]{1,2,0:T(8,128)(2,1)S(1)} %collective-permute-done.5), channel_id=1, source_target_pairs={{0,8},{8,16},{16,24},{24,32},{32,40},{40,48},{48,56},{56,0},{1,9},... | collective-permute-start | bytes 1013768 | tf_op jit(solution)/shard_map/ppermute | solution.py:117
  55.5 7.1 %collective-permute-start.4 = (bf16[5,1408,24]{1,2,0:T(8,128)(2,1)S(1)}, bf16[5,1408,24]{1,2,0:T(8,128)(2,1)S(1)}, u32[]{:S(2)}, u32[]{:S(2)}) collective-permute-start(bf16[5,1408,24]{1,2,0:T(8,128)(2,1)S(1)} %collective-permute-done.3), channel_id=1, source_target_pairs={{0,56},{8,0},{16,8},{24,16},{32,24},{40,32},{48,40},{56,48},{1,57}... | collective-permute-start | bytes 1013768 | tf_op jit(solution)/shard_map/ppermute | solution.py:114
  58.6 7.5 %collective-permute-start.7 = (bf16[5,1408,24]{1,2,0:T(8,128)(2,1)S(1)}, bf16[5,1408,24]{1,2,0:T(8,128)(2,1)S(1)}, u32[]{:S(2)}, u32[]{:S(2)}) collective-permute-start(bf16[5,1408,24]{1,2,0:T(8,128)(2,1)S(1)} %collective-permute-done.6), channel_id=1, source_target_pairs={{0,8},{8,16},{16,24},{24,32},{32,40},{40,48},{48,56},{56,0},{1,9},... | collective-permute-start | bytes 1013768 | tf_op jit(solution)/shard_map/ppermute | solution.py:117
  69.2 9.9 %collective-permute-start.8 = (bf16[2,1408]{1,0:T(2,128)(2,1)S(1)}, bf16[2,1408]{1,0:T(2,128)(2,1)S(1)}, u32[]{:S(2)}, u32[]{:S(2)}) collective-permute-start(bf16[2,1408]{1,0:T(2,128)(2,1)S(1)} %get-tuple-element.17), channel_id=1, source_target_pairs={{8,0},{16,8},{24,16},{32,24},{40,32},{48,40},{56,48},{9,1},{17,9},... | collective-permute-start | bytes 16904 | tf_op jit(solution)/shard_map/ppermute | solution.py:129
  70.5 8.6 %collective-permute-start = (bf16[2,1408]{1,0:T(2,128)(2,1)S(1)}, bf16[2,1408]{1,0:T(2,128)(2,1)S(1)}, u32[]{:S(2)}, u32[]{:S(2)}) collective-permute-start(bf16[2,1408]{1,0:T(2,128)(2,1)S(1)} %get-tuple-element.16), channel_id=1, source_target_pairs={{0,8},{8,16},{16,24},{24,32},{32,40},{40,48},{48,56},{1,9},{9,17},... | collective-permute-start | bytes 16904 | tf_op jit(solution)/shard_map/ppermute | solution.py:128
  85.9 16.1 %copy-start.3 = (f32[1536]{0:T(1024)S(1)}, f32[1536]{0:T(1024)}, u32[]{:S(2)}) copy-start(f32[1536]{0:T(1024)} %param.13) | copy-start | bytes 18436
  90.0 19.7 %all-to-all-start = ((bf16[8,96,192]{1,2,0:T(8,128)(2,1)}), bf16[8,96,192]{1,2,0:T(8,128)(2,1)S(1)}, u32[]{:S(2)}, u32[]{:S(2)}) async-start(bf16[8,96,192]{1,2,0:T(8,128)(2,1)} %copy.33), calls=%async_computation | async-start | bytes 786432 | tf_op jit(solution)/shard_map/all_to_all | solution.py:140
  102.0 66.3 %all-gather.9.cloned.1.call-start = ((), (), s32[]{:S(2)}) async-start(), calls=%async_computation.3 | async-start | bytes 3538944 | tf_op jit(solution)/shard_map/all_gather | solution.py:34
  128.5 71.3 %all-gather.11.cloned.1.call-start = ((), (), s32[]{:S(2)}) async-start(), calls=%async_computation.4 | async-start | bytes 3538944 | tf_op jit(solution)/shard_map/all_gather | solution.py:150
  (3 other events, 20.8 us)
Sparse Core Ops, SparseCore 0:
  11.0 39.2 all-gather.4
  52.1 33.4 all-gather.6
  128.6 39.5 all-gather.8
  169.9 29.7 all-gather.10

commit v6 on v5

--- a/solution.py
+++ b/solution.py
@@ -112,10 +112,13 @@
     ahead = behind = slots[0]
     for step in range(1, nz // 2 + 1):
         ahead = lax.ppermute(ahead, "sz", up)
-        slots[step % nz] = ahead
         if step <= (nz - 1) // 2:
             behind = lax.ppermute(behind, "sz", down)
+            ahead, behind = lax.optimization_barrier((ahead, behind))
             slots[(-step) % nz] = behind
+        else:
+            ahead = lax.optimization_barrier(ahead)
+        slots[step % nz] = ahead
     kernel = jnp.concatenate([slots[k][0] for k in range(nz)], axis=2)
     both_z = jnp.stack([slots[k][1] for k in range(nz)])
     proj_z = both_z[:, :proj_n].reshape(nz * proj_piece.shape[0], proj_piece.shape[1])
@@ -134,6 +137,8 @@
     bias = jnp.roll(bias, -me_z, axis=0).reshape(nz * width)
     levels = convolve(padded, kernel, plane_rows) + bias[None, :]
     pooled = pool_pairs(levels).astype(jnp.bfloat16)
+    pooled, out_z = lax.optimization_barrier((pooled, out_z))
+    out_weight = lax.all_gather(out_z, "sx", axis=0, tiled=True)
 
     coarse_rows = rows_here // 2
     pieces = pooled.reshape(nx, coarse_rows, nz * width)
@@ -145,9 +150,8 @@
     proj = jnp.dot(sx_major(attn_in, nz, nx, me_z), proj_weight, preferred_element_type=jnp.float32)
     queries = proj[:, :q_cols].astype(jnp.bfloat16)
     keyvals = proj[:, q_cols:].astype(jnp.bfloat16)
+    keyvals, out_weight = lax.optimization_barrier((keyvals, out_weight))
     key_block = gather_rows(keyvals)
-    key_block, out_z = lax.optimization_barrier((key_block, out_z))
-    out_weight = lax.all_gather(out_z, "sx", axis=0, tiled=True)
     context = attend(queries, key_block, head_scale)
     projected = jnp.dot(sx_major(context, nz, nx, me_z), out_weight, preferred_element_type=jnp.float32)
     return (coarse, projected.astype(jnp.bfloat16))

time: 210 us -> 215 us (1.024)
  waiting for transfers between devices: 84.2 us -> 102 us
  starting transfers between devices: 41.2 us -> 31.4 us
    all_gather x1, waiting for transfers between devices: 13.6 us -> 23.1 us  [shards(): out_weight = lax.all_gather(out_z, 'sx', axis=0, tiled=True)]
    ppermute x8, starting transfers between devices: 23.4 us -> 16.7 us  [shards(): ahead = lax.ppermute(ahead, 'sz', up)]
    all_gather x1, waiting for transfers between devices: 38.6 us -> 42.4 us  [gather_rows(): return lax.all_gather(inner, 'sz', axis=0, tiled=True)]
    ppermute x1, starting transfers between devices: 4.25 us -> 1.29 us  [shards(): low = lax.ppermute(plane[plane_rows - 2:], 'sz', forward)]
    ppermute x6, waiting for transfers between devices: 2.8 us -> 5.72 us  [shards(): behind = lax.ppermute(behind, 'sz', down)]
    all_to_all x1, starting transfers between devices: 12 us -> 9.23 us  [shards(): received = lax.all_to_all(pieces, 'sx', 0, 0, tiled=False)]
    ppermute x6, starting transfers between devices: 0.18 us -> 2.57 us  [shards(): behind = lax.ppermute(behind, 'sz', down)]
    unnamed x29 -> x41, local copies, waits for them, and re-layouts: 9.03 us -> 9.22 us
  transfers between devices with their start and end apart: 21 -> 21, of which waited for: 12 -> 10; matrix products, arithmetic and copies ran while one was open for 14% -> 13% of each run, Pallas kernels for 7% -> 0%
where the time goes in v6:
time: 215 us; the launch traced here: 214 us
  waiting for transfers between devices  102 us (47%)
  starting transfers between devices  31.4 us (15%)
  local copies, waits for them, and re-layouts  17.7 us (8%)
  Pallas kernels  15 us (7%)
  between operations  14.2 us (7%)
  blocking collectives  14.1 us (7%)
  matrix products  12.2 us (6%)
  other arithmetic  7.62 us (4%)
    all_gather x1, waiting for transfers between devices, gather_rows(): return lax.all_gather(inner, 'sz', axis=0, tiled=True)  42.4 us
    all_gather x1, waiting for transfers between devices, shards(): out_weight = lax.all_gather(out_z, 'sx', axis=0, tiled=True)  23.1 us
    ppermute x8, waiting for transfers between devices, shards(): ahead = lax.ppermute(ahead, 'sz', up)  22.8 us
    ppermute x8, starting transfers between devices, shards(): ahead = lax.ppermute(ahead, 'sz', up)  16.7 us
    pallas_call x1, Pallas kernels, attend(): pl.pallas_call(head_kernel, grid=(head_count,), in_specs=[pl.BlockSpec(me...  15 us
    all_gather x1, blocking collectives, gather_rows(): inner = lax.all_gather(block, 'sx', axis=0, tiled=True)  14.1 us
    all_to_all x1, starting transfers between devices, shards(): received = lax.all_to_all(pieces, 'sx', 0, 0, tiled=False)  9.23 us
    unnamed x41, local copies, waits for them, and re-layouts  9.22 us
  transfers between devices with their start and end apart: 21, of which 10 were waited for; matrix products, arithmetic and copies ran while one was open for 13% of the time, Pallas kernels for 0%

profile of v6, /device:TPU:1, one launch (start us, length us, event | category | flops | bytes accessed | tf_op | source)
XLA Modules:
  0.0 214.0 jit_solution(4701988299799535464)
XLA Ops:
  8.5 2.4 %fusion.28 = bf16[192,1408]{1,0:T(8,128)(2,1)} fusion(bf16[192,1408]{1,0:T(8,128)(2,1)} %param.9, f32[1408]{0:T(1024)} %param.10, f32[192]{0:T(256)S(1)} %add_rsqrt_fusion), kind=kLoop, calls=%fused_computation.25 | loop fusion | flops 3244032 | bytes 1087744 | tf_op jit(solution)/shard_map/convert_element_type | solution.py:99
  10.9 6.5 %collective-permute-start.1 = (bf16[5,1408,24]{1,2,0:T(8,128)(2,1)}, bf16[5,1408,24]{1,2,0:T(8,128)(2,1)S(1)}, u32[]{:S(2)}, u32[]{:S(2)}) collective-permute-start(bf16[5,1408,24]{1,2,0:T(8,128)(2,1)} %param.11), channel_id=1, source_target_pairs={{0,56},{8,0},{16,8},{24,16},{32,24},{40,32},{48,40},{56,48},{1,57}... | collective-permute-start | bytes 1013768 | tf_op jit(solution)/shard_map/ppermute | solution.py:114
  19.1 2.7 %collective-permute-start.2 = (bf16[216,256]{1,0:T(8,128)(2,1)S(1)}, bf16[216,256]{1,0:T(8,128)(2,1)S(1)}, u32[]{:S(2)}, u32[]{:S(2)}) collective-permute-start(bf16[216,256]{1,0:T(8,128)(2,1)S(1)} %constant_dynamic-update-slice_fusion), channel_id=1, source_target_pairs={{0,56},{8,0},{16,8},{24,16},{32,24},{40,32},{48,40},{56,48},{1,57}... | collective-permute-start | bytes 331784 | tf_op jit(solution)/shard_map/ppermute | solution.py:114
  21.9 4.7 %collective-permute-done.2 = bf16[216,256]{1,0:T(8,128)(2,1)S(1)} collective-permute-done((bf16[216,256]{1,0:T(8,128)(2,1)S(1)}, bf16[216,256]{1,0:T(8,128)(2,1)S(1)}, u32[]{:S(2)}, u32[]{:S(2)}) %collective-permute-start.2) | collective-permute-done | bytes 110624 | tf_op jit(solution)/shard_map/ppermute | solution.py:114
  26.6 3.1 %collective-permute-done.4 = bf16[216,256]{1,0:T(8,128)(2,1)S(1)} collective-permute-done((bf16[216,256]{1,0:T(8,128)(2,1)S(1)}, bf16[216,256]{1,0:T(8,128)(2,1)S(1)}, u32[]{:S(2)}, u32[]{:S(2)}) %collective-permute-start.4) | collective-permute-done | bytes 110624 | tf_op jit(solution)/shard_map/ppermute | solution.py:116
  32.7 7.1 %collective-permute-done.6 = bf16[216,256]{1,0:T(8,128)(2,1)S(1)} collective-permute-done((bf16[216,256]{1,0:T(8,128)(2,1)S(1)}, bf16[216,256]{1,0:T(8,128)(2,1)S(1)}, u32[]{:S(2)}, u32[]{:S(2)}) %collective-permute-start.6) | collective-permute-done | bytes 110624 | tf_op jit(solution)/shard_map/ppermute | solution.py:114
  41.4 2.7 %collective-permute-start.9 = (bf16[5,1408,24]{1,2,0:T(8,128)(2,1)S(1)}, bf16[5,1408,24]{1,2,0:T(8,128)(2,1)S(1)}, u32[]{:S(2)}, u32[]{:S(2)}) collective-permute-start(bf16[5,1408,24]{1,2,0:T(8,128)(2,1)S(1)} %collective-permute-done.5), channel_id=1, source_target_pairs={{0,56},{8,0},{16,8},{24,16},{32,24},{40,32},{48,40},{56,48},{1,57}... | collective-permute-start | bytes 1013768 | tf_op jit(solution)/shard_map/ppermute | solution.py:114
  45.7 5.2 %collective-permute-done.10 = bf16[216,256]{1,0:T(8,128)(2,1)S(1)} collective-permute-done((bf16[216,256]{1,0:T(8,128)(2,1)S(1)}, bf16[216,256]{1,0:T(8,128)(2,1)S(1)}, u32[]{:S(2)}, u32[]{:S(2)}) %collective-permute-start.10) | collective-permute-done | bytes 110624 | tf_op jit(solution)/shard_map/ppermute | solution.py:114
  52.0 2.5 %collective-permute-start.13 = (bf16[5,1408,24]{1,2,0:T(8,128)(2,1)S(1)}, bf16[5,1408,24]{1,2,0:T(8,128)(2,1)S(1)}, u32[]{:S(2)}, u32[]{:S(2)}) collective-permute-start(bf16[5,1408,24]{1,2,0:T(8,128)(2,1)S(1)} %collective-permute-done.9), channel_id=1, source_target_pairs={{0,56},{8,0},{16,8},{24,16},{32,24},{40,32},{48,40},{56,48},{1,57}... | collective-permute-start | bytes 1013768 | tf_op jit(solution)/shard_map/ppermute | solution.py:114
  54.7 5.7 %collective-permute-done.14 = bf16[216,256]{1,0:T(8,128)(2,1)S(1)} collective-permute-done((bf16[216,256]{1,0:T(8,128)(2,1)S(1)}, bf16[216,256]{1,0:T(8,128)(2,1)S(1)}, u32[]{:S(2)}, u32[]{:S(2)}) %collective-permute-start.14) | collective-permute-done | bytes 110624 | tf_op jit(solution)/shard_map/ppermute | solution.py:114
  63.4 1.6 copy-done.6
  72.9 3.0 %constant_dynamic-update-slice_fusion.11 = bf16[1538,1408]{1,0:T(8,128)(2,1)S(1)} fusion(bf16[1536,1408]{1,0:T(8,128)(2,1)} %all-gather.5.cloned.1.call-done), kind=kLoop, calls=%fused_computation.73 | loop fusion | bytes 8650752
  77.6 1.6 fusion.7
  79.2 1.6 fusion.3
  80.8 1.6 fusion.21
  82.4 1.6 fusion.15
  84.7 2.2 %reduce_max.9 = bf16[768,192]{1,0:T(8,128)(2,1)S(1)} reduce(bf16[768,2,192]{2,1,0:T(2,128)(2,1)S(1)} %reshape.75, bf16[]{:T(256)} %constant.198), dimensions={1}, to_apply=%region_1.2 | reduce | flops 147456 | bytes 884738 | tf_op jit(solution)/shard_map/reduce_max | solution.py:29
  87.9 9.2 %all-to-all-start = ((bf16[8,96,192]{1,2,0:T(8,128)(2,1)}), bf16[8,96,192]{1,2,0:T(8,128)(2,1)S(1)}, u32[]{:S(2)}, u32[]{:S(2)}) async-start(bf16[8,96,192]{1,2,0:T(8,128)(2,1)} %copy.25), calls=%async_computation | async-start | bytes 786432 | tf_op jit(solution)/shard_map/all_to_all | solution.py:145
  97.3 7.6 %all-to-all-done = bf16[8,96,192]{1,2,0:T(8,128)(2,1)S(1)} async-done(((bf16[8,96,192]{1,2,0:T(8,128)(2,1)}), bf16[8,96,192]{1,2,0:T(8,128)(2,1)S(1)}, u32[]{:S(2)}, u32[]{:S(2)}) %all-to-all-start) | async-done | bytes 294944 | tf_op jit(solution)/shard_map/all_to_all | solution.py:145
  105.7 2.8 %convolution_convert_fusion.1 = bf16[96,1280]{1,0:T(8,128)(2,1)S(1)} fusion(bf16[96,1536]{0,1:T(8,128)(2,1)S(1)} %bitcast.53, bf16[1536,1280]{1,0:T(8,128)(2,1)} %all-gather.7.cloned.1.call-done), kind=kOutput, calls=%fused_computation.17 | convolution fusion | flops 377610240 | bytes 4472832 | tf_op jit(solution)/shard_map/dot_general | solution.py:150
  108.5 23.1 %all-gather.9.cloned.1.call-done = bf16[1024,1536]{1,0:T(8,128)(2,1)} async-done(((bf16[128,1536]{1,0:T(8,128)(2,1)}), bf16[1024,1536]{1,0:T(8,128)(2,1)}) %all-gather.9.cloned.1.call-update) | async-done | bytes 3145744 | tf_op jit(solution)/shard_map/all_gather | solution.py:141
  131.6 14.1 %all_gather.18 = bf16[768,256]{1,0:T(8,128)(2,1)} all-gather(bf16[96,256]{1,0:T(8,128)(2,1)S(1)} %slice.80), channel_id=1, replica_groups=mesh['dp'=4,'sz'=8,'sx'=8] {'sx'}, dimensions={0}, use_global_device_ids=true | all-gather | bytes 442368 | tf_op jit(solution)/shard_map/all_gather | solution.py:33
  147.4 42.4 %all-gather.11.cloned.1.call-done.k_ref.v_ref = bf16[6144,256]{1,0:T(8,128)(2,1)} async-done(((bf16[768,256]{1,0:T(8,128)(2,1)}), bf16[6144,256]{1,0:T(8,128)(2,1)}) %all-gather.11.cloned.1.call-update) | async-done | bytes 3145744 | tf_op jit(solution)/shard_map/all_gather | solution.py:34
  189.8 15.0 %shard_map.104 = bf16[96,1024]{1,0:T(8,128)(2,1)} custom-call(f32[8]{0:T(128)} %scale_ref.1, bf16[96,1024]{1,0:T(8,128)(2,1)} %slice.79.q_ref, bf16[6144,256]{1,0:T(8,128)(2,1)} %all-gather.11.cloned.1.call-done.k_ref.v_ref, bf16[6144,256]{1,0:T(8,128)(2,1)} %all-gather.11.cloned.1.call-done.k_ref.v_ref), custom_call_target="tpu_custom_call" | custom-call | flops 2415919104 | bytes 3538944 | tf_op jit(solution)/shard_map/pallas_call | solution.py:61
  (108 shorter events, 29.7 us)
Async XLA Ops:
  7.2 62.1 %all-gather.5.cloned.1.call-start = ((), (), s32[]{:S(2)}) async-start(), calls=%async_computation.1 | async-start | bytes 4866048 | tf_op jit(solution)/shard_map/all_gather | solution.py:100
  10.8 51.7 %copy-start.8 = (f32[1536]{0:T(1024)S(1)}, f32[1536]{0:T(1024)}, u32[]{:S(2)}) copy-start(f32[1536]{0:T(1024)} %param.12) | copy-start | bytes 18436
  10.8 51.9 %copy-start.1 = (bf16[5,1408,24]{1,2,0:T(8,128)(2,1)S(1)}, bf16[5,1408,24]{1,2,0:T(8,128)(2,1)}, u32[]{:S(2)}) copy-start(bf16[5,1408,24]{1,2,0:T(8,128)(2,1)} %param.11) | copy-start | bytes 1013764
  10.8 94.9 %all-gather.7.cloned.1.call-start = ((), (), s32[]{:S(2)}) async-start(), calls=%async_computation.2 | async-start | bytes 4423680 | tf_op jit(solution)/shard_map/all_gather | solution.py:126
  10.9 18.8 %collective-permute-start.1 = (bf16[5,1408,24]{1,2,0:T(8,128)(2,1)}, bf16[5,1408,24]{1,2,0:T(8,128)(2,1)S(1)}, u32[]{:S(2)}, u32[]{:S(2)}) collective-permute-start(bf16[5,1408,24]{1,2,0:T(8,128)(2,1)} %param.11), channel_id=1, source_target_pairs={{0,56},{8,0},{16,8},{24,16},{32,24},{40,32},{48,40},{56,48},{1,57}... | collective-permute-start | bytes 1013768 | tf_op jit(solution)/shard_map/ppermute | solution.py:114
  17.4 12.3 %collective-permute-start.3 = (bf16[5,1408,24]{1,2,0:T(8,128)(2,1)}, bf16[5,1408,24]{1,2,0:T(8,128)(2,1)S(1)}, u32[]{:S(2)}, u32[]{:S(2)}) collective-permute-start(bf16[5,1408,24]{1,2,0:T(8,128)(2,1)} %param.11), channel_id=1, source_target_pairs={{0,8},{8,16},{16,24},{24,32},{32,40},{40,48},{48,56},{56,0},{1,9},... | collective-permute-start | bytes 1013768 | tf_op jit(solution)/shard_map/ppermute | solution.py:116
  19.1 7.4 %collective-permute-start.2 = (bf16[216,256]{1,0:T(8,128)(2,1)S(1)}, bf16[216,256]{1,0:T(8,128)(2,1)S(1)}, u32[]{:S(2)}, u32[]{:S(2)}) collective-permute-start(bf16[216,256]{1,0:T(8,128)(2,1)S(1)} %constant_dynamic-update-slice_fusion), channel_id=1, source_target_pairs={{0,56},{8,0},{16,8},{24,16},{32,24},{40,32},{48,40},{56,48},{1,57}... | collective-permute-start | bytes 331784 | tf_op jit(solution)/shard_map/ppermute | solution.py:114
  21.9 7.8 %collective-permute-start.4 = (bf16[216,256]{1,0:T(8,128)(2,1)S(1)}, bf16[216,256]{1,0:T(8,128)(2,1)S(1)}, u32[]{:S(2)}, u32[]{:S(2)}) collective-permute-start(bf16[216,256]{1,0:T(8,128)(2,1)S(1)} %constant_dynamic-update-slice_fusion), channel_id=1, source_target_pairs={{0,8},{8,16},{16,24},{24,32},{32,40},{40,48},{48,56},{56,0},{1,9},... | collective-permute-start | bytes 331784 | tf_op jit(solution)/shard_map/ppermute | solution.py:116
  29.7 11.7 %collective-permute-start.5 = (bf16[5,1408,24]{1,2,0:T(8,128)(2,1)S(1)}, bf16[5,1408,24]{1,2,0:T(8,128)(2,1)S(1)}, u32[]{:S(2)}, u32[]{:S(2)}) collective-permute-start(bf16[5,1408,24]{1,2,0:T(8,128)(2,1)S(1)} %collective-permute-done.1), channel_id=1, source_target_pairs={{0,56},{8,0},{16,8},{24,16},{32,24},{40,32},{48,40},{56,48},{1,57}... | collective-permute-start | bytes 1013768 | tf_op jit(solution)/shard_map/ppermute | solution.py:114
  30.1 11.4 %collective-permute-start.7 = (bf16[5,1408,24]{1,2,0:T(8,128)(2,1)S(1)}, bf16[5,1408,24]{1,2,0:T(8,128)(2,1)S(1)}, u32[]{:S(2)}, u32[]{:S(2)}) collective-permute-start(bf16[5,1408,24]{1,2,0:T(8,128)(2,1)S(1)} %collective-permute-done.3), channel_id=1, source_target_pairs={{0,8},{8,16},{16,24},{24,32},{32,40},{40,48},{48,56},{56,0},{1,9},... | collective-permute-start | bytes 1013768 | tf_op jit(solution)/shard_map/ppermute | solution.py:116
  31.2 8.7 %collective-permute-start.6 = (bf16[216,256]{1,0:T(8,128)(2,1)S(1)}, bf16[216,256]{1,0:T(8,128)(2,1)S(1)}, u32[]{:S(2)}, u32[]{:S(2)}) collective-permute-start(bf16[216,256]{1,0:T(8,128)(2,1)S(1)} %collective-permute-done.2), channel_id=1, source_target_pairs={{0,56},{8,0},{16,8},{24,16},{32,24},{40,32},{48,40},{56,48},{1,57}... | collective-permute-start | bytes 331784 | tf_op jit(solution)/shard_map/ppermute | solution.py:114
  32.7 8.7 %collective-permute-start.8 = (bf16[216,256]{1,0:T(8,128)(2,1)S(1)}, bf16[216,256]{1,0:T(8,128)(2,1)S(1)}, u32[]{:S(2)}, u32[]{:S(2)}) collective-permute-start(bf16[216,256]{1,0:T(8,128)(2,1)S(1)} %collective-permute-done.4), channel_id=1, source_target_pairs={{0,8},{8,16},{16,24},{24,32},{32,40},{40,48},{48,56},{56,0},{1,9},... | collective-permute-start | bytes 331784 | tf_op jit(solution)/shard_map/ppermute | solution.py:116
  41.4 10.5 %collective-permute-start.11 = (bf16[5,1408,24]{1,2,0:T(8,128)(2,1)S(1)}, bf16[5,1408,24]{1,2,0:T(8,128)(2,1)S(1)}, u32[]{:S(2)}, u32[]{:S(2)}) collective-permute-start(bf16[5,1408,24]{1,2,0:T(8,128)(2,1)S(1)} %collective-permute-done.7), channel_id=1, source_target_pairs={{0,8},{8,16},{16,24},{24,32},{32,40},{40,48},{48,56},{56,0},{1,9},... | collective-permute-start | bytes 1013768 | tf_op jit(solution)/shard_map/ppermute | solution.py:116
  41.4 10.5 %collective-permute-start.9 = (bf16[5,1408,24]{1,2,0:T(8,128)(2,1)S(1)}, bf16[5,1408,24]{1,2,0:T(8,128)(2,1)S(1)}, u32[]{:S(2)}, u32[]{:S(2)}) collective-permute-start(bf16[5,1408,24]{1,2,0:T(8,128)(2,1)S(1)} %collective-permute-done.5), channel_id=1, source_target_pairs={{0,56},{8,0},{16,8},{24,16},{32,24},{40,32},{48,40},{56,48},{1,57}... | collective-permute-start | bytes 1013768 | tf_op jit(solution)/shard_map/ppermute | solution.py:114
  44.1 6.8 %collective-permute-start.10 = (bf16[216,256]{1,0:T(8,128)(2,1)S(1)}, bf16[216,256]{1,0:T(8,128)(2,1)S(1)}, u32[]{:S(2)}, u32[]{:S(2)}) collective-permute-start(bf16[216,256]{1,0:T(8,128)(2,1)S(1)} %collective-permute-done.6), channel_id=1, source_target_pairs={{0,56},{8,0},{16,8},{24,16},{32,24},{40,32},{48,40},{56,48},{1,57}... | collective-permute-start | bytes 331784 | tf_op jit(solution)/shard_map/ppermute | solution.py:114
  44.2 7.7 %collective-permute-start.12 = (bf16[216,256]{1,0:T(8,128)(2,1)S(1)}, bf16[216,256]{1,0:T(8,128)(2,1)S(1)}, u32[]{:S(2)}, u32[]{:S(2)}) collective-permute-start(bf16[216,256]{1,0:T(8,128)(2,1)S(1)} %collective-permute-done.8), channel_id=1, source_target_pairs={{0,8},{8,16},{16,24},{24,32},{32,40},{40,48},{48,56},{56,0},{1,9},... | collective-permute-start | bytes 331784 | tf_op jit(solution)/shard_map/ppermute | solution.py:116
  52.0 8.5 %collective-permute-start.13 = (bf16[5,1408,24]{1,2,0:T(8,128)(2,1)S(1)}, bf16[5,1408,24]{1,2,0:T(8,128)(2,1)S(1)}, u32[]{:S(2)}, u32[]{:S(2)}) collective-permute-start(bf16[5,1408,24]{1,2,0:T(8,128)(2,1)S(1)} %collective-permute-done.9), channel_id=1, source_target_pairs={{0,56},{8,0},{16,8},{24,16},{32,24},{40,32},{48,40},{56,48},{1,57}... | collective-permute-start | bytes 1013768 | tf_op jit(solution)/shard_map/ppermute | solution.py:114
  54.4 6.0 %collective-permute-start.14 = (bf16[216,256]{1,0:T(8,128)(2,1)S(1)}, bf16[216,256]{1,0:T(8,128)(2,1)S(1)}, u32[]{:S(2)}, u32[]{:S(2)}) collective-permute-start(bf16[216,256]{1,0:T(8,128)(2,1)S(1)} %collective-permute-done.10), channel_id=1, source_target_pairs={{0,56},{8,0},{16,8},{24,16},{32,24},{40,32},{48,40},{56,48},{1,57}... | collective-permute-start | bytes 331784 | tf_op jit(solution)/shard_map/ppermute | solution.py:114
  62.4 69.2 %all-gather.9.cloned.1.call-start = ((), (), s32[]{:S(2)}) async-start(), calls=%async_computation.3 | async-start | bytes 3538944 | tf_op jit(solution)/shard_map/all_gather | solution.py:141
  70.0 7.6 %collective-permute-start = (bf16[2,1408]{1,0:T(2,128)(2,1)S(1)}, bf16[2,1408]{1,0:T(2,128)(2,1)S(1)}, u32[]{:S(2)}, u32[]{:S(2)}) collective-permute-start(bf16[2,1408]{1,0:T(2,128)(2,1)S(1)} %get-tuple-element.46), channel_id=1, source_target_pairs={{0,8},{8,16},{16,24},{24,32},{32,40},{40,48},{48,56},{1,9},{9,17},... | collective-permute-start | bytes 16904 | tf_op jit(solution)/shard_map/ppermute | solution.py:131
  71.3 6.2 %collective-permute-start.15 = (bf16[2,1408]{1,0:T(2,128)(2,1)S(1)}, bf16[2,1408]{1,0:T(2,128)(2,1)S(1)}, u32[]{:S(2)}, u32[]{:S(2)}) collective-permute-start(bf16[2,1408]{1,0:T(2,128)(2,1)S(1)} %get-tuple-element.47), channel_id=1, source_target_pairs={{8,0},{16,8},{24,16},{32,24},{40,32},{48,40},{56,48},{9,1},{17,9},... | collective-permute-start | bytes 16904 | tf_op jit(solution)/shard_map/ppermute | solution.py:132
  87.9 16.9 %all-to-all-start = ((bf16[8,96,192]{1,2,0:T(8,128)(2,1)}), bf16[8,96,192]{1,2,0:T(8,128)(2,1)S(1)}, u32[]{:S(2)}, u32[]{:S(2)}) async-start(bf16[8,96,192]{1,2,0:T(8,128)(2,1)} %copy.25), calls=%async_computation | async-start | bytes 786432 | tf_op jit(solution)/shard_map/all_to_all | solution.py:145
  97.2 92.7 %all-gather.11.cloned.1.call-start = ((), (), s32[]{:S(2)}) async-start(), calls=%async_computation.4 | async-start | bytes 3538944 | tf_op jit(solution)/shard_map/all_gather | solution.py:34
  147.4 58.7 %copy-start = (bf16[1024,1536]{1,0:T(8,128)(2,1)S(1)}, bf16[1024,1536]{1,0:T(8,128)(2,1)}, u32[]{:S(2)}) copy-start(bf16[1024,1536]{1,0:T(8,128)(2,1)} %all-gather.9.cloned.1.call-done) | copy-start | bytes 9437188
  (9 other events, 42.0 us)
Sparse Core Ops, SparseCore 0:
  11.0 39.2 all-gather.4
  62.6 36.9 all-gather.6
  101.4 30.1 all-gather.8
  145.9 43.8 all-gather.10

commit v7 on v5

--- a/solution.py
+++ b/solution.py
@@ -38,6 +38,23 @@
     rows = columns.shape[0]
     split = jnp.roll(columns.reshape(rows, nz, nx, -1), -me_z, axis=1)
     return split.transpose(0, 2, 1, 3).reshape(rows, columns.shape[1])
+
+
+def ring(value, axis, n):
+    up = [(i, (i - 1) % n) for i in range(n)]
+    down = [(i, (i + 1) % n) for i in range(n)]
+    slots = {0: value}
+    ahead = behind = value
+    for step in range(1, n // 2 + 1):
+        ahead = lax.ppermute(ahead, axis, up)
+        if step <= (n - 1) // 2:
+            behind = lax.ppermute(behind, axis, down)
+            ahead, behind = lax.optimization_barrier((ahead, behind))
+            slots[(-step) % n] = behind
+        else:
+            ahead = lax.optimization_barrier(ahead)
+        slots[step % n] = ahead
+    return [slots[k] for k in range(n)]
 
 
 def head_kernel(scale_ref, q_ref, k_ref, v_ref, o_ref):
@@ -106,18 +123,9 @@
     both = jnp.concatenate(
         [proj_piece.reshape(proj_n, lane), output_weight.reshape(-1, lane)], axis=0
     )
-    up = [(i, (i - 1) % nz) for i in range(nz)]
-    down = [(i, (i + 1) % nz) for i in range(nz)]
-    slots = {0: (conv_weight, both)}
-    ahead = behind = slots[0]
-    for step in range(1, nz // 2 + 1):
-        ahead = lax.ppermute(ahead, "sz", up)
-        slots[step % nz] = ahead
-        if step <= (nz - 1) // 2:
-            behind = lax.ppermute(behind, "sz", down)
-            slots[(-step) % nz] = behind
-    kernel = jnp.concatenate([slots[k][0] for k in range(nz)], axis=2)
-    both_z = jnp.stack([slots[k][1] for k in range(nz)])
+    slots = ring((conv_weight, both), "sz", nz)
+    kernel = jnp.concatenate([s[0] for s in slots], axis=2)
+    both_z = jnp.stack([s[1] for s in slots])
     proj_z = both_z[:, :proj_n].reshape(nz * proj_piece.shape[0], proj_piece.shape[1])
     out_z = both_z[:, proj_n:].reshape(nz * output_weight.shape[0], output_weight.shape[1])
     proj_weight = lax.all_gather(proj_z, "sx", axis=0, tiled=True)
@@ -145,11 +153,15 @@
     proj = jnp.dot(sx_major(attn_in, nz, nx, me_z), proj_weight, preferred_element_type=jnp.float32)
     queries = proj[:, :q_cols].astype(jnp.bfloat16)
     keyvals = proj[:, q_cols:].astype(jnp.bfloat16)
-    key_block = gather_rows(keyvals)
-    key_block, out_z = lax.optimization_barrier((key_block, out_z))
-    out_weight = lax.all_gather(out_z, "sx", axis=0, tiled=True)
+    kv_plane = lax.all_gather(keyvals, "sx", axis=0, tiled=True)
+    kv_plane, out_z = lax.optimization_barrier((kv_plane, out_z))
+    key_block = lax.all_gather(kv_plane, "sz", axis=0, tiled=True)
+    out_weight = jnp.concatenate(ring(out_z, "sx", nx), axis=0)
     context = attend(queries, key_block, head_scale)
-    projected = jnp.dot(sx_major(context, nz, nx, me_z), out_weight, preferred_element_type=jnp.float32)
+    rows = context.shape[0]
+    by_slot = jnp.roll(context.reshape(rows, nz, nx, -1), (-me_z, -me_x), axis=(1, 2))
+    by_slot = by_slot.transpose(0, 2, 1, 3).reshape(rows, context.shape[1])
+    projected = jnp.dot(by_slot, out_weight, preferred_element_type=jnp.float32)
     return (coarse, projected.astype(jnp.bfloat16))
 
 

time: 210 us -> 198 us (0.943)
  waiting for transfers between devices: 84.2 us -> 62.6 us
  local copies, waits for them, and re-layouts: 18 us -> 23.3 us
  matrix products: 14.2 us -> 17.6 us
    all_gather x2 -> x1, waiting for transfers between devices: 52.2 us -> 8.15 us  [shards(): key_block = lax.all_gather(kv_plane, 'sz', axis=0, tiled=True)]
    ppermute x14 -> x21, waiting for transfers between devices: 24.4 us -> 47.1 us  [the longest x12 40.2 us: ring(): ahead = lax.ppermute(ahead, axis, up)]
    unnamed x29 -> x52, local copies, waits for them, and re-layouts: 9.03 us -> 15 us
    dot_general x5, matrix products: 8.09 us -> 13.4 us  [convolve(): jnp.dot(padded[kernel_tap:kernel_tap + row_count], kernel[kernel_tap], pr...]
    ppermute x14 -> x21, starting transfers between devices: 23.5 us -> 27.3 us  [the longest x12 24 us: ring(): ahead = lax.ppermute(ahead, axis, up)]
    all_to_all x1, starting transfers between devices: 12 us -> 8.68 us  [shards(): received = lax.all_to_all(pieces, 'sx', 0, 0, tiled=False)]
  transfers between devices with their start and end apart: 21 -> 27, of which waited for: 12 -> 14; matrix products, arithmetic and copies ran while one was open for 14% -> 20% of each run, Pallas kernels for 7% -> 0%
where the time goes in v7:
time: 198 us; the launch traced here: 197 us
  waiting for transfers between devices  62.6 us (32%)
  starting transfers between devices  41.6 us (21%)
  local copies, waits for them, and re-layouts  23.3 us (12%)
  matrix products  17.6 us (9%)
  blocking collectives  15.1 us (8%)
  Pallas kernels  15 us (8%)
  between operations  14.3 us (7%)
  other arithmetic  7.78 us (4%)
    ppermute x12, waiting for transfers between devices, ring(): ahead = lax.ppermute(ahead, axis, up)  40.2 us
    ppermute x12, starting transfers between devices, ring(): ahead = lax.ppermute(ahead, axis, up)  24 us
    all_gather x1, blocking collectives, shards(): kv_plane = lax.all_gather(keyvals, 'sx', axis=0, tiled=True)  15.1 us
    unnamed x52, local copies, waits for them, and re-layouts  15 us
    pallas_call x1, Pallas kernels, attend(): pl.pallas_call(head_kernel, grid=(head_count,), in_specs=[pl.BlockSpec(me...  15 us
    dot_general x5, matrix products, convolve(): jnp.dot(padded[kernel_tap:kernel_tap + row_count], kernel[kernel_tap], pr...  13.4 us
    all_to_all x1, starting transfers between devices, shards(): received = lax.all_to_all(pieces, 'sx', 0, 0, tiled=False)  8.68 us
    all_gather x1, waiting for transfers between devices, shards(): key_block = lax.all_gather(kv_plane, 'sz', axis=0, tiled=True)  8.15 us
  transfers between devices with their start and end apart: 27, of which 14 were waited for; matrix products, arithmetic and copies ran while one was open for 20% of the time, Pallas kernels for 0%

profile of v7, /device:TPU:1, one launch (start us, length us, event | category | flops | bytes accessed | tf_op | source)
XLA Modules:
  0.0 197.2 jit_solution(13519621695232705084)
XLA Ops:
  10.9 6.5 %collective-permute-start.1 = (bf16[5,1408,24]{1,2,0:T(8,128)(2,1)}, bf16[5,1408,24]{1,2,0:T(8,128)(2,1)S(1)}, u32[]{:S(2)}, u32[]{:S(2)}) collective-permute-start(bf16[5,1408,24]{1,2,0:T(8,128)(2,1)} %param.11), channel_id=1, source_target_pairs={{0,56},{8,0},{16,8},{24,16},{32,24},{40,32},{48,40},{56,48},{1,57}... | collective-permute-start | bytes 1013768 | tf_op jit(solution)/shard_map/ppermute | solution.py:49
  19.2 2.7 %collective-permute-start.2 = (bf16[216,256]{1,0:T(8,128)(2,1)S(1)}, bf16[216,256]{1,0:T(8,128)(2,1)S(1)}, u32[]{:S(2)}, u32[]{:S(2)}) collective-permute-start(bf16[216,256]{1,0:T(8,128)(2,1)S(1)} %constant_dynamic-update-slice_fusion), channel_id=1, source_target_pairs={{0,56},{8,0},{16,8},{24,16},{32,24},{40,32},{48,40},{56,48},{1,57}... | collective-permute-start | bytes 331784 | tf_op jit(solution)/shard_map/ppermute | solution.py:49
  21.9 4.7 %collective-permute-done.2 = bf16[216,256]{1,0:T(8,128)(2,1)S(1)} collective-permute-done((bf16[216,256]{1,0:T(8,128)(2,1)S(1)}, bf16[216,256]{1,0:T(8,128)(2,1)S(1)}, u32[]{:S(2)}, u32[]{:S(2)}) %collective-permute-start.2) | collective-permute-done | bytes 110624 | tf_op jit(solution)/shard_map/ppermute | solution.py:49
  26.6 3.1 %collective-permute-done.4 = bf16[216,256]{1,0:T(8,128)(2,1)S(1)} collective-permute-done((bf16[216,256]{1,0:T(8,128)(2,1)S(1)}, bf16[216,256]{1,0:T(8,128)(2,1)S(1)}, u32[]{:S(2)}, u32[]{:S(2)}) %collective-permute-start.4) | collective-permute-done | bytes 110624 | tf_op jit(solution)/shard_map/ppermute | solution.py:51
  32.8 7.1 %collective-permute-done.6 = bf16[216,256]{1,0:T(8,128)(2,1)S(1)} collective-permute-done((bf16[216,256]{1,0:T(8,128)(2,1)S(1)}, bf16[216,256]{1,0:T(8,128)(2,1)S(1)}, u32[]{:S(2)}, u32[]{:S(2)}) %collective-permute-start.6) | collective-permute-done | bytes 110624 | tf_op jit(solution)/shard_map/ppermute | solution.py:49
  46.2 4.7 %collective-permute-done.10 = bf16[216,256]{1,0:T(8,128)(2,1)S(1)} collective-permute-done((bf16[216,256]{1,0:T(8,128)(2,1)}, bf16[216,256]{1,0:T(8,128)(2,1)S(1)}, u32[]{:S(2)}, u32[]{:S(2)}) %collective-permute-start.10) | collective-permute-done | bytes 110624 | tf_op jit(solution)/shard_map/ppermute | solution.py:49
  54.2 7.2 %collective-permute-done.14 = bf16[216,256]{1,0:T(8,128)(2,1)S(1)} collective-permute-done((bf16[216,256]{1,0:T(8,128)(2,1)S(1)}, bf16[216,256]{1,0:T(8,128)(2,1)S(1)}, u32[]{:S(2)}, u32[]{:S(2)}) %collective-permute-start.14) | collective-permute-done | bytes 110624 | tf_op jit(solution)/shard_map/ppermute | solution.py:49
  71.9 4.2 %collective-permute-start = (bf16[2,1408]{1,0:T(2,128)(2,1)S(1)}, bf16[2,1408]{1,0:T(2,128)(2,1)S(1)}, u32[]{:S(2)}, u32[]{:S(2)}) collective-permute-start(bf16[2,1408]{1,0:T(2,128)(2,1)S(1)} %get-tuple-element.56), channel_id=1, source_target_pairs={{0,8},{8,16},{16,24},{24,32},{32,40},{40,48},{48,56},{1,9},{9,17},... | collective-permute-start | bytes 16904 | tf_op jit(solution)/shard_map/ppermute | solution.py:136
  76.1 2.8 %constant_dynamic-update-slice_fusion.11 = bf16[1538,1408]{1,0:T(8,128)(2,1)S(1)} fusion(bf16[1536,1408]{1,0:T(8,128)(2,1)} %all-gather.4.cloned.1.call-done), kind=kLoop, calls=%fused_computation.76 | loop fusion | bytes 8650752
  84.3 2.7 %fusion.3 = f32[1536,192]{0,1:T(8,128)S(1)} fusion(bf16[1538,1408]{1,0:T(8,128)(2,1)S(1)} %constant_dynamic-update-slice_fusion.10, bf16[5,1408,192]{1,2,0:T(8,128)(2,1)} %constant_dynamic-update-slice_fusion.2), kind=kOutput, calls=%fused_computation.4 | convolution fusion | flops 830472192 | bytes 6045696 | tf_op jit(solution)/shard_map/dot_general | solution.py:20
  87.0 2.7 %fusion.21 = f32[1536,192]{0,1:T(8,128)S(1)} fusion(f32[1536,192]{0,1:T(8,128)S(1)} %fusion.37, f32[1536,192]{0,1:T(8,128)S(1)} %fusion.7, bf16[2,1408]{1,0:T(2,128)(2,1)S(1)} %collective-permute-done, bf16[1536,1408]{1,0:T(8,128)(2,1)S(1)} %bitcast.52, bf16[5,1408,192]{1,2,0:T(8,128)(2,1)} %constant_dynamic-update-slice_fusion.2), kind=kOutput, calls=%fused_computation.15 | convolution fusion | flops 839712768 | bytes 8410624 | tf_op jit(solution)/shard_map/dot_general | solution.py:20
  89.7 2.7 %fusion.15 = bf16[1536,192]{0,1:T(8,128)(2,1)S(1)} fusion(f32[1536,192]{0,1:T(8,128)S(1)} %fusion.3, f32[1536,192]{0,1:T(8,128)S(1)} %fusion.21, bf16[1538,1408]{1,0:T(8,128)(2,1)S(1)} %constant_dynamic-update-slice_fusion.10, f32[192]{0:T(256)S(1)} %add.105, bf16[5,1408,192]{1,2,0:T(8,128)(2,1)} %constant_dynamic-update-slice_fusion.2), kind=kOutput, calls=%fused_computation.13 | convolution fusion | flops 831651840 | bytes 7816192 | tf_op jit(solution)/shard_map/dot_general | solution.py:20
  96.8 8.7 %all-to-all-start = ((bf16[8,96,192]{1,2,0:T(8,128)(2,1)}), bf16[8,96,192]{1,2,0:T(8,128)(2,1)S(1)}, u32[]{:S(2)}, u32[]{:S(2)}) async-start(bf16[8,96,192]{1,2,0:T(8,128)(2,1)} %copy.33), calls=%async_computation | async-start | bytes 786432 | tf_op jit(solution)/shard_map/all_to_all | solution.py:148
  106.0 7.2 %all-to-all-done = bf16[8,96,192]{1,2,0:T(8,128)(2,1)S(1)} async-done(((bf16[8,96,192]{1,2,0:T(8,128)(2,1)}), bf16[8,96,192]{1,2,0:T(8,128)(2,1)S(1)}, u32[]{:S(2)}, u32[]{:S(2)}) %all-to-all-start) | async-done | bytes 294944 | tf_op jit(solution)/shard_map/all_to_all | solution.py:148
  114.1 2.8 %convolution_convert_fusion.1 = bf16[96,1280]{1,0:T(8,128)(2,1)S(1)} fusion(bf16[96,1536]{0,1:T(8,128)(2,1)S(1)} %bitcast.54, bf16[1536,1280]{1,0:T(8,128)(2,1)} %all-gather.6.cloned.1.call-done), kind=kOutput, calls=%fused_computation.17 | convolution fusion | flops 377610240 | bytes 4472832 | tf_op jit(solution)/shard_map/dot_general | solution.py:153
  116.9 15.1 %all_gather.14 = bf16[768,256]{1,0:T(8,128)(2,1)} all-gather(bf16[96,256]{1,0:T(8,128)(2,1)S(1)} %slice.79), channel_id=1, replica_groups=mesh['dp'=4,'sz'=8,'sx'=8] {'sx'}, dimensions={0}, use_global_device_ids=true | all-gather | bytes 442368 | tf_op jit(solution)/shard_map/all_gather | solution.py:156
  133.8 5.8 %collective-permute-done.16 = bf16[128,1536]{1,0:T(8,128)(2,1)S(1)} collective-permute-done((bf16[128,1536]{1,0:T(8,128)(2,1)S(1)}, bf16[128,1536]{1,0:T(8,128)(2,1)S(1)}, u32[]{:S(2)}, u32[]{:S(2)}) %collective-permute-start.16) | collective-permute-done | bytes 393248 | tf_op jit(solution)/shard_map/ppermute | solution.py:49
  143.4 3.8 %collective-permute-done.18 = bf16[128,1536]{1,0:T(8,128)(2,1)} collective-permute-done((bf16[128,1536]{1,0:T(8,128)(2,1)S(1)}, bf16[128,1536]{1,0:T(8,128)(2,1)}, u32[]{:S(2)}, u32[]{:S(2)}) %collective-permute-start.18) | collective-permute-done | bytes 393248 | tf_op jit(solution)/shard_map/ppermute | solution.py:49
  147.1 3.1 %collective-permute-start.20 = (bf16[128,1536]{1,0:T(8,128)(2,1)}, bf16[128,1536]{1,0:T(8,128)(2,1)S(1)}, u32[]{:S(2)}, u32[]{:S(2)}) collective-permute-start(bf16[128,1536]{1,0:T(8,128)(2,1)} %collective-permute-done.18), channel_id=1, source_target_pairs={{0,7},{1,0},{2,1},{3,2},{4,3},{5,4},{6,5},{7,6},{8,15},{9,8},{10,9... | collective-permute-start | bytes 1179656 | tf_op jit(solution)/shard_map/ppermute | solution.py:49
  151.4 3.7 %collective-permute-done.20 = bf16[128,1536]{1,0:T(8,128)(2,1)S(1)} collective-permute-done((bf16[128,1536]{1,0:T(8,128)(2,1)}, bf16[128,1536]{1,0:T(8,128)(2,1)S(1)}, u32[]{:S(2)}, u32[]{:S(2)}) %collective-permute-start.20) | collective-permute-done | bytes 393248 | tf_op jit(solution)/shard_map/ppermute | solution.py:49
  155.3 3.9 %collective-permute-start.22 = (bf16[128,1536]{1,0:T(8,128)(2,1)S(1)}, bf16[128,1536]{1,0:T(8,128)(2,1)S(1)}, u32[]{:S(2)}, u32[]{:S(2)}) collective-permute-start(bf16[128,1536]{1,0:T(8,128)(2,1)S(1)} %collective-permute-done.20), channel_id=1, source_target_pairs={{0,7},{1,0},{2,1},{3,2},{4,3},{5,4},{6,5},{7,6},{8,15},{9,8},{10,9... | collective-permute-start | bytes 1179656 | tf_op jit(solution)/shard_map/ppermute | solution.py:49
  160.2 3.3 %collective-permute-done.22 = bf16[128,1536]{1,0:T(8,128)(2,1)S(1)} collective-permute-done((bf16[128,1536]{1,0:T(8,128)(2,1)S(1)}, bf16[128,1536]{1,0:T(8,128)(2,1)S(1)}, u32[]{:S(2)}, u32[]{:S(2)}) %collective-permute-start.22) | collective-permute-done | bytes 393248 | tf_op jit(solution)/shard_map/ppermute | solution.py:49
  164.7 8.2 %all-gather.8.cloned.1.call-done.k_ref.v_ref = bf16[6144,256]{1,0:T(8,128)(2,1)} async-done(((bf16[768,256]{1,0:T(8,128)(2,1)}), bf16[6144,256]{1,0:T(8,128)(2,1)}) %all-gather.8.cloned.1.call-update) | async-done | bytes 3145744 | tf_op jit(solution)/shard_map/all_gather | solution.py:158
  172.8 15.0 %shard_map.104 = bf16[96,1024]{1,0:T(8,128)(2,1)} custom-call(f32[8]{0:T(128)} %scale_ref.1, bf16[96,1024]{1,0:T(8,128)(2,1)} %slice.78.q_ref, bf16[6144,256]{1,0:T(8,128)(2,1)} %all-gather.8.cloned.1.call-done.k_ref.v_ref, bf16[6144,256]{1,0:T(8,128)(2,1)} %all-gather.8.cloned.1.call-done.k_ref.v_ref), custom_call_target="tpu_custom_call" | custom-call | flops 2415919104 | bytes 3538944 | tf_op jit(solution)/shard_map/pallas_call | solution.py:78
  (134 shorter events, 51.3 us)
Async XLA Ops:
  7.2 62.6 %all-gather.4.cloned.1.call-start = ((), (), s32[]{:S(2)}) async-start(), calls=%async_computation.1 | async-start | bytes 4866048 | tf_op jit(solution)/shard_map/all_gather | solution.py:117
  10.9 103.2 %all-gather.6.cloned.1.call-start = ((), (), s32[]{:S(2)}) async-start(), calls=%async_computation.2 | async-start | bytes 4423680 | tf_op jit(solution)/shard_map/all_gather | solution.py:131
  10.9 18.8 %collective-permute-start.1 = (bf16[5,1408,24]{1,2,0:T(8,128)(2,1)}, bf16[5,1408,24]{1,2,0:T(8,128)(2,1)S(1)}, u32[]{:S(2)}, u32[]{:S(2)}) collective-permute-start(bf16[5,1408,24]{1,2,0:T(8,128)(2,1)} %param.11), channel_id=1, source_target_pairs={{0,56},{8,0},{16,8},{24,16},{32,24},{40,32},{48,40},{56,48},{1,57}... | collective-permute-start | bytes 1013768 | tf_op jit(solution)/shard_map/ppermute | solution.py:49
  17.4 12.3 %collective-permute-start.3 = (bf16[5,1408,24]{1,2,0:T(8,128)(2,1)}, bf16[5,1408,24]{1,2,0:T(8,128)(2,1)S(1)}, u32[]{:S(2)}, u32[]{:S(2)}) collective-permute-start(bf16[5,1408,24]{1,2,0:T(8,128)(2,1)} %param.11), channel_id=1, source_target_pairs={{0,8},{8,16},{16,24},{24,32},{32,40},{40,48},{48,56},{56,0},{1,9},... | collective-permute-start | bytes 1013768 | tf_op jit(solution)/shard_map/ppermute | solution.py:51
  19.2 7.4 %collective-permute-start.2 = (bf16[216,256]{1,0:T(8,128)(2,1)S(1)}, bf16[216,256]{1,0:T(8,128)(2,1)S(1)}, u32[]{:S(2)}, u32[]{:S(2)}) collective-permute-start(bf16[216,256]{1,0:T(8,128)(2,1)S(1)} %constant_dynamic-update-slice_fusion), channel_id=1, source_target_pairs={{0,56},{8,0},{16,8},{24,16},{32,24},{40,32},{48,40},{56,48},{1,57}... | collective-permute-start | bytes 331784 | tf_op jit(solution)/shard_map/ppermute | solution.py:49
  21.9 7.8 %collective-permute-start.4 = (bf16[216,256]{1,0:T(8,128)(2,1)S(1)}, bf16[216,256]{1,0:T(8,128)(2,1)S(1)}, u32[]{:S(2)}, u32[]{:S(2)}) collective-permute-start(bf16[216,256]{1,0:T(8,128)(2,1)S(1)} %constant_dynamic-update-slice_fusion), channel_id=1, source_target_pairs={{0,8},{8,16},{16,24},{24,32},{32,40},{40,48},{48,56},{56,0},{1,9},... | collective-permute-start | bytes 331784 | tf_op jit(solution)/shard_map/ppermute | solution.py:51
  29.7 11.7 %collective-permute-start.5 = (bf16[5,1408,24]{1,2,0:T(8,128)(2,1)S(1)}, bf16[5,1408,24]{1,2,0:T(8,128)(2,1)S(1)}, u32[]{:S(2)}, u32[]{:S(2)}) collective-permute-start(bf16[5,1408,24]{1,2,0:T(8,128)(2,1)S(1)} %collective-permute-done.1), channel_id=1, source_target_pairs={{0,56},{8,0},{16,8},{24,16},{32,24},{40,32},{48,40},{56,48},{1,57}... | collective-permute-start | bytes 1013768 | tf_op jit(solution)/shard_map/ppermute | solution.py:49
  30.1 11.4 %collective-permute-start.7 = (bf16[5,1408,24]{1,2,0:T(8,128)(2,1)S(1)}, bf16[5,1408,24]{1,2,0:T(8,128)(2,1)S(1)}, u32[]{:S(2)}, u32[]{:S(2)}) collective-permute-start(bf16[5,1408,24]{1,2,0:T(8,128)(2,1)S(1)} %collective-permute-done.3), channel_id=1, source_target_pairs={{0,8},{8,16},{16,24},{24,32},{32,40},{40,48},{48,56},{56,0},{1,9},... | collective-permute-start | bytes 1013768 | tf_op jit(solution)/shard_map/ppermute | solution.py:51
  31.2 8.7 %collective-permute-start.6 = (bf16[216,256]{1,0:T(8,128)(2,1)S(1)}, bf16[216,256]{1,0:T(8,128)(2,1)S(1)}, u32[]{:S(2)}, u32[]{:S(2)}) collective-permute-start(bf16[216,256]{1,0:T(8,128)(2,1)S(1)} %collective-permute-done.2), channel_id=1, source_target_pairs={{0,56},{8,0},{16,8},{24,16},{32,24},{40,32},{48,40},{56,48},{1,57}... | collective-permute-start | bytes 331784 | tf_op jit(solution)/shard_map/ppermute | solution.py:49
  32.8 8.7 %collective-permute-start.8 = (bf16[216,256]{1,0:T(8,128)(2,1)S(1)}, bf16[216,256]{1,0:T(8,128)(2,1)S(1)}, u32[]{:S(2)}, u32[]{:S(2)}) collective-permute-start(bf16[216,256]{1,0:T(8,128)(2,1)S(1)} %collective-permute-done.4), channel_id=1, source_target_pairs={{0,8},{8,16},{16,24},{24,32},{32,40},{40,48},{48,56},{56,0},{1,9},... | collective-permute-start | bytes 331784 | tf_op jit(solution)/shard_map/ppermute | solution.py:51
  41.5 11.4 %collective-permute-start.9 = (bf16[5,1408,24]{1,2,0:T(8,128)(2,1)S(1)}, bf16[5,1408,24]{1,2,0:T(8,128)(2,1)S(1)}, u32[]{:S(2)}, u32[]{:S(2)}) collective-permute-start(bf16[5,1408,24]{1,2,0:T(8,128)(2,1)S(1)} %collective-permute-done.5), channel_id=1, source_target_pairs={{0,56},{8,0},{16,8},{24,16},{32,24},{40,32},{48,40},{56,48},{1,57}... | collective-permute-start | bytes 1013768 | tf_op jit(solution)/shard_map/ppermute | solution.py:49
  42.4 10.5 %collective-permute-start.11 = (bf16[5,1408,24]{1,2,0:T(8,128)(2,1)S(1)}, bf16[5,1408,24]{1,2,0:T(8,128)(2,1)S(1)}, u32[]{:S(2)}, u32[]{:S(2)}) collective-permute-start(bf16[5,1408,24]{1,2,0:T(8,128)(2,1)S(1)} %collective-permute-done.7), channel_id=1, source_target_pairs={{0,8},{8,16},{16,24},{24,32},{32,40},{40,48},{48,56},{56,0},{1,9},... | collective-permute-start | bytes 1013768 | tf_op jit(solution)/shard_map/ppermute | solution.py:51
  43.2 7.7 %collective-permute-start.10 = (bf16[216,256]{1,0:T(8,128)(2,1)}, bf16[216,256]{1,0:T(8,128)(2,1)S(1)}, u32[]{:S(2)}, u32[]{:S(2)}) collective-permute-start(bf16[216,256]{1,0:T(8,128)(2,1)} %copy-done.9), channel_id=1, source_target_pairs={{0,56},{8,0},{16,8},{24,16},{32,24},{40,32},{48,40},{56,48},{1,57}... | collective-permute-start | bytes 331784 | tf_op jit(solution)/shard_map/ppermute | solution.py:49
  45.3 7.6 %collective-permute-start.12 = (bf16[216,256]{1,0:T(8,128)(2,1)S(1)}, bf16[216,256]{1,0:T(8,128)(2,1)S(1)}, u32[]{:S(2)}, u32[]{:S(2)}) collective-permute-start(bf16[216,256]{1,0:T(8,128)(2,1)S(1)} %collective-permute-done.8), channel_id=1, source_target_pairs={{0,8},{8,16},{16,24},{24,32},{32,40},{40,48},{48,56},{56,0},{1,9},... | collective-permute-start | bytes 331784 | tf_op jit(solution)/shard_map/ppermute | solution.py:51
  52.9 8.5 %collective-permute-start.13 = (bf16[5,1408,24]{1,2,0:T(8,128)(2,1)S(1)}, bf16[5,1408,24]{1,2,0:T(8,128)(2,1)S(1)}, u32[]{:S(2)}, u32[]{:S(2)}) collective-permute-start(bf16[5,1408,24]{1,2,0:T(8,128)(2,1)S(1)} %collective-permute-done.9), channel_id=1, source_target_pairs={{0,56},{8,0},{16,8},{24,16},{32,24},{40,32},{48,40},{56,48},{1,57}... | collective-permute-start | bytes 1013768 | tf_op jit(solution)/shard_map/ppermute | solution.py:49
  70.5 11.1 %collective-permute-start.15 = (bf16[2,1408]{1,0:T(2,128)(2,1)S(1)}, bf16[2,1408]{1,0:T(2,128)(2,1)S(1)}, u32[]{:S(2)}, u32[]{:S(2)}) collective-permute-start(bf16[2,1408]{1,0:T(2,128)(2,1)S(1)} %get-tuple-element.57), channel_id=1, source_target_pairs={{8,0},{16,8},{24,16},{32,24},{40,32},{48,40},{56,48},{9,1},{17,9},... | collective-permute-start | bytes 16904 | tf_op jit(solution)/shard_map/ppermute | solution.py:137
  71.9 9.8 %collective-permute-start = (bf16[2,1408]{1,0:T(2,128)(2,1)S(1)}, bf16[2,1408]{1,0:T(2,128)(2,1)S(1)}, u32[]{:S(2)}, u32[]{:S(2)}) collective-permute-start(bf16[2,1408]{1,0:T(2,128)(2,1)S(1)} %get-tuple-element.56), channel_id=1, source_target_pairs={{0,8},{8,16},{16,24},{24,32},{32,40},{40,48},{48,56},{1,9},{9,17},... | collective-permute-start | bytes 16904 | tf_op jit(solution)/shard_map/ppermute | solution.py:136
  96.8 16.4 %all-to-all-start = ((bf16[8,96,192]{1,2,0:T(8,128)(2,1)}), bf16[8,96,192]{1,2,0:T(8,128)(2,1)S(1)}, u32[]{:S(2)}, u32[]{:S(2)}) async-start(bf16[8,96,192]{1,2,0:T(8,128)(2,1)} %copy.33), calls=%async_computation | async-start | bytes 786432 | tf_op jit(solution)/shard_map/all_to_all | solution.py:148
  105.5 67.3 %all-gather.8.cloned.1.call-start = ((), (), s32[]{:S(2)}) async-start(), calls=%async_computation.3 | async-start | bytes 3538944 | tf_op jit(solution)/shard_map/all_gather | solution.py:158
  132.0 7.5 %collective-permute-start.16 = (bf16[128,1536]{1,0:T(8,128)(2,1)S(1)}, bf16[128,1536]{1,0:T(8,128)(2,1)S(1)}, u32[]{:S(2)}, u32[]{:S(2)}) collective-permute-start(bf16[128,1536]{1,0:T(8,128)(2,1)S(1)} %reshape.80), channel_id=1, source_target_pairs={{0,7},{1,0},{2,1},{3,2},{4,3},{5,4},{6,5},{7,6},{8,15},{9,8},{10,9... | collective-permute-start | bytes 1179656 | tf_op jit(solution)/shard_map/ppermute | solution.py:49
  132.2 7.3 %collective-permute-start.17 = (bf16[128,1536]{1,0:T(8,128)(2,1)S(1)}, bf16[128,1536]{1,0:T(8,128)(2,1)S(1)}, u32[]{:S(2)}, u32[]{:S(2)}) collective-permute-start(bf16[128,1536]{1,0:T(8,128)(2,1)S(1)} %reshape.80), channel_id=1, source_target_pairs={{0,1},{1,2},{2,3},{3,4},{4,5},{5,6},{6,7},{7,0},{8,9},{9,10},{10,1... | collective-permute-start | bytes 1179656 | tf_op jit(solution)/shard_map/ppermute | solution.py:51
  139.5 7.6 %collective-permute-start.18 = (bf16[128,1536]{1,0:T(8,128)(2,1)S(1)}, bf16[128,1536]{1,0:T(8,128)(2,1)}, u32[]{:S(2)}, u32[]{:S(2)}) collective-permute-start(bf16[128,1536]{1,0:T(8,128)(2,1)S(1)} %collective-permute-done.16), channel_id=1, source_target_pairs={{0,7},{1,0},{2,1},{3,2},{4,3},{5,4},{6,5},{7,6},{8,15},{9,8},{10,9... | collective-permute-start | bytes 1179656 | tf_op jit(solution)/shard_map/ppermute | solution.py:49
  147.1 8.0 %collective-permute-start.20 = (bf16[128,1536]{1,0:T(8,128)(2,1)}, bf16[128,1536]{1,0:T(8,128)(2,1)S(1)}, u32[]{:S(2)}, u32[]{:S(2)}) collective-permute-start(bf16[128,1536]{1,0:T(8,128)(2,1)} %collective-permute-done.18), channel_id=1, source_target_pairs={{0,7},{1,0},{2,1},{3,2},{4,3},{5,4},{6,5},{7,6},{8,15},{9,8},{10,9... | collective-permute-start | bytes 1179656 | tf_op jit(solution)/shard_map/ppermute | solution.py:49
  155.3 8.2 %collective-permute-start.22 = (bf16[128,1536]{1,0:T(8,128)(2,1)S(1)}, bf16[128,1536]{1,0:T(8,128)(2,1)S(1)}, u32[]{:S(2)}, u32[]{:S(2)}) collective-permute-start(bf16[128,1536]{1,0:T(8,128)(2,1)S(1)} %collective-permute-done.20), channel_id=1, source_target_pairs={{0,7},{1,0},{2,1},{3,2},{4,3},{5,4},{6,5},{7,6},{8,15},{9,8},{10,9... | collective-permute-start | bytes 1179656 | tf_op jit(solution)/shard_map/ppermute | solution.py:49
  (17 other events, 200.6 us)
Sparse Core Ops, SparseCore 0:
  11.0 39.2 all-gather.3
  63.5 35.1 all-gather.5
  132.1 40.6 all-gather.7

commit v8 on v7

--- a/solution.py
+++ b/solution.py
@@ -70,10 +70,10 @@
     o_ref[...] = (context / total).astype(o_ref.dtype)
 
 
-def attend(queries, key_block, scales):
+def attend(queries, keys_all, values_all, scales):
     row_count = queries.shape[0]
     head_count = scales.shape[0]
-    key_count = key_block.shape[0]
+    key_count = keys_all.shape[0]
     flops = 4 * head_count * row_count * key_count * HEAD_DIM
     return pl.pallas_call(
         head_kernel,
@@ -82,16 +82,16 @@
             pl.BlockSpec(memory_space=pltpu.SMEM),
             pl.BlockSpec((row_count, HEAD_DIM), lambda h: (0, h)),
             pl.BlockSpec((key_count, HEAD_DIM), lambda h: (0, 0)),
-            pl.BlockSpec((key_count, HEAD_DIM), lambda h: (0, 1)),
+            pl.BlockSpec((key_count, HEAD_DIM), lambda h: (0, 0)),
         ],
         out_specs=pl.BlockSpec((row_count, HEAD_DIM), lambda h: (0, h)),
         out_shape=jax.ShapeDtypeStruct((row_count, head_count * HEAD_DIM), jnp.bfloat16),
         cost_estimate=pl.CostEstimate(
             flops=flops,
             transcendentals=head_count * row_count * key_count,
-            bytes_accessed=2 * key_block.size + 4 * queries.size,
+            bytes_accessed=2 * (keys_all.size + values_all.size) + 4 * queries.size,
         ),
-    )(scales, queries, key_block, key_block)
+    )(scales, queries, keys_all, values_all)
 
 
 def shards(
@@ -155,9 +155,11 @@
     keyvals = proj[:, q_cols:].astype(jnp.bfloat16)
     kv_plane = lax.all_gather(keyvals, "sx", axis=0, tiled=True)
     kv_plane, out_z = lax.optimization_barrier((kv_plane, out_z))
-    key_block = lax.all_gather(kv_plane, "sz", axis=0, tiled=True)
+    keys_all = lax.all_gather(kv_plane[:, :HEAD_DIM], "sz", axis=0, tiled=True)
+    value_slots = jnp.stack(ring(kv_plane[:, HEAD_DIM:], "sz", nz))
+    values_all = jnp.roll(value_slots, me_z, axis=0).reshape(keys_all.shape)
     out_weight = jnp.concatenate(ring(out_z, "sx", nx), axis=0)
-    context = attend(queries, key_block, head_scale)
+    context = attend(queries, keys_all, values_all, head_scale)
     rows = context.shape[0]
     by_slot = jnp.roll(context.reshape(rows, nz, nx, -1), (-me_z, -me_x), axis=(1, 2))
     by_slot = by_slot.transpose(0, 2, 1, 3).reshape(rows, context.shape[1])

time: 198 us -> 214 us (1.081)
  local copies, waits for them, and re-layouts: 23.3 us -> 31.8 us
  starting transfers between devices: 41.6 us -> 47.8 us
    all_gather x1, waiting for transfers between devices: 8.15 us -> 0.02 us  [shards(): keys_all = lax.all_gather(kv_plane[:, :HEAD_DIM], 'sz', axis=0, tiled=True)]
    ppermute x9 -> x12, waiting for transfers between devices: 6.95 us -> 12.8 us  [ring(): behind = lax.ppermute(behind, axis, down)]
    ppermute x12 -> x16, waiting for transfers between devices: 40.2 us -> 44.1 us  [ring(): ahead = lax.ppermute(ahead, axis, up)]
    ppermute x9 -> x12, starting transfers between devices: 3.33 us -> 6.61 us  [ring(): behind = lax.ppermute(behind, axis, down)]
    unnamed x52 -> x57, local copies, waits for them, and re-layouts: 15 us -> 18.1 us
    ppermute x12 -> x16, starting transfers between devices: 24 us -> 27 us  [ring(): ahead = lax.ppermute(ahead, axis, up)]
  transfers between devices with their start and end apart: 27 -> 34, of which waited for: 14 -> 17; matrix products, arithmetic and copies ran while one was open for 20% -> 22% of each run, Pallas kernels for 0% -> 0%
where the time goes in v8:
time: 214 us; the launch traced here: 212 us
  waiting for transfers between devices  63.4 us (30%)
  starting transfers between devices  47.8 us (22%)
  local copies, waits for them, and re-layouts  31.8 us (15%)
  matrix products  17.6 us (8%)
  Pallas kernels  15 us (7%)
  between operations  14.3 us (7%)
  blocking collectives  14 us (7%)
  other arithmetic  7.82 us (4%)
    ppermute x16, waiting for transfers between devices, ring(): ahead = lax.ppermute(ahead, axis, up)  44.1 us
    ppermute x16, starting transfers between devices, ring(): ahead = lax.ppermute(ahead, axis, up)  27 us
    unnamed x57, local copies, waits for them, and re-layouts  18.1 us
    pallas_call x1, Pallas kernels, attend(): pl.pallas_call(head_kernel, grid=(head_count,), in_specs=[pl.BlockSpec(me...  15 us
    all_gather x1, blocking collectives, shards(): kv_plane = lax.all_gather(keyvals, 'sx', axis=0, tiled=True)  14 us
    dot_general x5, matrix products, convolve(): jnp.dot(padded[kernel_tap:kernel_tap + row_count], kernel[kernel_tap], pr...  13.4 us
    ppermute x12, waiting for transfers between devices, ring(): behind = lax.ppermute(behind, axis, down)  12.8 us
    all_to_all x1, starting transfers between devices, shards(): received = lax.all_to_all(pieces, 'sx', 0, 0, tiled=False)  8.65 us
  transfers between devices with their start and end apart: 34, of which 17 were waited for; matrix products, arithmetic and copies ran while one was open for 22% of the time, Pallas kernels for 0%

profile of v8, /device:TPU:1, one launch (start us, length us, event | category | flops | bytes accessed | tf_op | source)
XLA Modules:
  0.0 211.8 jit_solution(6522306131493212098)
XLA Ops:
  10.9 6.5 %collective-permute-start.1 = (bf16[5,1408,24]{1,2,0:T(8,128)(2,1)}, bf16[5,1408,24]{1,2,0:T(8,128)(2,1)S(1)}, u32[]{:S(2)}, u32[]{:S(2)}) collective-permute-start(bf16[5,1408,24]{1,2,0:T(8,128)(2,1)} %param.11), channel_id=1, source_target_pairs={{0,56},{8,0},{16,8},{24,16},{32,24},{40,32},{48,40},{56,48},{1,57}... | collective-permute-start | bytes 1013768 | tf_op jit(solution)/shard_map/ppermute | solution.py:49
  19.2 2.7 %collective-permute-start.2 = (bf16[216,256]{1,0:T(8,128)(2,1)S(1)}, bf16[216,256]{1,0:T(8,128)(2,1)S(1)}, u32[]{:S(2)}, u32[]{:S(2)}) collective-permute-start(bf16[216,256]{1,0:T(8,128)(2,1)S(1)} %constant_dynamic-update-slice_fusion), channel_id=1, source_target_pairs={{0,56},{8,0},{16,8},{24,16},{32,24},{40,32},{48,40},{56,48},{1,57}... | collective-permute-start | bytes 331784 | tf_op jit(solution)/shard_map/ppermute | solution.py:49
  21.9 4.7 %collective-permute-done.2 = bf16[216,256]{1,0:T(8,128)(2,1)S(1)} collective-permute-done((bf16[216,256]{1,0:T(8,128)(2,1)S(1)}, bf16[216,256]{1,0:T(8,128)(2,1)S(1)}, u32[]{:S(2)}, u32[]{:S(2)}) %collective-permute-start.2) | collective-permute-done | bytes 110624 | tf_op jit(solution)/shard_map/ppermute | solution.py:49
  26.6 3.1 %collective-permute-done.4 = bf16[216,256]{1,0:T(8,128)(2,1)S(1)} collective-permute-done((bf16[216,256]{1,0:T(8,128)(2,1)S(1)}, bf16[216,256]{1,0:T(8,128)(2,1)S(1)}, u32[]{:S(2)}, u32[]{:S(2)}) %collective-permute-start.4) | collective-permute-done | bytes 110624 | tf_op jit(solution)/shard_map/ppermute | solution.py:51
  32.8 7.1 %collective-permute-done.6 = bf16[216,256]{1,0:T(8,128)(2,1)S(1)} collective-permute-done((bf16[216,256]{1,0:T(8,128)(2,1)S(1)}, bf16[216,256]{1,0:T(8,128)(2,1)S(1)}, u32[]{:S(2)}, u32[]{:S(2)}) %collective-permute-start.6) | collective-permute-done | bytes 110624 | tf_op jit(solution)/shard_map/ppermute | solution.py:49
  46.9 4.0 %collective-permute-done.10 = bf16[216,256]{1,0:T(8,128)(2,1)S(1)} collective-permute-done((bf16[216,256]{1,0:T(8,128)(2,1)}, bf16[216,256]{1,0:T(8,128)(2,1)S(1)}, u32[]{:S(2)}, u32[]{:S(2)}) %collective-permute-start.10) | collective-permute-done | bytes 110624 | tf_op jit(solution)/shard_map/ppermute | solution.py:49
  54.3 7.2 %collective-permute-done.14 = bf16[216,256]{1,0:T(8,128)(2,1)S(1)} collective-permute-done((bf16[216,256]{1,0:T(8,128)(2,1)S(1)}, bf16[216,256]{1,0:T(8,128)(2,1)S(1)}, u32[]{:S(2)}, u32[]{:S(2)}) %collective-permute-start.14) | collective-permute-done | bytes 110624 | tf_op jit(solution)/shard_map/ppermute | solution.py:49
  72.8 4.2 %collective-permute-start = (bf16[2,1408]{1,0:T(2,128)(2,1)S(1)}, bf16[2,1408]{1,0:T(2,128)(2,1)S(1)}, u32[]{:S(2)}, u32[]{:S(2)}) collective-permute-start(bf16[2,1408]{1,0:T(2,128)(2,1)S(1)} %get-tuple-element.68), channel_id=1, source_target_pairs={{0,8},{8,16},{16,24},{24,32},{32,40},{40,48},{48,56},{1,9},{9,17},... | collective-permute-start | bytes 16904 | tf_op jit(solution)/shard_map/ppermute | solution.py:136
  77.0 2.9 %constant_dynamic-update-slice_fusion.11 = bf16[1538,1408]{1,0:T(8,128)(2,1)S(1)} fusion(bf16[1536,1408]{1,0:T(8,128)(2,1)} %all-gather.4.cloned.1.call-done), kind=kLoop, calls=%fused_computation.91 | loop fusion | bytes 8650752
  82.6 2.6 %fusion.7 = f32[1536,192]{0,1:T(8,128)S(1)} fusion(bf16[1536,1408]{1,0:T(8,128)(2,1)S(1)} %bitcast.77, bf16[2,1408]{1,0:T(2,128)(2,1)S(1)} %collective-permute-done, bf16[5,1408,192]{1,2,0:T(8,128)(2,1)} %constant_dynamic-update-slice_fusion.2), kind=kOutput, calls=%fused_computation.9 | convolution fusion | flops 839122944 | bytes 6051328 | tf_op jit(solution)/shard_map/dot_general | solution.py:20
  85.3 2.7 %fusion.3 = f32[1536,192]{0,1:T(8,128)S(1)} fusion(bf16[1538,1408]{1,0:T(8,128)(2,1)S(1)} %constant_dynamic-update-slice_fusion.10, bf16[5,1408,192]{1,2,0:T(8,128)(2,1)} %constant_dynamic-update-slice_fusion.2), kind=kOutput, calls=%fused_computation.4 | convolution fusion | flops 830472192 | bytes 6045696 | tf_op jit(solution)/shard_map/dot_general | solution.py:20
  88.0 2.7 %fusion.21 = f32[1536,192]{0,1:T(8,128)S(1)} fusion(f32[1536,192]{0,1:T(8,128)S(1)} %fusion.37, f32[1536,192]{0,1:T(8,128)S(1)} %fusion.7, bf16[2,1408]{1,0:T(2,128)(2,1)S(1)} %collective-permute-done, bf16[1536,1408]{1,0:T(8,128)(2,1)S(1)} %bitcast.77, bf16[5,1408,192]{1,2,0:T(8,128)(2,1)} %constant_dynamic-update-slice_fusion.2), kind=kOutput, calls=%fused_computation.15 | convolution fusion | flops 839712768 | bytes 8410624 | tf_op jit(solution)/shard_map/dot_general | solution.py:20
  90.7 2.8 %fusion.15 = bf16[1536,192]{0,1:T(8,128)(2,1)S(1)} fusion(f32[1536,192]{0,1:T(8,128)S(1)} %fusion.3, f32[1536,192]{0,1:T(8,128)S(1)} %fusion.21, bf16[1538,1408]{1,0:T(8,128)(2,1)S(1)} %constant_dynamic-update-slice_fusion.10, f32[192]{0:T(256)S(1)} %add.109, bf16[5,1408,192]{1,2,0:T(8,128)(2,1)} %constant_dynamic-update-slice_fusion.2), kind=kOutput, calls=%fused_computation.13 | convolution fusion | flops 831651840 | bytes 7816192 | tf_op jit(solution)/shard_map/dot_general | solution.py:20
  97.8 8.6 %all-to-all-start = ((bf16[8,96,192]{1,2,0:T(8,128)(2,1)}), bf16[8,96,192]{1,2,0:T(8,128)(2,1)S(1)}, u32[]{:S(2)}, u32[]{:S(2)}) async-start(bf16[8,96,192]{1,2,0:T(8,128)(2,1)} %copy.33), calls=%async_computation | async-start | bytes 786432 | tf_op jit(solution)/shard_map/all_to_all | solution.py:148
  107.7 6.4 %all-to-all-done = bf16[8,96,192]{1,2,0:T(8,128)(2,1)S(1)} async-done(((bf16[8,96,192]{1,2,0:T(8,128)(2,1)}), bf16[8,96,192]{1,2,0:T(8,128)(2,1)S(1)}, u32[]{:S(2)}, u32[]{:S(2)}) %all-to-all-start) | async-done | bytes 294944 | tf_op jit(solution)/shard_map/all_to_all | solution.py:148
  115.9 2.8 %convolution_convert_fusion.1 = bf16[96,1280]{1,0:T(8,128)(2,1)S(1)} fusion(bf16[96,1536]{0,1:T(8,128)(2,1)S(1)} %bitcast.79, bf16[1536,1280]{1,0:T(8,128)(2,1)} %all-gather.6.cloned.1.call-done), kind=kOutput, calls=%fused_computation.17 | convolution fusion | flops 377610240 | bytes 4472832 | tf_op jit(solution)/shard_map/dot_general | solution.py:153
  119.4 14.0 %all_gather.14 = bf16[768,256]{1,0:T(8,128)(2,1)S(1)} all-gather(bf16[96,256]{1,0:T(8,128)(2,1)S(1)} %slice.87), channel_id=1, replica_groups=mesh['dp'=4,'sz'=8,'sx'=8] {'sx'}, dimensions={0}, use_global_device_ids=true | all-gather | bytes 442368 | tf_op jit(solution)/shard_map/all_gather | solution.py:156
  144.5 3.2 %collective-permute-done.18 = bf16[768,128]{1,0:T(8,128)(2,1)S(1)} collective-permute-done((bf16[768,128]{1,0:T(8,128)(2,1)}, bf16[768,128]{1,0:T(8,128)(2,1)S(1)}, u32[]{:S(2)}, u32[]{:S(2)}) %collective-permute-start.18) | collective-permute-done | bytes 196640 | tf_op jit(solution)/shard_map/ppermute | solution.py:49
  155.9 3.3 %collective-permute-done.21 = bf16[768,128]{1,0:T(8,128)(2,1)S(1)} collective-permute-done((bf16[768,128]{1,0:T(8,128)(2,1)S(1)}, bf16[768,128]{1,0:T(8,128)(2,1)S(1)}, u32[]{:S(2)}, u32[]{:S(2)}) %collective-permute-start.21) | collective-permute-done | bytes 196640 | tf_op jit(solution)/shard_map/ppermute | solution.py:51
  160.4 7.0 %collective-permute-done.22 = bf16[768,128]{1,0:T(8,128)(2,1)S(1)} collective-permute-done((bf16[768,128]{1,0:T(8,128)(2,1)S(1)}, bf16[768,128]{1,0:T(8,128)(2,1)S(1)}, u32[]{:S(2)}, u32[]{:S(2)}) %collective-permute-start.22) | collective-permute-done | bytes 196640 | tf_op jit(solution)/shard_map/ppermute | solution.py:49
  169.5 4.2 %collective-permute-start.27 = (bf16[128,1536]{1,0:T(8,128)(2,1)S(1)}, bf16[128,1536]{1,0:T(8,128)(2,1)S(1)}, u32[]{:S(2)}, u32[]{:S(2)}) collective-permute-start(bf16[128,1536]{1,0:T(8,128)(2,1)S(1)} %collective-permute-done.25), channel_id=1, source_target_pairs={{0,7},{1,0},{2,1},{3,2},{4,3},{5,4},{6,5},{7,6},{8,15},{9,8},{10,9... | collective-permute-start | bytes 1179656 | tf_op jit(solution)/shard_map/ppermute | solution.py:49
  173.8 4.9 %collective-permute-done.27 = bf16[128,1536]{1,0:T(8,128)(2,1)S(1)} collective-permute-done((bf16[128,1536]{1,0:T(8,128)(2,1)S(1)}, bf16[128,1536]{1,0:T(8,128)(2,1)S(1)}, u32[]{:S(2)}, u32[]{:S(2)}) %collective-permute-start.27) | collective-permute-done | bytes 393248 | tf_op jit(solution)/shard_map/ppermute | solution.py:49
  178.8 3.3 %collective-permute-start.29 = (bf16[128,1536]{1,0:T(8,128)(2,1)S(1)}, bf16[128,1536]{1,0:T(8,128)(2,1)S(1)}, u32[]{:S(2)}, u32[]{:S(2)}) collective-permute-start(bf16[128,1536]{1,0:T(8,128)(2,1)S(1)} %collective-permute-done.27), channel_id=1, source_target_pairs={{0,7},{1,0},{2,1},{3,2},{4,3},{5,4},{6,5},{7,6},{8,15},{9,8},{10,9... | collective-permute-start | bytes 1179656 | tf_op jit(solution)/shard_map/ppermute | solution.py:49
  187.5 15.0 %shard_map.104 = bf16[96,1024]{1,0:T(8,128)(2,1)} custom-call(f32[8]{0:T(128)} %scale_ref.1, bf16[96,1024]{1,0:T(8,128)(2,1)} %slice.86.q_ref, bf16[6144,128]{1,0:T(8,128)(2,1)} %all-gather.8.cloned.1.call-done.k_ref, bf16[6144,128]{1,0:T(8,128)(2,1)} %bitcast.81), custom_call_target="tpu_custom_call" | custom-call | flops 2415919104 | bytes 3538944 | tf_op jit(solution)/shard_map/pallas_call | solution.py:78
  (156 shorter events, 71.4 us)
Async XLA Ops:
  7.2 63.5 %all-gather.4.cloned.1.call-start = ((), (), s32[]{:S(2)}) async-start(), calls=%async_computation.1 | async-start | bytes 4866048 | tf_op jit(solution)/shard_map/all_gather | solution.py:117
  10.9 105.0 %all-gather.6.cloned.1.call-start = ((), (), s32[]{:S(2)}) async-start(), calls=%async_computation.2 | async-start | bytes 4423680 | tf_op jit(solution)/shard_map/all_gather | solution.py:131
  10.9 18.8 %collective-permute-start.1 = (bf16[5,1408,24]{1,2,0:T(8,128)(2,1)}, bf16[5,1408,24]{1,2,0:T(8,128)(2,1)S(1)}, u32[]{:S(2)}, u32[]{:S(2)}) collective-permute-start(bf16[5,1408,24]{1,2,0:T(8,128)(2,1)} %param.11), channel_id=1, source_target_pairs={{0,56},{8,0},{16,8},{24,16},{32,24},{40,32},{48,40},{56,48},{1,57}... | collective-permute-start | bytes 1013768 | tf_op jit(solution)/shard_map/ppermute | solution.py:49
  17.4 12.3 %collective-permute-start.3 = (bf16[5,1408,24]{1,2,0:T(8,128)(2,1)}, bf16[5,1408,24]{1,2,0:T(8,128)(2,1)S(1)}, u32[]{:S(2)}, u32[]{:S(2)}) collective-permute-start(bf16[5,1408,24]{1,2,0:T(8,128)(2,1)} %param.11), channel_id=1, source_target_pairs={{0,8},{8,16},{16,24},{24,32},{32,40},{40,48},{48,56},{56,0},{1,9},... | collective-permute-start | bytes 1013768 | tf_op jit(solution)/shard_map/ppermute | solution.py:51
  21.9 7.8 %collective-permute-start.4 = (bf16[216,256]{1,0:T(8,128)(2,1)S(1)}, bf16[216,256]{1,0:T(8,128)(2,1)S(1)}, u32[]{:S(2)}, u32[]{:S(2)}) collective-permute-start(bf16[216,256]{1,0:T(8,128)(2,1)S(1)} %constant_dynamic-update-slice_fusion), channel_id=1, source_target_pairs={{0,8},{8,16},{16,24},{24,32},{32,40},{40,48},{48,56},{56,0},{1,9},... | collective-permute-start | bytes 331784 | tf_op jit(solution)/shard_map/ppermute | solution.py:51
  29.8 11.7 %collective-permute-start.5 = (bf16[5,1408,24]{1,2,0:T(8,128)(2,1)S(1)}, bf16[5,1408,24]{1,2,0:T(8,128)(2,1)S(1)}, u32[]{:S(2)}, u32[]{:S(2)}) collective-permute-start(bf16[5,1408,24]{1,2,0:T(8,128)(2,1)S(1)} %collective-permute-done.1), channel_id=1, source_target_pairs={{0,56},{8,0},{16,8},{24,16},{32,24},{40,32},{48,40},{56,48},{1,57}... | collective-permute-start | bytes 1013768 | tf_op jit(solution)/shard_map/ppermute | solution.py:49
  30.1 11.4 %collective-permute-start.7 = (bf16[5,1408,24]{1,2,0:T(8,128)(2,1)S(1)}, bf16[5,1408,24]{1,2,0:T(8,128)(2,1)S(1)}, u32[]{:S(2)}, u32[]{:S(2)}) collective-permute-start(bf16[5,1408,24]{1,2,0:T(8,128)(2,1)S(1)} %collective-permute-done.3), channel_id=1, source_target_pairs={{0,8},{8,16},{16,24},{24,32},{32,40},{40,48},{48,56},{56,0},{1,9},... | collective-permute-start | bytes 1013768 | tf_op jit(solution)/shard_map/ppermute | solution.py:51
  31.2 8.7 %collective-permute-start.6 = (bf16[216,256]{1,0:T(8,128)(2,1)S(1)}, bf16[216,256]{1,0:T(8,128)(2,1)S(1)}, u32[]{:S(2)}, u32[]{:S(2)}) collective-permute-start(bf16[216,256]{1,0:T(8,128)(2,1)S(1)} %collective-permute-done.2), channel_id=1, source_target_pairs={{0,56},{8,0},{16,8},{24,16},{32,24},{40,32},{48,40},{56,48},{1,57}... | collective-permute-start | bytes 331784 | tf_op jit(solution)/shard_map/ppermute | solution.py:49
  32.8 8.7 %collective-permute-start.8 = (bf16[216,256]{1,0:T(8,128)(2,1)S(1)}, bf16[216,256]{1,0:T(8,128)(2,1)S(1)}, u32[]{:S(2)}, u32[]{:S(2)}) collective-permute-start(bf16[216,256]{1,0:T(8,128)(2,1)S(1)} %collective-permute-done.4), channel_id=1, source_target_pairs={{0,8},{8,16},{16,24},{24,32},{32,40},{40,48},{48,56},{56,0},{1,9},... | collective-permute-start | bytes 331784 | tf_op jit(solution)/shard_map/ppermute | solution.py:51
  41.5 11.4 %collective-permute-start.9 = (bf16[5,1408,24]{1,2,0:T(8,128)(2,1)S(1)}, bf16[5,1408,24]{1,2,0:T(8,128)(2,1)S(1)}, u32[]{:S(2)}, u32[]{:S(2)}) collective-permute-start(bf16[5,1408,24]{1,2,0:T(8,128)(2,1)S(1)} %collective-permute-done.5), channel_id=1, source_target_pairs={{0,56},{8,0},{16,8},{24,16},{32,24},{40,32},{48,40},{56,48},{1,57}... | collective-permute-start | bytes 1013768 | tf_op jit(solution)/shard_map/ppermute | solution.py:49
  42.4 10.5 %collective-permute-start.11 = (bf16[5,1408,24]{1,2,0:T(8,128)(2,1)S(1)}, bf16[5,1408,24]{1,2,0:T(8,128)(2,1)S(1)}, u32[]{:S(2)}, u32[]{:S(2)}) collective-permute-start(bf16[5,1408,24]{1,2,0:T(8,128)(2,1)S(1)} %collective-permute-done.7), channel_id=1, source_target_pairs={{0,8},{8,16},{16,24},{24,32},{32,40},{40,48},{48,56},{56,0},{1,9},... | collective-permute-start | bytes 1013768 | tf_op jit(solution)/shard_map/ppermute | solution.py:51
  52.9 8.5 %collective-permute-start.13 = (bf16[5,1408,24]{1,2,0:T(8,128)(2,1)S(1)}, bf16[5,1408,24]{1,2,0:T(8,128)(2,1)S(1)}, u32[]{:S(2)}, u32[]{:S(2)}) collective-permute-start(bf16[5,1408,24]{1,2,0:T(8,128)(2,1)S(1)} %collective-permute-done.9), channel_id=1, source_target_pairs={{0,56},{8,0},{16,8},{24,16},{32,24},{40,32},{48,40},{56,48},{1,57}... | collective-permute-start | bytes 1013768 | tf_op jit(solution)/shard_map/ppermute | solution.py:49
  71.4 11.2 %collective-permute-start.15 = (bf16[2,1408]{1,0:T(2,128)(2,1)S(1)}, bf16[2,1408]{1,0:T(2,128)(2,1)S(1)}, u32[]{:S(2)}, u32[]{:S(2)}) collective-permute-start(bf16[2,1408]{1,0:T(2,128)(2,1)S(1)} %get-tuple-element.69), channel_id=1, source_target_pairs={{8,0},{16,8},{24,16},{32,24},{40,32},{48,40},{56,48},{9,1},{17,9},... | collective-permute-start | bytes 16904 | tf_op jit(solution)/shard_map/ppermute | solution.py:137
  72.8 9.9 %collective-permute-start = (bf16[2,1408]{1,0:T(2,128)(2,1)S(1)}, bf16[2,1408]{1,0:T(2,128)(2,1)S(1)}, u32[]{:S(2)}, u32[]{:S(2)}) collective-permute-start(bf16[2,1408]{1,0:T(2,128)(2,1)S(1)} %get-tuple-element.68), channel_id=1, source_target_pairs={{0,8},{8,16},{16,24},{24,32},{32,40},{40,48},{48,56},{1,9},{9,17},... | collective-permute-start | bytes 16904 | tf_op jit(solution)/shard_map/ppermute | solution.py:136
  97.8 16.3 %all-to-all-start = ((bf16[8,96,192]{1,2,0:T(8,128)(2,1)}), bf16[8,96,192]{1,2,0:T(8,128)(2,1)S(1)}, u32[]{:S(2)}, u32[]{:S(2)}) async-start(bf16[8,96,192]{1,2,0:T(8,128)(2,1)} %copy.33), calls=%async_computation | async-start | bytes 786432 | tf_op jit(solution)/shard_map/all_to_all | solution.py:148
  106.4 81.0 %all-gather.8.cloned.1.call-start = ((), (), s32[]{:S(2)}) async-start(), calls=%async_computation.3 | async-start | bytes 1769472 | tf_op jit(solution)/shard_map/all_gather | solution.py:158
  134.2 7.8 %collective-permute-start.17 = (bf16[768,128]{1,0:T(8,128)(2,1)}, bf16[768,128]{1,0:T(8,128)(2,1)}, u32[]{:S(2)}, u32[]{:S(2)}) collective-permute-start(bf16[768,128]{1,0:T(8,128)(2,1)} %get-tuple-element.70), channel_id=1, source_target_pairs={{0,8},{8,16},{16,24},{24,32},{32,40},{40,48},{48,56},{56,0},{1,9},... | collective-permute-start | bytes 589832 | tf_op jit(solution)/shard_map/ppermute | solution.py:51
  136.7 14.0 %collective-permute-start.23 = (bf16[128,1536]{1,0:T(8,128)(2,1)}, bf16[128,1536]{1,0:T(8,128)(2,1)}, u32[]{:S(2)}, u32[]{:S(2)}) collective-permute-start(bf16[128,1536]{1,0:T(8,128)(2,1)} %reshape.83), channel_id=1, source_target_pairs={{0,7},{1,0},{2,1},{3,2},{4,3},{5,4},{6,5},{7,6},{8,15},{9,8},{10,9... | collective-permute-start | bytes 1179656 | tf_op jit(solution)/shard_map/ppermute | solution.py:49
  137.5 13.2 %collective-permute-start.24 = (bf16[128,1536]{1,0:T(8,128)(2,1)}, bf16[128,1536]{1,0:T(8,128)(2,1)}, u32[]{:S(2)}, u32[]{:S(2)}) collective-permute-start(bf16[128,1536]{1,0:T(8,128)(2,1)} %reshape.83), channel_id=1, source_target_pairs={{0,1},{1,2},{2,3},{3,4},{4,5},{5,6},{6,7},{7,0},{8,9},{9,10},{10,1... | collective-permute-start | bytes 1179656 | tf_op jit(solution)/shard_map/ppermute | solution.py:51
  149.5 9.7 %collective-permute-start.21 = (bf16[768,128]{1,0:T(8,128)(2,1)S(1)}, bf16[768,128]{1,0:T(8,128)(2,1)S(1)}, u32[]{:S(2)}, u32[]{:S(2)}) collective-permute-start(bf16[768,128]{1,0:T(8,128)(2,1)S(1)} %collective-permute-done.19), channel_id=1, source_target_pairs={{0,8},{8,16},{16,24},{24,32},{32,40},{40,48},{48,56},{56,0},{1,9},... | collective-permute-start | bytes 589832 | tf_op jit(solution)/shard_map/ppermute | solution.py:51
  150.7 18.8 %collective-permute-start.25 = (bf16[128,1536]{1,0:T(8,128)(2,1)}, bf16[128,1536]{1,0:T(8,128)(2,1)S(1)}, u32[]{:S(2)}, u32[]{:S(2)}) collective-permute-start(bf16[128,1536]{1,0:T(8,128)(2,1)} %collective-permute-done.23), channel_id=1, source_target_pairs={{0,7},{1,0},{2,1},{3,2},{4,3},{5,4},{6,5},{7,6},{8,15},{9,8},{10,9... | collective-permute-start | bytes 1179656 | tf_op jit(solution)/shard_map/ppermute | solution.py:49
  154.2 15.3 %collective-permute-start.26 = (bf16[128,1536]{1,0:T(8,128)(2,1)}, bf16[128,1536]{1,0:T(8,128)(2,1)S(1)}, u32[]{:S(2)}, u32[]{:S(2)}) collective-permute-start(bf16[128,1536]{1,0:T(8,128)(2,1)} %collective-permute-done.24), channel_id=1, source_target_pairs={{0,1},{1,2},{2,3},{3,4},{4,5},{5,6},{6,7},{7,0},{8,9},{9,10},{10,1... | collective-permute-start | bytes 1179656 | tf_op jit(solution)/shard_map/ppermute | solution.py:51
  159.2 8.1 %collective-permute-start.22 = (bf16[768,128]{1,0:T(8,128)(2,1)S(1)}, bf16[768,128]{1,0:T(8,128)(2,1)S(1)}, u32[]{:S(2)}, u32[]{:S(2)}) collective-permute-start(bf16[768,128]{1,0:T(8,128)(2,1)S(1)} %collective-permute-done.20), channel_id=1, source_target_pairs={{0,56},{8,0},{16,8},{24,16},{32,24},{40,32},{48,40},{56,48},{1,57}... | collective-permute-start | bytes 589832 | tf_op jit(solution)/shard_map/ppermute | solution.py:49
  169.5 9.3 %collective-permute-start.27 = (bf16[128,1536]{1,0:T(8,128)(2,1)S(1)}, bf16[128,1536]{1,0:T(8,128)(2,1)S(1)}, u32[]{:S(2)}, u32[]{:S(2)}) collective-permute-start(bf16[128,1536]{1,0:T(8,128)(2,1)S(1)} %collective-permute-done.25), channel_id=1, source_target_pairs={{0,7},{1,0},{2,1},{3,2},{4,3},{5,4},{6,5},{7,6},{8,15},{9,8},{10,9... | collective-permute-start | bytes 1179656 | tf_op jit(solution)/shard_map/ppermute | solution.py:49
  (19 other events, 179.3 us)
Sparse Core Ops, SparseCore 0:
  11.0 39.2 all-gather.3
  63.6 35.1 all-gather.5
  138.6 37.1 all-gather.7

commit v9 on v7

--- a/solution.py
+++ b/solution.py
@@ -40,19 +40,36 @@
     return split.transpose(0, 2, 1, 3).reshape(rows, columns.shape[1])
 
 
+def split_at(a):
+    half = a.shape[0] // 2
+    return half if a.shape[0] < 32 else half // 16 * 16
+
+
 def ring(value, axis, n):
     up = [(i, (i - 1) % n) for i in range(n)]
     down = [(i, (i + 1) % n) for i in range(n)]
     slots = {0: value}
     ahead = behind = value
     for step in range(1, n // 2 + 1):
-        ahead = lax.ppermute(ahead, axis, up)
+        if step > (n - 1) // 2 and n > 2:
+            ahead = ahead
+        else:
+            ahead = lax.ppermute(ahead, axis, up)
         if step <= (n - 1) // 2:
             behind = lax.ppermute(behind, axis, down)
             ahead, behind = lax.optimization_barrier((ahead, behind))
             slots[(-step) % n] = behind
+        elif n == 2:
+            ahead = lax.optimization_barrier(ahead)
         else:
-            ahead = lax.optimization_barrier(ahead)
+            first = jax.tree.map(lambda a: a[: split_at(a)], ahead)
+            second = jax.tree.map(lambda a: a[split_at(a) :], behind)
+            first = lax.ppermute(first, axis, up)
+            second = lax.ppermute(second, axis, down)
+            first, second = lax.optimization_barrier((first, second))
+            ahead = jax.tree.map(lambda a, b: jnp.concatenate([a, b], axis=0), first, second)
+            slots[step % n] = ahead
+            continue
         slots[step % n] = ahead
     return [slots[k] for k in range(n)]
 

time: 198 us -> 200 us (1.010)
  waiting for transfers between devices: 62.6 us -> 56.6 us
  local copies, waits for them, and re-layouts: 23.3 us -> 27 us
  starting transfers between devices: 41.6 us -> 44.8 us
    ppermute x12 -> x9, waiting for transfers between devices: 40.2 us -> 26.9 us  [ring(): ahead = lax.ppermute(ahead, axis, up)]
    ppermute x0 -> x6, starting transfers between devices: none -> 7.17 us  [the longest x3 4.36 us: ring(): first = lax.ppermute(first, axis, up)]
    ppermute x0 -> x6, waiting for transfers between devices: none -> 6.47 us  [the longest x3 3.33 us: ring(): first = lax.ppermute(first, axis, up)]
    ppermute x12 -> x9, starting transfers between devices: 24 us -> 19.6 us  [ring(): ahead = lax.ppermute(ahead, axis, up)]
    unnamed x52 -> x43, local copies, waits for them, and re-layouts: 15 us -> 15.5 us
  transfers between devices with their start and end apart: 27 -> 30, of which waited for: 14 -> 16; matrix products, arithmetic and copies ran while one was open for 20% -> 22% of each run, Pallas kernels for 0% -> 0%
where the time goes in v9:
time: 200 us; the launch traced here: 199 us
  waiting for transfers between devices  56.6 us (28%)
  starting transfers between devices  44.8 us (22%)
  local copies, waits for them, and re-layouts  27 us (14%)
  matrix products  17.5 us (9%)
  blocking collectives  15.1 us (8%)
  Pallas kernels  15 us (8%)
  between operations  14.2 us (7%)
  other arithmetic  8.56 us (4%)
    ppermute x9, waiting for transfers between devices, ring(): ahead = lax.ppermute(ahead, axis, up)  26.9 us
    ppermute x9, starting transfers between devices, ring(): ahead = lax.ppermute(ahead, axis, up)  19.6 us
    unnamed x43, local copies, waits for them, and re-layouts  15.5 us
    all_gather x1, blocking collectives, shards(): kv_plane = lax.all_gather(keyvals, 'sx', axis=0, tiled=True)  15.1 us
    pallas_call x1, Pallas kernels, attend(): pl.pallas_call(head_kernel, grid=(head_count,), in_specs=[pl.BlockSpec(me...  15 us
    dot_general x5, matrix products, convolve(): jnp.dot(padded[kernel_tap:kernel_tap + row_count], kernel[kernel_tap], pr...  13.3 us
    all_to_all x1, starting transfers between devices, shards(): received = lax.all_to_all(pieces, 'sx', 0, 0, tiled=False)  9.07 us
    all_gather x1, waiting for transfers between devices, shards(): key_block = lax.all_gather(kv_plane, 'sz', axis=0, tiled=True)  9.07 us
  transfers between devices with their start and end apart: 30, of which 16 were waited for; matrix products, arithmetic and copies ran while one was open for 22% of the time, Pallas kernels for 0%

profile of v9, /device:TPU:1, one launch (start us, length us, event | category | flops | bytes accessed | tf_op | source)
XLA Modules:
  0.0 198.8 jit_solution(3407070110002915254)
XLA Ops:
  10.9 6.5 %collective-permute-start.1 = (bf16[5,1408,24]{1,2,0:T(8,128)(2,1)}, bf16[5,1408,24]{1,2,0:T(8,128)(2,1)S(1)}, u32[]{:S(2)}, u32[]{:S(2)}) collective-permute-start(bf16[5,1408,24]{1,2,0:T(8,128)(2,1)} %param.11), channel_id=1, source_target_pairs={{0,56},{8,0},{16,8},{24,16},{32,24},{40,32},{48,40},{56,48},{1,57}... | collective-permute-start | bytes 1013768 | tf_op jit(solution)/shard_map/ppermute | solution.py:57
  19.2 2.7 %collective-permute-start.2 = (bf16[216,256]{1,0:T(8,128)(2,1)S(1)}, bf16[216,256]{1,0:T(8,128)(2,1)S(1)}, u32[]{:S(2)}, u32[]{:S(2)}) collective-permute-start(bf16[216,256]{1,0:T(8,128)(2,1)S(1)} %constant_dynamic-update-slice_fusion), channel_id=1, source_target_pairs={{0,56},{8,0},{16,8},{24,16},{32,24},{40,32},{48,40},{56,48},{1,57}... | collective-permute-start | bytes 331784 | tf_op jit(solution)/shard_map/ppermute | solution.py:57
  21.9 4.7 %collective-permute-done.2 = bf16[216,256]{1,0:T(8,128)(2,1)S(1)} collective-permute-done((bf16[216,256]{1,0:T(8,128)(2,1)S(1)}, bf16[216,256]{1,0:T(8,128)(2,1)S(1)}, u32[]{:S(2)}, u32[]{:S(2)}) %collective-permute-start.2) | collective-permute-done | bytes 110624 | tf_op jit(solution)/shard_map/ppermute | solution.py:57
  26.6 3.1 %collective-permute-done.4 = bf16[216,256]{1,0:T(8,128)(2,1)S(1)} collective-permute-done((bf16[216,256]{1,0:T(8,128)(2,1)S(1)}, bf16[216,256]{1,0:T(8,128)(2,1)S(1)}, u32[]{:S(2)}, u32[]{:S(2)}) %collective-permute-start.4) | collective-permute-done | bytes 110624 | tf_op jit(solution)/shard_map/ppermute | solution.py:59
  34.2 5.7 %collective-permute-done.6 = bf16[216,256]{1,0:T(8,128)(2,1)S(1)} collective-permute-done((bf16[216,256]{1,0:T(8,128)(2,1)S(1)}, bf16[216,256]{1,0:T(8,128)(2,1)S(1)}, u32[]{:S(2)}, u32[]{:S(2)}) %collective-permute-start.6) | collective-permute-done | bytes 110624 | tf_op jit(solution)/shard_map/ppermute | solution.py:57
  46.9 4.0 %collective-permute-done.10 = bf16[216,256]{1,0:T(8,128)(2,1)S(1)} collective-permute-done((bf16[216,256]{1,0:T(8,128)(2,1)}, bf16[216,256]{1,0:T(8,128)(2,1)S(1)}, u32[]{:S(2)}, u32[]{:S(2)}) %collective-permute-start.10) | collective-permute-done | bytes 110624 | tf_op jit(solution)/shard_map/ppermute | solution.py:57
  57.4 2.7 %collective-permute-done.16 = bf16[120,256]{1,0:T(8,128)(2,1)S(1)} collective-permute-done((bf16[120,256]{1,0:T(8,128)(2,1)S(1)}, bf16[120,256]{1,0:T(8,128)(2,1)S(1)}, u32[]{:S(2)}, u32[]{:S(2)}) %collective-permute-start.16) | collective-permute-done | bytes 61472 | tf_op jit(solution)/shard_map/ppermute | solution.py:68
  72.5 4.2 %collective-permute-start = (bf16[2,1408]{1,0:T(2,128)(2,1)S(1)}, bf16[2,1408]{1,0:T(2,128)(2,1)S(1)}, u32[]{:S(2)}, u32[]{:S(2)}) collective-permute-start(bf16[2,1408]{1,0:T(2,128)(2,1)S(1)} %get-tuple-element.64), channel_id=1, source_target_pairs={{0,8},{8,16},{16,24},{24,32},{32,40},{40,48},{48,56},{1,9},{9,17},... | collective-permute-start | bytes 16904 | tf_op jit(solution)/shard_map/ppermute | solution.py:153
  76.8 3.0 %constant_dynamic-update-slice_fusion.10 = bf16[1538,1408]{1,0:T(8,128)(2,1)S(1)} fusion(bf16[1536,1408]{1,0:T(8,128)(2,1)} %all-gather.4.cloned.1.call-done), kind=kLoop, calls=%fused_computation.77 | loop fusion | bytes 8650752
  82.4 2.6 %fusion.7 = f32[1536,192]{0,1:T(8,128)S(1)} fusion(bf16[1536,1408]{1,0:T(8,128)(2,1)S(1)} %bitcast.54, bf16[2,1408]{1,0:T(2,128)(2,1)S(1)} %collective-permute-done, bf16[5,1408,192]{1,2,0:T(8,128)(2,1)} %constant_dynamic-update-slice_fusion.2), kind=kOutput, calls=%fused_computation.9 | convolution fusion | flops 839122944 | bytes 6051328 | tf_op jit(solution)/shard_map/dot_general | solution.py:20
  85.1 2.7 %fusion.3 = f32[1536,192]{0,1:T(8,128)S(1)} fusion(bf16[1538,1408]{1,0:T(8,128)(2,1)S(1)} %constant_dynamic-update-slice_fusion.9, bf16[5,1408,192]{1,2,0:T(8,128)(2,1)} %constant_dynamic-update-slice_fusion.2), kind=kOutput, calls=%fused_computation.4 | convolution fusion | flops 830472192 | bytes 6045696 | tf_op jit(solution)/shard_map/dot_general | solution.py:20
  87.7 2.7 %fusion.21 = f32[1536,192]{0,1:T(8,128)S(1)} fusion(f32[1536,192]{0,1:T(8,128)S(1)} %fusion.37, f32[1536,192]{0,1:T(8,128)S(1)} %fusion.7, bf16[2,1408]{1,0:T(2,128)(2,1)S(1)} %collective-permute-done, bf16[1536,1408]{1,0:T(8,128)(2,1)S(1)} %bitcast.54, bf16[5,1408,192]{1,2,0:T(8,128)(2,1)} %constant_dynamic-update-slice_fusion.2), kind=kOutput, calls=%fused_computation.15 | convolution fusion | flops 839712768 | bytes 8410624 | tf_op jit(solution)/shard_map/dot_general | solution.py:20
  90.5 2.7 %fusion.15 = bf16[1536,192]{0,1:T(8,128)(2,1)S(1)} fusion(f32[1536,192]{0,1:T(8,128)S(1)} %fusion.3, f32[1536,192]{0,1:T(8,128)S(1)} %fusion.21, bf16[1538,1408]{1,0:T(8,128)(2,1)S(1)} %constant_dynamic-update-slice_fusion.9, f32[192]{0:T(256)S(1)} %add.105, bf16[5,1408,192]{1,2,0:T(8,128)(2,1)} %constant_dynamic-update-slice_fusion.2), kind=kOutput, calls=%fused_computation.13 | convolution fusion | flops 831651840 | bytes 7816192 | tf_op jit(solution)/shard_map/dot_general | solution.py:20
  97.5 9.1 %all-to-all-start = ((bf16[8,96,192]{1,2,0:T(8,128)(2,1)}), bf16[8,96,192]{1,2,0:T(8,128)(2,1)S(1)}, u32[]{:S(2)}, u32[]{:S(2)}) async-start(bf16[8,96,192]{1,2,0:T(8,128)(2,1)} %copy.33), calls=%async_computation | async-start | bytes 786432 | tf_op jit(solution)/shard_map/all_to_all | solution.py:165
  107.1 7.2 %all-to-all-done = bf16[8,96,192]{1,2,0:T(8,128)(2,1)S(1)} async-done(((bf16[8,96,192]{1,2,0:T(8,128)(2,1)}), bf16[8,96,192]{1,2,0:T(8,128)(2,1)S(1)}, u32[]{:S(2)}, u32[]{:S(2)}) %all-to-all-start) | async-done | bytes 294944 | tf_op jit(solution)/shard_map/all_to_all | solution.py:165
  115.2 2.8 %convolution_convert_fusion.1 = bf16[96,1280]{1,0:T(8,128)(2,1)S(1)} fusion(bf16[96,1536]{0,1:T(8,128)(2,1)S(1)} %bitcast.56, bf16[1536,1280]{1,0:T(8,128)(2,1)} %all-gather.6.cloned.1.call-done), kind=kOutput, calls=%fused_computation.17 | convolution fusion | flops 377610240 | bytes 4472832 | tf_op jit(solution)/shard_map/dot_general | solution.py:170
  118.0 15.1 %all_gather.14 = bf16[768,256]{1,0:T(8,128)(2,1)} all-gather(bf16[96,256]{1,0:T(8,128)(2,1)S(1)} %slice.103), channel_id=1, replica_groups=mesh['dp'=4,'sz'=8,'sx'=8] {'sx'}, dimensions={0}, use_global_device_ids=true | all-gather | bytes 442368 | tf_op jit(solution)/shard_map/all_gather | solution.py:173
  134.9 5.9 %collective-permute-done.18 = bf16[128,1536]{1,0:T(8,128)(2,1)} collective-permute-done((bf16[128,1536]{1,0:T(8,128)(2,1)S(1)}, bf16[128,1536]{1,0:T(8,128)(2,1)}, u32[]{:S(2)}, u32[]{:S(2)}) %collective-permute-start.18) | collective-permute-done | bytes 393248 | tf_op jit(solution)/shard_map/ppermute | solution.py:57
  144.6 4.0 %collective-permute-done.20 = bf16[128,1536]{1,0:T(8,128)(2,1)} collective-permute-done((bf16[128,1536]{1,0:T(8,128)(2,1)}, bf16[128,1536]{1,0:T(8,128)(2,1)}, u32[]{:S(2)}, u32[]{:S(2)}) %collective-permute-start.20) | collective-permute-done | bytes 393248 | tf_op jit(solution)/shard_map/ppermute | solution.py:57
  148.5 3.1 %collective-permute-start.22 = (bf16[128,1536]{1,0:T(8,128)(2,1)}, bf16[128,1536]{1,0:T(8,128)(2,1)S(1)}, u32[]{:S(2)}, u32[]{:S(2)}) collective-permute-start(bf16[128,1536]{1,0:T(8,128)(2,1)} %collective-permute-done.20), channel_id=1, source_target_pairs={{0,7},{1,0},{2,1},{3,2},{4,3},{5,4},{6,5},{7,6},{8,15},{9,8},{10,9... | collective-permute-start | bytes 1179656 | tf_op jit(solution)/shard_map/ppermute | solution.py:57
  153.7 2.8 %collective-permute-done.22 = bf16[128,1536]{1,0:T(8,128)(2,1)S(1)} collective-permute-done((bf16[128,1536]{1,0:T(8,128)(2,1)}, bf16[128,1536]{1,0:T(8,128)(2,1)S(1)}, u32[]{:S(2)}, u32[]{:S(2)}) %collective-permute-start.22) | collective-permute-done | bytes 393248 | tf_op jit(solution)/shard_map/ppermute | solution.py:57
  156.7 3.9 %collective-permute-start.24 = (bf16[64,1536]{1,0:T(8,128)(2,1)S(1)}, bf16[64,1536]{1,0:T(8,128)(2,1)S(1)}, u32[]{:S(2)}, u32[]{:S(2)}) collective-permute-start(bf16[64,1536]{1,0:T(8,128)(2,1)S(1)} %slice.88), channel_id=1, source_target_pairs={{0,7},{1,0},{2,1},{3,2},{4,3},{5,4},{6,5},{7,6},{8,15},{9,8},{10,9... | collective-permute-start | bytes 589832 | tf_op jit(solution)/shard_map/ppermute | solution.py:67
  165.4 9.1 %all-gather.8.cloned.1.call-done.k_ref.v_ref = bf16[6144,256]{1,0:T(8,128)(2,1)} async-done(((bf16[768,256]{1,0:T(8,128)(2,1)}), bf16[6144,256]{1,0:T(8,128)(2,1)}) %all-gather.8.cloned.1.call-update) | async-done | bytes 3145744 | tf_op jit(solution)/shard_map/all_gather | solution.py:175
  174.5 15.0 %shard_map.104 = bf16[96,1024]{1,0:T(8,128)(2,1)} custom-call(f32[8]{0:T(128)} %scale_ref.1, bf16[96,1024]{1,0:T(8,128)(2,1)} %slice.102.q_ref, bf16[6144,256]{1,0:T(8,128)(2,1)} %all-gather.8.cloned.1.call-done.k_ref.v_ref, bf16[6144,256]{1,0:T(8,128)(2,1)} %all-gather.8.cloned.1.call-done.k_ref.v_ref), custom_call_target="tpu_custom_call" | custom-call | flops 2415919104 | bytes 3538944 | tf_op jit(solution)/shard_map/pallas_call | solution.py:95
  (139 shorter events, 59.4 us)
Async XLA Ops:
  7.2 63.2 %all-gather.4.cloned.1.call-start = ((), (), s32[]{:S(2)}) async-start(), calls=%async_computation.1 | async-start | bytes 4866048 | tf_op jit(solution)/shard_map/all_gather | solution.py:134
  10.9 104.3 %all-gather.6.cloned.1.call-start = ((), (), s32[]{:S(2)}) async-start(), calls=%async_computation.2 | async-start | bytes 4423680 | tf_op jit(solution)/shard_map/all_gather | solution.py:148
  10.9 18.8 %collective-permute-start.1 = (bf16[5,1408,24]{1,2,0:T(8,128)(2,1)}, bf16[5,1408,24]{1,2,0:T(8,128)(2,1)S(1)}, u32[]{:S(2)}, u32[]{:S(2)}) collective-permute-start(bf16[5,1408,24]{1,2,0:T(8,128)(2,1)} %param.11), channel_id=1, source_target_pairs={{0,56},{8,0},{16,8},{24,16},{32,24},{40,32},{48,40},{56,48},{1,57}... | collective-permute-start | bytes 1013768 | tf_op jit(solution)/shard_map/ppermute | solution.py:57
  17.4 12.3 %collective-permute-start.3 = (bf16[5,1408,24]{1,2,0:T(8,128)(2,1)}, bf16[5,1408,24]{1,2,0:T(8,128)(2,1)S(1)}, u32[]{:S(2)}, u32[]{:S(2)}) collective-permute-start(bf16[5,1408,24]{1,2,0:T(8,128)(2,1)} %param.11), channel_id=1, source_target_pairs={{0,8},{8,16},{16,24},{24,32},{32,40},{40,48},{48,56},{56,0},{1,9},... | collective-permute-start | bytes 1013768 | tf_op jit(solution)/shard_map/ppermute | solution.py:59
  19.2 7.4 %collective-permute-start.2 = (bf16[216,256]{1,0:T(8,128)(2,1)S(1)}, bf16[216,256]{1,0:T(8,128)(2,1)S(1)}, u32[]{:S(2)}, u32[]{:S(2)}) collective-permute-start(bf16[216,256]{1,0:T(8,128)(2,1)S(1)} %constant_dynamic-update-slice_fusion), channel_id=1, source_target_pairs={{0,56},{8,0},{16,8},{24,16},{32,24},{40,32},{48,40},{56,48},{1,57}... | collective-permute-start | bytes 331784 | tf_op jit(solution)/shard_map/ppermute | solution.py:57
  21.9 7.8 %collective-permute-start.4 = (bf16[216,256]{1,0:T(8,128)(2,1)S(1)}, bf16[216,256]{1,0:T(8,128)(2,1)S(1)}, u32[]{:S(2)}, u32[]{:S(2)}) collective-permute-start(bf16[216,256]{1,0:T(8,128)(2,1)S(1)} %constant_dynamic-update-slice_fusion), channel_id=1, source_target_pairs={{0,8},{8,16},{16,24},{24,32},{32,40},{40,48},{48,56},{56,0},{1,9},... | collective-permute-start | bytes 331784 | tf_op jit(solution)/shard_map/ppermute | solution.py:59
  29.7 11.7 %collective-permute-start.5 = (bf16[5,1408,24]{1,2,0:T(8,128)(2,1)S(1)}, bf16[5,1408,24]{1,2,0:T(8,128)(2,1)S(1)}, u32[]{:S(2)}, u32[]{:S(2)}) collective-permute-start(bf16[5,1408,24]{1,2,0:T(8,128)(2,1)S(1)} %collective-permute-done.1), channel_id=1, source_target_pairs={{0,56},{8,0},{16,8},{24,16},{32,24},{40,32},{48,40},{56,48},{1,57}... | collective-permute-start | bytes 1013768 | tf_op jit(solution)/shard_map/ppermute | solution.py:57
  30.1 11.4 %collective-permute-start.7 = (bf16[5,1408,24]{1,2,0:T(8,128)(2,1)S(1)}, bf16[5,1408,24]{1,2,0:T(8,128)(2,1)S(1)}, u32[]{:S(2)}, u32[]{:S(2)}) collective-permute-start(bf16[5,1408,24]{1,2,0:T(8,128)(2,1)S(1)} %collective-permute-done.3), channel_id=1, source_target_pairs={{0,8},{8,16},{16,24},{24,32},{32,40},{40,48},{48,56},{56,0},{1,9},... | collective-permute-start | bytes 1013768 | tf_op jit(solution)/shard_map/ppermute | solution.py:59
  31.2 8.7 %collective-permute-start.6 = (bf16[216,256]{1,0:T(8,128)(2,1)S(1)}, bf16[216,256]{1,0:T(8,128)(2,1)S(1)}, u32[]{:S(2)}, u32[]{:S(2)}) collective-permute-start(bf16[216,256]{1,0:T(8,128)(2,1)S(1)} %collective-permute-done.2), channel_id=1, source_target_pairs={{0,56},{8,0},{16,8},{24,16},{32,24},{40,32},{48,40},{56,48},{1,57}... | collective-permute-start | bytes 331784 | tf_op jit(solution)/shard_map/ppermute | solution.py:57
  32.8 8.7 %collective-permute-start.8 = (bf16[216,256]{1,0:T(8,128)(2,1)S(1)}, bf16[216,256]{1,0:T(8,128)(2,1)S(1)}, u32[]{:S(2)}, u32[]{:S(2)}) collective-permute-start(bf16[216,256]{1,0:T(8,128)(2,1)S(1)} %collective-permute-done.4), channel_id=1, source_target_pairs={{0,8},{8,16},{16,24},{24,32},{32,40},{40,48},{48,56},{56,0},{1,9},... | collective-permute-start | bytes 331784 | tf_op jit(solution)/shard_map/ppermute | solution.py:59
  41.5 11.4 %collective-permute-start.9 = (bf16[5,1408,24]{1,2,0:T(8,128)(2,1)S(1)}, bf16[5,1408,24]{1,2,0:T(8,128)(2,1)S(1)}, u32[]{:S(2)}, u32[]{:S(2)}) collective-permute-start(bf16[5,1408,24]{1,2,0:T(8,128)(2,1)S(1)} %collective-permute-done.5), channel_id=1, source_target_pairs={{0,56},{8,0},{16,8},{24,16},{32,24},{40,32},{48,40},{56,48},{1,57}... | collective-permute-start | bytes 1013768 | tf_op jit(solution)/shard_map/ppermute | solution.py:57
  42.4 10.5 %collective-permute-start.11 = (bf16[5,1408,24]{1,2,0:T(8,128)(2,1)S(1)}, bf16[5,1408,24]{1,2,0:T(8,128)(2,1)S(1)}, u32[]{:S(2)}, u32[]{:S(2)}) collective-permute-start(bf16[5,1408,24]{1,2,0:T(8,128)(2,1)S(1)} %collective-permute-done.7), channel_id=1, source_target_pairs={{0,8},{8,16},{16,24},{24,32},{32,40},{40,48},{48,56},{56,0},{1,9},... | collective-permute-start | bytes 1013768 | tf_op jit(solution)/shard_map/ppermute | solution.py:59
  43.9 6.9 %collective-permute-start.10 = (bf16[216,256]{1,0:T(8,128)(2,1)}, bf16[216,256]{1,0:T(8,128)(2,1)S(1)}, u32[]{:S(2)}, u32[]{:S(2)}) collective-permute-start(bf16[216,256]{1,0:T(8,128)(2,1)} %copy-done.6), channel_id=1, source_target_pairs={{0,56},{8,0},{16,8},{24,16},{32,24},{40,32},{48,40},{56,48},{1,57}... | collective-permute-start | bytes 331784 | tf_op jit(solution)/shard_map/ppermute | solution.py:57
  46.0 6.9 %collective-permute-start.12 = (bf16[216,256]{1,0:T(8,128)(2,1)S(1)}, bf16[216,256]{1,0:T(8,128)(2,1)S(1)}, u32[]{:S(2)}, u32[]{:S(2)}) collective-permute-start(bf16[216,256]{1,0:T(8,128)(2,1)S(1)} %collective-permute-done.8), channel_id=1, source_target_pairs={{0,8},{8,16},{16,24},{24,32},{32,40},{40,48},{48,56},{56,0},{1,9},... | collective-permute-start | bytes 331784 | tf_op jit(solution)/shard_map/ppermute | solution.py:59
  52.9 7.2 %collective-permute-start.13 = (bf16[2,1408,24]{1,2,0:T(8,128)(2,1)S(1)}, bf16[2,1408,24]{1,2,0:T(8,128)(2,1)S(1)}, u32[]{:S(2)}, u32[]{:S(2)}) collective-permute-start(bf16[2,1408,24]{1,2,0:T(8,128)(2,1)S(1)} %slice.71), channel_id=1, source_target_pairs={{0,56},{8,0},{16,8},{24,16},{32,24},{40,32},{48,40},{56,48},{1,57}... | collective-permute-start | bytes 405512 | tf_op jit(solution)/shard_map/ppermute | solution.py:67
  53.4 6.7 %collective-permute-start.15 = (bf16[3,1408,24]{1,2,0:T(8,128)(2,1)S(1)}, bf16[3,1408,24]{1,2,0:T(8,128)(2,1)S(1)}, u32[]{:S(2)}, u32[]{:S(2)}) collective-permute-start(bf16[3,1408,24]{1,2,0:T(8,128)(2,1)S(1)} %slice.73), channel_id=1, source_target_pairs={{0,8},{8,16},{16,24},{24,32},{32,40},{40,48},{48,56},{56,0},{1,9},... | collective-permute-start | bytes 608264 | tf_op jit(solution)/shard_map/ppermute | solution.py:68
  71.2 11.2 %collective-permute-start.17 = (bf16[2,1408]{1,0:T(2,128)(2,1)S(1)}, bf16[2,1408]{1,0:T(2,128)(2,1)S(1)}, u32[]{:S(2)}, u32[]{:S(2)}) collective-permute-start(bf16[2,1408]{1,0:T(2,128)(2,1)S(1)} %get-tuple-element.65), channel_id=1, source_target_pairs={{8,0},{16,8},{24,16},{32,24},{40,32},{48,40},{56,48},{9,1},{17,9},... | collective-permute-start | bytes 16904 | tf_op jit(solution)/shard_map/ppermute | solution.py:154
  72.5 9.9 %collective-permute-start = (bf16[2,1408]{1,0:T(2,128)(2,1)S(1)}, bf16[2,1408]{1,0:T(2,128)(2,1)S(1)}, u32[]{:S(2)}, u32[]{:S(2)}) collective-permute-start(bf16[2,1408]{1,0:T(2,128)(2,1)S(1)} %get-tuple-element.64), channel_id=1, source_target_pairs={{0,8},{8,16},{16,24},{24,32},{32,40},{40,48},{48,56},{1,9},{9,17},... | collective-permute-start | bytes 16904 | tf_op jit(solution)/shard_map/ppermute | solution.py:153
  97.5 16.8 %all-to-all-start = ((bf16[8,96,192]{1,2,0:T(8,128)(2,1)}), bf16[8,96,192]{1,2,0:T(8,128)(2,1)S(1)}, u32[]{:S(2)}, u32[]{:S(2)}) async-start(bf16[8,96,192]{1,2,0:T(8,128)(2,1)} %copy.33), calls=%async_computation | async-start | bytes 786432 | tf_op jit(solution)/shard_map/all_to_all | solution.py:165
  106.6 67.8 %all-gather.8.cloned.1.call-start = ((), (), s32[]{:S(2)}) async-start(), calls=%async_computation.3 | async-start | bytes 3538944 | tf_op jit(solution)/shard_map/all_gather | solution.py:175
  133.1 7.6 %collective-permute-start.18 = (bf16[128,1536]{1,0:T(8,128)(2,1)S(1)}, bf16[128,1536]{1,0:T(8,128)(2,1)}, u32[]{:S(2)}, u32[]{:S(2)}) collective-permute-start(bf16[128,1536]{1,0:T(8,128)(2,1)S(1)} %reshape.80), channel_id=1, source_target_pairs={{0,7},{1,0},{2,1},{3,2},{4,3},{5,4},{6,5},{7,6},{8,15},{9,8},{10,9... | collective-permute-start | bytes 1179656 | tf_op jit(solution)/shard_map/ppermute | solution.py:57
  133.3 7.4 %collective-permute-start.19 = (bf16[128,1536]{1,0:T(8,128)(2,1)S(1)}, bf16[128,1536]{1,0:T(8,128)(2,1)}, u32[]{:S(2)}, u32[]{:S(2)}) collective-permute-start(bf16[128,1536]{1,0:T(8,128)(2,1)S(1)} %reshape.80), channel_id=1, source_target_pairs={{0,1},{1,2},{2,3},{3,4},{4,5},{5,6},{6,7},{7,0},{8,9},{9,10},{10,1... | collective-permute-start | bytes 1179656 | tf_op jit(solution)/shard_map/ppermute | solution.py:59
  140.7 7.8 %collective-permute-start.20 = (bf16[128,1536]{1,0:T(8,128)(2,1)}, bf16[128,1536]{1,0:T(8,128)(2,1)}, u32[]{:S(2)}, u32[]{:S(2)}) collective-permute-start(bf16[128,1536]{1,0:T(8,128)(2,1)} %collective-permute-done.18), channel_id=1, source_target_pairs={{0,7},{1,0},{2,1},{3,2},{4,3},{5,4},{6,5},{7,6},{8,15},{9,8},{10,9... | collective-permute-start | bytes 1179656 | tf_op jit(solution)/shard_map/ppermute | solution.py:57
  148.5 8.0 %collective-permute-start.22 = (bf16[128,1536]{1,0:T(8,128)(2,1)}, bf16[128,1536]{1,0:T(8,128)(2,1)S(1)}, u32[]{:S(2)}, u32[]{:S(2)}) collective-permute-start(bf16[128,1536]{1,0:T(8,128)(2,1)} %collective-permute-done.20), channel_id=1, source_target_pairs={{0,7},{1,0},{2,1},{3,2},{4,3},{5,4},{6,5},{7,6},{8,15},{9,8},{10,9... | collective-permute-start | bytes 1179656 | tf_op jit(solution)/shard_map/ppermute | solution.py:57
  (16 other events, 162.4 us)
Sparse Core Ops, SparseCore 0:
  11.0 39.2 all-gather.3
  62.5 36.6 all-gather.5
  133.2 41.1 all-gather.7

commit v10 on v7

--- a/solution.py
+++ b/solution.py
@@ -114,7 +114,12 @@
 
     me_z = lax.axis_index("sz")
     normed = jax.nn.gelu(normalize(features.astype(jnp.float32), norm_gain)).astype(jnp.bfloat16)
-    plane = lax.all_gather(normed, "sx", axis=0, tiled=True)
+    count = nz * nx
+    after = [(i, i + 1) for i in range(count - 1)]
+    before = [(i + 1, i) for i in range(count - 1)]
+    low = lax.ppermute(normed[rows_here - 2 :], ("sz", "sx"), after)
+    high = lax.ppermute(normed[:2], ("sz", "sx"), before)
+    framed = lax.all_gather(jnp.concatenate([low, normed, high], axis=0), "sx", axis=0, tiled=False)
 
     q_cols = query_weight.shape[1]
     lane = 256
@@ -130,12 +135,11 @@
     out_z = both_z[:, proj_n:].reshape(nz * output_weight.shape[0], output_weight.shape[1])
     proj_weight = lax.all_gather(proj_z, "sx", axis=0, tiled=True)
 
-    plane_rows = plane.shape[0]
-    forward = [(i, i + 1) for i in range(nz - 1)]
-    backward = [(i + 1, i) for i in range(nz - 1)]
-    low = lax.ppermute(plane[plane_rows - 2 :], "sz", forward)
-    high = lax.ppermute(plane[:2], "sz", backward)
-    padded = jnp.concatenate([low, plane, high], axis=0)
+    plane_rows = nx * rows_here
+    padded = jnp.concatenate(
+        [framed[0, :2], framed[:, 2 : rows_here + 2].reshape(plane_rows, -1), framed[nx - 1, rows_here + 2 :]],
+        axis=0,
+    )
 
     bias_all = conv_bias.reshape(nz, nx, width).transpose(1, 0, 2)
     bias = lax.dynamic_index_in_dim(bias_all, me_x, axis=0, keepdims=False)

time: 198 us -> 206 us (1.040)
  starting transfers between devices: 41.6 us -> 49 us
    all_to_all x1, starting transfers between devices: 8.68 us -> 14.3 us  [shards(): received = lax.all_to_all(pieces, 'sx', 0, 0, tiled=False)]
    unnamed x52 -> x47, local copies, waits for them, and re-layouts: 15 us -> 11.3 us
    slice x1 -> x2, local copies, waits for them, and re-layouts: 0.76 us -> 3.32 us  [the longest x1 3.31 us: shards(): framed[:, 2:rows_here + 2].reshape(plane_rows, -1)]
  transfers between devices with their start and end apart: 27 -> 27, of which waited for: 14 -> 15; matrix products, arithmetic and copies ran while one was open for 20% -> 18% of each run, Pallas kernels for 0% -> 0%
where the time goes in v10:
time: 206 us; the launch traced here: 205 us
  waiting for transfers between devices  64.4 us (31%)
  starting transfers between devices  49 us (24%)
  local copies, waits for them, and re-layouts  22.1 us (11%)
  matrix products  17.6 us (9%)
  blocking collectives  15.1 us (7%)
  Pallas kernels  15 us (7%)
  between operations  14.3 us (7%)
  other arithmetic  7.3 us (4%)
    ppermute x12, waiting for transfers between devices, ring(): ahead = lax.ppermute(ahead, axis, up)  38.9 us
    ppermute x12, starting transfers between devices, ring(): ahead = lax.ppermute(ahead, axis, up)  22.7 us
    all_gather x1, blocking collectives, shards(): kv_plane = lax.all_gather(keyvals, 'sx', axis=0, tiled=True)  15.1 us
    pallas_call x1, Pallas kernels, attend(): pl.pallas_call(head_kernel, grid=(head_count,), in_specs=[pl.BlockSpec(me...  15 us
    all_to_all x1, starting transfers between devices, shards(): received = lax.all_to_all(pieces, 'sx', 0, 0, tiled=False)  14.3 us
    dot_general x5, matrix products, convolve(): jnp.dot(padded[kernel_tap:kernel_tap + row_count], kernel[kernel_tap], pr...  13.5 us
    unnamed x47, local copies, waits for them, and re-layouts  11.3 us
    all_gather x1, waiting for transfers between devices, shards(): key_block = lax.all_gather(kv_plane, 'sz', axis=0, tiled=True)  9.7 us
  transfers between devices with their start and end apart: 27, of which 15 were waited for; matrix products, arithmetic and copies ran while one was open for 18% of the time, Pallas kernels for 0%

profile of v10, /device:TPU:1, one launch (start us, length us, event | category | flops | bytes accessed | tf_op | source)
XLA Modules:
  0.0 204.8 jit_solution(2396783165711970627)
XLA Ops:
  10.2 5.1 %collective-permute-start.1 = (bf16[2,1408]{1,0:T(2,128)(2,1)S(1)}, bf16[2,1408]{1,0:T(2,128)(2,1)S(1)}, u32[]{:S(2)}, u32[]{:S(2)}) collective-permute-start(bf16[2,1408]{1,0:T(2,128)(2,1)S(1)} %get-tuple-element.59), channel_id=1, source_target_pairs={{1,0},{2,1},{3,2},{4,3},{5,4},{6,5},{7,6},{8,7},{9,8},{10,9},{11,1... | collective-permute-start | bytes 16904 | tf_op jit(solution)/shard_map/ppermute | solution.py:121
  19.4 6.1 %collective-permute-start.2 = (bf16[5,1408,24]{1,2,0:T(8,128)(2,1)S(1)}, bf16[5,1408,24]{1,2,0:T(8,128)(2,1)S(1)}, u32[]{:S(2)}, u32[]{:S(2)}) collective-permute-start(bf16[5,1408,24]{1,2,0:T(8,128)(2,1)S(1)} %copy-done.3), channel_id=1, source_target_pairs={{0,56},{8,0},{16,8},{24,16},{32,24},{40,32},{48,40},{56,48},{1,57}... | collective-permute-start | bytes 1013768 | tf_op jit(solution)/shard_map/ppermute | solution.py:49
  25.7 2.7 %collective-permute-start.3 = (bf16[216,256]{1,0:T(8,128)(2,1)S(1)}, bf16[216,256]{1,0:T(8,128)(2,1)S(1)}, u32[]{:S(2)}, u32[]{:S(2)}) collective-permute-start(bf16[216,256]{1,0:T(8,128)(2,1)S(1)} %constant_dynamic-update-slice_fusion), channel_id=1, source_target_pairs={{0,56},{8,0},{16,8},{24,16},{32,24},{40,32},{48,40},{56,48},{1,57}... | collective-permute-start | bytes 331784 | tf_op jit(solution)/shard_map/ppermute | solution.py:49
  30.8 3.1 %collective-permute-done.5 = bf16[216,256]{1,0:T(8,128)(2,1)S(1)} collective-permute-done((bf16[216,256]{1,0:T(8,128)(2,1)S(1)}, bf16[216,256]{1,0:T(8,128)(2,1)S(1)}, u32[]{:S(2)}, u32[]{:S(2)}) %collective-permute-start.5) | collective-permute-done | bytes 110624 | tf_op jit(solution)/shard_map/ppermute | solution.py:51
  36.8 4.7 %collective-permute-done.7 = bf16[216,256]{1,0:T(8,128)(2,1)S(1)} collective-permute-done((bf16[216,256]{1,0:T(8,128)(2,1)S(1)}, bf16[216,256]{1,0:T(8,128)(2,1)S(1)}, u32[]{:S(2)}, u32[]{:S(2)}) %collective-permute-start.7) | collective-permute-done | bytes 110624 | tf_op jit(solution)/shard_map/ppermute | solution.py:49
  41.5 2.8 %collective-permute-done.9 = bf16[216,256]{1,0:T(8,128)(2,1)S(1)} collective-permute-done((bf16[216,256]{1,0:T(8,128)(2,1)S(1)}, bf16[216,256]{1,0:T(8,128)(2,1)S(1)}, u32[]{:S(2)}, u32[]{:S(2)}) %collective-permute-start.9) | collective-permute-done | bytes 110624 | tf_op jit(solution)/shard_map/ppermute | solution.py:51
  47.4 6.8 %collective-permute-done.11 = bf16[216,256]{1,0:T(8,128)(2,1)S(1)} collective-permute-done((bf16[216,256]{1,0:T(8,128)(2,1)S(1)}, bf16[216,256]{1,0:T(8,128)(2,1)S(1)}, u32[]{:S(2)}, u32[]{:S(2)}) %collective-permute-start.11) | collective-permute-done | bytes 110624 | tf_op jit(solution)/shard_map/ppermute | solution.py:49
  57.4 8.4 %collective-permute-done.15 = bf16[216,256]{1,0:T(8,128)(2,1)S(1)} collective-permute-done((bf16[216,256]{1,0:T(8,128)(2,1)S(1)}, bf16[216,256]{1,0:T(8,128)(2,1)S(1)}, u32[]{:S(2)}, u32[]{:S(2)}) %collective-permute-start.15) | collective-permute-done | bytes 110624 | tf_op jit(solution)/shard_map/ppermute | solution.py:49
  75.2 3.3 %slice.81 = bf16[8,192,1408]{2,1,0:T(8,128)(2,1)S(1)} slice(bf16[8,196,1408]{2,1,0:T(8,128)(2,1)} %all-gather.10.cloned.1.call-done), slice={[0:8], [2:194], [0:1408]} | slice | bytes 8650752 | tf_op jit(solution)/shard_map/slice | solution.py:140
  81.9 2.7 %fusion.1 = f32[1536,192]{0,1:T(8,128)S(1)} fusion(bf16[1536,1408]{1,0:T(8,128)(2,1)S(1)} %bitcast.59, bf16[2,1408]{1,0:T(2,128)(2,1)S(1)} %get-tuple-element.57, bf16[5,1408,192]{1,2,0:T(8,128)(2,1)} %constant_dynamic-update-slice_fusion.2), kind=kOutput, calls=%fused_computation.5 | convolution fusion | flops 839122944 | bytes 6051328 | tf_op jit(solution)/shard_map/dot_general | solution.py:20
  87.2 2.7 %fusion.12 = f32[1536,192]{0,1:T(8,128)S(1)} fusion(f32[1536,192]{0,1:T(8,128)S(1)} %fusion.1, f32[1536,192]{0,1:T(8,128)S(1)} %fusion.28, f32[1536,192]{0,1:T(8,128)S(1)} %fusion.4, bf16[1536,1408]{1,0:T(8,128)(2,1)S(1)} %bitcast.61, bf16[2,1408]{1,0:T(2,128)(2,1)S(1)} %get-tuple-element.56, bf16[5,1408,192]{1,2,0:T(8,128)(2,1)} %constant_dynamic-update-slice_fusion.2), kind=kOutput, calls=%fused_computation.16 | convolution fusion | flops 840007680 | bytes 9590272 | tf_op jit(solution)/shard_map/dot_general | solution.py:20
  89.9 2.8 %fusion.14 = bf16[1536,192]{0,1:T(8,128)(2,1)S(1)} fusion(f32[1536,192]{0,1:T(8,128)S(1)} %fusion.12, bf16[2,1408]{1,0:T(2,128)(2,1)S(1)} %get-tuple-element.57, bf16[1536,1408]{1,0:T(8,128)(2,1)S(1)} %bitcast.62, f32[192]{0:T(256)S(1)} %add.105, bf16[5,1408,192]{1,2,0:T(8,128)(2,1)} %constant_dynamic-update-slice_fusion.2), kind=kOutput, calls=%fused_computation.18 | convolution fusion | flops 840007680 | bytes 6641920 | tf_op jit(solution)/shard_map/dot_general | solution.py:20
  97.2 14.3 %all-to-all-start = ((bf16[8,96,192]{1,2,0:T(8,128)(2,1)}), bf16[8,96,192]{1,2,0:T(8,128)(2,1)S(1)}, u32[]{:S(2)}, u32[]{:S(2)}) async-start(bf16[8,96,192]{1,2,0:T(8,128)(2,1)} %copy.33), calls=%async_computation | async-start | bytes 786432 | tf_op jit(solution)/shard_map/all_to_all | solution.py:152
  112.1 7.2 %all-to-all-done = bf16[8,96,192]{1,2,0:T(8,128)(2,1)S(1)} async-done(((bf16[8,96,192]{1,2,0:T(8,128)(2,1)}), bf16[8,96,192]{1,2,0:T(8,128)(2,1)S(1)}, u32[]{:S(2)}, u32[]{:S(2)}) %all-to-all-start) | async-done | bytes 294944 | tf_op jit(solution)/shard_map/all_to_all | solution.py:152
  120.1 2.8 %convolution_convert_fusion.1 = bf16[96,1280]{1,0:T(8,128)(2,1)S(1)} fusion(bf16[96,1536]{0,1:T(8,128)(2,1)S(1)} %bitcast.64, bf16[1536,1280]{1,0:T(8,128)(2,1)} %all-gather.6.cloned.1.call-done), kind=kOutput, calls=%fused_computation.20 | convolution fusion | flops 377610240 | bytes 4472832 | tf_op jit(solution)/shard_map/dot_general | solution.py:157
  122.9 15.1 %all_gather.18 = bf16[768,256]{1,0:T(8,128)(2,1)} all-gather(bf16[96,256]{1,0:T(8,128)(2,1)S(1)} %slice.94), channel_id=1, replica_groups=mesh['dp'=4,'sz'=8,'sx'=8] {'sx'}, dimensions={0}, use_global_device_ids=true | all-gather | bytes 442368 | tf_op jit(solution)/shard_map/all_gather | solution.py:160
  139.8 5.8 %collective-permute-done.16 = bf16[128,1536]{1,0:T(8,128)(2,1)S(1)} collective-permute-done((bf16[128,1536]{1,0:T(8,128)(2,1)S(1)}, bf16[128,1536]{1,0:T(8,128)(2,1)S(1)}, u32[]{:S(2)}, u32[]{:S(2)}) %collective-permute-start.16) | collective-permute-done | bytes 393248 | tf_op jit(solution)/shard_map/ppermute | solution.py:49
  149.4 3.8 %collective-permute-done.18 = bf16[128,1536]{1,0:T(8,128)(2,1)} collective-permute-done((bf16[128,1536]{1,0:T(8,128)(2,1)S(1)}, bf16[128,1536]{1,0:T(8,128)(2,1)}, u32[]{:S(2)}, u32[]{:S(2)}) %collective-permute-start.18) | collective-permute-done | bytes 393248 | tf_op jit(solution)/shard_map/ppermute | solution.py:49
  153.2 3.1 %collective-permute-start.20 = (bf16[128,1536]{1,0:T(8,128)(2,1)}, bf16[128,1536]{1,0:T(8,128)(2,1)S(1)}, u32[]{:S(2)}, u32[]{:S(2)}) collective-permute-start(bf16[128,1536]{1,0:T(8,128)(2,1)} %collective-permute-done.18), channel_id=1, source_target_pairs={{0,7},{1,0},{2,1},{3,2},{4,3},{5,4},{6,5},{7,6},{8,15},{9,8},{10,9... | collective-permute-start | bytes 1179656 | tf_op jit(solution)/shard_map/ppermute | solution.py:49
  157.4 3.7 %collective-permute-done.20 = bf16[128,1536]{1,0:T(8,128)(2,1)S(1)} collective-permute-done((bf16[128,1536]{1,0:T(8,128)(2,1)}, bf16[128,1536]{1,0:T(8,128)(2,1)S(1)}, u32[]{:S(2)}, u32[]{:S(2)}) %collective-permute-start.20) | collective-permute-done | bytes 393248 | tf_op jit(solution)/shard_map/ppermute | solution.py:49
  161.3 3.9 %collective-permute-start.22 = (bf16[128,1536]{1,0:T(8,128)(2,1)S(1)}, bf16[128,1536]{1,0:T(8,128)(2,1)S(1)}, u32[]{:S(2)}, u32[]{:S(2)}) collective-permute-start(bf16[128,1536]{1,0:T(8,128)(2,1)S(1)} %collective-permute-done.20), channel_id=1, source_target_pairs={{0,7},{1,0},{2,1},{3,2},{4,3},{5,4},{6,5},{7,6},{8,15},{9,8},{10,9... | collective-permute-start | bytes 1179656 | tf_op jit(solution)/shard_map/ppermute | solution.py:49
  166.3 3.3 %collective-permute-done.22 = bf16[128,1536]{1,0:T(8,128)(2,1)S(1)} collective-permute-done((bf16[128,1536]{1,0:T(8,128)(2,1)S(1)}, bf16[128,1536]{1,0:T(8,128)(2,1)S(1)}, u32[]{:S(2)}, u32[]{:S(2)}) %collective-permute-start.22) | collective-permute-done | bytes 393248 | tf_op jit(solution)/shard_map/ppermute | solution.py:49
  170.7 9.7 %all-gather.8.cloned.1.call-done.k_ref.v_ref = bf16[6144,256]{1,0:T(8,128)(2,1)} async-done(((bf16[768,256]{1,0:T(8,128)(2,1)}), bf16[6144,256]{1,0:T(8,128)(2,1)}) %all-gather.8.cloned.1.call-update) | async-done | bytes 3145744 | tf_op jit(solution)/shard_map/all_gather | solution.py:162
  180.4 15.0 %shard_map.104 = bf16[96,1024]{1,0:T(8,128)(2,1)} custom-call(f32[8]{0:T(128)} %scale_ref.1, bf16[96,1024]{1,0:T(8,128)(2,1)} %slice.93.q_ref, bf16[6144,256]{1,0:T(8,128)(2,1)} %all-gather.8.cloned.1.call-done.k_ref.v_ref, bf16[6144,256]{1,0:T(8,128)(2,1)} %all-gather.8.cloned.1.call-done.k_ref.v_ref), custom_call_target="tpu_custom_call" | custom-call | flops 2415919104 | bytes 3538944 | tf_op jit(solution)/shard_map/pallas_call | solution.py:78
  (130 shorter events, 51.6 us)
Async XLA Ops:
  7.2 68.0 %all-gather.10.cloned.1.call-start = ((), (), s32[]{:S(2)}) async-start(), calls=%async_computation.3 | async-start | bytes 5068800 | tf_op jit(solution)/shard_map/all_gather | solution.py:122
  10.2 7.1 %collective-permute-start.1 = (bf16[2,1408]{1,0:T(2,128)(2,1)S(1)}, bf16[2,1408]{1,0:T(2,128)(2,1)S(1)}, u32[]{:S(2)}, u32[]{:S(2)}) collective-permute-start(bf16[2,1408]{1,0:T(2,128)(2,1)S(1)} %get-tuple-element.59), channel_id=1, source_target_pairs={{1,0},{2,1},{3,2},{4,3},{5,4},{6,5},{7,6},{8,7},{9,8},{10,9},{11,1... | collective-permute-start | bytes 16904 | tf_op jit(solution)/shard_map/ppermute | solution.py:121
  19.3 100.8 %all-gather.6.cloned.1.call-start = ((), (), s32[]{:S(2)}) async-start(), calls=%async_computation.1 | async-start | bytes 4423680 | tf_op jit(solution)/shard_map/all_gather | solution.py:136
  19.4 14.5 %collective-permute-start.2 = (bf16[5,1408,24]{1,2,0:T(8,128)(2,1)S(1)}, bf16[5,1408,24]{1,2,0:T(8,128)(2,1)S(1)}, u32[]{:S(2)}, u32[]{:S(2)}) collective-permute-start(bf16[5,1408,24]{1,2,0:T(8,128)(2,1)S(1)} %copy-done.3), channel_id=1, source_target_pairs={{0,56},{8,0},{16,8},{24,16},{32,24},{40,32},{48,40},{56,48},{1,57}... | collective-permute-start | bytes 1013768 | tf_op jit(solution)/shard_map/ppermute | solution.py:49
  25.5 8.4 %collective-permute-start.4 = (bf16[5,1408,24]{1,2,0:T(8,128)(2,1)S(1)}, bf16[5,1408,24]{1,2,0:T(8,128)(2,1)S(1)}, u32[]{:S(2)}, u32[]{:S(2)}) collective-permute-start(bf16[5,1408,24]{1,2,0:T(8,128)(2,1)S(1)} %copy-done.3), channel_id=1, source_target_pairs={{0,8},{8,16},{16,24},{24,32},{32,40},{40,48},{48,56},{56,0},{1,9},... | collective-permute-start | bytes 1013768 | tf_op jit(solution)/shard_map/ppermute | solution.py:51
  28.4 5.5 %collective-permute-start.5 = (bf16[216,256]{1,0:T(8,128)(2,1)S(1)}, bf16[216,256]{1,0:T(8,128)(2,1)S(1)}, u32[]{:S(2)}, u32[]{:S(2)}) collective-permute-start(bf16[216,256]{1,0:T(8,128)(2,1)S(1)} %constant_dynamic-update-slice_fusion), channel_id=1, source_target_pairs={{0,8},{8,16},{16,24},{24,32},{32,40},{40,48},{48,56},{56,0},{1,9},... | collective-permute-start | bytes 331784 | tf_op jit(solution)/shard_map/ppermute | solution.py:51
  33.9 10.4 %collective-permute-start.6 = (bf16[5,1408,24]{1,2,0:T(8,128)(2,1)S(1)}, bf16[5,1408,24]{1,2,0:T(8,128)(2,1)S(1)}, u32[]{:S(2)}, u32[]{:S(2)}) collective-permute-start(bf16[5,1408,24]{1,2,0:T(8,128)(2,1)S(1)} %collective-permute-done.2), channel_id=1, source_target_pairs={{0,56},{8,0},{16,8},{24,16},{32,24},{40,32},{48,40},{56,48},{1,57}... | collective-permute-start | bytes 1013768 | tf_op jit(solution)/shard_map/ppermute | solution.py:49
  34.0 10.3 %collective-permute-start.8 = (bf16[5,1408,24]{1,2,0:T(8,128)(2,1)S(1)}, bf16[5,1408,24]{1,2,0:T(8,128)(2,1)S(1)}, u32[]{:S(2)}, u32[]{:S(2)}) collective-permute-start(bf16[5,1408,24]{1,2,0:T(8,128)(2,1)S(1)} %collective-permute-done.4), channel_id=1, source_target_pairs={{0,8},{8,16},{16,24},{24,32},{32,40},{40,48},{48,56},{56,0},{1,9},... | collective-permute-start | bytes 1013768 | tf_op jit(solution)/shard_map/ppermute | solution.py:51
  35.4 6.2 %collective-permute-start.7 = (bf16[216,256]{1,0:T(8,128)(2,1)S(1)}, bf16[216,256]{1,0:T(8,128)(2,1)S(1)}, u32[]{:S(2)}, u32[]{:S(2)}) collective-permute-start(bf16[216,256]{1,0:T(8,128)(2,1)S(1)} %collective-permute-done.3), channel_id=1, source_target_pairs={{0,56},{8,0},{16,8},{24,16},{32,24},{40,32},{48,40},{56,48},{1,57}... | collective-permute-start | bytes 331784 | tf_op jit(solution)/shard_map/ppermute | solution.py:49
  36.7 7.7 %collective-permute-start.9 = (bf16[216,256]{1,0:T(8,128)(2,1)S(1)}, bf16[216,256]{1,0:T(8,128)(2,1)S(1)}, u32[]{:S(2)}, u32[]{:S(2)}) collective-permute-start(bf16[216,256]{1,0:T(8,128)(2,1)S(1)} %collective-permute-done.5), channel_id=1, source_target_pairs={{0,8},{8,16},{16,24},{24,32},{32,40},{40,48},{48,56},{56,0},{1,9},... | collective-permute-start | bytes 331784 | tf_op jit(solution)/shard_map/ppermute | solution.py:51
  44.3 11.2 %collective-permute-start.10 = (bf16[5,1408,24]{1,2,0:T(8,128)(2,1)S(1)}, bf16[5,1408,24]{1,2,0:T(8,128)(2,1)S(1)}, u32[]{:S(2)}, u32[]{:S(2)}) collective-permute-start(bf16[5,1408,24]{1,2,0:T(8,128)(2,1)S(1)} %collective-permute-done.6), channel_id=1, source_target_pairs={{0,56},{8,0},{16,8},{24,16},{32,24},{40,32},{48,40},{56,48},{1,57}... | collective-permute-start | bytes 1013768 | tf_op jit(solution)/shard_map/ppermute | solution.py:49
  44.4 11.2 %collective-permute-start.12 = (bf16[5,1408,24]{1,2,0:T(8,128)(2,1)S(1)}, bf16[5,1408,24]{1,2,0:T(8,128)(2,1)S(1)}, u32[]{:S(2)}, u32[]{:S(2)}) collective-permute-start(bf16[5,1408,24]{1,2,0:T(8,128)(2,1)S(1)} %collective-permute-done.8), channel_id=1, source_target_pairs={{0,8},{8,16},{16,24},{24,32},{32,40},{40,48},{48,56},{56,0},{1,9},... | collective-permute-start | bytes 1013768 | tf_op jit(solution)/shard_map/ppermute | solution.py:51
  45.8 8.4 %collective-permute-start.11 = (bf16[216,256]{1,0:T(8,128)(2,1)S(1)}, bf16[216,256]{1,0:T(8,128)(2,1)S(1)}, u32[]{:S(2)}, u32[]{:S(2)}) collective-permute-start(bf16[216,256]{1,0:T(8,128)(2,1)S(1)} %collective-permute-done.7), channel_id=1, source_target_pairs={{0,56},{8,0},{16,8},{24,16},{32,24},{40,32},{48,40},{56,48},{1,57}... | collective-permute-start | bytes 331784 | tf_op jit(solution)/shard_map/ppermute | solution.py:49
  47.2 8.3 %collective-permute-start.13 = (bf16[216,256]{1,0:T(8,128)(2,1)S(1)}, bf16[216,256]{1,0:T(8,128)(2,1)S(1)}, u32[]{:S(2)}, u32[]{:S(2)}) collective-permute-start(bf16[216,256]{1,0:T(8,128)(2,1)S(1)} %collective-permute-done.9), channel_id=1, source_target_pairs={{0,8},{8,16},{16,24},{24,32},{32,40},{40,48},{48,56},{56,0},{1,9},... | collective-permute-start | bytes 331784 | tf_op jit(solution)/shard_map/ppermute | solution.py:51
  55.5 10.2 %collective-permute-start.14 = (bf16[5,1408,24]{1,2,0:T(8,128)(2,1)S(1)}, bf16[5,1408,24]{1,2,0:T(8,128)(2,1)S(1)}, u32[]{:S(2)}, u32[]{:S(2)}) collective-permute-start(bf16[5,1408,24]{1,2,0:T(8,128)(2,1)S(1)} %collective-permute-done.10), channel_id=1, source_target_pairs={{0,56},{8,0},{16,8},{24,16},{32,24},{40,32},{48,40},{56,48},{1,57}... | collective-permute-start | bytes 1013768 | tf_op jit(solution)/shard_map/ppermute | solution.py:49
  55.8 10.0 %collective-permute-start.15 = (bf16[216,256]{1,0:T(8,128)(2,1)S(1)}, bf16[216,256]{1,0:T(8,128)(2,1)S(1)}, u32[]{:S(2)}, u32[]{:S(2)}) collective-permute-start(bf16[216,256]{1,0:T(8,128)(2,1)S(1)} %collective-permute-done.11), channel_id=1, source_target_pairs={{0,56},{8,0},{16,8},{24,16},{32,24},{40,32},{48,40},{56,48},{1,57}... | collective-permute-start | bytes 331784 | tf_op jit(solution)/shard_map/ppermute | solution.py:49
  97.2 22.0 %all-to-all-start = ((bf16[8,96,192]{1,2,0:T(8,128)(2,1)}), bf16[8,96,192]{1,2,0:T(8,128)(2,1)S(1)}, u32[]{:S(2)}, u32[]{:S(2)}) async-start(bf16[8,96,192]{1,2,0:T(8,128)(2,1)} %copy.33), calls=%async_computation | async-start | bytes 786432 | tf_op jit(solution)/shard_map/all_to_all | solution.py:152
  111.5 68.9 %all-gather.8.cloned.1.call-start = ((), (), s32[]{:S(2)}) async-start(), calls=%async_computation.2 | async-start | bytes 3538944 | tf_op jit(solution)/shard_map/all_gather | solution.py:162
  138.1 7.5 %collective-permute-start.16 = (bf16[128,1536]{1,0:T(8,128)(2,1)S(1)}, bf16[128,1536]{1,0:T(8,128)(2,1)S(1)}, u32[]{:S(2)}, u32[]{:S(2)}) collective-permute-start(bf16[128,1536]{1,0:T(8,128)(2,1)S(1)} %reshape.84), channel_id=1, source_target_pairs={{0,7},{1,0},{2,1},{3,2},{4,3},{5,4},{6,5},{7,6},{8,15},{9,8},{10,9... | collective-permute-start | bytes 1179656 | tf_op jit(solution)/shard_map/ppermute | solution.py:49
  138.2 7.3 %collective-permute-start.17 = (bf16[128,1536]{1,0:T(8,128)(2,1)S(1)}, bf16[128,1536]{1,0:T(8,128)(2,1)S(1)}, u32[]{:S(2)}, u32[]{:S(2)}) collective-permute-start(bf16[128,1536]{1,0:T(8,128)(2,1)S(1)} %reshape.84), channel_id=1, source_target_pairs={{0,1},{1,2},{2,3},{3,4},{4,5},{5,6},{6,7},{7,0},{8,9},{9,10},{10,1... | collective-permute-start | bytes 1179656 | tf_op jit(solution)/shard_map/ppermute | solution.py:51
  145.6 7.6 %collective-permute-start.18 = (bf16[128,1536]{1,0:T(8,128)(2,1)S(1)}, bf16[128,1536]{1,0:T(8,128)(2,1)}, u32[]{:S(2)}, u32[]{:S(2)}) collective-permute-start(bf16[128,1536]{1,0:T(8,128)(2,1)S(1)} %collective-permute-done.16), channel_id=1, source_target_pairs={{0,7},{1,0},{2,1},{3,2},{4,3},{5,4},{6,5},{7,6},{8,15},{9,8},{10,9... | collective-permute-start | bytes 1179656 | tf_op jit(solution)/shard_map/ppermute | solution.py:49
  147.8 5.4 %collective-permute-start.19 = (bf16[128,1536]{1,0:T(8,128)(2,1)S(1)}, bf16[128,1536]{1,0:T(8,128)(2,1)}, u32[]{:S(2)}, u32[]{:S(2)}) collective-permute-start(bf16[128,1536]{1,0:T(8,128)(2,1)S(1)} %collective-permute-done.17), channel_id=1, source_target_pairs={{0,1},{1,2},{2,3},{3,4},{4,5},{5,6},{6,7},{7,0},{8,9},{9,10},{10,1... | collective-permute-start | bytes 1179656 | tf_op jit(solution)/shard_map/ppermute | solution.py:51
  153.2 8.0 %collective-permute-start.20 = (bf16[128,1536]{1,0:T(8,128)(2,1)}, bf16[128,1536]{1,0:T(8,128)(2,1)S(1)}, u32[]{:S(2)}, u32[]{:S(2)}) collective-permute-start(bf16[128,1536]{1,0:T(8,128)(2,1)} %collective-permute-done.18), channel_id=1, source_target_pairs={{0,7},{1,0},{2,1},{3,2},{4,3},{5,4},{6,5},{7,6},{8,15},{9,8},{10,9... | collective-permute-start | bytes 1179656 | tf_op jit(solution)/shard_map/ppermute | solution.py:49
  161.3 8.2 %collective-permute-start.22 = (bf16[128,1536]{1,0:T(8,128)(2,1)S(1)}, bf16[128,1536]{1,0:T(8,128)(2,1)S(1)}, u32[]{:S(2)}, u32[]{:S(2)}) collective-permute-start(bf16[128,1536]{1,0:T(8,128)(2,1)S(1)} %collective-permute-done.20), channel_id=1, source_target_pairs={{0,7},{1,0},{2,1},{3,2},{4,3},{5,4},{6,5},{7,6},{8,15},{9,8},{10,9... | collective-permute-start | bytes 1179656 | tf_op jit(solution)/shard_map/ppermute | solution.py:49
  (15 other events, 202.7 us)
Sparse Core Ops, SparseCore 0:
  19.4 41.3 all-gather.9
  67.8 43.1 all-gather.5
  138.2 42.1 all-gather.7

commit v11 on v7

--- a/solution.py
+++ b/solution.py
@@ -15,8 +15,8 @@
 
 
 def convolve(padded, kernel, row_count):
-    summed = jnp.zeros((row_count, kernel.shape[2]), jnp.float32)
-    for kernel_tap in range(kernel.shape[0]):
+    summed = jnp.zeros((row_count, kernel[0].shape[1]), jnp.float32)
+    for kernel_tap in range(len(kernel)):
         summed = summed + jnp.dot(
             padded[kernel_tap : kernel_tap + row_count],
             kernel[kernel_tap],
@@ -109,7 +109,7 @@
     nx = lax.axis_size("sx")
     me_x = lax.axis_index("sx")
     rows_here = features.shape[0]
-    width = conv_weight.shape[2]
+    taps, _, width = conv_weight.shape
     ch_out = conv_bias.shape[0]
 
     me_z = lax.axis_index("sz")
@@ -124,7 +124,7 @@
         [proj_piece.reshape(proj_n, lane), output_weight.reshape(-1, lane)], axis=0
     )
     slots = ring((conv_weight, both), "sz", nz)
-    kernel = jnp.concatenate([s[0] for s in slots], axis=2)
+    kernel = [jnp.concatenate([s[0][tap] for s in slots], axis=1) for tap in range(taps)]
     both_z = jnp.stack([s[1] for s in slots])
     proj_z = both_z[:, :proj_n].reshape(nz * proj_piece.shape[0], proj_piece.shape[1])
     out_z = both_z[:, proj_n:].reshape(nz * output_weight.shape[0], output_weight.shape[1])

time: 198 us -> 191 us (0.965)
  matrix products: 17.6 us -> 12.2 us
    dot_general x5, matrix products: 13.4 us -> 8.06 us  [convolve(): jnp.dot(padded[kernel_tap:kernel_tap + row_count], kernel[kernel_tap], pr...]
    ppermute x12, waiting for transfers between devices: 40.2 us -> 35.5 us  [ring(): ahead = lax.ppermute(ahead, axis, up)]
    all_gather x1, waiting for transfers between devices: 8.15 us -> 12.7 us  [shards(): key_block = lax.all_gather(kv_plane, 'sz', axis=0, tiled=True)]
    ppermute x1, starting transfers between devices: 4.25 us -> 1.97 us  [shards(): low = lax.ppermute(plane[plane_rows - 2:], 'sz', forward)]
    unnamed x52 -> x48, local copies, waits for them, and re-layouts: 15 us -> 13 us
  transfers between devices with their start and end apart: 27 -> 27, of which waited for: 14 -> 14; matrix products, arithmetic and copies ran while one was open for 20% -> 17% of each run, Pallas kernels for 0% -> 0%
where the time goes in v11:
time: 191 us; the launch traced here: 190 us
  waiting for transfers between devices  61.3 us (32%)
  starting transfers between devices  42.3 us (22%)
  local copies, waits for them, and re-layouts  21.9 us (11%)
  blocking collectives  15.1 us (8%)
  Pallas kernels  15 us (8%)
  between operations  14.3 us (7%)
  matrix products  12.2 us (6%)
  other arithmetic  7.83 us (4%)
    ppermute x12, waiting for transfers between devices, ring(): ahead = lax.ppermute(ahead, axis, up)  35.5 us
    ppermute x12, starting transfers between devices, ring(): ahead = lax.ppermute(ahead, axis, up)  25.5 us
    all_gather x1, blocking collectives, shards(): kv_plane = lax.all_gather(keyvals, 'sx', axis=0, tiled=True)  15.1 us
    pallas_call x1, Pallas kernels, attend(): pl.pallas_call(head_kernel, grid=(head_count,), in_specs=[pl.BlockSpec(me...  15 us
    unnamed x48, local copies, waits for them, and re-layouts  13 us
    all_gather x1, waiting for transfers between devices, shards(): key_block = lax.all_gather(kv_plane, 'sz', axis=0, tiled=True)  12.7 us
    all_to_all x1, starting transfers between devices, shards(): received = lax.all_to_all(pieces, 'sx', 0, 0, tiled=False)  9.02 us
    dot_general x5, matrix products, convolve(): jnp.dot(padded[kernel_tap:kernel_tap + row_count], kernel[kernel_tap], pr...  8.06 us
  transfers between devices with their start and end apart: 27, of which 14 were waited for; matrix products, arithmetic and copies ran while one was open for 17% of the time, Pallas kernels for 0%

profile of v11, /device:TPU:1, one launch (start us, length us, event | category | flops | bytes accessed | tf_op | source)
XLA Modules:
  0.0 190.0 jit_solution(8683569209888877911)
XLA Ops:
  8.5 2.4 %fusion.28 = bf16[192,1408]{1,0:T(8,128)(2,1)} fusion(bf16[192,1408]{1,0:T(8,128)(2,1)} %param.9, f32[1408]{0:T(1024)} %param.10, f32[192]{0:T(256)S(1)} %add_rsqrt_fusion), kind=kLoop, calls=%fused_computation.25 | loop fusion | flops 3244032 | bytes 1087744 | tf_op jit(solution)/shard_map/convert_element_type | solution.py:116
  12.7 6.5 %collective-permute-start.2 = (bf16[216,256]{1,0:T(8,128)(2,1)S(1)}, bf16[216,256]{1,0:T(8,128)(2,1)S(1)}, u32[]{:S(2)}, u32[]{:S(2)}) collective-permute-start(bf16[216,256]{1,0:T(8,128)(2,1)S(1)} %constant_dynamic-update-slice_fusion), channel_id=1, source_target_pairs={{0,56},{8,0},{16,8},{24,16},{32,24},{40,32},{48,40},{56,48},{1,57}... | collective-permute-start | bytes 331784 | tf_op jit(solution)/shard_map/ppermute | solution.py:49
  19.2 2.7 %collective-permute-start.1 = (bf16[5,1408,24]{1,2,0:T(8,128)(2,1)}, bf16[5,1408,24]{1,2,0:T(8,128)(2,1)S(1)}, u32[]{:S(2)}, u32[]{:S(2)}) collective-permute-start(bf16[5,1408,24]{1,2,0:T(8,128)(2,1)} %param.11), channel_id=1, source_target_pairs={{0,56},{8,0},{16,8},{24,16},{32,24},{40,32},{48,40},{56,48},{1,57}... | collective-permute-start | bytes 1013768 | tf_op jit(solution)/shard_map/ppermute | solution.py:49
  24.5 3.7 %collective-permute-done.1 = bf16[5,1408,24]{1,2,0:T(8,128)(2,1)S(1)} collective-permute-done((bf16[5,1408,24]{1,2,0:T(8,128)(2,1)}, bf16[5,1408,24]{1,2,0:T(8,128)(2,1)S(1)}, u32[]{:S(2)}, u32[]{:S(2)}) %collective-permute-start.1) | collective-permute-done | bytes 337952 | tf_op jit(solution)/shard_map/ppermute | solution.py:49
  28.2 3.0 %collective-permute-done.3 = bf16[5,1408,24]{1,2,0:T(8,128)(2,1)S(1)} collective-permute-done((bf16[5,1408,24]{1,2,0:T(8,128)(2,1)}, bf16[5,1408,24]{1,2,0:T(8,128)(2,1)S(1)}, u32[]{:S(2)}, u32[]{:S(2)}) %collective-permute-start.3) | collective-permute-done | bytes 337952 | tf_op jit(solution)/shard_map/ppermute | solution.py:51
  34.9 5.9 %collective-permute-done.6 = bf16[216,256]{1,0:T(8,128)(2,1)S(1)} collective-permute-done((bf16[216,256]{1,0:T(8,128)(2,1)S(1)}, bf16[216,256]{1,0:T(8,128)(2,1)S(1)}, u32[]{:S(2)}, u32[]{:S(2)}) %collective-permute-start.6) | collective-permute-done | bytes 110624 | tf_op jit(solution)/shard_map/ppermute | solution.py:49
  42.4 2.7 %collective-permute-start.9 = (bf16[5,1408,24]{1,2,0:T(8,128)(2,1)S(1)}, bf16[5,1408,24]{1,2,0:T(8,128)(2,1)S(1)}, u32[]{:S(2)}, u32[]{:S(2)}) collective-permute-start(bf16[5,1408,24]{1,2,0:T(8,128)(2,1)S(1)} %collective-permute-done.5), channel_id=1, source_target_pairs={{0,56},{8,0},{16,8},{24,16},{32,24},{40,32},{48,40},{56,48},{1,57}... | collective-permute-start | bytes 1013768 | tf_op jit(solution)/shard_map/ppermute | solution.py:49
  47.3 4.0 %collective-permute-done.10 = bf16[216,256]{1,0:T(8,128)(2,1)S(1)} collective-permute-done((bf16[216,256]{1,0:T(8,128)(2,1)S(1)}, bf16[216,256]{1,0:T(8,128)(2,1)S(1)}, u32[]{:S(2)}, u32[]{:S(2)}) %collective-permute-start.10) | collective-permute-done | bytes 110624 | tf_op jit(solution)/shard_map/ppermute | solution.py:49
  52.3 2.5 %collective-permute-start.13 = (bf16[5,1408,24]{1,2,0:T(8,128)(2,1)S(1)}, bf16[5,1408,24]{1,2,0:T(8,128)(2,1)S(1)}, u32[]{:S(2)}, u32[]{:S(2)}) collective-permute-start(bf16[5,1408,24]{1,2,0:T(8,128)(2,1)S(1)} %collective-permute-done.9), channel_id=1, source_target_pairs={{0,56},{8,0},{16,8},{24,16},{32,24},{40,32},{48,40},{56,48},{1,57}... | collective-permute-start | bytes 1013768 | tf_op jit(solution)/shard_map/ppermute | solution.py:49
  55.1 5.1 %collective-permute-done.14 = bf16[216,256]{1,0:T(8,128)(2,1)S(1)} collective-permute-done((bf16[216,256]{1,0:T(8,128)(2,1)S(1)}, bf16[216,256]{1,0:T(8,128)(2,1)S(1)}, u32[]{:S(2)}, u32[]{:S(2)}) %collective-permute-start.14) | collective-permute-done | bytes 110624 | tf_op jit(solution)/shard_map/ppermute | solution.py:49
  69.5 2.5 %constant_dynamic-update-slice_fusion.27 = bf16[1538,1408]{1,0:T(8,128)(2,1)S(1)} fusion(bf16[1536,1408]{1,0:T(8,128)(2,1)} %all-gather.4.cloned.1.call-done), kind=kLoop, calls=%fused_computation.77 | loop fusion | bytes 8650752
  81.0 2.2 %reduce_max.9 = bf16[768,192]{1,0:T(8,128)(2,1)S(1)} reduce(bf16[768,2,192]{2,1,0:T(2,128)(2,1)S(1)} %reshape.75, bf16[]{:T(256)} %constant.291), dimensions={1}, to_apply=%region_1.2 | reduce | flops 147456 | bytes 884738 | tf_op jit(solution)/shard_map/reduce_max | solution.py:29
  84.7 9.0 %all-to-all-start = ((bf16[8,96,192]{1,2,0:T(8,128)(2,1)}), bf16[8,96,192]{1,2,0:T(8,128)(2,1)S(1)}, u32[]{:S(2)}, u32[]{:S(2)}) async-start(bf16[8,96,192]{1,2,0:T(8,128)(2,1)} %copy.33), calls=%async_computation | async-start | bytes 786432 | tf_op jit(solution)/shard_map/all_to_all | solution.py:148
  94.2 7.2 %all-to-all-done = bf16[8,96,192]{1,2,0:T(8,128)(2,1)S(1)} async-done(((bf16[8,96,192]{1,2,0:T(8,128)(2,1)}), bf16[8,96,192]{1,2,0:T(8,128)(2,1)S(1)}, u32[]{:S(2)}, u32[]{:S(2)}) %all-to-all-start) | async-done | bytes 294944 | tf_op jit(solution)/shard_map/all_to_all | solution.py:148
  102.3 2.8 %convolution_convert_fusion.1 = bf16[96,1280]{1,0:T(8,128)(2,1)S(1)} fusion(bf16[96,1536]{0,1:T(8,128)(2,1)S(1)} %bitcast.124, bf16[1536,1280]{1,0:T(8,128)(2,1)} %all-gather.6.cloned.1.call-done), kind=kOutput, calls=%fused_computation.17 | convolution fusion | flops 377610240 | bytes 4472832 | tf_op jit(solution)/shard_map/dot_general | solution.py:153
  105.1 15.1 %all_gather.14 = bf16[768,256]{1,0:T(8,128)(2,1)} all-gather(bf16[96,256]{1,0:T(8,128)(2,1)S(1)} %slice.214), channel_id=1, replica_groups=mesh['dp'=4,'sz'=8,'sx'=8] {'sx'}, dimensions={0}, use_global_device_ids=true | all-gather | bytes 442368 | tf_op jit(solution)/shard_map/all_gather | solution.py:156
  122.0 5.8 %collective-permute-done.16 = bf16[128,1536]{1,0:T(8,128)(2,1)S(1)} collective-permute-done((bf16[128,1536]{1,0:T(8,128)(2,1)S(1)}, bf16[128,1536]{1,0:T(8,128)(2,1)S(1)}, u32[]{:S(2)}, u32[]{:S(2)}) %collective-permute-start.16) | collective-permute-done | bytes 393248 | tf_op jit(solution)/shard_map/ppermute | solution.py:49
  131.6 3.8 %collective-permute-done.18 = bf16[128,1536]{1,0:T(8,128)(2,1)} collective-permute-done((bf16[128,1536]{1,0:T(8,128)(2,1)S(1)}, bf16[128,1536]{1,0:T(8,128)(2,1)}, u32[]{:S(2)}, u32[]{:S(2)}) %collective-permute-start.18) | collective-permute-done | bytes 393248 | tf_op jit(solution)/shard_map/ppermute | solution.py:49
  135.4 3.1 %collective-permute-start.20 = (bf16[128,1536]{1,0:T(8,128)(2,1)}, bf16[128,1536]{1,0:T(8,128)(2,1)S(1)}, u32[]{:S(2)}, u32[]{:S(2)}) collective-permute-start(bf16[128,1536]{1,0:T(8,128)(2,1)} %collective-permute-done.18), channel_id=1, source_target_pairs={{0,7},{1,0},{2,1},{3,2},{4,3},{5,4},{6,5},{7,6},{8,15},{9,8},{10,9... | collective-permute-start | bytes 1179656 | tf_op jit(solution)/shard_map/ppermute | solution.py:49
  139.6 3.7 %collective-permute-done.20 = bf16[128,1536]{1,0:T(8,128)(2,1)S(1)} collective-permute-done((bf16[128,1536]{1,0:T(8,128)(2,1)}, bf16[128,1536]{1,0:T(8,128)(2,1)S(1)}, u32[]{:S(2)}, u32[]{:S(2)}) %collective-permute-start.20) | collective-permute-done | bytes 393248 | tf_op jit(solution)/shard_map/ppermute | solution.py:49
  143.5 3.6 %collective-permute-start.22 = (bf16[128,1536]{1,0:T(8,128)(2,1)S(1)}, bf16[128,1536]{1,0:T(8,128)(2,1)S(1)}, u32[]{:S(2)}, u32[]{:S(2)}) collective-permute-start(bf16[128,1536]{1,0:T(8,128)(2,1)S(1)} %collective-permute-done.20), channel_id=1, source_target_pairs={{0,7},{1,0},{2,1},{3,2},{4,3},{5,4},{6,5},{7,6},{8,15},{9,8},{10,9... | collective-permute-start | bytes 1179656 | tf_op jit(solution)/shard_map/ppermute | solution.py:49
  148.2 3.6 %collective-permute-done.22 = bf16[128,1536]{1,0:T(8,128)(2,1)S(1)} collective-permute-done((bf16[128,1536]{1,0:T(8,128)(2,1)S(1)}, bf16[128,1536]{1,0:T(8,128)(2,1)S(1)}, u32[]{:S(2)}, u32[]{:S(2)}) %collective-permute-start.22) | collective-permute-done | bytes 393248 | tf_op jit(solution)/shard_map/ppermute | solution.py:49
  152.9 12.7 %all-gather.8.cloned.1.call-done.k_ref.v_ref = bf16[6144,256]{1,0:T(8,128)(2,1)} async-done(((bf16[768,256]{1,0:T(8,128)(2,1)}), bf16[6144,256]{1,0:T(8,128)(2,1)}) %all-gather.8.cloned.1.call-update) | async-done | bytes 3145744 | tf_op jit(solution)/shard_map/all_gather | solution.py:158
  165.6 15.0 %shard_map.104 = bf16[96,1024]{1,0:T(8,128)(2,1)} custom-call(f32[8]{0:T(128)} %scale_ref.1, bf16[96,1024]{1,0:T(8,128)(2,1)} %slice.213.q_ref, bf16[6144,256]{1,0:T(8,128)(2,1)} %all-gather.8.cloned.1.call-done.k_ref.v_ref, bf16[6144,256]{1,0:T(8,128)(2,1)} %all-gather.8.cloned.1.call-done.k_ref.v_ref), custom_call_target="tpu_custom_call" | custom-call | flops 2415919104 | bytes 3538944 | tf_op jit(solution)/shard_map/pallas_call | solution.py:78
  (130 shorter events, 47.1 us)
Async XLA Ops:
  7.2 58.0 %all-gather.4.cloned.1.call-start = ((), (), s32[]{:S(2)}) async-start(), calls=%async_computation.1 | async-start | bytes 4866048 | tf_op jit(solution)/shard_map/all_gather | solution.py:117
  10.9 91.4 %all-gather.6.cloned.1.call-start = ((), (), s32[]{:S(2)}) async-start(), calls=%async_computation.2 | async-start | bytes 4423680 | tf_op jit(solution)/shard_map/all_gather | solution.py:131
  12.7 11.8 %collective-permute-start.2 = (bf16[216,256]{1,0:T(8,128)(2,1)S(1)}, bf16[216,256]{1,0:T(8,128)(2,1)S(1)}, u32[]{:S(2)}, u32[]{:S(2)}) collective-permute-start(bf16[216,256]{1,0:T(8,128)(2,1)S(1)} %constant_dynamic-update-slice_fusion), channel_id=1, source_target_pairs={{0,56},{8,0},{16,8},{24,16},{32,24},{40,32},{48,40},{56,48},{1,57}... | collective-permute-start | bytes 331784 | tf_op jit(solution)/shard_map/ppermute | solution.py:49
  19.2 9.0 %collective-permute-start.1 = (bf16[5,1408,24]{1,2,0:T(8,128)(2,1)}, bf16[5,1408,24]{1,2,0:T(8,128)(2,1)S(1)}, u32[]{:S(2)}, u32[]{:S(2)}) collective-permute-start(bf16[5,1408,24]{1,2,0:T(8,128)(2,1)} %param.11), channel_id=1, source_target_pairs={{0,56},{8,0},{16,8},{24,16},{32,24},{40,32},{48,40},{56,48},{1,57}... | collective-permute-start | bytes 1013768 | tf_op jit(solution)/shard_map/ppermute | solution.py:49
  21.9 9.4 %collective-permute-start.3 = (bf16[5,1408,24]{1,2,0:T(8,128)(2,1)}, bf16[5,1408,24]{1,2,0:T(8,128)(2,1)S(1)}, u32[]{:S(2)}, u32[]{:S(2)}) collective-permute-start(bf16[5,1408,24]{1,2,0:T(8,128)(2,1)} %param.11), channel_id=1, source_target_pairs={{0,8},{8,16},{16,24},{24,32},{32,40},{40,48},{48,56},{56,0},{1,9},... | collective-permute-start | bytes 1013768 | tf_op jit(solution)/shard_map/ppermute | solution.py:51
  31.3 11.1 %collective-permute-start.5 = (bf16[5,1408,24]{1,2,0:T(8,128)(2,1)S(1)}, bf16[5,1408,24]{1,2,0:T(8,128)(2,1)S(1)}, u32[]{:S(2)}, u32[]{:S(2)}) collective-permute-start(bf16[5,1408,24]{1,2,0:T(8,128)(2,1)S(1)} %collective-permute-done.1), channel_id=1, source_target_pairs={{0,56},{8,0},{16,8},{24,16},{32,24},{40,32},{48,40},{56,48},{1,57}... | collective-permute-start | bytes 1013768 | tf_op jit(solution)/shard_map/ppermute | solution.py:49
  31.5 10.8 %collective-permute-start.7 = (bf16[5,1408,24]{1,2,0:T(8,128)(2,1)S(1)}, bf16[5,1408,24]{1,2,0:T(8,128)(2,1)S(1)}, u32[]{:S(2)}, u32[]{:S(2)}) collective-permute-start(bf16[5,1408,24]{1,2,0:T(8,128)(2,1)S(1)} %collective-permute-done.3), channel_id=1, source_target_pairs={{0,8},{8,16},{16,24},{24,32},{32,40},{40,48},{48,56},{56,0},{1,9},... | collective-permute-start | bytes 1013768 | tf_op jit(solution)/shard_map/ppermute | solution.py:51
  32.7 8.1 %collective-permute-start.6 = (bf16[216,256]{1,0:T(8,128)(2,1)S(1)}, bf16[216,256]{1,0:T(8,128)(2,1)S(1)}, u32[]{:S(2)}, u32[]{:S(2)}) collective-permute-start(bf16[216,256]{1,0:T(8,128)(2,1)S(1)} %collective-permute-done.2), channel_id=1, source_target_pairs={{0,56},{8,0},{16,8},{24,16},{32,24},{40,32},{48,40},{56,48},{1,57}... | collective-permute-start | bytes 331784 | tf_op jit(solution)/shard_map/ppermute | solution.py:49
  34.2 8.1 %collective-permute-start.8 = (bf16[216,256]{1,0:T(8,128)(2,1)S(1)}, bf16[216,256]{1,0:T(8,128)(2,1)S(1)}, u32[]{:S(2)}, u32[]{:S(2)}) collective-permute-start(bf16[216,256]{1,0:T(8,128)(2,1)S(1)} %collective-permute-done.4), channel_id=1, source_target_pairs={{0,8},{8,16},{16,24},{24,32},{32,40},{40,48},{48,56},{56,0},{1,9},... | collective-permute-start | bytes 331784 | tf_op jit(solution)/shard_map/ppermute | solution.py:51
  42.4 9.9 %collective-permute-start.11 = (bf16[5,1408,24]{1,2,0:T(8,128)(2,1)S(1)}, bf16[5,1408,24]{1,2,0:T(8,128)(2,1)S(1)}, u32[]{:S(2)}, u32[]{:S(2)}) collective-permute-start(bf16[5,1408,24]{1,2,0:T(8,128)(2,1)S(1)} %collective-permute-done.7), channel_id=1, source_target_pairs={{0,8},{8,16},{16,24},{24,32},{32,40},{40,48},{48,56},{56,0},{1,9},... | collective-permute-start | bytes 1013768 | tf_op jit(solution)/shard_map/ppermute | solution.py:51
  42.4 9.9 %collective-permute-start.9 = (bf16[5,1408,24]{1,2,0:T(8,128)(2,1)S(1)}, bf16[5,1408,24]{1,2,0:T(8,128)(2,1)S(1)}, u32[]{:S(2)}, u32[]{:S(2)}) collective-permute-start(bf16[5,1408,24]{1,2,0:T(8,128)(2,1)S(1)} %collective-permute-done.5), channel_id=1, source_target_pairs={{0,56},{8,0},{16,8},{24,16},{32,24},{40,32},{48,40},{56,48},{1,57}... | collective-permute-start | bytes 1013768 | tf_op jit(solution)/shard_map/ppermute | solution.py:49
  45.0 6.3 %collective-permute-start.10 = (bf16[216,256]{1,0:T(8,128)(2,1)S(1)}, bf16[216,256]{1,0:T(8,128)(2,1)S(1)}, u32[]{:S(2)}, u32[]{:S(2)}) collective-permute-start(bf16[216,256]{1,0:T(8,128)(2,1)S(1)} %collective-permute-done.6), channel_id=1, source_target_pairs={{0,56},{8,0},{16,8},{24,16},{32,24},{40,32},{48,40},{56,48},{1,57}... | collective-permute-start | bytes 331784 | tf_op jit(solution)/shard_map/ppermute | solution.py:49
  45.1 7.2 %collective-permute-start.12 = (bf16[216,256]{1,0:T(8,128)(2,1)S(1)}, bf16[216,256]{1,0:T(8,128)(2,1)S(1)}, u32[]{:S(2)}, u32[]{:S(2)}) collective-permute-start(bf16[216,256]{1,0:T(8,128)(2,1)S(1)} %collective-permute-done.8), channel_id=1, source_target_pairs={{0,8},{8,16},{16,24},{24,32},{32,40},{40,48},{48,56},{56,0},{1,9},... | collective-permute-start | bytes 331784 | tf_op jit(solution)/shard_map/ppermute | solution.py:51
  52.3 7.9 %collective-permute-start.13 = (bf16[5,1408,24]{1,2,0:T(8,128)(2,1)S(1)}, bf16[5,1408,24]{1,2,0:T(8,128)(2,1)S(1)}, u32[]{:S(2)}, u32[]{:S(2)}) collective-permute-start(bf16[5,1408,24]{1,2,0:T(8,128)(2,1)S(1)} %collective-permute-done.9), channel_id=1, source_target_pairs={{0,56},{8,0},{16,8},{24,16},{32,24},{40,32},{48,40},{56,48},{1,57}... | collective-permute-start | bytes 1013768 | tf_op jit(solution)/shard_map/ppermute | solution.py:49
  66.0 7.8 %collective-permute-start = (bf16[2,1408]{1,0:T(2,128)(2,1)S(1)}, bf16[2,1408]{1,0:T(2,128)(2,1)S(1)}, u32[]{:S(2)}, u32[]{:S(2)}) collective-permute-start(bf16[2,1408]{1,0:T(2,128)(2,1)S(1)} %get-tuple-element.56), channel_id=1, source_target_pairs={{0,8},{8,16},{16,24},{24,32},{32,40},{40,48},{48,56},{1,9},{9,17},... | collective-permute-start | bytes 16904 | tf_op jit(solution)/shard_map/ppermute | solution.py:136
  68.0 5.7 %collective-permute-start.15 = (bf16[2,1408]{1,0:T(2,128)(2,1)S(1)}, bf16[2,1408]{1,0:T(2,128)(2,1)S(1)}, u32[]{:S(2)}, u32[]{:S(2)}) collective-permute-start(bf16[2,1408]{1,0:T(2,128)(2,1)S(1)} %get-tuple-element.57), channel_id=1, source_target_pairs={{8,0},{16,8},{24,16},{32,24},{40,32},{48,40},{56,48},{9,1},{17,9},... | collective-permute-start | bytes 16904 | tf_op jit(solution)/shard_map/ppermute | solution.py:137
  84.7 16.7 %all-to-all-start = ((bf16[8,96,192]{1,2,0:T(8,128)(2,1)}), bf16[8,96,192]{1,2,0:T(8,128)(2,1)S(1)}, u32[]{:S(2)}, u32[]{:S(2)}) async-start(bf16[8,96,192]{1,2,0:T(8,128)(2,1)} %copy.33), calls=%async_computation | async-start | bytes 786432 | tf_op jit(solution)/shard_map/all_to_all | solution.py:148
  93.7 71.9 %all-gather.8.cloned.1.call-start = ((), (), s32[]{:S(2)}) async-start(), calls=%async_computation.3 | async-start | bytes 3538944 | tf_op jit(solution)/shard_map/all_gather | solution.py:158
  120.2 7.5 %collective-permute-start.16 = (bf16[128,1536]{1,0:T(8,128)(2,1)S(1)}, bf16[128,1536]{1,0:T(8,128)(2,1)S(1)}, u32[]{:S(2)}, u32[]{:S(2)}) collective-permute-start(bf16[128,1536]{1,0:T(8,128)(2,1)S(1)} %reshape.80), channel_id=1, source_target_pairs={{0,7},{1,0},{2,1},{3,2},{4,3},{5,4},{6,5},{7,6},{8,15},{9,8},{10,9... | collective-permute-start | bytes 1179656 | tf_op jit(solution)/shard_map/ppermute | solution.py:49
  120.4 7.3 %collective-permute-start.17 = (bf16[128,1536]{1,0:T(8,128)(2,1)S(1)}, bf16[128,1536]{1,0:T(8,128)(2,1)S(1)}, u32[]{:S(2)}, u32[]{:S(2)}) collective-permute-start(bf16[128,1536]{1,0:T(8,128)(2,1)S(1)} %reshape.80), channel_id=1, source_target_pairs={{0,1},{1,2},{2,3},{3,4},{4,5},{5,6},{6,7},{7,0},{8,9},{9,10},{10,1... | collective-permute-start | bytes 1179656 | tf_op jit(solution)/shard_map/ppermute | solution.py:51
  127.8 7.6 %collective-permute-start.18 = (bf16[128,1536]{1,0:T(8,128)(2,1)S(1)}, bf16[128,1536]{1,0:T(8,128)(2,1)}, u32[]{:S(2)}, u32[]{:S(2)}) collective-permute-start(bf16[128,1536]{1,0:T(8,128)(2,1)S(1)} %collective-permute-done.16), channel_id=1, source_target_pairs={{0,7},{1,0},{2,1},{3,2},{4,3},{5,4},{6,5},{7,6},{8,15},{9,8},{10,9... | collective-permute-start | bytes 1179656 | tf_op jit(solution)/shard_map/ppermute | solution.py:49
  130.0 5.4 %collective-permute-start.19 = (bf16[128,1536]{1,0:T(8,128)(2,1)S(1)}, bf16[128,1536]{1,0:T(8,128)(2,1)}, u32[]{:S(2)}, u32[]{:S(2)}) collective-permute-start(bf16[128,1536]{1,0:T(8,128)(2,1)S(1)} %collective-permute-done.17), channel_id=1, source_target_pairs={{0,1},{1,2},{2,3},{3,4},{4,5},{5,6},{6,7},{7,0},{8,9},{9,10},{10,1... | collective-permute-start | bytes 1179656 | tf_op jit(solution)/shard_map/ppermute | solution.py:51
  135.4 8.0 %collective-permute-start.20 = (bf16[128,1536]{1,0:T(8,128)(2,1)}, bf16[128,1536]{1,0:T(8,128)(2,1)S(1)}, u32[]{:S(2)}, u32[]{:S(2)}) collective-permute-start(bf16[128,1536]{1,0:T(8,128)(2,1)} %collective-permute-done.18), channel_id=1, source_target_pairs={{0,7},{1,0},{2,1},{3,2},{4,3},{5,4},{6,5},{7,6},{8,15},{9,8},{10,9... | collective-permute-start | bytes 1179656 | tf_op jit(solution)/shard_map/ppermute | solution.py:49
  143.5 8.2 %collective-permute-start.22 = (bf16[128,1536]{1,0:T(8,128)(2,1)S(1)}, bf16[128,1536]{1,0:T(8,128)(2,1)S(1)}, u32[]{:S(2)}, u32[]{:S(2)}) collective-permute-start(bf16[128,1536]{1,0:T(8,128)(2,1)S(1)} %collective-permute-done.20), channel_id=1, source_target_pairs={{0,7},{1,0},{2,1},{3,2},{4,3},{5,4},{6,5},{7,6},{8,15},{9,8},{10,9... | collective-permute-start | bytes 1179656 | tf_op jit(solution)/shard_map/ppermute | solution.py:49
  (15 other events, 96.7 us)
Sparse Core Ops, SparseCore 0:
  11.0 39.2 all-gather.3
  61.6 37.5 all-gather.5
  120.4 45.2 all-gather.7

commit v12 on v11

--- a/solution.py
+++ b/solution.py
@@ -26,7 +26,7 @@
 
 
 def pool_pairs(levels):
-    return jnp.max(levels.reshape(-1, 2, levels.shape[1]), axis=1)
+    return jnp.maximum(levels[0::2], levels[1::2])
 
 
 def gather_rows(block):

time: 191 us -> 209 us (1.094)
  local copies, waits for them, and re-layouts: 21.9 us -> 42.6 us
  other arithmetic: 7.83 us -> 5.67 us
    slice x0 -> x2, local copies, waits for them, and re-layouts: none -> 21.5 us  [pool_pairs(): return jnp.maximum(levels[0::2], levels[1::2])]
    reduce_max x1 -> x0, other arithmetic: 2.22 us -> none  [pool_pairs(): return jnp.max(levels.reshape(-1, 2, levels.shape[1]), axis=1)]
  transfers between devices with their start and end apart: 27 -> 27, of which waited for: 14 -> 14; matrix products, arithmetic and copies ran while one was open for 17% -> 25% of each run, Pallas kernels for 0% -> 0%
where the time goes in v12:
time: 209 us
  waiting for transfers between devices  61.3 us (29%)
  local copies, waits for them, and re-layouts  42.6 us (20%)
  starting transfers between devices  42.3 us (20%)
  blocking collectives  15.1 us (7%)
  Pallas kernels  15 us (7%)
  between operations  14.3 us (7%)
  matrix products  12.2 us (6%)
  other arithmetic  5.67 us (3%)
    ppermute x12, waiting for transfers between devices, ring(): ahead = lax.ppermute(ahead, axis, up)  35.6 us
    ppermute x12, starting transfers between devices, ring(): ahead = lax.ppermute(ahead, axis, up)  25.4 us
    slice x2, local copies, waits for them, and re-layouts, pool_pairs(): return jnp.maximum(levels[0::2], levels[1::2])  21.5 us
    all_gather x1, blocking collectives, shards(): kv_plane = lax.all_gather(keyvals, 'sx', axis=0, tiled=True)  15.1 us
    pallas_call x1, Pallas kernels, attend(): pl.pallas_call(head_kernel, grid=(head_count,), in_specs=[pl.BlockSpec(me...  15 us
    unnamed x48, local copies, waits for them, and re-layouts  13 us
    all_gather x1, waiting for transfers between devices, shards(): key_block = lax.all_gather(kv_plane, 'sz', axis=0, tiled=True)  12.7 us
    all_to_all x1, starting transfers between devices, shards(): received = lax.all_to_all(pieces, 'sx', 0, 0, tiled=False)  9.02 us
  transfers between devices with their start and end apart: 27, of which 14 were waited for; matrix products, arithmetic and copies ran while one was open for 25% of the time, Pallas kernels for 0%

profile of v12, /device:TPU:1, one launch (start us, length us, event | category | flops | bytes accessed | tf_op | source)
XLA Modules:
  0.0 208.6 jit_solution(8378408924212536784)
XLA Ops:
  12.7 6.5 %collective-permute-start.2 = (bf16[216,256]{1,0:T(8,128)(2,1)S(1)}, bf16[216,256]{1,0:T(8,128)(2,1)S(1)}, u32[]{:S(2)}, u32[]{:S(2)}) collective-permute-start(bf16[216,256]{1,0:T(8,128)(2,1)S(1)} %constant_dynamic-update-slice_fusion), channel_id=1, source_target_pairs={{0,56},{8,0},{16,8},{24,16},{32,24},{40,32},{48,40},{56,48},{1,57}... | collective-permute-start | bytes 331784 | tf_op jit(solution)/shard_map/ppermute | solution.py:49
  19.2 2.7 %collective-permute-start.1 = (bf16[5,1408,24]{1,2,0:T(8,128)(2,1)}, bf16[5,1408,24]{1,2,0:T(8,128)(2,1)S(1)}, u32[]{:S(2)}, u32[]{:S(2)}) collective-permute-start(bf16[5,1408,24]{1,2,0:T(8,128)(2,1)} %param.11), channel_id=1, source_target_pairs={{0,56},{8,0},{16,8},{24,16},{32,24},{40,32},{48,40},{56,48},{1,57}... | collective-permute-start | bytes 1013768 | tf_op jit(solution)/shard_map/ppermute | solution.py:49
  24.5 3.7 %collective-permute-done.1 = bf16[5,1408,24]{1,2,0:T(8,128)(2,1)S(1)} collective-permute-done((bf16[5,1408,24]{1,2,0:T(8,128)(2,1)}, bf16[5,1408,24]{1,2,0:T(8,128)(2,1)S(1)}, u32[]{:S(2)}, u32[]{:S(2)}) %collective-permute-start.1) | collective-permute-done | bytes 337952 | tf_op jit(solution)/shard_map/ppermute | solution.py:49
  28.2 3.0 %collective-permute-done.3 = bf16[5,1408,24]{1,2,0:T(8,128)(2,1)S(1)} collective-permute-done((bf16[5,1408,24]{1,2,0:T(8,128)(2,1)}, bf16[5,1408,24]{1,2,0:T(8,128)(2,1)S(1)}, u32[]{:S(2)}, u32[]{:S(2)}) %collective-permute-start.3) | collective-permute-done | bytes 337952 | tf_op jit(solution)/shard_map/ppermute | solution.py:51
  34.9 5.9 %collective-permute-done.6 = bf16[216,256]{1,0:T(8,128)(2,1)S(1)} collective-permute-done((bf16[216,256]{1,0:T(8,128)(2,1)S(1)}, bf16[216,256]{1,0:T(8,128)(2,1)S(1)}, u32[]{:S(2)}, u32[]{:S(2)}) %collective-permute-start.6) | collective-permute-done | bytes 110624 | tf_op jit(solution)/shard_map/ppermute | solution.py:49
  42.3 2.7 %collective-permute-start.9 = (bf16[5,1408,24]{1,2,0:T(8,128)(2,1)S(1)}, bf16[5,1408,24]{1,2,0:T(8,128)(2,1)S(1)}, u32[]{:S(2)}, u32[]{:S(2)}) collective-permute-start(bf16[5,1408,24]{1,2,0:T(8,128)(2,1)S(1)} %collective-permute-done.5), channel_id=1, source_target_pairs={{0,56},{8,0},{16,8},{24,16},{32,24},{40,32},{48,40},{56,48},{1,57}... | collective-permute-start | bytes 1013768 | tf_op jit(solution)/shard_map/ppermute | solution.py:49
  47.2 4.1 %collective-permute-done.10 = bf16[216,256]{1,0:T(8,128)(2,1)S(1)} collective-permute-done((bf16[216,256]{1,0:T(8,128)(2,1)S(1)}, bf16[216,256]{1,0:T(8,128)(2,1)S(1)}, u32[]{:S(2)}, u32[]{:S(2)}) %collective-permute-start.10) | collective-permute-done | bytes 110624 | tf_op jit(solution)/shard_map/ppermute | solution.py:49
  52.3 2.5 %collective-permute-start.13 = (bf16[5,1408,24]{1,2,0:T(8,128)(2,1)S(1)}, bf16[5,1408,24]{1,2,0:T(8,128)(2,1)S(1)}, u32[]{:S(2)}, u32[]{:S(2)}) collective-permute-start(bf16[5,1408,24]{1,2,0:T(8,128)(2,1)S(1)} %collective-permute-done.9), channel_id=1, source_target_pairs={{0,56},{8,0},{16,8},{24,16},{32,24},{40,32},{48,40},{56,48},{1,57}... | collective-permute-start | bytes 1013768 | tf_op jit(solution)/shard_map/ppermute | solution.py:49
  55.1 5.1 %collective-permute-done.14 = bf16[216,256]{1,0:T(8,128)(2,1)S(1)} collective-permute-done((bf16[216,256]{1,0:T(8,128)(2,1)S(1)}, bf16[216,256]{1,0:T(8,128)(2,1)S(1)}, u32[]{:S(2)}, u32[]{:S(2)}) %collective-permute-start.14) | collective-permute-done | bytes 110624 | tf_op jit(solution)/shard_map/ppermute | solution.py:49
  69.6 2.5 %constant_dynamic-update-slice_fusion.27 = bf16[1538,1408]{1,0:T(8,128)(2,1)S(1)} fusion(bf16[1536,1408]{1,0:T(8,128)(2,1)} %all-gather.4.cloned.1.call-done), kind=kLoop, calls=%fused_computation.78 | loop fusion | bytes 8650752
  80.4 10.8 %slice.208 = bf16[768,192]{0,1:T(8,128)(2,1)S(1)} slice(bf16[1536,192]{0,1:T(8,128)(2,1)S(1)} %fusion.15), slice={[0:1536:2], [0:192:1]} | slice | bytes 589824 | tf_op jit(solution)/shard_map/slice | solution.py:29
  91.2 10.8 %slice.209 = bf16[768,192]{0,1:T(8,128)(2,1)S(1)} slice(bf16[1536,192]{0,1:T(8,128)(2,1)S(1)} %fusion.15), slice={[1:1536:2], [0:192:1]} | slice | bytes 589824 | tf_op jit(solution)/shard_map/slice | solution.py:29
  103.3 9.0 %all-to-all-start = ((bf16[8,96,192]{1,2,0:T(8,128)(2,1)}), bf16[8,96,192]{1,2,0:T(8,128)(2,1)S(1)}, u32[]{:S(2)}, u32[]{:S(2)}) async-start(bf16[8,96,192]{1,2,0:T(8,128)(2,1)} %copy.24), calls=%async_computation | async-start | bytes 786432 | tf_op jit(solution)/shard_map/all_to_all | solution.py:148
  112.8 7.2 %all-to-all-done = bf16[8,96,192]{1,2,0:T(8,128)(2,1)S(1)} async-done(((bf16[8,96,192]{1,2,0:T(8,128)(2,1)}), bf16[8,96,192]{1,2,0:T(8,128)(2,1)S(1)}, u32[]{:S(2)}, u32[]{:S(2)}) %all-to-all-start) | async-done | bytes 294944 | tf_op jit(solution)/shard_map/all_to_all | solution.py:148
  120.9 2.8 %convolution_convert_fusion.1 = bf16[96,1280]{1,0:T(8,128)(2,1)S(1)} fusion(bf16[96,1536]{0,1:T(8,128)(2,1)S(1)} %bitcast.124, bf16[1536,1280]{1,0:T(8,128)(2,1)} %all-gather.6.cloned.1.call-done), kind=kOutput, calls=%fused_computation.17 | convolution fusion | flops 377610240 | bytes 4472832 | tf_op jit(solution)/shard_map/dot_general | solution.py:153
  123.7 15.1 %all_gather.14 = bf16[768,256]{1,0:T(8,128)(2,1)} all-gather(bf16[96,256]{1,0:T(8,128)(2,1)S(1)} %slice.222), channel_id=1, replica_groups=mesh['dp'=4,'sz'=8,'sx'=8] {'sx'}, dimensions={0}, use_global_device_ids=true | all-gather | bytes 442368 | tf_op jit(solution)/shard_map/all_gather | solution.py:156
  140.6 5.8 %collective-permute-done.16 = bf16[128,1536]{1,0:T(8,128)(2,1)S(1)} collective-permute-done((bf16[128,1536]{1,0:T(8,128)(2,1)S(1)}, bf16[128,1536]{1,0:T(8,128)(2,1)S(1)}, u32[]{:S(2)}, u32[]{:S(2)}) %collective-permute-start.16) | collective-permute-done | bytes 393248 | tf_op jit(solution)/shard_map/ppermute | solution.py:49
  150.2 3.8 %collective-permute-done.18 = bf16[128,1536]{1,0:T(8,128)(2,1)} collective-permute-done((bf16[128,1536]{1,0:T(8,128)(2,1)S(1)}, bf16[128,1536]{1,0:T(8,128)(2,1)}, u32[]{:S(2)}, u32[]{:S(2)}) %collective-permute-start.18) | collective-permute-done | bytes 393248 | tf_op jit(solution)/shard_map/ppermute | solution.py:49
  153.9 3.1 %collective-permute-start.20 = (bf16[128,1536]{1,0:T(8,128)(2,1)}, bf16[128,1536]{1,0:T(8,128)(2,1)S(1)}, u32[]{:S(2)}, u32[]{:S(2)}) collective-permute-start(bf16[128,1536]{1,0:T(8,128)(2,1)} %collective-permute-done.18), channel_id=1, source_target_pairs={{0,7},{1,0},{2,1},{3,2},{4,3},{5,4},{6,5},{7,6},{8,15},{9,8},{10,9... | collective-permute-start | bytes 1179656 | tf_op jit(solution)/shard_map/ppermute | solution.py:49
  158.2 3.7 %collective-permute-done.20 = bf16[128,1536]{1,0:T(8,128)(2,1)S(1)} collective-permute-done((bf16[128,1536]{1,0:T(8,128)(2,1)}, bf16[128,1536]{1,0:T(8,128)(2,1)S(1)}, u32[]{:S(2)}, u32[]{:S(2)}) %collective-permute-start.20) | collective-permute-done | bytes 393248 | tf_op jit(solution)/shard_map/ppermute | solution.py:49
  162.1 3.6 %collective-permute-start.22 = (bf16[128,1536]{1,0:T(8,128)(2,1)S(1)}, bf16[128,1536]{1,0:T(8,128)(2,1)S(1)}, u32[]{:S(2)}, u32[]{:S(2)}) collective-permute-start(bf16[128,1536]{1,0:T(8,128)(2,1)S(1)} %collective-permute-done.20), channel_id=1, source_target_pairs={{0,7},{1,0},{2,1},{3,2},{4,3},{5,4},{6,5},{7,6},{8,15},{9,8},{10,9... | collective-permute-start | bytes 1179656 | tf_op jit(solution)/shard_map/ppermute | solution.py:49
  166.8 3.6 %collective-permute-done.22 = bf16[128,1536]{1,0:T(8,128)(2,1)S(1)} collective-permute-done((bf16[128,1536]{1,0:T(8,128)(2,1)S(1)}, bf16[128,1536]{1,0:T(8,128)(2,1)S(1)}, u32[]{:S(2)}, u32[]{:S(2)}) %collective-permute-start.22) | collective-permute-done | bytes 393248 | tf_op jit(solution)/shard_map/ppermute | solution.py:49
  171.5 12.7 %all-gather.8.cloned.1.call-done.k_ref.v_ref = bf16[6144,256]{1,0:T(8,128)(2,1)} async-done(((bf16[768,256]{1,0:T(8,128)(2,1)}), bf16[6144,256]{1,0:T(8,128)(2,1)}) %all-gather.8.cloned.1.call-update) | async-done | bytes 3145744 | tf_op jit(solution)/shard_map/all_gather | solution.py:158
  184.2 15.0 %shard_map.104 = bf16[96,1024]{1,0:T(8,128)(2,1)} custom-call(f32[8]{0:T(128)} %scale_ref.1, bf16[96,1024]{1,0:T(8,128)(2,1)} %slice.221.q_ref, bf16[6144,256]{1,0:T(8,128)(2,1)} %all-gather.8.cloned.1.call-done.k_ref.v_ref, bf16[6144,256]{1,0:T(8,128)(2,1)} %all-gather.8.cloned.1.call-done.k_ref.v_ref), custom_call_target="tpu_custom_call" | custom-call | flops 2415919104 | bytes 3538944 | tf_op jit(solution)/shard_map/pallas_call | solution.py:78
  (129 shorter events, 48.7 us)
Async XLA Ops:
  7.2 58.1 %all-gather.4.cloned.1.call-start = ((), (), s32[]{:S(2)}) async-start(), calls=%async_computation.1 | async-start | bytes 4866048 | tf_op jit(solution)/shard_map/all_gather | solution.py:117
  10.9 110.0 %all-gather.6.cloned.1.call-start = ((), (), s32[]{:S(2)}) async-start(), calls=%async_computation.2 | async-start | bytes 4423680 | tf_op jit(solution)/shard_map/all_gather | solution.py:131
  12.7 11.8 %collective-permute-start.2 = (bf16[216,256]{1,0:T(8,128)(2,1)S(1)}, bf16[216,256]{1,0:T(8,128)(2,1)S(1)}, u32[]{:S(2)}, u32[]{:S(2)}) collective-permute-start(bf16[216,256]{1,0:T(8,128)(2,1)S(1)} %constant_dynamic-update-slice_fusion), channel_id=1, source_target_pairs={{0,56},{8,0},{16,8},{24,16},{32,24},{40,32},{48,40},{56,48},{1,57}... | collective-permute-start | bytes 331784 | tf_op jit(solution)/shard_map/ppermute | solution.py:49
  19.2 9.0 %collective-permute-start.1 = (bf16[5,1408,24]{1,2,0:T(8,128)(2,1)}, bf16[5,1408,24]{1,2,0:T(8,128)(2,1)S(1)}, u32[]{:S(2)}, u32[]{:S(2)}) collective-permute-start(bf16[5,1408,24]{1,2,0:T(8,128)(2,1)} %param.11), channel_id=1, source_target_pairs={{0,56},{8,0},{16,8},{24,16},{32,24},{40,32},{48,40},{56,48},{1,57}... | collective-permute-start | bytes 1013768 | tf_op jit(solution)/shard_map/ppermute | solution.py:49
  21.9 9.4 %collective-permute-start.3 = (bf16[5,1408,24]{1,2,0:T(8,128)(2,1)}, bf16[5,1408,24]{1,2,0:T(8,128)(2,1)S(1)}, u32[]{:S(2)}, u32[]{:S(2)}) collective-permute-start(bf16[5,1408,24]{1,2,0:T(8,128)(2,1)} %param.11), channel_id=1, source_target_pairs={{0,8},{8,16},{16,24},{24,32},{32,40},{40,48},{48,56},{56,0},{1,9},... | collective-permute-start | bytes 1013768 | tf_op jit(solution)/shard_map/ppermute | solution.py:51
  31.3 11.1 %collective-permute-start.5 = (bf16[5,1408,24]{1,2,0:T(8,128)(2,1)S(1)}, bf16[5,1408,24]{1,2,0:T(8,128)(2,1)S(1)}, u32[]{:S(2)}, u32[]{:S(2)}) collective-permute-start(bf16[5,1408,24]{1,2,0:T(8,128)(2,1)S(1)} %collective-permute-done.1), channel_id=1, source_target_pairs={{0,56},{8,0},{16,8},{24,16},{32,24},{40,32},{48,40},{56,48},{1,57}... | collective-permute-start | bytes 1013768 | tf_op jit(solution)/shard_map/ppermute | solution.py:49
  31.5 10.8 %collective-permute-start.7 = (bf16[5,1408,24]{1,2,0:T(8,128)(2,1)S(1)}, bf16[5,1408,24]{1,2,0:T(8,128)(2,1)S(1)}, u32[]{:S(2)}, u32[]{:S(2)}) collective-permute-start(bf16[5,1408,24]{1,2,0:T(8,128)(2,1)S(1)} %collective-permute-done.3), channel_id=1, source_target_pairs={{0,8},{8,16},{16,24},{24,32},{32,40},{40,48},{48,56},{56,0},{1,9},... | collective-permute-start | bytes 1013768 | tf_op jit(solution)/shard_map/ppermute | solution.py:51
  32.7 8.1 %collective-permute-start.6 = (bf16[216,256]{1,0:T(8,128)(2,1)S(1)}, bf16[216,256]{1,0:T(8,128)(2,1)S(1)}, u32[]{:S(2)}, u32[]{:S(2)}) collective-permute-start(bf16[216,256]{1,0:T(8,128)(2,1)S(1)} %collective-permute-done.2), channel_id=1, source_target_pairs={{0,56},{8,0},{16,8},{24,16},{32,24},{40,32},{48,40},{56,48},{1,57}... | collective-permute-start | bytes 331784 | tf_op jit(solution)/shard_map/ppermute | solution.py:49
  34.2 8.1 %collective-permute-start.8 = (bf16[216,256]{1,0:T(8,128)(2,1)S(1)}, bf16[216,256]{1,0:T(8,128)(2,1)S(1)}, u32[]{:S(2)}, u32[]{:S(2)}) collective-permute-start(bf16[216,256]{1,0:T(8,128)(2,1)S(1)} %collective-permute-done.4), channel_id=1, source_target_pairs={{0,8},{8,16},{16,24},{24,32},{32,40},{40,48},{48,56},{56,0},{1,9},... | collective-permute-start | bytes 331784 | tf_op jit(solution)/shard_map/ppermute | solution.py:51
  42.3 9.9 %collective-permute-start.11 = (bf16[5,1408,24]{1,2,0:T(8,128)(2,1)S(1)}, bf16[5,1408,24]{1,2,0:T(8,128)(2,1)S(1)}, u32[]{:S(2)}, u32[]{:S(2)}) collective-permute-start(bf16[5,1408,24]{1,2,0:T(8,128)(2,1)S(1)} %collective-permute-done.7), channel_id=1, source_target_pairs={{0,8},{8,16},{16,24},{24,32},{32,40},{40,48},{48,56},{56,0},{1,9},... | collective-permute-start | bytes 1013768 | tf_op jit(solution)/shard_map/ppermute | solution.py:51
  42.3 9.9 %collective-permute-start.9 = (bf16[5,1408,24]{1,2,0:T(8,128)(2,1)S(1)}, bf16[5,1408,24]{1,2,0:T(8,128)(2,1)S(1)}, u32[]{:S(2)}, u32[]{:S(2)}) collective-permute-start(bf16[5,1408,24]{1,2,0:T(8,128)(2,1)S(1)} %collective-permute-done.5), channel_id=1, source_target_pairs={{0,56},{8,0},{16,8},{24,16},{32,24},{40,32},{48,40},{56,48},{1,57}... | collective-permute-start | bytes 1013768 | tf_op jit(solution)/shard_map/ppermute | solution.py:49
  45.0 6.3 %collective-permute-start.10 = (bf16[216,256]{1,0:T(8,128)(2,1)S(1)}, bf16[216,256]{1,0:T(8,128)(2,1)S(1)}, u32[]{:S(2)}, u32[]{:S(2)}) collective-permute-start(bf16[216,256]{1,0:T(8,128)(2,1)S(1)} %collective-permute-done.6), channel_id=1, source_target_pairs={{0,56},{8,0},{16,8},{24,16},{32,24},{40,32},{48,40},{56,48},{1,57}... | collective-permute-start | bytes 331784 | tf_op jit(solution)/shard_map/ppermute | solution.py:49
  45.0 7.2 %collective-permute-start.12 = (bf16[216,256]{1,0:T(8,128)(2,1)S(1)}, bf16[216,256]{1,0:T(8,128)(2,1)S(1)}, u32[]{:S(2)}, u32[]{:S(2)}) collective-permute-start(bf16[216,256]{1,0:T(8,128)(2,1)S(1)} %collective-permute-done.8), channel_id=1, source_target_pairs={{0,8},{8,16},{16,24},{24,32},{32,40},{40,48},{48,56},{56,0},{1,9},... | collective-permute-start | bytes 331784 | tf_op jit(solution)/shard_map/ppermute | solution.py:51
  52.3 7.9 %collective-permute-start.13 = (bf16[5,1408,24]{1,2,0:T(8,128)(2,1)S(1)}, bf16[5,1408,24]{1,2,0:T(8,128)(2,1)S(1)}, u32[]{:S(2)}, u32[]{:S(2)}) collective-permute-start(bf16[5,1408,24]{1,2,0:T(8,128)(2,1)S(1)} %collective-permute-done.9), channel_id=1, source_target_pairs={{0,56},{8,0},{16,8},{24,16},{32,24},{40,32},{48,40},{56,48},{1,57}... | collective-permute-start | bytes 1013768 | tf_op jit(solution)/shard_map/ppermute | solution.py:49
  66.0 7.8 %collective-permute-start = (bf16[2,1408]{1,0:T(2,128)(2,1)S(1)}, bf16[2,1408]{1,0:T(2,128)(2,1)S(1)}, u32[]{:S(2)}, u32[]{:S(2)}) collective-permute-start(bf16[2,1408]{1,0:T(2,128)(2,1)S(1)} %get-tuple-element.54), channel_id=1, source_target_pairs={{0,8},{8,16},{16,24},{24,32},{32,40},{40,48},{48,56},{1,9},{9,17},... | collective-permute-start | bytes 16904 | tf_op jit(solution)/shard_map/ppermute | solution.py:136
  68.0 5.7 %collective-permute-start.15 = (bf16[2,1408]{1,0:T(2,128)(2,1)S(1)}, bf16[2,1408]{1,0:T(2,128)(2,1)S(1)}, u32[]{:S(2)}, u32[]{:S(2)}) collective-permute-start(bf16[2,1408]{1,0:T(2,128)(2,1)S(1)} %get-tuple-element.55), channel_id=1, source_target_pairs={{8,0},{16,8},{24,16},{32,24},{40,32},{48,40},{56,48},{9,1},{17,9},... | collective-permute-start | bytes 16904 | tf_op jit(solution)/shard_map/ppermute | solution.py:137
  103.3 16.7 %all-to-all-start = ((bf16[8,96,192]{1,2,0:T(8,128)(2,1)}), bf16[8,96,192]{1,2,0:T(8,128)(2,1)S(1)}, u32[]{:S(2)}, u32[]{:S(2)}) async-start(bf16[8,96,192]{1,2,0:T(8,128)(2,1)} %copy.24), calls=%async_computation | async-start | bytes 786432 | tf_op jit(solution)/shard_map/all_to_all | solution.py:148
  112.3 71.9 %all-gather.8.cloned.1.call-start = ((), (), s32[]{:S(2)}) async-start(), calls=%async_computation.3 | async-start | bytes 3538944 | tf_op jit(solution)/shard_map/all_gather | solution.py:158
  138.8 7.5 %collective-permute-start.16 = (bf16[128,1536]{1,0:T(8,128)(2,1)S(1)}, bf16[128,1536]{1,0:T(8,128)(2,1)S(1)}, u32[]{:S(2)}, u32[]{:S(2)}) collective-permute-start(bf16[128,1536]{1,0:T(8,128)(2,1)S(1)} %reshape.77), channel_id=1, source_target_pairs={{0,7},{1,0},{2,1},{3,2},{4,3},{5,4},{6,5},{7,6},{8,15},{9,8},{10,9... | collective-permute-start | bytes 1179656 | tf_op jit(solution)/shard_map/ppermute | solution.py:49
  139.0 7.3 %collective-permute-start.17 = (bf16[128,1536]{1,0:T(8,128)(2,1)S(1)}, bf16[128,1536]{1,0:T(8,128)(2,1)S(1)}, u32[]{:S(2)}, u32[]{:S(2)}) collective-permute-start(bf16[128,1536]{1,0:T(8,128)(2,1)S(1)} %reshape.77), channel_id=1, source_target_pairs={{0,1},{1,2},{2,3},{3,4},{4,5},{5,6},{6,7},{7,0},{8,9},{9,10},{10,1... | collective-permute-start | bytes 1179656 | tf_op jit(solution)/shard_map/ppermute | solution.py:51
  146.3 7.6 %collective-permute-start.18 = (bf16[128,1536]{1,0:T(8,128)(2,1)S(1)}, bf16[128,1536]{1,0:T(8,128)(2,1)}, u32[]{:S(2)}, u32[]{:S(2)}) collective-permute-start(bf16[128,1536]{1,0:T(8,128)(2,1)S(1)} %collective-permute-done.16), channel_id=1, source_target_pairs={{0,7},{1,0},{2,1},{3,2},{4,3},{5,4},{6,5},{7,6},{8,15},{9,8},{10,9... | collective-permute-start | bytes 1179656 | tf_op jit(solution)/shard_map/ppermute | solution.py:49
  148.5 5.4 %collective-permute-start.19 = (bf16[128,1536]{1,0:T(8,128)(2,1)S(1)}, bf16[128,1536]{1,0:T(8,128)(2,1)}, u32[]{:S(2)}, u32[]{:S(2)}) collective-permute-start(bf16[128,1536]{1,0:T(8,128)(2,1)S(1)} %collective-permute-done.17), channel_id=1, source_target_pairs={{0,1},{1,2},{2,3},{3,4},{4,5},{5,6},{6,7},{7,0},{8,9},{9,10},{10,1... | collective-permute-start | bytes 1179656 | tf_op jit(solution)/shard_map/ppermute | solution.py:51
  153.9 8.0 %collective-permute-start.20 = (bf16[128,1536]{1,0:T(8,128)(2,1)}, bf16[128,1536]{1,0:T(8,128)(2,1)S(1)}, u32[]{:S(2)}, u32[]{:S(2)}) collective-permute-start(bf16[128,1536]{1,0:T(8,128)(2,1)} %collective-permute-done.18), channel_id=1, source_target_pairs={{0,7},{1,0},{2,1},{3,2},{4,3},{5,4},{6,5},{7,6},{8,15},{9,8},{10,9... | collective-permute-start | bytes 1179656 | tf_op jit(solution)/shard_map/ppermute | solution.py:49
  162.1 8.2 %collective-permute-start.22 = (bf16[128,1536]{1,0:T(8,128)(2,1)S(1)}, bf16[128,1536]{1,0:T(8,128)(2,1)S(1)}, u32[]{:S(2)}, u32[]{:S(2)}) collective-permute-start(bf16[128,1536]{1,0:T(8,128)(2,1)S(1)} %collective-permute-done.20), channel_id=1, source_target_pairs={{0,7},{1,0},{2,1},{3,2},{4,3},{5,4},{6,5},{7,6},{8,15},{9,8},{10,9... | collective-permute-start | bytes 1179656 | tf_op jit(solution)/shard_map/ppermute | solution.py:49
  (15 other events, 115.6 us)
Sparse Core Ops, SparseCore 0:
  11.0 39.2 all-gather.3
  61.6 37.5 all-gather.5
  138.9 45.2 all-gather.7

commit v13 on v11

--- a/solution.py
+++ b/solution.py
@@ -58,16 +58,19 @@
 
 
 def head_kernel(scale_ref, q_ref, k_ref, v_ref, o_ref):
-    head = pl.program_id(0)
-    scores = lax.dot_general(
-        q_ref[...], k_ref[...], (((1,), (1,)), ((), ())), preferred_element_type=jnp.float32
-    )
-    scores = scores * scale_ref[head] * HEAD_DIM ** (-0.5)
-    biggest = jnp.max(scores, axis=1, keepdims=True)
-    expon = jnp.exp(scores - biggest)
-    total = jnp.sum(expon, axis=1, keepdims=True)
-    context = jnp.dot(expon.astype(jnp.bfloat16), v_ref[...], preferred_element_type=jnp.float32)
-    o_ref[...] = (context / total).astype(o_ref.dtype)
+    pair = pl.program_id(0)
+    for inner in range(2):
+        head = pair * 2 + inner
+        cols = slice(inner * HEAD_DIM, (inner + 1) * HEAD_DIM)
+        scores = lax.dot_general(
+            q_ref[:, cols], k_ref[...], (((1,), (1,)), ((), ())), preferred_element_type=jnp.float32
+        )
+        scores = scores * scale_ref[head] * HEAD_DIM ** (-0.5)
+        biggest = jnp.max(scores, axis=1, keepdims=True)
+        expon = jnp.exp(scores - biggest)
+        total = jnp.sum(expon, axis=1, keepdims=True)
+        context = jnp.dot(expon.astype(jnp.bfloat16), v_ref[...], preferred_element_type=jnp.float32)
+        o_ref[:, cols] = (context / total).astype(o_ref.dtype)
 
 
 def attend(queries, key_block, scales):
@@ -77,14 +80,14 @@
     flops = 4 * head_count * row_count * key_count * HEAD_DIM
     return pl.pallas_call(
         head_kernel,
-        grid=(head_count,),
+        grid=(head_count // 2,),
         in_specs=[
             pl.BlockSpec(memory_space=pltpu.SMEM),
-            pl.BlockSpec((row_count, HEAD_DIM), lambda h: (0, h)),
+            pl.BlockSpec((row_count, 2 * HEAD_DIM), lambda h: (0, h)),
             pl.BlockSpec((key_count, HEAD_DIM), lambda h: (0, 0)),
             pl.BlockSpec((key_count, HEAD_DIM), lambda h: (0, 1)),
         ],
-        out_specs=pl.BlockSpec((row_count, HEAD_DIM), lambda h: (0, h)),
+        out_specs=pl.BlockSpec((row_count, 2 * HEAD_DIM), lambda h: (0, h)),
         out_shape=jax.ShapeDtypeStruct((row_count, head_count * HEAD_DIM), jnp.bfloat16),
         cost_estimate=pl.CostEstimate(
             flops=flops,

time: 191 us -> 189 us (0.990)
  no operation moved by 1% of the time
where the time goes in v13:
time: 189 us; the launch traced here: 188 us
  waiting for transfers between devices  61.3 us (32%)
  starting transfers between devices  42.3 us (22%)
  local copies, waits for them, and re-layouts  21.9 us (12%)
  blocking collectives  15.1 us (8%)
  between operations  14.3 us (8%)
  Pallas kernels  13.4 us (7%)
  matrix products  12.3 us (7%)
  other arithmetic  7.83 us (4%)
    ppermute x12, waiting for transfers between devices, ring(): ahead = lax.ppermute(ahead, axis, up)  35.5 us
    ppermute x12, starting transfers between devices, ring(): ahead = lax.ppermute(ahead, axis, up)  25.5 us
    all_gather x1, blocking collectives, shards(): kv_plane = lax.all_gather(keyvals, 'sx', axis=0, tiled=True)  15.1 us
    pallas_call x1, Pallas kernels, attend(): pl.pallas_call(head_kernel, grid=(head_count // 2,), in_specs=[pl.BlockSp...  13.4 us
    unnamed x48, local copies, waits for them, and re-layouts  13 us
    all_gather x1, waiting for transfers between devices, shards(): key_block = lax.all_gather(kv_plane, 'sz', axis=0, tiled=True)  12.7 us
    all_to_all x1, starting transfers between devices, shards(): received = lax.all_to_all(pieces, 'sx', 0, 0, tiled=False)  9.02 us
    dot_general x5, matrix products, convolve(): jnp.dot(padded[kernel_tap:kernel_tap + row_count], kernel[kernel_tap], pr...  8.06 us
  transfers between devices with their start and end apart: 27, of which 14 were waited for; matrix products, arithmetic and copies ran while one was open for 17% of the time, Pallas kernels for 0%

profile of v13, /device:TPU:1, one launch (start us, length us, event | category | flops | bytes accessed | tf_op | source)
XLA Modules:
  0.0 188.4 jit_solution(7205471060718979581)
XLA Ops:
  8.5 2.4 %fusion.28 = bf16[192,1408]{1,0:T(8,128)(2,1)} fusion(bf16[192,1408]{1,0:T(8,128)(2,1)} %param.9, f32[1408]{0:T(1024)} %param.10, f32[192]{0:T(256)S(1)} %add_rsqrt_fusion), kind=kLoop, calls=%fused_computation.25 | loop fusion | flops 3244032 | bytes 1087744 | tf_op jit(solution)/shard_map/convert_element_type | solution.py:119
  12.7 6.5 %collective-permute-start.2 = (bf16[216,256]{1,0:T(8,128)(2,1)S(1)}, bf16[216,256]{1,0:T(8,128)(2,1)S(1)}, u32[]{:S(2)}, u32[]{:S(2)}) collective-permute-start(bf16[216,256]{1,0:T(8,128)(2,1)S(1)} %constant_dynamic-update-slice_fusion), channel_id=1, source_target_pairs={{0,56},{8,0},{16,8},{24,16},{32,24},{40,32},{48,40},{56,48},{1,57}... | collective-permute-start | bytes 331784 | tf_op jit(solution)/shard_map/ppermute | solution.py:49
  19.2 2.7 %collective-permute-start.1 = (bf16[5,1408,24]{1,2,0:T(8,128)(2,1)}, bf16[5,1408,24]{1,2,0:T(8,128)(2,1)S(1)}, u32[]{:S(2)}, u32[]{:S(2)}) collective-permute-start(bf16[5,1408,24]{1,2,0:T(8,128)(2,1)} %param.11), channel_id=1, source_target_pairs={{0,56},{8,0},{16,8},{24,16},{32,24},{40,32},{48,40},{56,48},{1,57}... | collective-permute-start | bytes 1013768 | tf_op jit(solution)/shard_map/ppermute | solution.py:49
  24.5 3.7 %collective-permute-done.1 = bf16[5,1408,24]{1,2,0:T(8,128)(2,1)S(1)} collective-permute-done((bf16[5,1408,24]{1,2,0:T(8,128)(2,1)}, bf16[5,1408,24]{1,2,0:T(8,128)(2,1)S(1)}, u32[]{:S(2)}, u32[]{:S(2)}) %collective-permute-start.1) | collective-permute-done | bytes 337952 | tf_op jit(solution)/shard_map/ppermute | solution.py:49
  28.2 3.0 %collective-permute-done.3 = bf16[5,1408,24]{1,2,0:T(8,128)(2,1)S(1)} collective-permute-done((bf16[5,1408,24]{1,2,0:T(8,128)(2,1)}, bf16[5,1408,24]{1,2,0:T(8,128)(2,1)S(1)}, u32[]{:S(2)}, u32[]{:S(2)}) %collective-permute-start.3) | collective-permute-done | bytes 337952 | tf_op jit(solution)/shard_map/ppermute | solution.py:51
  34.9 5.9 %collective-permute-done.6 = bf16[216,256]{1,0:T(8,128)(2,1)S(1)} collective-permute-done((bf16[216,256]{1,0:T(8,128)(2,1)S(1)}, bf16[216,256]{1,0:T(8,128)(2,1)S(1)}, u32[]{:S(2)}, u32[]{:S(2)}) %collective-permute-start.6) | collective-permute-done | bytes 110624 | tf_op jit(solution)/shard_map/ppermute | solution.py:49
  42.4 2.7 %collective-permute-start.9 = (bf16[5,1408,24]{1,2,0:T(8,128)(2,1)S(1)}, bf16[5,1408,24]{1,2,0:T(8,128)(2,1)S(1)}, u32[]{:S(2)}, u32[]{:S(2)}) collective-permute-start(bf16[5,1408,24]{1,2,0:T(8,128)(2,1)S(1)} %collective-permute-done.5), channel_id=1, source_target_pairs={{0,56},{8,0},{16,8},{24,16},{32,24},{40,32},{48,40},{56,48},{1,57}... | collective-permute-start | bytes 1013768 | tf_op jit(solution)/shard_map/ppermute | solution.py:49
  47.3 4.0 %collective-permute-done.10 = bf16[216,256]{1,0:T(8,128)(2,1)S(1)} collective-permute-done((bf16[216,256]{1,0:T(8,128)(2,1)S(1)}, bf16[216,256]{1,0:T(8,128)(2,1)S(1)}, u32[]{:S(2)}, u32[]{:S(2)}) %collective-permute-start.10) | collective-permute-done | bytes 110624 | tf_op jit(solution)/shard_map/ppermute | solution.py:49
  52.3 2.5 %collective-permute-start.13 = (bf16[5,1408,24]{1,2,0:T(8,128)(2,1)S(1)}, bf16[5,1408,24]{1,2,0:T(8,128)(2,1)S(1)}, u32[]{:S(2)}, u32[]{:S(2)}) collective-permute-start(bf16[5,1408,24]{1,2,0:T(8,128)(2,1)S(1)} %collective-permute-done.9), channel_id=1, source_target_pairs={{0,56},{8,0},{16,8},{24,16},{32,24},{40,32},{48,40},{56,48},{1,57}... | collective-permute-start | bytes 1013768 | tf_op jit(solution)/shard_map/ppermute | solution.py:49
  55.1 5.1 %collective-permute-done.14 = bf16[216,256]{1,0:T(8,128)(2,1)S(1)} collective-permute-done((bf16[216,256]{1,0:T(8,128)(2,1)S(1)}, bf16[216,256]{1,0:T(8,128)(2,1)S(1)}, u32[]{:S(2)}, u32[]{:S(2)}) %collective-permute-start.14) | collective-permute-done | bytes 110624 | tf_op jit(solution)/shard_map/ppermute | solution.py:49
  69.5 2.5 %constant_dynamic-update-slice_fusion.27 = bf16[1538,1408]{1,0:T(8,128)(2,1)S(1)} fusion(bf16[1536,1408]{1,0:T(8,128)(2,1)} %all-gather.4.cloned.1.call-done), kind=kLoop, calls=%fused_computation.77 | loop fusion | bytes 8650752
  81.0 2.2 %reduce_max.9 = bf16[768,192]{1,0:T(8,128)(2,1)S(1)} reduce(bf16[768,2,192]{2,1,0:T(2,128)(2,1)S(1)} %reshape.75, bf16[]{:T(256)} %constant.291), dimensions={1}, to_apply=%region_1.2 | reduce | flops 147456 | bytes 884738 | tf_op jit(solution)/shard_map/reduce_max | solution.py:29
  84.7 9.0 %all-to-all-start = ((bf16[8,96,192]{1,2,0:T(8,128)(2,1)}), bf16[8,96,192]{1,2,0:T(8,128)(2,1)S(1)}, u32[]{:S(2)}, u32[]{:S(2)}) async-start(bf16[8,96,192]{1,2,0:T(8,128)(2,1)} %copy.33), calls=%async_computation | async-start | bytes 786432 | tf_op jit(solution)/shard_map/all_to_all | solution.py:151
  94.2 7.2 %all-to-all-done = bf16[8,96,192]{1,2,0:T(8,128)(2,1)S(1)} async-done(((bf16[8,96,192]{1,2,0:T(8,128)(2,1)}), bf16[8,96,192]{1,2,0:T(8,128)(2,1)S(1)}, u32[]{:S(2)}, u32[]{:S(2)}) %all-to-all-start) | async-done | bytes 294944 | tf_op jit(solution)/shard_map/all_to_all | solution.py:151
  102.3 2.8 %convolution_convert_fusion.1 = bf16[96,1280]{1,0:T(8,128)(2,1)S(1)} fusion(bf16[96,1536]{0,1:T(8,128)(2,1)S(1)} %bitcast.124, bf16[1536,1280]{1,0:T(8,128)(2,1)} %all-gather.6.cloned.1.call-done), kind=kOutput, calls=%fused_computation.17 | convolution fusion | flops 377610240 | bytes 4472832 | tf_op jit(solution)/shard_map/dot_general | solution.py:156
  105.1 15.1 %all_gather.14 = bf16[768,256]{1,0:T(8,128)(2,1)} all-gather(bf16[96,256]{1,0:T(8,128)(2,1)S(1)} %slice.214), channel_id=1, replica_groups=mesh['dp'=4,'sz'=8,'sx'=8] {'sx'}, dimensions={0}, use_global_device_ids=true | all-gather | bytes 442368 | tf_op jit(solution)/shard_map/all_gather | solution.py:159
  122.0 5.8 %collective-permute-done.16 = bf16[128,1536]{1,0:T(8,128)(2,1)S(1)} collective-permute-done((bf16[128,1536]{1,0:T(8,128)(2,1)S(1)}, bf16[128,1536]{1,0:T(8,128)(2,1)S(1)}, u32[]{:S(2)}, u32[]{:S(2)}) %collective-permute-start.16) | collective-permute-done | bytes 393248 | tf_op jit(solution)/shard_map/ppermute | solution.py:49
  131.6 3.8 %collective-permute-done.18 = bf16[128,1536]{1,0:T(8,128)(2,1)} collective-permute-done((bf16[128,1536]{1,0:T(8,128)(2,1)S(1)}, bf16[128,1536]{1,0:T(8,128)(2,1)}, u32[]{:S(2)}, u32[]{:S(2)}) %collective-permute-start.18) | collective-permute-done | bytes 393248 | tf_op jit(solution)/shard_map/ppermute | solution.py:49
  135.4 3.1 %collective-permute-start.20 = (bf16[128,1536]{1,0:T(8,128)(2,1)}, bf16[128,1536]{1,0:T(8,128)(2,1)S(1)}, u32[]{:S(2)}, u32[]{:S(2)}) collective-permute-start(bf16[128,1536]{1,0:T(8,128)(2,1)} %collective-permute-done.18), channel_id=1, source_target_pairs={{0,7},{1,0},{2,1},{3,2},{4,3},{5,4},{6,5},{7,6},{8,15},{9,8},{10,9... | collective-permute-start | bytes 1179656 | tf_op jit(solution)/shard_map/ppermute | solution.py:49
  139.6 3.7 %collective-permute-done.20 = bf16[128,1536]{1,0:T(8,128)(2,1)S(1)} collective-permute-done((bf16[128,1536]{1,0:T(8,128)(2,1)}, bf16[128,1536]{1,0:T(8,128)(2,1)S(1)}, u32[]{:S(2)}, u32[]{:S(2)}) %collective-permute-start.20) | collective-permute-done | bytes 393248 | tf_op jit(solution)/shard_map/ppermute | solution.py:49
  143.5 3.6 %collective-permute-start.22 = (bf16[128,1536]{1,0:T(8,128)(2,1)S(1)}, bf16[128,1536]{1,0:T(8,128)(2,1)S(1)}, u32[]{:S(2)}, u32[]{:S(2)}) collective-permute-start(bf16[128,1536]{1,0:T(8,128)(2,1)S(1)} %collective-permute-done.20), channel_id=1, source_target_pairs={{0,7},{1,0},{2,1},{3,2},{4,3},{5,4},{6,5},{7,6},{8,15},{9,8},{10,9... | collective-permute-start | bytes 1179656 | tf_op jit(solution)/shard_map/ppermute | solution.py:49
  148.2 3.6 %collective-permute-done.22 = bf16[128,1536]{1,0:T(8,128)(2,1)S(1)} collective-permute-done((bf16[128,1536]{1,0:T(8,128)(2,1)S(1)}, bf16[128,1536]{1,0:T(8,128)(2,1)S(1)}, u32[]{:S(2)}, u32[]{:S(2)}) %collective-permute-start.22) | collective-permute-done | bytes 393248 | tf_op jit(solution)/shard_map/ppermute | solution.py:49
  152.9 12.7 %all-gather.8.cloned.1.call-done.k_ref.v_ref = bf16[6144,256]{1,0:T(8,128)(2,1)} async-done(((bf16[768,256]{1,0:T(8,128)(2,1)}), bf16[6144,256]{1,0:T(8,128)(2,1)}) %all-gather.8.cloned.1.call-update) | async-done | bytes 3145744 | tf_op jit(solution)/shard_map/all_gather | solution.py:161
  165.6 13.4 %shard_map.104 = bf16[96,1024]{1,0:T(8,128)(2,1)} custom-call(f32[8]{0:T(128)} %scale_ref.1, bf16[96,1024]{1,0:T(8,128)(2,1)} %slice.213.q_ref, bf16[6144,256]{1,0:T(8,128)(2,1)} %all-gather.8.cloned.1.call-done.k_ref.v_ref, bf16[6144,256]{1,0:T(8,128)(2,1)} %all-gather.8.cloned.1.call-done.k_ref.v_ref), custom_call_target="tpu_custom_call" | custom-call | flops 2415919104 | bytes 3538944 | tf_op jit(solution)/shard_map/pallas_call | solution.py:81
  (130 shorter events, 47.1 us)
Async XLA Ops:
  7.2 58.0 %all-gather.4.cloned.1.call-start = ((), (), s32[]{:S(2)}) async-start(), calls=%async_computation.1 | async-start | bytes 4866048 | tf_op jit(solution)/shard_map/all_gather | solution.py:120
  10.9 91.4 %all-gather.6.cloned.1.call-start = ((), (), s32[]{:S(2)}) async-start(), calls=%async_computation.2 | async-start | bytes 4423680 | tf_op jit(solution)/shard_map/all_gather | solution.py:134
  12.7 11.8 %collective-permute-start.2 = (bf16[216,256]{1,0:T(8,128)(2,1)S(1)}, bf16[216,256]{1,0:T(8,128)(2,1)S(1)}, u32[]{:S(2)}, u32[]{:S(2)}) collective-permute-start(bf16[216,256]{1,0:T(8,128)(2,1)S(1)} %constant_dynamic-update-slice_fusion), channel_id=1, source_target_pairs={{0,56},{8,0},{16,8},{24,16},{32,24},{40,32},{48,40},{56,48},{1,57}... | collective-permute-start | bytes 331784 | tf_op jit(solution)/shard_map/ppermute | solution.py:49
  19.2 9.0 %collective-permute-start.1 = (bf16[5,1408,24]{1,2,0:T(8,128)(2,1)}, bf16[5,1408,24]{1,2,0:T(8,128)(2,1)S(1)}, u32[]{:S(2)}, u32[]{:S(2)}) collective-permute-start(bf16[5,1408,24]{1,2,0:T(8,128)(2,1)} %param.11), channel_id=1, source_target_pairs={{0,56},{8,0},{16,8},{24,16},{32,24},{40,32},{48,40},{56,48},{1,57}... | collective-permute-start | bytes 1013768 | tf_op jit(solution)/shard_map/ppermute | solution.py:49
  21.9 9.4 %collective-permute-start.3 = (bf16[5,1408,24]{1,2,0:T(8,128)(2,1)}, bf16[5,1408,24]{1,2,0:T(8,128)(2,1)S(1)}, u32[]{:S(2)}, u32[]{:S(2)}) collective-permute-start(bf16[5,1408,24]{1,2,0:T(8,128)(2,1)} %param.11), channel_id=1, source_target_pairs={{0,8},{8,16},{16,24},{24,32},{32,40},{40,48},{48,56},{56,0},{1,9},... | collective-permute-start | bytes 1013768 | tf_op jit(solution)/shard_map/ppermute | solution.py:51
  31.3 11.1 %collective-permute-start.5 = (bf16[5,1408,24]{1,2,0:T(8,128)(2,1)S(1)}, bf16[5,1408,24]{1,2,0:T(8,128)(2,1)S(1)}, u32[]{:S(2)}, u32[]{:S(2)}) collective-permute-start(bf16[5,1408,24]{1,2,0:T(8,128)(2,1)S(1)} %collective-permute-done.1), channel_id=1, source_target_pairs={{0,56},{8,0},{16,8},{24,16},{32,24},{40,32},{48,40},{56,48},{1,57}... | collective-permute-start | bytes 1013768 | tf_op jit(solution)/shard_map/ppermute | solution.py:49
  31.5 10.8 %collective-permute-start.7 = (bf16[5,1408,24]{1,2,0:T(8,128)(2,1)S(1)}, bf16[5,1408,24]{1,2,0:T(8,128)(2,1)S(1)}, u32[]{:S(2)}, u32[]{:S(2)}) collective-permute-start(bf16[5,1408,24]{1,2,0:T(8,128)(2,1)S(1)} %collective-permute-done.3), channel_id=1, source_target_pairs={{0,8},{8,16},{16,24},{24,32},{32,40},{40,48},{48,56},{56,0},{1,9},... | collective-permute-start | bytes 1013768 | tf_op jit(solution)/shard_map/ppermute | solution.py:51
  32.7 8.1 %collective-permute-start.6 = (bf16[216,256]{1,0:T(8,128)(2,1)S(1)}, bf16[216,256]{1,0:T(8,128)(2,1)S(1)}, u32[]{:S(2)}, u32[]{:S(2)}) collective-permute-start(bf16[216,256]{1,0:T(8,128)(2,1)S(1)} %collective-permute-done.2), channel_id=1, source_target_pairs={{0,56},{8,0},{16,8},{24,16},{32,24},{40,32},{48,40},{56,48},{1,57}... | collective-permute-start | bytes 331784 | tf_op jit(solution)/shard_map/ppermute | solution.py:49
  34.2 8.1 %collective-permute-start.8 = (bf16[216,256]{1,0:T(8,128)(2,1)S(1)}, bf16[216,256]{1,0:T(8,128)(2,1)S(1)}, u32[]{:S(2)}, u32[]{:S(2)}) collective-permute-start(bf16[216,256]{1,0:T(8,128)(2,1)S(1)} %collective-permute-done.4), channel_id=1, source_target_pairs={{0,8},{8,16},{16,24},{24,32},{32,40},{40,48},{48,56},{56,0},{1,9},... | collective-permute-start | bytes 331784 | tf_op jit(solution)/shard_map/ppermute | solution.py:51
  42.4 9.9 %collective-permute-start.11 = (bf16[5,1408,24]{1,2,0:T(8,128)(2,1)S(1)}, bf16[5,1408,24]{1,2,0:T(8,128)(2,1)S(1)}, u32[]{:S(2)}, u32[]{:S(2)}) collective-permute-start(bf16[5,1408,24]{1,2,0:T(8,128)(2,1)S(1)} %collective-permute-done.7), channel_id=1, source_target_pairs={{0,8},{8,16},{16,24},{24,32},{32,40},{40,48},{48,56},{56,0},{1,9},... | collective-permute-start | bytes 1013768 | tf_op jit(solution)/shard_map/ppermute | solution.py:51
  42.4 9.9 %collective-permute-start.9 = (bf16[5,1408,24]{1,2,0:T(8,128)(2,1)S(1)}, bf16[5,1408,24]{1,2,0:T(8,128)(2,1)S(1)}, u32[]{:S(2)}, u32[]{:S(2)}) collective-permute-start(bf16[5,1408,24]{1,2,0:T(8,128)(2,1)S(1)} %collective-permute-done.5), channel_id=1, source_target_pairs={{0,56},{8,0},{16,8},{24,16},{32,24},{40,32},{48,40},{56,48},{1,57}... | collective-permute-start | bytes 1013768 | tf_op jit(solution)/shard_map/ppermute | solution.py:49
  45.0 6.3 %collective-permute-start.10 = (bf16[216,256]{1,0:T(8,128)(2,1)S(1)}, bf16[216,256]{1,0:T(8,128)(2,1)S(1)}, u32[]{:S(2)}, u32[]{:S(2)}) collective-permute-start(bf16[216,256]{1,0:T(8,128)(2,1)S(1)} %collective-permute-done.6), channel_id=1, source_target_pairs={{0,56},{8,0},{16,8},{24,16},{32,24},{40,32},{48,40},{56,48},{1,57}... | collective-permute-start | bytes 331784 | tf_op jit(solution)/shard_map/ppermute | solution.py:49
  45.1 7.2 %collective-permute-start.12 = (bf16[216,256]{1,0:T(8,128)(2,1)S(1)}, bf16[216,256]{1,0:T(8,128)(2,1)S(1)}, u32[]{:S(2)}, u32[]{:S(2)}) collective-permute-start(bf16[216,256]{1,0:T(8,128)(2,1)S(1)} %collective-permute-done.8), channel_id=1, source_target_pairs={{0,8},{8,16},{16,24},{24,32},{32,40},{40,48},{48,56},{56,0},{1,9},... | collective-permute-start | bytes 331784 | tf_op jit(solution)/shard_map/ppermute | solution.py:51
  52.3 7.9 %collective-permute-start.13 = (bf16[5,1408,24]{1,2,0:T(8,128)(2,1)S(1)}, bf16[5,1408,24]{1,2,0:T(8,128)(2,1)S(1)}, u32[]{:S(2)}, u32[]{:S(2)}) collective-permute-start(bf16[5,1408,24]{1,2,0:T(8,128)(2,1)S(1)} %collective-permute-done.9), channel_id=1, source_target_pairs={{0,56},{8,0},{16,8},{24,16},{32,24},{40,32},{48,40},{56,48},{1,57}... | collective-permute-start | bytes 1013768 | tf_op jit(solution)/shard_map/ppermute | solution.py:49
  66.0 7.8 %collective-permute-start = (bf16[2,1408]{1,0:T(2,128)(2,1)S(1)}, bf16[2,1408]{1,0:T(2,128)(2,1)S(1)}, u32[]{:S(2)}, u32[]{:S(2)}) collective-permute-start(bf16[2,1408]{1,0:T(2,128)(2,1)S(1)} %get-tuple-element.56), channel_id=1, source_target_pairs={{0,8},{8,16},{16,24},{24,32},{32,40},{40,48},{48,56},{1,9},{9,17},... | collective-permute-start | bytes 16904 | tf_op jit(solution)/shard_map/ppermute | solution.py:139
  68.0 5.7 %collective-permute-start.15 = (bf16[2,1408]{1,0:T(2,128)(2,1)S(1)}, bf16[2,1408]{1,0:T(2,128)(2,1)S(1)}, u32[]{:S(2)}, u32[]{:S(2)}) collective-permute-start(bf16[2,1408]{1,0:T(2,128)(2,1)S(1)} %get-tuple-element.57), channel_id=1, source_target_pairs={{8,0},{16,8},{24,16},{32,24},{40,32},{48,40},{56,48},{9,1},{17,9},... | collective-permute-start | bytes 16904 | tf_op jit(solution)/shard_map/ppermute | solution.py:140
  84.7 16.7 %all-to-all-start = ((bf16[8,96,192]{1,2,0:T(8,128)(2,1)}), bf16[8,96,192]{1,2,0:T(8,128)(2,1)S(1)}, u32[]{:S(2)}, u32[]{:S(2)}) async-start(bf16[8,96,192]{1,2,0:T(8,128)(2,1)} %copy.33), calls=%async_computation | async-start | bytes 786432 | tf_op jit(solution)/shard_map/all_to_all | solution.py:151
  93.7 71.9 %all-gather.8.cloned.1.call-start = ((), (), s32[]{:S(2)}) async-start(), calls=%async_computation.3 | async-start | bytes 3538944 | tf_op jit(solution)/shard_map/all_gather | solution.py:161
  120.2 7.5 %collective-permute-start.16 = (bf16[128,1536]{1,0:T(8,128)(2,1)S(1)}, bf16[128,1536]{1,0:T(8,128)(2,1)S(1)}, u32[]{:S(2)}, u32[]{:S(2)}) collective-permute-start(bf16[128,1536]{1,0:T(8,128)(2,1)S(1)} %reshape.80), channel_id=1, source_target_pairs={{0,7},{1,0},{2,1},{3,2},{4,3},{5,4},{6,5},{7,6},{8,15},{9,8},{10,9... | collective-permute-start | bytes 1179656 | tf_op jit(solution)/shard_map/ppermute | solution.py:49
  120.4 7.3 %collective-permute-start.17 = (bf16[128,1536]{1,0:T(8,128)(2,1)S(1)}, bf16[128,1536]{1,0:T(8,128)(2,1)S(1)}, u32[]{:S(2)}, u32[]{:S(2)}) collective-permute-start(bf16[128,1536]{1,0:T(8,128)(2,1)S(1)} %reshape.80), channel_id=1, source_target_pairs={{0,1},{1,2},{2,3},{3,4},{4,5},{5,6},{6,7},{7,0},{8,9},{9,10},{10,1... | collective-permute-start | bytes 1179656 | tf_op jit(solution)/shard_map/ppermute | solution.py:51
  127.8 7.6 %collective-permute-start.18 = (bf16[128,1536]{1,0:T(8,128)(2,1)S(1)}, bf16[128,1536]{1,0:T(8,128)(2,1)}, u32[]{:S(2)}, u32[]{:S(2)}) collective-permute-start(bf16[128,1536]{1,0:T(8,128)(2,1)S(1)} %collective-permute-done.16), channel_id=1, source_target_pairs={{0,7},{1,0},{2,1},{3,2},{4,3},{5,4},{6,5},{7,6},{8,15},{9,8},{10,9... | collective-permute-start | bytes 1179656 | tf_op jit(solution)/shard_map/ppermute | solution.py:49
  130.0 5.4 %collective-permute-start.19 = (bf16[128,1536]{1,0:T(8,128)(2,1)S(1)}, bf16[128,1536]{1,0:T(8,128)(2,1)}, u32[]{:S(2)}, u32[]{:S(2)}) collective-permute-start(bf16[128,1536]{1,0:T(8,128)(2,1)S(1)} %collective-permute-done.17), channel_id=1, source_target_pairs={{0,1},{1,2},{2,3},{3,4},{4,5},{5,6},{6,7},{7,0},{8,9},{9,10},{10,1... | collective-permute-start | bytes 1179656 | tf_op jit(solution)/shard_map/ppermute | solution.py:51
  135.4 8.0 %collective-permute-start.20 = (bf16[128,1536]{1,0:T(8,128)(2,1)}, bf16[128,1536]{1,0:T(8,128)(2,1)S(1)}, u32[]{:S(2)}, u32[]{:S(2)}) collective-permute-start(bf16[128,1536]{1,0:T(8,128)(2,1)} %collective-permute-done.18), channel_id=1, source_target_pairs={{0,7},{1,0},{2,1},{3,2},{4,3},{5,4},{6,5},{7,6},{8,15},{9,8},{10,9... | collective-permute-start | bytes 1179656 | tf_op jit(solution)/shard_map/ppermute | solution.py:49
  143.5 8.2 %collective-permute-start.22 = (bf16[128,1536]{1,0:T(8,128)(2,1)S(1)}, bf16[128,1536]{1,0:T(8,128)(2,1)S(1)}, u32[]{:S(2)}, u32[]{:S(2)}) collective-permute-start(bf16[128,1536]{1,0:T(8,128)(2,1)S(1)} %collective-permute-done.20), channel_id=1, source_target_pairs={{0,7},{1,0},{2,1},{3,2},{4,3},{5,4},{6,5},{7,6},{8,15},{9,8},{10,9... | collective-permute-start | bytes 1179656 | tf_op jit(solution)/shard_map/ppermute | solution.py:49
  (15 other events, 96.7 us)
Sparse Core Ops, SparseCore 0:
  11.0 39.2 all-gather.3
  61.6 37.5 all-gather.5
  120.4 45.2 all-gather.7

commit v14 on v13

--- a/solution.py
+++ b/solution.py
@@ -65,7 +65,7 @@
         scores = lax.dot_general(
             q_ref[:, cols], k_ref[...], (((1,), (1,)), ((), ())), preferred_element_type=jnp.float32
         )
-        scores = scores * scale_ref[head] * HEAD_DIM ** (-0.5)
+        scores = scores * (scale_ref[head] * HEAD_DIM ** (-0.5))
         biggest = jnp.max(scores, axis=1, keepdims=True)
         expon = jnp.exp(scores - biggest)
         total = jnp.sum(expon, axis=1, keepdims=True)

time: 189 us -> 189 us (level)
  no operation moved by 1% of the time
where the time goes in v14:
time: 189 us; the launch traced here: 188 us
  waiting for transfers between devices  61.3 us (32%)
  starting transfers between devices  42.3 us (22%)
  local copies, waits for them, and re-layouts  21.9 us (12%)
  blocking collectives  15.1 us (8%)
  between operations  14.3 us (8%)
  Pallas kernels  12.8 us (7%)
  matrix products  12.2 us (6%)
  other arithmetic  7.83 us (4%)
    ppermute x12, waiting for transfers between devices, ring(): ahead = lax.ppermute(ahead, axis, up)  35.5 us
    ppermute x12, starting transfers between devices, ring(): ahead = lax.ppermute(ahead, axis, up)  25.5 us
    all_gather x1, blocking collectives, shards(): kv_plane = lax.all_gather(keyvals, 'sx', axis=0, tiled=True)  15.1 us
    unnamed x48, local copies, waits for them, and re-layouts  13 us
    pallas_call x1, Pallas kernels, attend(): pl.pallas_call(head_kernel, grid=(head_count // 2,), in_specs=[pl.BlockSp...  12.8 us
    all_gather x1, waiting for transfers between devices, shards(): key_block = lax.all_gather(kv_plane, 'sz', axis=0, tiled=True)  12.7 us
    all_to_all x1, starting transfers between devices, shards(): received = lax.all_to_all(pieces, 'sx', 0, 0, tiled=False)  9.02 us
    dot_general x5, matrix products, convolve(): jnp.dot(padded[kernel_tap:kernel_tap + row_count], kernel[kernel_tap], pr...  8.06 us
  transfers between devices with their start and end apart: 27, of which 14 were waited for; matrix products, arithmetic and copies ran while one was open for 17% of the time, Pallas kernels for 0%

profile of v14, /device:TPU:1, one launch (start us, length us, event | category | flops | bytes accessed | tf_op | source)
XLA Modules:
  0.0 187.8 jit_solution(11581291508107848492)
XLA Ops:
  8.5 2.4 %fusion.28 = bf16[192,1408]{1,0:T(8,128)(2,1)} fusion(bf16[192,1408]{1,0:T(8,128)(2,1)} %param.9, f32[1408]{0:T(1024)} %param.10, f32[192]{0:T(256)S(1)} %add_rsqrt_fusion), kind=kLoop, calls=%fused_computation.25 | loop fusion | flops 3244032 | bytes 1087744 | tf_op jit(solution)/shard_map/convert_element_type | solution.py:119
  12.7 6.5 %collective-permute-start.2 = (bf16[216,256]{1,0:T(8,128)(2,1)S(1)}, bf16[216,256]{1,0:T(8,128)(2,1)S(1)}, u32[]{:S(2)}, u32[]{:S(2)}) collective-permute-start(bf16[216,256]{1,0:T(8,128)(2,1)S(1)} %constant_dynamic-update-slice_fusion), channel_id=1, source_target_pairs={{0,56},{8,0},{16,8},{24,16},{32,24},{40,32},{48,40},{56,48},{1,57}... | collective-permute-start | bytes 331784 | tf_op jit(solution)/shard_map/ppermute | solution.py:49
  19.2 2.7 %collective-permute-start.1 = (bf16[5,1408,24]{1,2,0:T(8,128)(2,1)}, bf16[5,1408,24]{1,2,0:T(8,128)(2,1)S(1)}, u32[]{:S(2)}, u32[]{:S(2)}) collective-permute-start(bf16[5,1408,24]{1,2,0:T(8,128)(2,1)} %param.11), channel_id=1, source_target_pairs={{0,56},{8,0},{16,8},{24,16},{32,24},{40,32},{48,40},{56,48},{1,57}... | collective-permute-start | bytes 1013768 | tf_op jit(solution)/shard_map/ppermute | solution.py:49
  24.5 3.7 %collective-permute-done.1 = bf16[5,1408,24]{1,2,0:T(8,128)(2,1)S(1)} collective-permute-done((bf16[5,1408,24]{1,2,0:T(8,128)(2,1)}, bf16[5,1408,24]{1,2,0:T(8,128)(2,1)S(1)}, u32[]{:S(2)}, u32[]{:S(2)}) %collective-permute-start.1) | collective-permute-done | bytes 337952 | tf_op jit(solution)/shard_map/ppermute | solution.py:49
  28.2 3.0 %collective-permute-done.3 = bf16[5,1408,24]{1,2,0:T(8,128)(2,1)S(1)} collective-permute-done((bf16[5,1408,24]{1,2,0:T(8,128)(2,1)}, bf16[5,1408,24]{1,2,0:T(8,128)(2,1)S(1)}, u32[]{:S(2)}, u32[]{:S(2)}) %collective-permute-start.3) | collective-permute-done | bytes 337952 | tf_op jit(solution)/shard_map/ppermute | solution.py:51
  34.9 5.9 %collective-permute-done.6 = bf16[216,256]{1,0:T(8,128)(2,1)S(1)} collective-permute-done((bf16[216,256]{1,0:T(8,128)(2,1)S(1)}, bf16[216,256]{1,0:T(8,128)(2,1)S(1)}, u32[]{:S(2)}, u32[]{:S(2)}) %collective-permute-start.6) | collective-permute-done | bytes 110624 | tf_op jit(solution)/shard_map/ppermute | solution.py:49
  42.4 2.7 %collective-permute-start.9 = (bf16[5,1408,24]{1,2,0:T(8,128)(2,1)S(1)}, bf16[5,1408,24]{1,2,0:T(8,128)(2,1)S(1)}, u32[]{:S(2)}, u32[]{:S(2)}) collective-permute-start(bf16[5,1408,24]{1,2,0:T(8,128)(2,1)S(1)} %collective-permute-done.5), channel_id=1, source_target_pairs={{0,56},{8,0},{16,8},{24,16},{32,24},{40,32},{48,40},{56,48},{1,57}... | collective-permute-start | bytes 1013768 | tf_op jit(solution)/shard_map/ppermute | solution.py:49
  47.3 4.0 %collective-permute-done.10 = bf16[216,256]{1,0:T(8,128)(2,1)S(1)} collective-permute-done((bf16[216,256]{1,0:T(8,128)(2,1)S(1)}, bf16[216,256]{1,0:T(8,128)(2,1)S(1)}, u32[]{:S(2)}, u32[]{:S(2)}) %collective-permute-start.10) | collective-permute-done | bytes 110624 | tf_op jit(solution)/shard_map/ppermute | solution.py:49
  52.3 2.5 %collective-permute-start.13 = (bf16[5,1408,24]{1,2,0:T(8,128)(2,1)S(1)}, bf16[5,1408,24]{1,2,0:T(8,128)(2,1)S(1)}, u32[]{:S(2)}, u32[]{:S(2)}) collective-permute-start(bf16[5,1408,24]{1,2,0:T(8,128)(2,1)S(1)} %collective-permute-done.9), channel_id=1, source_target_pairs={{0,56},{8,0},{16,8},{24,16},{32,24},{40,32},{48,40},{56,48},{1,57}... | collective-permute-start | bytes 1013768 | tf_op jit(solution)/shard_map/ppermute | solution.py:49
  55.1 5.1 %collective-permute-done.14 = bf16[216,256]{1,0:T(8,128)(2,1)S(1)} collective-permute-done((bf16[216,256]{1,0:T(8,128)(2,1)S(1)}, bf16[216,256]{1,0:T(8,128)(2,1)S(1)}, u32[]{:S(2)}, u32[]{:S(2)}) %collective-permute-start.14) | collective-permute-done | bytes 110624 | tf_op jit(solution)/shard_map/ppermute | solution.py:49
  69.5 2.5 %constant_dynamic-update-slice_fusion.27 = bf16[1538,1408]{1,0:T(8,128)(2,1)S(1)} fusion(bf16[1536,1408]{1,0:T(8,128)(2,1)} %all-gather.4.cloned.1.call-done), kind=kLoop, calls=%fused_computation.77 | loop fusion | bytes 8650752
  81.0 2.2 %reduce_max.9 = bf16[768,192]{1,0:T(8,128)(2,1)S(1)} reduce(bf16[768,2,192]{2,1,0:T(2,128)(2,1)S(1)} %reshape.75, bf16[]{:T(256)} %constant.291), dimensions={1}, to_apply=%region_1.2 | reduce | flops 147456 | bytes 884738 | tf_op jit(solution)/shard_map/reduce_max | solution.py:29
  84.7 9.0 %all-to-all-start = ((bf16[8,96,192]{1,2,0:T(8,128)(2,1)}), bf16[8,96,192]{1,2,0:T(8,128)(2,1)S(1)}, u32[]{:S(2)}, u32[]{:S(2)}) async-start(bf16[8,96,192]{1,2,0:T(8,128)(2,1)} %copy.33), calls=%async_computation | async-start | bytes 786432 | tf_op jit(solution)/shard_map/all_to_all | solution.py:151
  94.2 7.2 %all-to-all-done = bf16[8,96,192]{1,2,0:T(8,128)(2,1)S(1)} async-done(((bf16[8,96,192]{1,2,0:T(8,128)(2,1)}), bf16[8,96,192]{1,2,0:T(8,128)(2,1)S(1)}, u32[]{:S(2)}, u32[]{:S(2)}) %all-to-all-start) | async-done | bytes 294944 | tf_op jit(solution)/shard_map/all_to_all | solution.py:151
  102.3 2.8 %convolution_convert_fusion.1 = bf16[96,1280]{1,0:T(8,128)(2,1)S(1)} fusion(bf16[96,1536]{0,1:T(8,128)(2,1)S(1)} %bitcast.124, bf16[1536,1280]{1,0:T(8,128)(2,1)} %all-gather.6.cloned.1.call-done), kind=kOutput, calls=%fused_computation.17 | convolution fusion | flops 377610240 | bytes 4472832 | tf_op jit(solution)/shard_map/dot_general | solution.py:156
  105.1 15.1 %all_gather.14 = bf16[768,256]{1,0:T(8,128)(2,1)} all-gather(bf16[96,256]{1,0:T(8,128)(2,1)S(1)} %slice.214), channel_id=1, replica_groups=mesh['dp'=4,'sz'=8,'sx'=8] {'sx'}, dimensions={0}, use_global_device_ids=true | all-gather | bytes 442368 | tf_op jit(solution)/shard_map/all_gather | solution.py:159
  122.0 5.8 %collective-permute-done.16 = bf16[128,1536]{1,0:T(8,128)(2,1)S(1)} collective-permute-done((bf16[128,1536]{1,0:T(8,128)(2,1)S(1)}, bf16[128,1536]{1,0:T(8,128)(2,1)S(1)}, u32[]{:S(2)}, u32[]{:S(2)}) %collective-permute-start.16) | collective-permute-done | bytes 393248 | tf_op jit(solution)/shard_map/ppermute | solution.py:49
  131.6 3.8 %collective-permute-done.18 = bf16[128,1536]{1,0:T(8,128)(2,1)} collective-permute-done((bf16[128,1536]{1,0:T(8,128)(2,1)S(1)}, bf16[128,1536]{1,0:T(8,128)(2,1)}, u32[]{:S(2)}, u32[]{:S(2)}) %collective-permute-start.18) | collective-permute-done | bytes 393248 | tf_op jit(solution)/shard_map/ppermute | solution.py:49
  135.4 3.1 %collective-permute-start.20 = (bf16[128,1536]{1,0:T(8,128)(2,1)}, bf16[128,1536]{1,0:T(8,128)(2,1)S(1)}, u32[]{:S(2)}, u32[]{:S(2)}) collective-permute-start(bf16[128,1536]{1,0:T(8,128)(2,1)} %collective-permute-done.18), channel_id=1, source_target_pairs={{0,7},{1,0},{2,1},{3,2},{4,3},{5,4},{6,5},{7,6},{8,15},{9,8},{10,9... | collective-permute-start | bytes 1179656 | tf_op jit(solution)/shard_map/ppermute | solution.py:49
  139.6 3.7 %collective-permute-done.20 = bf16[128,1536]{1,0:T(8,128)(2,1)S(1)} collective-permute-done((bf16[128,1536]{1,0:T(8,128)(2,1)}, bf16[128,1536]{1,0:T(8,128)(2,1)S(1)}, u32[]{:S(2)}, u32[]{:S(2)}) %collective-permute-start.20) | collective-permute-done | bytes 393248 | tf_op jit(solution)/shard_map/ppermute | solution.py:49
  143.5 3.6 %collective-permute-start.22 = (bf16[128,1536]{1,0:T(8,128)(2,1)S(1)}, bf16[128,1536]{1,0:T(8,128)(2,1)S(1)}, u32[]{:S(2)}, u32[]{:S(2)}) collective-permute-start(bf16[128,1536]{1,0:T(8,128)(2,1)S(1)} %collective-permute-done.20), channel_id=1, source_target_pairs={{0,7},{1,0},{2,1},{3,2},{4,3},{5,4},{6,5},{7,6},{8,15},{9,8},{10,9... | collective-permute-start | bytes 1179656 | tf_op jit(solution)/shard_map/ppermute | solution.py:49
  148.2 3.6 %collective-permute-done.22 = bf16[128,1536]{1,0:T(8,128)(2,1)S(1)} collective-permute-done((bf16[128,1536]{1,0:T(8,128)(2,1)S(1)}, bf16[128,1536]{1,0:T(8,128)(2,1)S(1)}, u32[]{:S(2)}, u32[]{:S(2)}) %collective-permute-start.22) | collective-permute-done | bytes 393248 | tf_op jit(solution)/shard_map/ppermute | solution.py:49
  152.9 12.7 %all-gather.8.cloned.1.call-done.k_ref.v_ref = bf16[6144,256]{1,0:T(8,128)(2,1)} async-done(((bf16[768,256]{1,0:T(8,128)(2,1)}), bf16[6144,256]{1,0:T(8,128)(2,1)}) %all-gather.8.cloned.1.call-update) | async-done | bytes 3145744 | tf_op jit(solution)/shard_map/all_gather | solution.py:161
  165.6 12.8 %shard_map.104 = bf16[96,1024]{1,0:T(8,128)(2,1)} custom-call(f32[8]{0:T(128)} %scale_ref.1, bf16[96,1024]{1,0:T(8,128)(2,1)} %slice.213.q_ref, bf16[6144,256]{1,0:T(8,128)(2,1)} %all-gather.8.cloned.1.call-done.k_ref.v_ref, bf16[6144,256]{1,0:T(8,128)(2,1)} %all-gather.8.cloned.1.call-done.k_ref.v_ref), custom_call_target="tpu_custom_call" | custom-call | flops 2415919104 | bytes 3538944 | tf_op jit(solution)/shard_map/pallas_call | solution.py:81
  (130 shorter events, 47.1 us)
Async XLA Ops:
  7.2 58.0 %all-gather.4.cloned.1.call-start = ((), (), s32[]{:S(2)}) async-start(), calls=%async_computation.1 | async-start | bytes 4866048 | tf_op jit(solution)/shard_map/all_gather | solution.py:120
  10.9 91.4 %all-gather.6.cloned.1.call-start = ((), (), s32[]{:S(2)}) async-start(), calls=%async_computation.2 | async-start | bytes 4423680 | tf_op jit(solution)/shard_map/all_gather | solution.py:134
  12.7 11.8 %collective-permute-start.2 = (bf16[216,256]{1,0:T(8,128)(2,1)S(1)}, bf16[216,256]{1,0:T(8,128)(2,1)S(1)}, u32[]{:S(2)}, u32[]{:S(2)}) collective-permute-start(bf16[216,256]{1,0:T(8,128)(2,1)S(1)} %constant_dynamic-update-slice_fusion), channel_id=1, source_target_pairs={{0,56},{8,0},{16,8},{24,16},{32,24},{40,32},{48,40},{56,48},{1,57}... | collective-permute-start | bytes 331784 | tf_op jit(solution)/shard_map/ppermute | solution.py:49
  19.2 9.0 %collective-permute-start.1 = (bf16[5,1408,24]{1,2,0:T(8,128)(2,1)}, bf16[5,1408,24]{1,2,0:T(8,128)(2,1)S(1)}, u32[]{:S(2)}, u32[]{:S(2)}) collective-permute-start(bf16[5,1408,24]{1,2,0:T(8,128)(2,1)} %param.11), channel_id=1, source_target_pairs={{0,56},{8,0},{16,8},{24,16},{32,24},{40,32},{48,40},{56,48},{1,57}... | collective-permute-start | bytes 1013768 | tf_op jit(solution)/shard_map/ppermute | solution.py:49
  21.9 9.4 %collective-permute-start.3 = (bf16[5,1408,24]{1,2,0:T(8,128)(2,1)}, bf16[5,1408,24]{1,2,0:T(8,128)(2,1)S(1)}, u32[]{:S(2)}, u32[]{:S(2)}) collective-permute-start(bf16[5,1408,24]{1,2,0:T(8,128)(2,1)} %param.11), channel_id=1, source_target_pairs={{0,8},{8,16},{16,24},{24,32},{32,40},{40,48},{48,56},{56,0},{1,9},... | collective-permute-start | bytes 1013768 | tf_op jit(solution)/shard_map/ppermute | solution.py:51
  31.3 11.1 %collective-permute-start.5 = (bf16[5,1408,24]{1,2,0:T(8,128)(2,1)S(1)}, bf16[5,1408,24]{1,2,0:T(8,128)(2,1)S(1)}, u32[]{:S(2)}, u32[]{:S(2)}) collective-permute-start(bf16[5,1408,24]{1,2,0:T(8,128)(2,1)S(1)} %collective-permute-done.1), channel_id=1, source_target_pairs={{0,56},{8,0},{16,8},{24,16},{32,24},{40,32},{48,40},{56,48},{1,57}... | collective-permute-start | bytes 1013768 | tf_op jit(solution)/shard_map/ppermute | solution.py:49
  31.5 10.8 %collective-permute-start.7 = (bf16[5,1408,24]{1,2,0:T(8,128)(2,1)S(1)}, bf16[5,1408,24]{1,2,0:T(8,128)(2,1)S(1)}, u32[]{:S(2)}, u32[]{:S(2)}) collective-permute-start(bf16[5,1408,24]{1,2,0:T(8,128)(2,1)S(1)} %collective-permute-done.3), channel_id=1, source_target_pairs={{0,8},{8,16},{16,24},{24,32},{32,40},{40,48},{48,56},{56,0},{1,9},... | collective-permute-start | bytes 1013768 | tf_op jit(solution)/shard_map/ppermute | solution.py:51
  32.7 8.1 %collective-permute-start.6 = (bf16[216,256]{1,0:T(8,128)(2,1)S(1)}, bf16[216,256]{1,0:T(8,128)(2,1)S(1)}, u32[]{:S(2)}, u32[]{:S(2)}) collective-permute-start(bf16[216,256]{1,0:T(8,128)(2,1)S(1)} %collective-permute-done.2), channel_id=1, source_target_pairs={{0,56},{8,0},{16,8},{24,16},{32,24},{40,32},{48,40},{56,48},{1,57}... | collective-permute-start | bytes 331784 | tf_op jit(solution)/shard_map/ppermute | solution.py:49
  34.2 8.1 %collective-permute-start.8 = (bf16[216,256]{1,0:T(8,128)(2,1)S(1)}, bf16[216,256]{1,0:T(8,128)(2,1)S(1)}, u32[]{:S(2)}, u32[]{:S(2)}) collective-permute-start(bf16[216,256]{1,0:T(8,128)(2,1)S(1)} %collective-permute-done.4), channel_id=1, source_target_pairs={{0,8},{8,16},{16,24},{24,32},{32,40},{40,48},{48,56},{56,0},{1,9},... | collective-permute-start | bytes 331784 | tf_op jit(solution)/shard_map/ppermute | solution.py:51
  42.4 9.9 %collective-permute-start.11 = (bf16[5,1408,24]{1,2,0:T(8,128)(2,1)S(1)}, bf16[5,1408,24]{1,2,0:T(8,128)(2,1)S(1)}, u32[]{:S(2)}, u32[]{:S(2)}) collective-permute-start(bf16[5,1408,24]{1,2,0:T(8,128)(2,1)S(1)} %collective-permute-done.7), channel_id=1, source_target_pairs={{0,8},{8,16},{16,24},{24,32},{32,40},{40,48},{48,56},{56,0},{1,9},... | collective-permute-start | bytes 1013768 | tf_op jit(solution)/shard_map/ppermute | solution.py:51
  42.4 9.9 %collective-permute-start.9 = (bf16[5,1408,24]{1,2,0:T(8,128)(2,1)S(1)}, bf16[5,1408,24]{1,2,0:T(8,128)(2,1)S(1)}, u32[]{:S(2)}, u32[]{:S(2)}) collective-permute-start(bf16[5,1408,24]{1,2,0:T(8,128)(2,1)S(1)} %collective-permute-done.5), channel_id=1, source_target_pairs={{0,56},{8,0},{16,8},{24,16},{32,24},{40,32},{48,40},{56,48},{1,57}... | collective-permute-start | bytes 1013768 | tf_op jit(solution)/shard_map/ppermute | solution.py:49
  45.0 6.3 %collective-permute-start.10 = (bf16[216,256]{1,0:T(8,128)(2,1)S(1)}, bf16[216,256]{1,0:T(8,128)(2,1)S(1)}, u32[]{:S(2)}, u32[]{:S(2)}) collective-permute-start(bf16[216,256]{1,0:T(8,128)(2,1)S(1)} %collective-permute-done.6), channel_id=1, source_target_pairs={{0,56},{8,0},{16,8},{24,16},{32,24},{40,32},{48,40},{56,48},{1,57}... | collective-permute-start | bytes 331784 | tf_op jit(solution)/shard_map/ppermute | solution.py:49
  45.1 7.2 %collective-permute-start.12 = (bf16[216,256]{1,0:T(8,128)(2,1)S(1)}, bf16[216,256]{1,0:T(8,128)(2,1)S(1)}, u32[]{:S(2)}, u32[]{:S(2)}) collective-permute-start(bf16[216,256]{1,0:T(8,128)(2,1)S(1)} %collective-permute-done.8), channel_id=1, source_target_pairs={{0,8},{8,16},{16,24},{24,32},{32,40},{40,48},{48,56},{56,0},{1,9},... | collective-permute-start | bytes 331784 | tf_op jit(solution)/shard_map/ppermute | solution.py:51
  52.3 7.9 %collective-permute-start.13 = (bf16[5,1408,24]{1,2,0:T(8,128)(2,1)S(1)}, bf16[5,1408,24]{1,2,0:T(8,128)(2,1)S(1)}, u32[]{:S(2)}, u32[]{:S(2)}) collective-permute-start(bf16[5,1408,24]{1,2,0:T(8,128)(2,1)S(1)} %collective-permute-done.9), channel_id=1, source_target_pairs={{0,56},{8,0},{16,8},{24,16},{32,24},{40,32},{48,40},{56,48},{1,57}... | collective-permute-start | bytes 1013768 | tf_op jit(solution)/shard_map/ppermute | solution.py:49
  66.0 7.8 %collective-permute-start = (bf16[2,1408]{1,0:T(2,128)(2,1)S(1)}, bf16[2,1408]{1,0:T(2,128)(2,1)S(1)}, u32[]{:S(2)}, u32[]{:S(2)}) collective-permute-start(bf16[2,1408]{1,0:T(2,128)(2,1)S(1)} %get-tuple-element.56), channel_id=1, source_target_pairs={{0,8},{8,16},{16,24},{24,32},{32,40},{40,48},{48,56},{1,9},{9,17},... | collective-permute-start | bytes 16904 | tf_op jit(solution)/shard_map/ppermute | solution.py:139
  68.0 5.7 %collective-permute-start.15 = (bf16[2,1408]{1,0:T(2,128)(2,1)S(1)}, bf16[2,1408]{1,0:T(2,128)(2,1)S(1)}, u32[]{:S(2)}, u32[]{:S(2)}) collective-permute-start(bf16[2,1408]{1,0:T(2,128)(2,1)S(1)} %get-tuple-element.57), channel_id=1, source_target_pairs={{8,0},{16,8},{24,16},{32,24},{40,32},{48,40},{56,48},{9,1},{17,9},... | collective-permute-start | bytes 16904 | tf_op jit(solution)/shard_map/ppermute | solution.py:140
  84.7 16.7 %all-to-all-start = ((bf16[8,96,192]{1,2,0:T(8,128)(2,1)}), bf16[8,96,192]{1,2,0:T(8,128)(2,1)S(1)}, u32[]{:S(2)}, u32[]{:S(2)}) async-start(bf16[8,96,192]{1,2,0:T(8,128)(2,1)} %copy.33), calls=%async_computation | async-start | bytes 786432 | tf_op jit(solution)/shard_map/all_to_all | solution.py:151
  93.7 71.9 %all-gather.8.cloned.1.call-start = ((), (), s32[]{:S(2)}) async-start(), calls=%async_computation.3 | async-start | bytes 3538944 | tf_op jit(solution)/shard_map/all_gather | solution.py:161
  120.2 7.5 %collective-permute-start.16 = (bf16[128,1536]{1,0:T(8,128)(2,1)S(1)}, bf16[128,1536]{1,0:T(8,128)(2,1)S(1)}, u32[]{:S(2)}, u32[]{:S(2)}) collective-permute-start(bf16[128,1536]{1,0:T(8,128)(2,1)S(1)} %reshape.80), channel_id=1, source_target_pairs={{0,7},{1,0},{2,1},{3,2},{4,3},{5,4},{6,5},{7,6},{8,15},{9,8},{10,9... | collective-permute-start | bytes 1179656 | tf_op jit(solution)/shard_map/ppermute | solution.py:49
  120.4 7.3 %collective-permute-start.17 = (bf16[128,1536]{1,0:T(8,128)(2,1)S(1)}, bf16[128,1536]{1,0:T(8,128)(2,1)S(1)}, u32[]{:S(2)}, u32[]{:S(2)}) collective-permute-start(bf16[128,1536]{1,0:T(8,128)(2,1)S(1)} %reshape.80), channel_id=1, source_target_pairs={{0,1},{1,2},{2,3},{3,4},{4,5},{5,6},{6,7},{7,0},{8,9},{9,10},{10,1... | collective-permute-start | bytes 1179656 | tf_op jit(solution)/shard_map/ppermute | solution.py:51
  127.8 7.6 %collective-permute-start.18 = (bf16[128,1536]{1,0:T(8,128)(2,1)S(1)}, bf16[128,1536]{1,0:T(8,128)(2,1)}, u32[]{:S(2)}, u32[]{:S(2)}) collective-permute-start(bf16[128,1536]{1,0:T(8,128)(2,1)S(1)} %collective-permute-done.16), channel_id=1, source_target_pairs={{0,7},{1,0},{2,1},{3,2},{4,3},{5,4},{6,5},{7,6},{8,15},{9,8},{10,9... | collective-permute-start | bytes 1179656 | tf_op jit(solution)/shard_map/ppermute | solution.py:49
  130.0 5.4 %collective-permute-start.19 = (bf16[128,1536]{1,0:T(8,128)(2,1)S(1)}, bf16[128,1536]{1,0:T(8,128)(2,1)}, u32[]{:S(2)}, u32[]{:S(2)}) collective-permute-start(bf16[128,1536]{1,0:T(8,128)(2,1)S(1)} %collective-permute-done.17), channel_id=1, source_target_pairs={{0,1},{1,2},{2,3},{3,4},{4,5},{5,6},{6,7},{7,0},{8,9},{9,10},{10,1... | collective-permute-start | bytes 1179656 | tf_op jit(solution)/shard_map/ppermute | solution.py:51
  135.4 8.0 %collective-permute-start.20 = (bf16[128,1536]{1,0:T(8,128)(2,1)}, bf16[128,1536]{1,0:T(8,128)(2,1)S(1)}, u32[]{:S(2)}, u32[]{:S(2)}) collective-permute-start(bf16[128,1536]{1,0:T(8,128)(2,1)} %collective-permute-done.18), channel_id=1, source_target_pairs={{0,7},{1,0},{2,1},{3,2},{4,3},{5,4},{6,5},{7,6},{8,15},{9,8},{10,9... | collective-permute-start | bytes 1179656 | tf_op jit(solution)/shard_map/ppermute | solution.py:49
  143.5 8.2 %collective-permute-start.22 = (bf16[128,1536]{1,0:T(8,128)(2,1)S(1)}, bf16[128,1536]{1,0:T(8,128)(2,1)S(1)}, u32[]{:S(2)}, u32[]{:S(2)}) collective-permute-start(bf16[128,1536]{1,0:T(8,128)(2,1)S(1)} %collective-permute-done.20), channel_id=1, source_target_pairs={{0,7},{1,0},{2,1},{3,2},{4,3},{5,4},{6,5},{7,6},{8,15},{9,8},{10,9... | collective-permute-start | bytes 1179656 | tf_op jit(solution)/shard_map/ppermute | solution.py:49
  (15 other events, 96.7 us)
Sparse Core Ops, SparseCore 0:
  11.0 39.2 all-gather.3
  61.6 37.5 all-gather.5
  120.4 45.2 all-gather.7
